TPU v7x, 128 devices: a whole 4x4x4 slice. The times are simulated.
128 devices in a mesh: gx: 16 (over z, x), gy: 8 (over y, core).
Axes of the slice: x: 4, y: 4, z: 4, core: 2. Of those that a mesh axis runs over, the one named last changes fastest.
Arguments:
- parent_field: float32 [8, 2048, 4096], P(None, 'gx', 'gy'), may hold values from -6 to 6
- parent_sppt: bfloat16 [2048, 4096], P('gx', 'gy'), may hold values from -0.796875 to 0.796875
- child_storm: float32 [8, 2048, 3072], P(None, 'gx', 'gy'), may hold values from -6 to 6
- child_sppt: bfloat16 [2048, 3072], P('gx', 'gy'), may hold values from -0.796875 to 0.796875
- wind: float32 [2, 8], replicated, may hold values from -0.3 to 0.3
- strip_dest: int32 [16384, 1], replicated, may hold values from 0 to 127; in each aligned block of 128 rows (0 to 127, 128 to 255, ...) at most 2 rows name the same one
- strip_row: int32 [16384], replicated, may hold values from 0 to 511
- strip_target: int32 [16384], replicated, may hold values from 0 to 127
- storm_shift: int32 [2, 4], replicated, may hold values from 0 to 15, as said below
Outputs:
- new_parent: float32 [8, 2048, 4096], P(None, 'gx', 'gy')
- child: float32 [8, 2048, 3072], P(None, 'gx', 'gy')
Inputs may be any that keep to these rules, and one draw needn't show every extreme that they name: `strip_dest`: among the 128 strips of one parent device no owner appears more than 2 times. `storm_shift`: row 0 lies in 0 to 16 - 1 and holds 16 - 1 at least once; row 1 lies in 0 to 8 - 1 and holds 8 - 1 at least once.
All inputs are finite; a program needn't handle non-finite values.
Results may differ from a plain program's by a relative error of at most 0.0003.
Values sent between devices are 32-bit elements; how exact they have to be, the bound alone decides.
No kernel may reach another device: no remote copies, remote signals or barrier semaphores. Data moves between devices by JAX's collectives and lax.ppermute only.
A program may use at most 64 MiB of HBM per device.

v0:
```python
import jax
import jax.numpy as jnp
from jax import lax
from jax.sharding import PartitionSpec as P

SUBSTEPS = 3
STRIP = 128
CAP = 2


KAPPA = 0.1
VERTICAL = 0.1
NUDGE = 0.5


def padded_2(block, sides, width):
    for axis, dim in sides:
        count = lax.axis_size(axis)
        forward = [(i, i + 1) for i in range(count - 1)]
        backward = [(target, source) for source, target in forward]
        low = lax.ppermute(
            lax.slice_in_dim(block, block.shape[dim] - width, None, axis=dim), axis, forward
        )
        high = lax.ppermute(lax.slice_in_dim(block, 0, width, axis=dim), axis, backward)
        block = jnp.concatenate([low, block, high], axis=dim)
    return block


def from_behind(value, axis, steps):
    count = lax.axis_size(axis)
    pairs = [(source, (source + steps) % count) for source in range(count)]
    return lax.ppermute(value, axis, pairs)


def refine_table(strip):
    coarse = jnp.arange(strip).astype(jnp.float32)
    finer = jnp.arange(3 * strip).astype(jnp.float32)
    position = jnp.clip((finer + 0.5) / 3.0 - 0.5, 0.0, strip - 1.0)
    return jnp.maximum(0.0, 1.0 - jnp.abs(position[None, :] - coarse[:, None]))


def tendency(padded, wind_x, wind_y):
    centre = padded[..., 1:-1, 1:-1]
    north = padded[..., 2:, 1:-1]
    south = padded[..., :-2, 1:-1]
    east = padded[..., 1:-1, 2:]
    west = padded[..., 1:-1, :-2]
    laplace = north + south + east + west - 4.0 * centre
    return KAPPA * laplace - wind_x * (0.5 * (north - south)) - wind_y * (0.5 * (east - west))


def vertical(field):
    upper = jnp.concatenate([field[1:], field[-1:]], axis=0)
    lower = jnp.concatenate([field[:1], field[:-1]], axis=0)
    return upper + lower - 2.0 * field


def shards(
    parent_field,
    parent_sppt,
    child_storm,
    child_sppt,
    wind,
    strip_dest,
    strip_row,
    strip_target,
    storm_shift,
):
    devices = lax.axis_size(("gx", "gy"))
    my_index = lax.axis_index(("gx", "gy"))
    wind_x = wind[0][:, None, None]
    wind_y = wind[1][:, None, None]
    padded = padded_2(parent_field, (("gx", 1), ("gy", 2)), 1)
    new_parent = parent_field + (1.0 + parent_sppt.astype(jnp.float32)) * (
        tendency(padded, wind_x, wind_y) + VERTICAL * vertical(parent_field)
    )
    levels, crows, widths = child_storm.shape
    npiece = storm_shift.shape[1]
    band_rows = crows // npiece
    col_count = lax.axis_size("gy")
    child = child_storm
    for bit in range((col_count - 1).bit_length()):
        moved = from_behind(child, "gy", 1 << bit)
        taken = jnp.repeat(storm_shift[1] >> bit & 1, band_rows) == 1
        child = jnp.where(taken[None, :, None], moved, child)
    for bit in range((lax.axis_size("gx") - 1).bit_length()):
        moved = from_behind(child, "gx", 1 << bit)
        taken = jnp.repeat(storm_shift[0] >> bit & 1, band_rows) == 1
        child = jnp.where(taken[None, :, None], moved, child)
    dest_table = strip_dest.reshape(devices, -1)
    row_table = strip_row.reshape(devices, -1)
    target_table = strip_target.reshape(devices, -1)
    slots = dest_table.shape[1]
    my_dest = lax.dynamic_index_in_dim(dest_table, my_index, 0, keepdims=False)
    my_rows = lax.dynamic_index_in_dim(row_table, my_index, 0, keepdims=False)
    same_owner = my_dest[:, None] == my_dest[None, :]
    earlier = jnp.arange(slots)[None, :] < jnp.arange(slots)[:, None]
    rank = jnp.sum((same_owner & earlier).astype(jnp.int32), axis=1)
    slot_index = my_dest * CAP + rank
    send_select = (jnp.arange(devices * CAP)[:, None] == slot_index[None, :]).astype(jnp.float32)
    both_states = jnp.stack([parent_field, new_parent]).reshape(2, levels, -1, STRIP)
    picked = jnp.take(both_states, my_rows, axis=2)
    strip_values = jnp.moveaxis(picked, 2, 0).reshape(slots, -1)
    outgoing_strips = jnp.dot(
        send_select,
        strip_values,
        precision=lax.Precision.HIGHEST,
        preferred_element_type=jnp.float32,
    )
    incoming = lax.all_to_all(
        outgoing_strips, ("gx", "gy"), split_axis=0, concat_axis=0, tiled=True
    )
    mine = dest_table == my_index
    rank_all = jnp.cumsum(mine.astype(jnp.int32), axis=1) - 1
    slot_ids = jnp.arange(CAP)
    hits = mine[:, None, :] & (rank_all[:, None, :] == slot_ids[None, :, None])
    chosen = jnp.sum(jnp.where(hits, target_table[:, None, :], 0), axis=2)
    target_rows = jnp.where(jnp.any(hits, axis=2), chosen, -1).reshape(-1)
    row_select = (jnp.arange(crows)[:, None] == target_rows[None, :]).astype(jnp.float32)
    coarse = jnp.dot(
        row_select, incoming, precision=lax.Precision.HIGHEST, preferred_element_type=jnp.float32
    )
    counts = jnp.sum(row_select, axis=1)
    boundary = jnp.einsum(
        "tald,de->alte",
        coarse.reshape(crows, 2, levels, STRIP),
        refine_table(STRIP),
        precision=lax.Precision.HIGHEST,
    )
    divisor = 1.0 + NUDGE * counts[None, :, None]
    factor = 1.0 + child_sppt.astype(jnp.float32)
    for substep in range(SUBSTEPS):
        padded_child = padded_2(child, (("gx", 1), ("gy", 2)), 1)
        weight = (substep + 1) / 3.0
        target_value = boundary[0] + weight * (boundary[1] - boundary[0])
        child = (
            child + factor * tendency(padded_child, wind_x, wind_y) + NUDGE * target_value
        ) / divisor
    return (new_parent, child)


def solution(mesh):
    placed = (
        P(None, "gx", "gy"),
        P("gx", "gy"),
        P(None, "gx", "gy"),
        P("gx", "gy"),
        P(),
        P(),
        P(),
        P(),
        P(),
    )
    return jax.shard_map(
        shards,
        mesh=mesh,
        in_specs=placed,
        out_specs=(P(None, "gx", "gy"), P(None, "gx", "gy")),
        check_vma=False,
    )
```

profile of v0, /device:TPU:33, one launch (start us, length us, event | category | flops | bytes accessed | tf_op | source)
XLA Modules:
  0.0 368.3 jit_solution(9390122672830269516)
XLA Ops:
  0.6 1.9 collective-permute-start.4
  3.4 16.7 %collective-permute-done.4 = f32[8,128,384]{2,1,0:T(8,128)S(1)} collective-permute-done((f32[8,128,384]{2,1,0:T(8,128)}, f32[8,128,384]{2,1,0:T(8,128)S(1)}, u32[]{:S(2)}, u32[]{:S(2)}) %collective-permute-start.4) | collective-permute-done | bytes 1572896 | tf_op jit(solution)/shard_map/ppermute | solution.py:32
  20.2 1.6 broadcast_select_fusion
  23.3 33.4 %collective-permute-done.5 = f32[8,128,384]{2,1,0:T(8,128)} collective-permute-done((f32[8,128,384]{2,1,0:T(8,128)S(1)}, f32[8,128,384]{2,1,0:T(8,128)}, u32[]{:S(2)}, u32[]{:S(2)}) %collective-permute-start.5) | collective-permute-done | bytes 1572896 | tf_op jit(solution)/shard_map/ppermute | solution.py:32
  56.7 1.6 broadcast_select_fusion.1
  58.4 2.4 collective-permute-start.6
  61.0 31.8 %collective-permute-done.6 = f32[8,128,384]{2,1,0:T(8,128)} collective-permute-done((f32[8,128,384]{2,1,0:T(8,128)S(1)}, f32[8,128,384]{2,1,0:T(8,128)}, u32[]{:S(2)}, u32[]{:S(2)}) %collective-permute-start.6) | collective-permute-done | bytes 1572896 | tf_op jit(solution)/shard_map/ppermute | solution.py:32
  92.8 1.6 broadcast_select_fusion.2
  96.7 4.3 %collective-permute-start = (f32[8,1,512]{2,0,1:T(8,128)S(1)}, f32[8,1,512]{2,0,1:T(8,128)S(1)}, u32[]{:S(2)}, u32[]{:S(2)}) collective-permute-start(f32[8,1,512]{2,0,1:T(8,128)S(1)} %copy.133), channel_id=1, source_target_pairs={{8,0},{16,8},{24,16},{32,24},{40,32},{48,40},{56,48},{64,56},{72,6... | collective-permute-start | bytes 49160 | tf_op jit(solution)/shard_map/ppermute | solution.py:24
  101.0 1.9 collective-permute-start.1
  103.9 24.5 %collective-permute-done.7 = f32[8,128,384]{2,1,0:T(8,128)S(1)} collective-permute-done((f32[8,128,384]{2,1,0:T(8,128)S(1)}, f32[8,128,384]{2,1,0:T(8,128)S(1)}, u32[]{:S(2)}, u32[]{:S(2)}) %collective-permute-start.7) | collective-permute-done | bytes 1572896 | tf_op jit(solution)/shard_map/ppermute | solution.py:32
  128.4 1.4 broadcast_select_fusion.3
  130.4 2.1 copy.109
  133.7 2.3 fusion.34
  136.2 2.0 copy.96
  138.3 2.0 copy.98
  141.1 9.7 %collective-permute-start.3 = (f32[8,130,1]{1,0,2:T(8,128)S(1)}, f32[8,130,1]{1,0,2:T(8,128)S(1)}, u32[]{:S(2)}, u32[]{:S(2)}) collective-permute-start(f32[8,130,1]{1,0,2:T(8,128)S(1)} %get-tuple-element.11), channel_id=1, source_target_pairs={{0,1},{1,2},{2,3},{3,4},{4,5},{5,6},{6,7},{8,9},{9,10},{10,11},{11... | collective-permute-start | bytes 12488 | tf_op jit(solution)/shard_map/ppermute | solution.py:21
  150.8 1.9 collective-permute-start.2
  152.7 10.6 %collective-permute-done.8 = f32[8,128,384]{2,1,0:T(8,128)} collective-permute-done((f32[8,128,384]{2,1,0:T(8,128)}, f32[8,128,384]{2,1,0:T(8,128)}, u32[]{:S(2)}, u32[]{:S(2)}) %collective-permute-start.8) | collective-permute-done | bytes 1572896 | tf_op jit(solution)/shard_map/ppermute | solution.py:32
  163.3 3.2 broadcast_select_fusion.4
  166.6 1.6 collective-permute-start.9
  168.9 2.7 stack.9
  172.0 4.3 %copy.118 = f32[1,8,512,128]{3,1,2,0:T(8,128)} copy(f32[1,8,512,128]{3,2,1,0:T(8,128)} %stack.9) | data formatting | bytes 4194304 | tf_op jit(solution)/shard_map/stack | solution.py:101
  176.3 7.1 %fusion.4 = f32[8,128,512]{1,0,2:T(8,128)} fusion(f32[8,128,512]{1,0,2:T(8,128)S(1)} %copy.109, f32[1,128,512]{1,0,2:T(1,128)S(1)} %copy.105, f32[7,128,512]{1,0,2:T(8,128)} %get-tuple-element.17, f32[7,128,512]{1,0,2:T(8,128)} %get-tuple-element.16, f32[1,128,512]{1,0,2:T(1,128)S(1)} %copy.107, f32[8,1,512]{1,0,2:T(8,128)S(1)} %copy-done, ...), kind=kLoop, calls=%fused_computation.15 | loop fusion | flops 15204352 | bytes 8691904 | tf_op jit(solution)/shard_map/add | solution.py:74
  183.4 1.9 copy.130
  185.3 1.5 stack.10
  187.3 3.0 copy.119
  190.3 2.2 pad_maximum_fusion
  192.5 2.9 gather_fusion
  196.8 3.0 copy.120
  199.8 16.1 %all-to-all-start = ((f32[128,2,2048]{2,1,0:T(2,128)}), f32[128,2,2048]{2,1,0:T(2,128)S(1)}, u32[]{:S(2)}, u32[]{:S(2)}) async-start(f32[128,2,2048]{2,1,0:T(2,128)} %copy.120), calls=%async_computation | async-start | bytes 4194304 | tf_op jit(solution)/shard_map/all_to_all | solution.py:110
  216.1 3.3 broadcast_select_fusion.5
  219.3 2.3 collective-permute-start.10
  222.9 22.1 %all-to-all-done = f32[128,2,2048]{2,1,0:T(2,128)S(1)} async-done(((f32[128,2,2048]{2,1,0:T(2,128)}), f32[128,2,2048]{2,1,0:T(2,128)S(1)}, u32[]{:S(2)}, u32[]{:S(2)}) %all-to-all-start) | async-done | bytes 2097184 | tf_op jit(solution)/shard_map/all_to_all | solution.py:110
  245.0 2.4 all_to_all.7
  247.4 1.9 copy.121
  249.3 26.2 %collective-permute-done.10 = f32[8,128,384]{2,1,0:T(8,128)} collective-permute-done((f32[8,128,384]{2,1,0:T(8,128)}, f32[8,128,384]{2,1,0:T(8,128)}, u32[]{:S(2)}, u32[]{:S(2)}) %collective-permute-start.10) | collective-permute-done | bytes 1572896 | tf_op jit(solution)/shard_map/ppermute | solution.py:32
  275.5 2.1 broadcast_select_fusion.6
  277.7 4.7 %collective-permute-start.11 = (f32[8,1,384]{2,1,0:T(1,128)S(1)}, f32[8,1,384]{2,1,0:T(1,128)S(1)}, u32[]{:S(2)}, u32[]{:S(2)}) collective-permute-start(f32[8,1,384]{2,1,0:T(1,128)S(1)} %get-tuple-element.29), channel_id=1, source_target_pairs={{8,0},{16,8},{24,16},{32,24},{40,32},{48,40},{56,48},{64,56},{72,6... | collective-permute-start | bytes 36872 | tf_op jit(solution)/shard_map/ppermute | solution.py:24
  282.4 1.9 collective-permute-start.12
  284.3 2.3 fusion.12
  286.6 2.4 collective-permute-done.12
  289.5 4.7 %collective-permute-start.14 = (f32[8,130,1]{1,0,2:T(8,128)S(1)}, f32[8,130,1]{1,0,2:T(8,128)S(1)}, u32[]{:S(2)}, u32[]{:S(2)}) collective-permute-start(f32[8,130,1]{1,0,2:T(8,128)S(1)} %copy.112), channel_id=1, source_target_pairs={{0,1},{1,2},{2,3},{3,4},{4,5},{5,6},{6,7},{8,9},{9,10},{10,11},{11... | collective-permute-start | bytes 12488 | tf_op jit(solution)/shard_map/ppermute | solution.py:21
  294.5 1.9 collective-permute-start.13
  296.4 3.9 %convolution_bitcast_fusion = f32[2,8,128,384]{3,2,1,0:T(8,128)S(1)} fusion(f32[128,2,8,128]{3,0,2,1:T(8,128)} %fusion.12, f32[128]{0:T(128)S(1)} %iota_convert_fusion, f32[384]{0:T(512)S(1)} %add_clamp_fusion), kind=kOutput, calls=%fused_computation.16 | convolution fusion | flops 1208156160 | bytes 4196352 | tf_op jit(solution)/shard_map/tald,de->alte/dot_general | solution.py:124
  302.5 6.5 %add_divide_fusion.2 = f32[8,128,384]{2,1,0:T(8,128)S(1)} fusion(f32[8,128,384]{2,1,0:T(8,128)} %copy-done.2, f32[8,1,384]{2,1,0:T(1,128)S(1)} %collective-permute-done.11, f32[8,1,384]{2,1,0:T(1,128)S(1)} %collective-permute-done.12, f32[8,130,1]{2,1,0:T(8,128)} %copy.113, f32[8,130,1]{2,1,0:T(8,128)} %copy.111, ...), kind=kLoop, calls=%fused_computation.46 | loop fusion | flops 11010048 | bytes 6521536 | tf_op jit(solution)/shard_map/div | solution.py:136
  309.0 2.3 collective-permute-start.15
  311.3 3.0 collective-permute-start.16
  314.3 3.5 collective-permute-done.16
  319.1 1.4 copy.124
  320.4 5.1 %collective-permute-start.18 = (f32[8,130,1]{1,0,2:T(8,128)S(1)}, f32[8,130,1]{1,0,2:T(8,128)S(1)}, u32[]{:S(2)}, u32[]{:S(2)}) collective-permute-start(f32[8,130,1]{1,0,2:T(8,128)S(1)} %copy.124), channel_id=1, source_target_pairs={{0,1},{1,2},{2,3},{3,4},{4,5},{5,6},{6,7},{8,9},{9,10},{10,11},{11... | collective-permute-start | bytes 12488 | tf_op jit(solution)/shard_map/ppermute | solution.py:21
  325.5 1.4 copy.122
  326.9 1.9 collective-permute-start.17
  329.9 2.0 collective-permute-done.17
  332.9 6.5 %add_divide_fusion.1 = f32[8,128,384]{2,1,0:T(8,128)S(1)} fusion(f32[8,128,384]{2,1,0:T(8,128)} %copy-done.4, f32[8,1,384]{2,1,0:T(1,128)S(1)} %collective-permute-done.15, f32[8,1,384]{2,1,0:T(1,128)S(1)} %collective-permute-done.16, f32[8,130,1]{2,1,0:T(8,128)} %copy.125, f32[8,130,1]{2,1,0:T(8,128)} %copy.123, ...), kind=kLoop, calls=%fused_computation.45 | loop fusion | flops 11010048 | bytes 6521536 | tf_op jit(solution)/shard_map/div | solution.py:136
  339.5 1.9 collective-permute-start.19
  341.4 3.4 collective-permute-start.20
  344.8 3.2 collective-permute-done.20
  349.1 1.4 copy.128
  350.5 3.1 collective-permute-start.22
  353.6 1.4 copy.126
  355.0 1.9 collective-permute-start.21
  358.0 2.0 collective-permute-done.21
  361.1 7.2 %add_divide_fusion = f32[8,128,384]{2,1,0:T(8,128)} fusion(f32[8,128,384]{2,1,0:T(8,128)} %copy-done.3, f32[8,1,384]{2,1,0:T(1,128)S(1)} %collective-permute-done.19, f32[8,1,384]{2,1,0:T(1,128)S(1)} %collective-permute-done.20, f32[8,130,1]{2,1,0:T(8,128)} %copy.129, f32[8,130,1]{2,1,0:T(8,128)} %copy.127, ...), kind=kLoop, calls=%fused_computation.44 | loop fusion | flops 10616832 | bytes 6521536 | tf_op jit(solution)/shard_map/div | solution.py:136
  (103 shorter events, 22.7 us)
Async XLA Ops:
  0.6 19.5 %collective-permute-start.4 = (f32[8,128,384]{2,1,0:T(8,128)}, f32[8,128,384]{2,1,0:T(8,128)S(1)}, u32[]{:S(2)}, u32[]{:S(2)}) collective-permute-start(f32[8,128,384]{2,1,0:T(8,128)} %param.11), channel_id=1, source_target_pairs={{0,1},{1,2},{2,3},{3,4},{4,5},{5,6},{6,7},{7,0},{8,9},{9,10},{10,1... | collective-permute-start | bytes 4718600 | tf_op jit(solution)/shard_map/ppermute | solution.py:32
  21.8 34.9 %collective-permute-start.5 = (f32[8,128,384]{2,1,0:T(8,128)S(1)}, f32[8,128,384]{2,1,0:T(8,128)}, u32[]{:S(2)}, u32[]{:S(2)}) collective-permute-start(f32[8,128,384]{2,1,0:T(8,128)S(1)} %broadcast_select_fusion), channel_id=1, source_target_pairs={{0,2},{1,3},{2,4},{3,5},{4,6},{5,7},{6,0},{7,1},{8,10},{9,11},{10,... | collective-permute-start | bytes 4718600 | tf_op jit(solution)/shard_map/ppermute | solution.py:32
  58.4 34.4 %collective-permute-start.6 = (f32[8,128,384]{2,1,0:T(8,128)S(1)}, f32[8,128,384]{2,1,0:T(8,128)}, u32[]{:S(2)}, u32[]{:S(2)}) collective-permute-start(f32[8,128,384]{2,1,0:T(8,128)S(1)} %broadcast_select_fusion.1), channel_id=1, source_target_pairs={{0,4},{1,5},{2,6},{3,7},{4,0},{5,1},{6,2},{7,3},{8,12},{9,13},{10,... | collective-permute-start | bytes 4718600 | tf_op jit(solution)/shard_map/ppermute | solution.py:32
  61.0 42.8 %copy-start.9 = (s32[16384,1]{0,1:T(1,128)S(1)}, s32[16384,1]{0,1:T(1,128)}, u32[]{:S(2)}) copy-start(s32[16384,1]{0,1:T(1,128)} %param.14) | copy-start | bytes 196612
  94.4 34.0 %collective-permute-start.7 = (f32[8,128,384]{2,1,0:T(8,128)S(1)}, f32[8,128,384]{2,1,0:T(8,128)S(1)}, u32[]{:S(2)}, u32[]{:S(2)}) collective-permute-start(f32[8,128,384]{2,1,0:T(8,128)S(1)} %broadcast_select_fusion.2), channel_id=1, source_target_pairs={{0,8},{8,16},{16,24},{24,32},{32,40},{40,48},{48,56},{56,64},{64,7... | collective-permute-start | bytes 4718600 | tf_op jit(solution)/shard_map/ppermute | solution.py:32
  96.7 39.5 %collective-permute-start = (f32[8,1,512]{2,0,1:T(8,128)S(1)}, f32[8,1,512]{2,0,1:T(8,128)S(1)}, u32[]{:S(2)}, u32[]{:S(2)}) collective-permute-start(f32[8,1,512]{2,0,1:T(8,128)S(1)} %copy.133), channel_id=1, source_target_pairs={{8,0},{16,8},{24,16},{32,24},{40,32},{48,40},{56,48},{64,56},{72,6... | collective-permute-start | bytes 49160 | tf_op jit(solution)/shard_map/ppermute | solution.py:24
  101.0 37.3 %collective-permute-start.1 = (f32[8,1,512]{2,0,1:T(8,128)S(1)}, f32[8,1,512]{2,0,1:T(8,128)S(1)}, u32[]{:S(2)}, u32[]{:S(2)}) collective-permute-start(f32[8,1,512]{2,0,1:T(8,128)S(1)} %copy.134), channel_id=1, source_target_pairs={{0,8},{8,16},{16,24},{24,32},{32,40},{40,48},{48,56},{56,64},{64,7... | collective-permute-start | bytes 49160 | tf_op jit(solution)/shard_map/ppermute | solution.py:21
  129.8 33.5 %collective-permute-start.8 = (f32[8,128,384]{2,1,0:T(8,128)}, f32[8,128,384]{2,1,0:T(8,128)}, u32[]{:S(2)}, u32[]{:S(2)}) collective-permute-start(f32[8,128,384]{2,1,0:T(8,128)} %broadcast_select_fusion.3), channel_id=1, source_target_pairs={{0,16},{8,24},{16,32},{24,40},{32,48},{40,56},{48,64},{56,72},{64,... | collective-permute-start | bytes 4718600 | tf_op jit(solution)/shard_map/ppermute | solution.py:32
  130.4 2.2 copy-start.11
  130.4 2.2 copy-start.7
  141.1 35.2 %collective-permute-start.3 = (f32[8,130,1]{1,0,2:T(8,128)S(1)}, f32[8,130,1]{1,0,2:T(8,128)S(1)}, u32[]{:S(2)}, u32[]{:S(2)}) collective-permute-start(f32[8,130,1]{1,0,2:T(8,128)S(1)} %get-tuple-element.11), channel_id=1, source_target_pairs={{0,1},{1,2},{2,3},{3,4},{4,5},{5,6},{6,7},{8,9},{9,10},{10,11},{11... | collective-permute-start | bytes 12488 | tf_op jit(solution)/shard_map/ppermute | solution.py:21
  150.8 25.5 %collective-permute-start.2 = (f32[8,130,1]{1,0,2:T(8,128)S(1)}, f32[8,130,1]{1,0,2:T(8,128)S(1)}, u32[]{:S(2)}, u32[]{:S(2)}) collective-permute-start(f32[8,130,1]{1,0,2:T(8,128)S(1)} %get-tuple-element.10), channel_id=1, source_target_pairs={{1,0},{2,1},{3,2},{4,3},{5,4},{6,5},{7,6},{9,8},{10,9},{11,10},{12... | collective-permute-start | bytes 12488 | tf_op jit(solution)/shard_map/ppermute | solution.py:24
  166.6 49.5 %collective-permute-start.9 = (f32[8,128,384]{2,1,0:T(8,128)}, f32[8,128,384]{2,1,0:T(8,128)}, u32[]{:S(2)}, u32[]{:S(2)}) collective-permute-start(f32[8,128,384]{2,1,0:T(8,128)} %broadcast_select_fusion.4), channel_id=1, source_target_pairs={{0,32},{8,40},{16,48},{24,56},{32,64},{40,72},{48,80},{56,88},{64,... | collective-permute-start | bytes 4718600 | tf_op jit(solution)/shard_map/ppermute | solution.py:32
  172.0 4.3 %copy-start = (f32[8,1,512]{1,0,2:T(8,128)S(1)}, f32[8,1,512]{1,0,2:T(8,128)}, u32[]{:S(2)}) copy-start(f32[8,1,512]{1,0,2:T(8,128)} %copy.96) | copy-start | bytes 49156
  172.0 4.3 %copy-start.1 = (f32[8,1,512]{1,0,2:T(8,128)S(1)}, f32[8,1,512]{1,0,2:T(8,128)}, u32[]{:S(2)}) copy-start(f32[8,1,512]{1,0,2:T(8,128)} %copy.98) | copy-start | bytes 49156
  185.3 2.0 copy-start.5
  187.3 3.0 copy-start.6
  199.8 45.2 %all-to-all-start = ((f32[128,2,2048]{2,1,0:T(2,128)}), f32[128,2,2048]{2,1,0:T(2,128)S(1)}, u32[]{:S(2)}, u32[]{:S(2)}) async-start(f32[128,2,2048]{2,1,0:T(2,128)} %copy.120), calls=%async_computation | async-start | bytes 4194304 | tf_op jit(solution)/shard_map/all_to_all | solution.py:110
  216.0 6.3 %copy-start.10 = (s32[16384]{0:T(1024)S(1)}, s32[16384]{0:T(1024)}, u32[]{:S(2)}) copy-start(s32[16384]{0:T(1024)} %param.16) | copy-start | bytes 196612
  216.0 6.8 %copy-start.8 = (bf16[128,384]{1,0:T(8,128)(2,1)S(1)}, bf16[128,384]{1,0:T(8,128)(2,1)}, u32[]{:S(2)}) copy-start(bf16[128,384]{1,0:T(8,128)(2,1)} %param.12) | copy-start | bytes 294916
  219.3 56.2 %collective-permute-start.10 = (f32[8,128,384]{2,1,0:T(8,128)}, f32[8,128,384]{2,1,0:T(8,128)}, u32[]{:S(2)}, u32[]{:S(2)}) collective-permute-start(f32[8,128,384]{2,1,0:T(8,128)} %broadcast_select_fusion.5), channel_id=1, source_target_pairs={{0,64},{8,72},{16,80},{24,88},{32,96},{40,104},{48,112},{56,120},{... | collective-permute-start | bytes 4718600 | tf_op jit(solution)/shard_map/ppermute | solution.py:32
  277.7 11.3 %copy-start.2 = (f32[8,128,384]{2,1,0:T(8,128)}, f32[8,128,384]{2,1,0:T(8,128)S(1)}, u32[]{:S(2)}) copy-start(f32[8,128,384]{2,1,0:T(8,128)S(1)} %broadcast_select_fusion.6) | copy-start | bytes 4718596
  277.7 8.9 %collective-permute-start.11 = (f32[8,1,384]{2,1,0:T(1,128)S(1)}, f32[8,1,384]{2,1,0:T(1,128)S(1)}, u32[]{:S(2)}, u32[]{:S(2)}) collective-permute-start(f32[8,1,384]{2,1,0:T(1,128)S(1)} %get-tuple-element.29), channel_id=1, source_target_pairs={{8,0},{16,8},{24,16},{32,24},{40,32},{48,40},{56,48},{64,56},{72,6... | collective-permute-start | bytes 36872 | tf_op jit(solution)/shard_map/ppermute | solution.py:24
  282.4 6.5 %collective-permute-start.12 = (f32[8,1,384]{2,1,0:T(1,128)S(1)}, f32[8,1,384]{2,1,0:T(1,128)S(1)}, u32[]{:S(2)}, u32[]{:S(2)}) collective-permute-start(f32[8,1,384]{2,1,0:T(1,128)S(1)} %get-tuple-element.28), channel_id=1, source_target_pairs={{0,8},{8,16},{16,24},{24,32},{32,40},{40,48},{48,56},{56,64},{64,7... | collective-permute-start | bytes 36872 | tf_op jit(solution)/shard_map/ppermute | solution.py:21
  289.5 10.9 %collective-permute-start.14 = (f32[8,130,1]{1,0,2:T(8,128)S(1)}, f32[8,130,1]{1,0,2:T(8,128)S(1)}, u32[]{:S(2)}, u32[]{:S(2)}) collective-permute-start(f32[8,130,1]{1,0,2:T(8,128)S(1)} %copy.112), channel_id=1, source_target_pairs={{0,1},{1,2},{2,3},{3,4},{4,5},{5,6},{6,7},{8,9},{9,10},{10,11},{11... | collective-permute-start | bytes 12488 | tf_op jit(solution)/shard_map/ppermute | solution.py:21
  294.5 6.9 %collective-permute-start.13 = (f32[8,130,1]{1,0,2:T(8,128)S(1)}, f32[8,130,1]{1,0,2:T(8,128)S(1)}, u32[]{:S(2)}, u32[]{:S(2)}) collective-permute-start(f32[8,130,1]{1,0,2:T(8,128)S(1)} %copy.110), channel_id=1, source_target_pairs={{1,0},{2,1},{3,2},{4,3},{5,4},{6,5},{7,6},{9,8},{10,9},{11,10},{12... | collective-permute-start | bytes 12488 | tf_op jit(solution)/shard_map/ppermute | solution.py:24
  309.0 8.9 %copy-start.4 = (f32[8,128,384]{2,1,0:T(8,128)}, f32[8,128,384]{2,1,0:T(8,128)S(1)}, u32[]{:S(2)}) copy-start(f32[8,128,384]{2,1,0:T(8,128)S(1)} %add_divide_fusion.2) | copy-start | bytes 4718596
  309.0 5.3 %collective-permute-start.15 = (f32[8,1,384]{2,1,0:T(1,128)S(1)}, f32[8,1,384]{2,1,0:T(1,128)S(1)}, u32[]{:S(2)}, u32[]{:S(2)}) collective-permute-start(f32[8,1,384]{2,1,0:T(1,128)S(1)} %get-tuple-element.27), channel_id=1, source_target_pairs={{8,0},{16,8},{24,16},{32,24},{40,32},{48,40},{56,48},{64,56},{72,6... | collective-permute-start | bytes 36872 | tf_op jit(solution)/shard_map/ppermute | solution.py:24
  311.3 6.5 %collective-permute-start.16 = (f32[8,1,384]{2,1,0:T(1,128)S(1)}, f32[8,1,384]{2,1,0:T(1,128)S(1)}, u32[]{:S(2)}, u32[]{:S(2)}) collective-permute-start(f32[8,1,384]{2,1,0:T(1,128)S(1)} %get-tuple-element.26), channel_id=1, source_target_pairs={{0,8},{8,16},{16,24},{24,32},{32,40},{40,48},{48,56},{56,64},{64,7... | collective-permute-start | bytes 36872 | tf_op jit(solution)/shard_map/ppermute | solution.py:21
  320.4 8.4 %collective-permute-start.18 = (f32[8,130,1]{1,0,2:T(8,128)S(1)}, f32[8,130,1]{1,0,2:T(8,128)S(1)}, u32[]{:S(2)}, u32[]{:S(2)}) collective-permute-start(f32[8,130,1]{1,0,2:T(8,128)S(1)} %copy.124), channel_id=1, source_target_pairs={{0,1},{1,2},{2,3},{3,4},{4,5},{5,6},{6,7},{8,9},{9,10},{10,11},{11... | collective-permute-start | bytes 12488 | tf_op jit(solution)/shard_map/ppermute | solution.py:21
  326.9 5.0 %collective-permute-start.17 = (f32[8,130,1]{1,0,2:T(8,128)S(1)}, f32[8,130,1]{1,0,2:T(8,128)S(1)}, u32[]{:S(2)}, u32[]{:S(2)}) collective-permute-start(f32[8,130,1]{1,0,2:T(8,128)S(1)} %copy.122), channel_id=1, source_target_pairs={{1,0},{2,1},{3,2},{4,3},{5,4},{6,5},{7,6},{9,8},{10,9},{11,10},{12... | collective-permute-start | bytes 12488 | tf_op jit(solution)/shard_map/ppermute | solution.py:24
  339.4 8.5 %copy-start.3 = (f32[8,128,384]{2,1,0:T(8,128)}, f32[8,128,384]{2,1,0:T(8,128)S(1)}, u32[]{:S(2)}) copy-start(f32[8,128,384]{2,1,0:T(8,128)S(1)} %add_divide_fusion.1) | copy-start | bytes 4718596
  339.5 5.3 %collective-permute-start.19 = (f32[8,1,384]{2,1,0:T(1,128)S(1)}, f32[8,1,384]{2,1,0:T(1,128)S(1)}, u32[]{:S(2)}, u32[]{:S(2)}) collective-permute-start(f32[8,1,384]{2,1,0:T(1,128)S(1)} %get-tuple-element.25), channel_id=1, source_target_pairs={{8,0},{16,8},{24,16},{32,24},{40,32},{48,40},{56,48},{64,56},{72,6... | collective-permute-start | bytes 36872 | tf_op jit(solution)/shard_map/ppermute | solution.py:24
  341.4 6.5 %collective-permute-start.20 = (f32[8,1,384]{2,1,0:T(1,128)S(1)}, f32[8,1,384]{2,1,0:T(1,128)S(1)}, u32[]{:S(2)}, u32[]{:S(2)}) collective-permute-start(f32[8,1,384]{2,1,0:T(1,128)S(1)} %get-tuple-element.24), channel_id=1, source_target_pairs={{0,8},{8,16},{16,24},{24,32},{32,40},{40,48},{48,56},{56,64},{64,7... | collective-permute-start | bytes 36872 | tf_op jit(solution)/shard_map/ppermute | solution.py:21
  350.5 6.4 %collective-permute-start.22 = (f32[8,130,1]{1,0,2:T(8,128)S(1)}, f32[8,130,1]{1,0,2:T(8,128)S(1)}, u32[]{:S(2)}, u32[]{:S(2)}) collective-permute-start(f32[8,130,1]{1,0,2:T(8,128)S(1)} %copy.128), channel_id=1, source_target_pairs={{0,1},{1,2},{2,3},{3,4},{4,5},{5,6},{6,7},{8,9},{9,10},{10,11},{11... | collective-permute-start | bytes 12488 | tf_op jit(solution)/shard_map/ppermute | solution.py:21
  355.0 5.0 %collective-permute-start.21 = (f32[8,130,1]{1,0,2:T(8,128)S(1)}, f32[8,130,1]{1,0,2:T(8,128)S(1)}, u32[]{:S(2)}, u32[]{:S(2)}) collective-permute-start(f32[8,130,1]{1,0,2:T(8,128)S(1)} %copy.126), channel_id=1, source_target_pairs={{1,0},{2,1},{3,2},{4,3},{5,4},{6,5},{7,6},{9,8},{10,9},{11,10},{12... | collective-permute-start | bytes 12488 | tf_op jit(solution)/shard_map/ppermute | solution.py:24
where the time goes:
time: 370 us; the launch traced here: 368 us
  waiting for transfers between devices  178 us (48%)
  starting transfers between devices  81.2 us (22%)
  other arithmetic  51 us (14%)
  local copies, waits for them, and re-layouts  49.4 us (13%)
  matrix products  7.21 us (2%)
    ppermute x7, waiting for transfers between devices, from_behind(): return lax.ppermute(value, axis, pairs)  143 us
    ppermute x8, starting transfers between devices, padded_2(): lax.ppermute(lax.slice_in_dim(block, block.shape[dim] - width, None, axis...  32.8 us
    all_to_all x1, waiting for transfers between devices, shards(): lax.all_to_all(outgoing_strips, ('gx', 'gy'), split_axis=0, concat_axis=0...  22.1 us
    ppermute x8, starting transfers between devices, padded_2(): lax.ppermute(lax.slice_in_dim(block, 0, width, axis=dim), axis, backward)  20.8 us
    div x3, other arithmetic, shards(): (child + factor * tendency(padded_child, wind_x, wind_y) + NUDGE * target...  20.2 us
    all_to_all x1, starting transfers between devices, shards(): lax.all_to_all(outgoing_strips, ('gx', 'gy'), split_axis=0, concat_axis=0...  16.1 us
    select_n x7, other arithmetic, shards(): child = jnp.where(taken[None, :, None], moved, child)  14.9 us
    ppermute x7, starting transfers between devices, from_behind(): return lax.ppermute(value, axis, pairs)  11.5 us
  transfers between devices with their start and end apart: 24, of which 12 were waited for; matrix products, arithmetic and copies ran while one was open for 19% of the time, Pallas kernels for 0%

commit v1 on v0

--- a/solution.py
+++ b/solution.py
@@ -30,6 +30,28 @@
     count = lax.axis_size(axis)
     pairs = [(source, (source + steps) % count) for source in range(count)]
     return lax.ppermute(value, axis, pairs)
+
+
+def storm_pieces(child, npiece, devices):
+    levels, crows, widths = child.shape
+    band_rows = crows // npiece
+    per_level = devices // levels
+    pieces = child.reshape(levels, npiece, per_level, band_rows // per_level, widths)
+    return jnp.transpose(pieces, (0, 2, 1, 3, 4)).reshape(devices, npiece, -1)
+
+
+def storm_unpieces(pieces, levels, crows, widths):
+    devices, npiece = pieces.shape[:2]
+    per_level = devices // levels
+    child = pieces.reshape(levels, per_level, npiece, crows // npiece // per_level, widths)
+    return jnp.transpose(child, (0, 2, 1, 3, 4)).reshape(levels, crows, widths)
+
+
+def storm_sources(storm_shift, nx, ny):
+    dest = jnp.arange(nx * ny)
+    src_x = (dest[:, None] // ny - storm_shift[0][None, :]) % nx
+    src_y = (dest[:, None] % ny - storm_shift[1][None, :]) % ny
+    return src_x * ny + src_y
 
 
 def refine_table(strip):
@@ -78,15 +100,12 @@
     npiece = storm_shift.shape[1]
     band_rows = crows // npiece
     col_count = lax.axis_size("gy")
-    child = child_storm
-    for bit in range((col_count - 1).bit_length()):
-        moved = from_behind(child, "gy", 1 << bit)
-        taken = jnp.repeat(storm_shift[1] >> bit & 1, band_rows) == 1
-        child = jnp.where(taken[None, :, None], moved, child)
-    for bit in range((lax.axis_size("gx") - 1).bit_length()):
-        moved = from_behind(child, "gx", 1 << bit)
-        taken = jnp.repeat(storm_shift[0] >> bit & 1, band_rows) == 1
-        child = jnp.where(taken[None, :, None], moved, child)
+    nx, ny = lax.axis_size("gx"), lax.axis_size("gy")
+    gathered = lax.all_to_all(
+        storm_pieces(child_storm, npiece, devices), ("gx", "gy"), 0, 0, tiled=True
+    )
+    sources = storm_sources(storm_shift, nx, ny)
+    storm_out = jnp.take_along_axis(gathered, sources[:, :, None], axis=0)
     dest_table = strip_dest.reshape(devices, -1)
     row_table = strip_row.reshape(devices, -1)
     target_table = strip_target.reshape(devices, -1)
@@ -107,8 +126,15 @@
         precision=lax.Precision.HIGHEST,
         preferred_element_type=jnp.float32,
     )
-    incoming = lax.all_to_all(
-        outgoing_strips, ("gx", "gy"), split_axis=0, concat_axis=0, tiled=True
+    strip_width = outgoing_strips.shape[1]
+    outgoing = jnp.concatenate(
+        [outgoing_strips.reshape(devices, -1), storm_out.reshape(devices, -1)], axis=1
+    )
+    arrived = lax.all_to_all(outgoing, ("gx", "gy"), split_axis=0, concat_axis=0, tiled=True)
+    strip_part = CAP * strip_width
+    incoming = arrived[:, :strip_part].reshape(devices * CAP, strip_width)
+    child = storm_unpieces(
+        arrived[:, strip_part:].reshape(devices, npiece, -1), levels, crows, widths
     )
     mine = dest_table == my_index
     rank_all = jnp.cumsum(mine.astype(jnp.int32), axis=1) - 1

time: 370 us -> 261 us (0.71)
  waiting for transfers between devices: 178 us -> 52 us
  local copies, waits for them, and re-layouts: 49.4 us -> 80.8 us
  starting transfers between devices: 81.2 us -> 70.6 us
  other arithmetic: 51 us -> 44.2 us
    ppermute x7 -> x0, waiting for transfers between devices: 143 us -> none  [from_behind(): return lax.ppermute(value, axis, pairs)]
    all_to_all x1 -> x2, waiting for transfers between devices: 22.1 us -> 44.1 us  [the longest x1 44.1 us: shards(): lax.all_to_all(outgoing, ('gx', 'gy'), split_axis=0, concat_axis=0, tiled...]
    reshape x1 -> x7, local copies, waits for them, and re-layouts: 0.16 us -> 16.3 us  [the longest x2 5.64 us: shards(): incoming = arrived[:, :strip_part].reshape(devices * CAP, strip_width)]
    select_n x7 -> x2, other arithmetic: 14.9 us -> 0.43 us  [the longest x1 0.42 us: shards(): storm_out = jnp.take_along_axis(gathered, sources[:, :, None], axis=0)]
    ppermute x8, starting transfers between devices: 32.8 us -> 20 us  [padded_2(): lax.ppermute(lax.slice_in_dim(block, block.shape[dim] - width, None, axis...]
    ppermute x7 -> x0, starting transfers between devices: 11.5 us -> none  [from_behind(): return lax.ppermute(value, axis, pairs)]
    ppermute x8, starting transfers between devices: 20.8 us -> 28.5 us  [padded_2(): lax.ppermute(lax.slice_in_dim(block, 0, width, axis=dim), axis, backward)]
    add x1, other arithmetic: 7.1 us -> 14.1 us  [shards(): parent_field + (1.0 + parent_sppt.astype(jnp.float32)) * (tendency(padded...]
  transfers between devices with their start and end apart: 24 -> 18, of which waited for: 12 -> 3; matrix products, arithmetic and copies ran while one was open for 19% -> 33% of each run, Pallas kernels for 0% -> 0%
where the time goes in v1:
time: 261 us; the launch traced here: 259 us
  local copies, waits for them, and re-layouts  80.8 us (31%)
  starting transfers between devices  70.6 us (27%)
  waiting for transfers between devices  52 us (20%)
  other arithmetic  44.2 us (17%)
  matrix products  10.2 us (4%)
    all_to_all x1, waiting for transfers between devices, shards(): lax.all_to_all(outgoing, ('gx', 'gy'), split_axis=0, concat_axis=0, tiled...  44.1 us
    ppermute x8, starting transfers between devices, padded_2(): lax.ppermute(lax.slice_in_dim(block, 0, width, axis=dim), axis, backward)  28.5 us
    div x3, other arithmetic, shards(): (child + factor * tendency(padded_child, wind_x, wind_y) + NUDGE * target...  20.1 us
    ppermute x8, starting transfers between devices, padded_2(): lax.ppermute(lax.slice_in_dim(block, block.shape[dim] - width, None, axis...  20 us
    add x1, other arithmetic, shards(): parent_field + (1.0 + parent_sppt.astype(jnp.float32)) * (tendency(padded...  14.1 us
    another operation x4, local copies, waits for them, and re-layouts, shards(): jnp.stack([parent_field, new_parent]).reshape(2, levels, -1, STRIP)  12.4 us
    all_to_all x1, starting transfers between devices, shards(): lax.all_to_all(storm_pieces(child_storm, npiece, devices), ('gx', 'gy'),...  12.2 us
    unnamed x28, local copies, waits for them, and re-layouts  10.1 us
  transfers between devices with their start and end apart: 18, of which 3 were waited for; matrix products, arithmetic and copies ran while one was open for 33% of the time, Pallas kernels for 0%

profile of v1, /device:TPU:33, one launch (start us, length us, event | category | flops | bytes accessed | tf_op | source)
XLA Modules:
  0.0 259.1 jit_solution(12640938532327635423)
XLA Ops:
  1.6 3.9 %collective-permute-start = (f32[8,1,512]{2,0,1:T(8,128)S(1)}, f32[8,1,512]{2,0,1:T(8,128)S(1)}, u32[]{:S(2)}, u32[]{:S(2)}) collective-permute-start(f32[8,1,512]{2,0,1:T(8,128)S(1)} %copy.186), channel_id=1, source_target_pairs={{8,0},{16,8},{24,16},{32,24},{40,32},{48,40},{56,48},{64,56},{72,6... | collective-permute-start | bytes 49160 | tf_op jit(solution)/shard_map/ppermute | solution.py:24
  5.6 1.9 collective-permute-start.1
  7.5 2.2 reshape.414
  10.3 2.7 %reshape.415 = f32[128,4,768]{2,1,0:T(4,128)} reshape(f32[8,16,4,2,384]{4,3,2,1,0:T(2,128)S(1)} %bitcast.88) | data formatting | bytes 3145728 | tf_op jit(solution)/shard_map/reshape | solution.py:40
  13.0 12.2 %all-to-all-start = ((f32[128,4,768]{2,1,0:T(4,128)}), f32[128,4,768]{2,1,0:T(4,128)S(1)}, u32[]{:S(2)}, u32[]{:S(2)}) async-start(f32[128,4,768]{2,1,0:T(4,128)} %reshape.415), calls=%async_computation | async-start | bytes 3145728 | tf_op jit(solution)/shard_map/all_to_all | solution.py:104
  25.2 2.9 %copy.158 = f32[8,128,512]{1,0,2:T(8,128)} copy(f32[8,128,512]{2,1,0:T(8,128)} %param.9) | data formatting | bytes 4194304 | tf_op args[0]
  29.5 4.5 %fusion.43 = (f32[7,128,512]{1,0,2:T(8,128)}, f32[7,128,512]{1,0,2:T(8,128)}) fusion(f32[8,128,512]{1,0,2:T(8,128)} %copy.158), kind=kLoop, calls=%fused_computation.156 | loop fusion | bytes 7340032 | tf_op jit(solution)/shard_map/slice | solution.py:76
  35.0 2.1 copy.145
  37.1 2.0 copy.147
  39.9 2.3 collective-permute-start.2
  42.2 3.4 %collective-permute-start.3 = (f32[8,130,1]{1,0,2:T(8,128)S(1)}, f32[8,130,1]{1,0,2:T(8,128)S(1)}, u32[]{:S(2)}, u32[]{:S(2)}) collective-permute-start(f32[8,130,1]{1,0,2:T(8,128)S(1)} %get-tuple-element.13), channel_id=1, source_target_pairs={{0,1},{1,2},{2,3},{3,4},{4,5},{5,6},{6,7},{8,9},{9,10},{10,11},{11... | collective-permute-start | bytes 12488 | tf_op jit(solution)/shard_map/ppermute | solution.py:21
  46.3 2.6 %stack.9 = f32[1,8,512,128]{3,2,1,0:T(8,128)} reshape(f32[8,128,512]{2,1,0:T(8,128)} %param.9) | data formatting | bytes 4194304 | tf_op jit(solution)/shard_map/stack | solution.py:120
  49.4 4.2 %copy.160 = f32[1,8,512,128]{3,1,2,0:T(8,128)} copy(f32[1,8,512,128]{3,2,1,0:T(8,128)} %stack.9) | data formatting | bytes 4194304 | tf_op jit(solution)/shard_map/stack | solution.py:120
  53.8 14.1 %fusion.4 = f32[8,128,512]{1,0,2:T(8,128)} fusion(f32[8,128,512]{1,0,2:T(8,128)} %copy.158, f32[1,128,512]{1,0,2:T(1,128)S(1)} %copy.154, f32[7,128,512]{1,0,2:T(8,128)} %get-tuple-element.19, f32[7,128,512]{1,0,2:T(8,128)} %get-tuple-element.18, f32[1,128,512]{1,0,2:T(1,128)S(1)} %copy.156, f32[8,1,512]{1,0,2:T(8,128)} %copy.145, f32[8,1,512]{1,0,2:T(8,128)} %copy.147, ...), kind=kLoop, calls=%fused_computation.18 | loop fusion | flops 15204352 | bytes 8691904 | tf_op jit(solution)/shard_map/add | solution.py:96
  67.9 2.9 %copy.182 = f32[8,128,512]{2,1,0:T(8,128)} copy(f32[8,128,512]{1,0,2:T(8,128)} %fusion.4) | data formatting | bytes 4194304
  70.8 2.6 %stack.10 = f32[1,8,512,128]{3,2,1,0:T(8,128)} reshape(f32[8,128,512]{2,1,0:T(8,128)} %copy.182) | data formatting | bytes 4194304 | tf_op jit(solution)/shard_map/stack | solution.py:120
  73.4 3.0 %copy.161 = f32[1,8,512,128]{3,1,2,0:T(8,128)S(1)} copy(f32[1,8,512,128]{3,2,1,0:T(8,128)} %stack.10) | data formatting | bytes 4194304 | tf_op jit(solution)/shard_map/stack | solution.py:120
  76.4 2.2 pad_maximum_fusion
  78.6 2.9 %gather_fusion = f32[128,2,8,128]{3,2,1,0:T(8,128)S(1)} fusion(f32[2,8,512,128]{3,1,2,0:T(8,128)} %pad_maximum_fusion, s32[1024]{0:T(1024)S(1)} %pad_clamp_fusion), kind=kCustom, calls=%fused_computation | custom fusion | bytes 2097664 | tf_op jit(solution)/shard_map/jit(_take)/gather | solution.py:121
  81.5 1.2 broadcast_select_fusion.1
  82.7 1.6 copy.162
  84.3 2.4 fusion.12
  86.6 2.9 %reshape.413 = f32[128,4096]{1,0:T(8,128)} reshape(f32[256,2048]{1,0:T(8,128)} %fusion.12) | data formatting | bytes 4194304 | tf_op jit(solution)/shard_map/reshape | solution.py:131
  89.5 4.2 %gather_fusion.1 = f32[512,768]{1,0:T(8,128)S(1)} fusion(f32[128,4,768]{2,1,0:T(4,128)S(1)} %all-to-all-done, s32[512]{0:T(512)S(1)} %reshape.426), kind=kCustom, calls=%fused_computation.1 | custom fusion | bytes 3149824 | tf_op jit(solution)/shard_map/jit(take_along_axis)/gather | solution.py:108
  94.9 1.3 copy-done.3
  96.5 3.7 %all_to_all.12 = f32[128,1,7168]{2,1,0:T(1,128)} reshape(f32[128,7168]{1,0:T(8,128)S(1)} %pad_maximum_fusion.1) | data formatting | bytes 7340032 | tf_op jit(solution)/shard_map/all_to_all | solution.py:133
  100.3 9.9 %all-to-all-start.1 = ((f32[128,1,7168]{2,1,0:T(1,128)}), f32[128,1,7168]{2,1,0:T(1,128)}, u32[]{:S(2)}, u32[]{:S(2)}) async-start(f32[128,1,7168]{2,1,0:T(1,128)} %all_to_all.12), calls=%async_computation.1 | async-start | bytes 7340032 | tf_op jit(solution)/shard_map/all_to_all | solution.py:133
  111.2 44.1 %all-to-all-done.1 = f32[128,1,7168]{2,1,0:T(1,128)} async-done(((f32[128,1,7168]{2,1,0:T(1,128)}), f32[128,1,7168]{2,1,0:T(1,128)}, u32[]{:S(2)}, u32[]{:S(2)}) %all-to-all-start.1) | async-done | bytes 3670048 | tf_op jit(solution)/shard_map/all_to_all | solution.py:133
  155.4 2.7 %copy.192 = f32[128,1,7168]{2,0,1:T(8,128)S(1)} copy(f32[128,1,7168]{2,1,0:T(1,128)} %all-to-all-done.1) | data formatting | bytes 7340032
  158.2 1.5 slice.208
  159.6 1.3 reshape_reshape.3
  161.0 1.9 copy.193
  162.9 2.4 reshape.416
  165.3 4.0 %collective-permute-start.4 = (f32[8,1,384]{2,1,0:T(1,128)S(1)}, f32[8,1,384]{2,1,0:T(1,128)S(1)}, u32[]{:S(2)}, u32[]{:S(2)}) collective-permute-start(f32[8,1,384]{2,1,0:T(1,128)S(1)} %get-tuple-element.31), channel_id=1, source_target_pairs={{8,0},{16,8},{24,16},{32,24},{40,32},{48,40},{56,48},{64,56},{72,6... | collective-permute-start | bytes 36872 | tf_op jit(solution)/shard_map/ppermute | solution.py:24
  169.3 1.9 collective-permute-start.5
  171.3 2.8 %reshape.417 = f32[256,2048]{1,0:T(8,128)} reshape(f32[128,4096]{1,0:T(8,128)} %slice.208) | data formatting | bytes 4194304 | tf_op jit(solution)/shard_map/reshape | solution.py:135
  174.0 2.9 %copy.173 = f32[256,2048]{0,1:T(8,128)} copy(f32[256,2048]{1,0:T(8,128)} %reshape.417) | data formatting | bytes 4194304 | tf_op jit(solution)/shard_map/reshape | solution.py:135
  176.9 3.9 %fusion.13 = f32[128,2,8,128]{3,0,2,1:T(8,128)} fusion(f32[2,8,128,256]{3,2,1,0:T(8,128)} %bitcast.85, s32[256]{0:T(256)S(1)} %select_n.143), kind=kOutput, calls=%fused_computation.78 | convolution fusion | flops 805339136 | bytes 3146752 | tf_op jit(solution)/shard_map/dot_general | solution.py:146
  181.3 3.5 %collective-permute-start.6 = (f32[8,130,1]{1,0,2:T(8,128)S(1)}, f32[8,130,1]{1,0,2:T(8,128)S(1)}, u32[]{:S(2)}, u32[]{:S(2)}) collective-permute-start(f32[8,130,1]{1,0,2:T(8,128)S(1)} %copy.166), channel_id=1, source_target_pairs={{1,0},{2,1},{3,2},{4,3},{5,4},{6,5},{7,6},{9,8},{10,9},{11,10},{12... | collective-permute-start | bytes 12488 | tf_op jit(solution)/shard_map/ppermute | solution.py:24
  185.1 2.1 collective-permute-start.7
  187.3 3.9 %convolution_bitcast_fusion = f32[2,8,128,384]{3,2,1,0:T(8,128)S(1)} fusion(f32[128,2,8,128]{3,0,2,1:T(8,128)} %fusion.13, f32[128]{0:T(128)S(1)} %iota_convert_fusion, f32[384]{0:T(512)S(1)} %add_clamp_fusion), kind=kOutput, calls=%fused_computation.19 | convolution fusion | flops 1208156160 | bytes 4196352 | tf_op jit(solution)/shard_map/tald,de->alte/dot_general | solution.py:150
  191.2 1.1 copy.167
  192.3 1.1 copy.169
  193.4 6.5 %add_divide_fusion.2 = f32[8,128,384]{2,1,0:T(8,128)S(1)} fusion(f32[8,128,384]{2,1,0:T(8,128)} %copy-done, f32[8,1,384]{2,1,0:T(1,128)S(1)} %collective-permute-done.4, f32[8,1,384]{2,1,0:T(1,128)S(1)} %collective-permute-done.5, f32[8,130,1]{2,1,0:T(8,128)} %copy.169, f32[8,130,1]{2,1,0:T(8,128)} %copy.167, ...), kind=kLoop, calls=%fused_computation.51 | loop fusion | flops 11010048 | bytes 6521536 | tf_op jit(solution)/shard_map/div | solution.py:162
  199.9 5.5 %collective-permute-start.8 = (f32[8,1,384]{2,1,0:T(1,128)S(1)}, f32[8,1,384]{2,1,0:T(1,128)S(1)}, u32[]{:S(2)}, u32[]{:S(2)}) collective-permute-start(f32[8,1,384]{2,1,0:T(1,128)S(1)} %get-tuple-element.29), channel_id=1, source_target_pairs={{8,0},{16,8},{24,16},{32,24},{40,32},{48,40},{56,48},{64,56},{72,6... | collective-permute-start | bytes 36872 | tf_op jit(solution)/shard_map/ppermute | solution.py:24
  205.4 1.9 collective-permute-start.9
  207.3 4.6 %collective-permute-done.9 = f32[8,1,384]{2,1,0:T(1,128)S(1)} collective-permute-done((f32[8,1,384]{2,1,0:T(1,128)S(1)}, f32[8,1,384]{2,1,0:T(1,128)S(1)}, u32[]{:S(2)}, u32[]{:S(2)}) %collective-permute-start.9) | collective-permute-done | bytes 12320 | tf_op jit(solution)/shard_map/ppermute | solution.py:21
  211.9 1.2 pad_maximum_fusion.39
  213.2 1.4 copy.174
  214.5 3.8 %collective-permute-start.10 = (f32[8,130,1]{1,0,2:T(8,128)S(1)}, f32[8,130,1]{1,0,2:T(8,128)S(1)}, u32[]{:S(2)}, u32[]{:S(2)}) collective-permute-start(f32[8,130,1]{1,0,2:T(8,128)S(1)} %copy.174), channel_id=1, source_target_pairs={{1,0},{2,1},{3,2},{4,3},{5,4},{6,5},{7,6},{9,8},{10,9},{11,10},{12... | collective-permute-start | bytes 12488 | tf_op jit(solution)/shard_map/ppermute | solution.py:24
  218.4 1.4 copy.176
  219.8 2.2 collective-permute-start.11
  222.0 1.1 copy.175
  223.0 1.1 copy.177
  224.1 6.5 %add_divide_fusion.1 = f32[8,128,384]{2,1,0:T(8,128)S(1)} fusion(f32[8,128,384]{2,1,0:T(8,128)} %copy-done.2, f32[8,1,384]{2,1,0:T(1,128)S(1)} %collective-permute-done.8, f32[8,1,384]{2,1,0:T(1,128)S(1)} %collective-permute-done.9, f32[8,130,1]{2,1,0:T(8,128)} %copy.177, f32[8,130,1]{2,1,0:T(8,128)} %copy.175, ...), kind=kLoop, calls=%fused_computation.50 | loop fusion | flops 11010048 | bytes 6521536 | tf_op jit(solution)/shard_map/div | solution.py:162
  230.6 1.9 collective-permute-start.12
  232.5 3.4 %collective-permute-start.13 = (f32[8,1,384]{2,1,0:T(1,128)S(1)}, f32[8,1,384]{2,1,0:T(1,128)S(1)}, u32[]{:S(2)}, u32[]{:S(2)}) collective-permute-start(f32[8,1,384]{2,1,0:T(1,128)S(1)} %get-tuple-element.26), channel_id=1, source_target_pairs={{0,8},{8,16},{16,24},{24,32},{32,40},{40,48},{48,56},{56,64},{64,7... | collective-permute-start | bytes 36872 | tf_op jit(solution)/shard_map/ppermute | solution.py:21
  235.9 3.2 %collective-permute-done.13 = f32[8,1,384]{2,1,0:T(1,128)S(1)} collective-permute-done((f32[8,1,384]{2,1,0:T(1,128)S(1)}, f32[8,1,384]{2,1,0:T(1,128)S(1)}, u32[]{:S(2)}, u32[]{:S(2)}) %collective-permute-start.13) | collective-permute-done | bytes 12320 | tf_op jit(solution)/shard_map/ppermute | solution.py:21
  239.1 1.2 pad_maximum_fusion.36
  240.3 1.4 copy.178
  241.7 3.6 %collective-permute-start.14 = (f32[8,130,1]{1,0,2:T(8,128)S(1)}, f32[8,130,1]{1,0,2:T(8,128)S(1)}, u32[]{:S(2)}, u32[]{:S(2)}) collective-permute-start(f32[8,130,1]{1,0,2:T(8,128)S(1)} %copy.178), channel_id=1, source_target_pairs={{1,0},{2,1},{3,2},{4,3},{5,4},{6,5},{7,6},{9,8},{10,9},{11,10},{12... | collective-permute-start | bytes 12488 | tf_op jit(solution)/shard_map/ppermute | solution.py:24
  245.2 1.4 copy.180
  246.6 3.1 %collective-permute-start.15 = (f32[8,130,1]{1,0,2:T(8,128)S(1)}, f32[8,130,1]{1,0,2:T(8,128)S(1)}, u32[]{:S(2)}, u32[]{:S(2)}) collective-permute-start(f32[8,130,1]{1,0,2:T(8,128)S(1)} %copy.180), channel_id=1, source_target_pairs={{0,1},{1,2},{2,3},{3,4},{4,5},{5,6},{6,7},{8,9},{9,10},{10,11},{11... | collective-permute-start | bytes 12488 | tf_op jit(solution)/shard_map/ppermute | solution.py:21
  251.9 7.2 %add_divide_fusion = f32[8,128,384]{2,1,0:T(8,128)} fusion(f32[8,128,384]{2,1,0:T(8,128)} %copy-done.1, f32[8,1,384]{2,1,0:T(1,128)S(1)} %collective-permute-done.12, f32[8,1,384]{2,1,0:T(1,128)S(1)} %collective-permute-done.13, f32[8,130,1]{2,1,0:T(8,128)} %copy.181, f32[8,130,1]{2,1,0:T(8,128)} %copy.179, ...), kind=kLoop, calls=%fused_computation.49 | loop fusion | flops 10616832 | bytes 6521536 | tf_op jit(solution)/shard_map/div | solution.py:162
  (87 shorter events, 11.7 us)
Async XLA Ops:
  1.6 33.3 %collective-permute-start = (f32[8,1,512]{2,0,1:T(8,128)S(1)}, f32[8,1,512]{2,0,1:T(8,128)S(1)}, u32[]{:S(2)}, u32[]{:S(2)}) collective-permute-start(f32[8,1,512]{2,0,1:T(8,128)S(1)} %copy.186), channel_id=1, source_target_pairs={{8,0},{16,8},{24,16},{32,24},{40,32},{48,40},{56,48},{64,56},{72,6... | collective-permute-start | bytes 49160 | tf_op jit(solution)/shard_map/ppermute | solution.py:24
  5.6 31.5 %collective-permute-start.1 = (f32[8,1,512]{2,0,1:T(8,128)S(1)}, f32[8,1,512]{2,0,1:T(8,128)S(1)}, u32[]{:S(2)}, u32[]{:S(2)}) collective-permute-start(f32[8,1,512]{2,0,1:T(8,128)S(1)} %copy.187), channel_id=1, source_target_pairs={{0,8},{8,16},{16,24},{24,32},{32,40},{40,48},{48,56},{56,64},{64,7... | collective-permute-start | bytes 49160 | tf_op jit(solution)/shard_map/ppermute | solution.py:21
  13.0 76.5 %all-to-all-start = ((f32[128,4,768]{2,1,0:T(4,128)}), f32[128,4,768]{2,1,0:T(4,128)S(1)}, u32[]{:S(2)}, u32[]{:S(2)}) async-start(f32[128,4,768]{2,1,0:T(4,128)} %reshape.415), calls=%async_computation | async-start | bytes 3145728 | tf_op jit(solution)/shard_map/all_to_all | solution.py:104
  25.2 4.0 %copy-start.9 = (s32[2,4]{1,0:T(2,128)S(1)}, s32[2,4]{1,0:T(2,128)}, u32[]{:S(2)}) copy-start(s32[2,4]{1,0:T(2,128)} %param.17) | copy-start | bytes 100
  25.2 4.3 %copy-start.10 = (f32[2,8]{1,0:T(2,128)S(1)}, f32[2,8]{1,0:T(2,128)}, u32[]{:S(2)}) copy-start(f32[2,8]{1,0:T(2,128)} %param.13) | copy-start | bytes 196
  29.5 4.6 %copy-start.5 = (bf16[128,512]{1,0:T(8,128)(2,1)S(1)}, bf16[128,512]{1,0:T(8,128)(2,1)}, u32[]{:S(2)}) copy-start(bf16[128,512]{1,0:T(8,128)(2,1)} %param.10) | copy-start | bytes 393220
  29.5 5.3 %copy-start.7 = (s32[16384,1]{0,1:T(1,128)S(1)}, s32[16384,1]{0,1:T(1,128)}, u32[]{:S(2)}) copy-start(s32[16384,1]{0,1:T(1,128)} %param.14) | copy-start | bytes 196612
  39.9 13.9 %collective-permute-start.2 = (f32[8,130,1]{1,0,2:T(8,128)S(1)}, f32[8,130,1]{1,0,2:T(8,128)S(1)}, u32[]{:S(2)}, u32[]{:S(2)}) collective-permute-start(f32[8,130,1]{1,0,2:T(8,128)S(1)} %get-tuple-element.12), channel_id=1, source_target_pairs={{1,0},{2,1},{3,2},{4,3},{5,4},{6,5},{7,6},{9,8},{10,9},{11,10},{12... | collective-permute-start | bytes 12488 | tf_op jit(solution)/shard_map/ppermute | solution.py:24
  42.2 11.6 %collective-permute-start.3 = (f32[8,130,1]{1,0,2:T(8,128)S(1)}, f32[8,130,1]{1,0,2:T(8,128)S(1)}, u32[]{:S(2)}, u32[]{:S(2)}) collective-permute-start(f32[8,130,1]{1,0,2:T(8,128)S(1)} %get-tuple-element.13), channel_id=1, source_target_pairs={{0,1},{1,2},{2,3},{3,4},{4,5},{5,6},{6,7},{8,9},{9,10},{10,11},{11... | collective-permute-start | bytes 12488 | tf_op jit(solution)/shard_map/ppermute | solution.py:21
  73.4 3.0 %copy-start.4 = (f32[1,8,512,128]{3,1,2,0:T(8,128)S(1)}, f32[1,8,512,128]{3,1,2,0:T(8,128)}, u32[]{:S(2)}) copy-start(f32[1,8,512,128]{3,1,2,0:T(8,128)} %copy.160) | copy-start | bytes 6291460
  94.6 1.6 copy-start.3
  100.2 10.4 %copy-start.8 = (s32[16384]{0:T(1024)S(1)}, s32[16384]{0:T(1024)}, u32[]{:S(2)}) copy-start(s32[16384]{0:T(1024)} %param.16) | copy-start | bytes 196612
  100.2 11.0 %copy-start.6 = (bf16[128,384]{1,0:T(8,128)(2,1)S(1)}, bf16[128,384]{1,0:T(8,128)(2,1)}, u32[]{:S(2)}) copy-start(bf16[128,384]{1,0:T(8,128)(2,1)} %param.12) | copy-start | bytes 294916
  100.3 55.1 %all-to-all-start.1 = ((f32[128,1,7168]{2,1,0:T(1,128)}), f32[128,1,7168]{2,1,0:T(1,128)}, u32[]{:S(2)}, u32[]{:S(2)}) async-start(f32[128,1,7168]{2,1,0:T(1,128)} %all_to_all.12), calls=%async_computation.1 | async-start | bytes 7340032 | tf_op jit(solution)/shard_map/all_to_all | solution.py:133
  165.3 15.5 %copy-start = (f32[8,128,384]{2,1,0:T(8,128)}, f32[8,128,384]{2,1,0:T(8,128)S(1)}, u32[]{:S(2)}) copy-start(f32[8,128,384]{2,1,0:T(8,128)S(1)} %reshape.416) | copy-start | bytes 4718596
  165.3 15.4 %collective-permute-start.4 = (f32[8,1,384]{2,1,0:T(1,128)S(1)}, f32[8,1,384]{2,1,0:T(1,128)S(1)}, u32[]{:S(2)}, u32[]{:S(2)}) collective-permute-start(f32[8,1,384]{2,1,0:T(1,128)S(1)} %get-tuple-element.31), channel_id=1, source_target_pairs={{8,0},{16,8},{24,16},{32,24},{40,32},{48,40},{56,48},{64,56},{72,6... | collective-permute-start | bytes 36872 | tf_op jit(solution)/shard_map/ppermute | solution.py:24
  169.3 11.4 %collective-permute-start.5 = (f32[8,1,384]{2,1,0:T(1,128)S(1)}, f32[8,1,384]{2,1,0:T(1,128)S(1)}, u32[]{:S(2)}, u32[]{:S(2)}) collective-permute-start(f32[8,1,384]{2,1,0:T(1,128)S(1)} %get-tuple-element.30), channel_id=1, source_target_pairs={{0,8},{8,16},{16,24},{24,32},{32,40},{40,48},{48,56},{56,64},{64,7... | collective-permute-start | bytes 36872 | tf_op jit(solution)/shard_map/ppermute | solution.py:21
  181.3 9.8 %collective-permute-start.6 = (f32[8,130,1]{1,0,2:T(8,128)S(1)}, f32[8,130,1]{1,0,2:T(8,128)S(1)}, u32[]{:S(2)}, u32[]{:S(2)}) collective-permute-start(f32[8,130,1]{1,0,2:T(8,128)S(1)} %copy.166), channel_id=1, source_target_pairs={{1,0},{2,1},{3,2},{4,3},{5,4},{6,5},{7,6},{9,8},{10,9},{11,10},{12... | collective-permute-start | bytes 12488 | tf_op jit(solution)/shard_map/ppermute | solution.py:24
  185.1 7.1 %collective-permute-start.7 = (f32[8,130,1]{1,0,2:T(8,128)S(1)}, f32[8,130,1]{1,0,2:T(8,128)S(1)}, u32[]{:S(2)}, u32[]{:S(2)}) collective-permute-start(f32[8,130,1]{1,0,2:T(8,128)S(1)} %copy.168), channel_id=1, source_target_pairs={{0,1},{1,2},{2,3},{3,4},{4,5},{5,6},{6,7},{8,9},{9,10},{10,11},{11... | collective-permute-start | bytes 12488 | tf_op jit(solution)/shard_map/ppermute | solution.py:21
  199.8 12.1 %copy-start.2 = (f32[8,128,384]{2,1,0:T(8,128)}, f32[8,128,384]{2,1,0:T(8,128)S(1)}, u32[]{:S(2)}) copy-start(f32[8,128,384]{2,1,0:T(8,128)S(1)} %add_divide_fusion.2) | copy-start | bytes 4718596
  199.9 7.5 %collective-permute-start.8 = (f32[8,1,384]{2,1,0:T(1,128)S(1)}, f32[8,1,384]{2,1,0:T(1,128)S(1)}, u32[]{:S(2)}, u32[]{:S(2)}) collective-permute-start(f32[8,1,384]{2,1,0:T(1,128)S(1)} %get-tuple-element.29), channel_id=1, source_target_pairs={{8,0},{16,8},{24,16},{32,24},{40,32},{48,40},{56,48},{64,56},{72,6... | collective-permute-start | bytes 36872 | tf_op jit(solution)/shard_map/ppermute | solution.py:24
  205.4 6.5 %collective-permute-start.9 = (f32[8,1,384]{2,1,0:T(1,128)S(1)}, f32[8,1,384]{2,1,0:T(1,128)S(1)}, u32[]{:S(2)}, u32[]{:S(2)}) collective-permute-start(f32[8,1,384]{2,1,0:T(1,128)S(1)} %get-tuple-element.28), channel_id=1, source_target_pairs={{0,8},{8,16},{16,24},{24,32},{32,40},{40,48},{48,56},{56,64},{64,7... | collective-permute-start | bytes 36872 | tf_op jit(solution)/shard_map/ppermute | solution.py:21
  214.5 7.4 %collective-permute-start.10 = (f32[8,130,1]{1,0,2:T(8,128)S(1)}, f32[8,130,1]{1,0,2:T(8,128)S(1)}, u32[]{:S(2)}, u32[]{:S(2)}) collective-permute-start(f32[8,130,1]{1,0,2:T(8,128)S(1)} %copy.174), channel_id=1, source_target_pairs={{1,0},{2,1},{3,2},{4,3},{5,4},{6,5},{7,6},{9,8},{10,9},{11,10},{12... | collective-permute-start | bytes 12488 | tf_op jit(solution)/shard_map/ppermute | solution.py:24
  219.8 3.3 %collective-permute-start.11 = (f32[8,130,1]{1,0,2:T(8,128)S(1)}, f32[8,130,1]{1,0,2:T(8,128)S(1)}, u32[]{:S(2)}, u32[]{:S(2)}) collective-permute-start(f32[8,130,1]{1,0,2:T(8,128)S(1)} %copy.176), channel_id=1, source_target_pairs={{0,1},{1,2},{2,3},{3,4},{4,5},{5,6},{6,7},{8,9},{9,10},{10,11},{11... | collective-permute-start | bytes 12488 | tf_op jit(solution)/shard_map/ppermute | solution.py:21
  230.6 8.5 %copy-start.1 = (f32[8,128,384]{2,1,0:T(8,128)}, f32[8,128,384]{2,1,0:T(8,128)S(1)}, u32[]{:S(2)}) copy-start(f32[8,128,384]{2,1,0:T(8,128)S(1)} %add_divide_fusion.1) | copy-start | bytes 4718596
  230.6 5.3 %collective-permute-start.12 = (f32[8,1,384]{2,1,0:T(1,128)S(1)}, f32[8,1,384]{2,1,0:T(1,128)S(1)}, u32[]{:S(2)}, u32[]{:S(2)}) collective-permute-start(f32[8,1,384]{2,1,0:T(1,128)S(1)} %get-tuple-element.27), channel_id=1, source_target_pairs={{8,0},{16,8},{24,16},{32,24},{40,32},{48,40},{56,48},{64,56},{72,6... | collective-permute-start | bytes 36872 | tf_op jit(solution)/shard_map/ppermute | solution.py:24
  232.5 6.5 %collective-permute-start.13 = (f32[8,1,384]{2,1,0:T(1,128)S(1)}, f32[8,1,384]{2,1,0:T(1,128)S(1)}, u32[]{:S(2)}, u32[]{:S(2)}) collective-permute-start(f32[8,1,384]{2,1,0:T(1,128)S(1)} %get-tuple-element.26), channel_id=1, source_target_pairs={{0,8},{8,16},{16,24},{24,32},{32,40},{40,48},{48,56},{56,64},{64,7... | collective-permute-start | bytes 36872 | tf_op jit(solution)/shard_map/ppermute | solution.py:21
  241.7 8.1 %collective-permute-start.14 = (f32[8,130,1]{1,0,2:T(8,128)S(1)}, f32[8,130,1]{1,0,2:T(8,128)S(1)}, u32[]{:S(2)}, u32[]{:S(2)}) collective-permute-start(f32[8,130,1]{1,0,2:T(8,128)S(1)} %copy.178), channel_id=1, source_target_pairs={{1,0},{2,1},{3,2},{4,3},{5,4},{6,5},{7,6},{9,8},{10,9},{11,10},{12... | collective-permute-start | bytes 12488 | tf_op jit(solution)/shard_map/ppermute | solution.py:24
  246.6 4.2 %collective-permute-start.15 = (f32[8,130,1]{1,0,2:T(8,128)S(1)}, f32[8,130,1]{1,0,2:T(8,128)S(1)}, u32[]{:S(2)}, u32[]{:S(2)}) collective-permute-start(f32[8,130,1]{1,0,2:T(8,128)S(1)} %copy.180), channel_id=1, source_target_pairs={{0,1},{1,2},{2,3},{3,4},{4,5},{5,6},{6,7},{8,9},{9,10},{10,11},{11... | collective-permute-start | bytes 12488 | tf_op jit(solution)/shard_map/ppermute | solution.py:21

commit v2 on v1

--- a/solution.py
+++ b/solution.py
@@ -13,17 +13,29 @@
 NUDGE = 0.5
 
 
-def padded_2(block, sides, width):
-    for axis, dim in sides:
+def edge_halos(block):
+    def swap(edge, axis, forward):
         count = lax.axis_size(axis)
-        forward = [(i, i + 1) for i in range(count - 1)]
-        backward = [(target, source) for source, target in forward]
-        low = lax.ppermute(
-            lax.slice_in_dim(block, block.shape[dim] - width, None, axis=dim), axis, forward
-        )
-        high = lax.ppermute(lax.slice_in_dim(block, 0, width, axis=dim), axis, backward)
-        block = jnp.concatenate([low, block, high], axis=dim)
-    return block
+        pairs = [(i, i + 1) for i in range(count - 1)]
+        if not forward:
+            pairs = [(target, source) for source, target in pairs]
+        return lax.ppermute(edge, axis, pairs)
+
+    before_x = swap(block[:, -1, :], "gx", True)
+    after_x = swap(block[:, 0, :], "gx", False)
+    before_y = swap(block[:, :, -1], "gy", True)
+    after_y = swap(block[:, :, 0], "gy", False)
+    return before_x, after_x, before_y, after_y
+
+
+def halo_tendency(block, wind_x, wind_y):
+    before_x, after_x, before_y, after_y = edge_halos(block)
+    north = jnp.concatenate([block[:, 1:, :], after_x[:, None, :]], axis=1)
+    south = jnp.concatenate([before_x[:, None, :], block[:, :-1, :]], axis=1)
+    east = jnp.concatenate([block[:, :, 1:], after_y[:, :, None]], axis=2)
+    west = jnp.concatenate([before_y[:, :, None], block[:, :, :-1]], axis=2)
+    laplace = north + south + east + west - 4.0 * block
+    return KAPPA * laplace - wind_x * (0.5 * (north - south)) - wind_y * (0.5 * (east - west))
 
 
 def from_behind(value, axis, steps):
@@ -61,16 +73,6 @@
     return jnp.maximum(0.0, 1.0 - jnp.abs(position[None, :] - coarse[:, None]))
 
 
-def tendency(padded, wind_x, wind_y):
-    centre = padded[..., 1:-1, 1:-1]
-    north = padded[..., 2:, 1:-1]
-    south = padded[..., :-2, 1:-1]
-    east = padded[..., 1:-1, 2:]
-    west = padded[..., 1:-1, :-2]
-    laplace = north + south + east + west - 4.0 * centre
-    return KAPPA * laplace - wind_x * (0.5 * (north - south)) - wind_y * (0.5 * (east - west))
-
-
 def vertical(field):
     upper = jnp.concatenate([field[1:], field[-1:]], axis=0)
     lower = jnp.concatenate([field[:1], field[:-1]], axis=0)
@@ -92,14 +94,12 @@
     my_index = lax.axis_index(("gx", "gy"))
     wind_x = wind[0][:, None, None]
     wind_y = wind[1][:, None, None]
-    padded = padded_2(parent_field, (("gx", 1), ("gy", 2)), 1)
     new_parent = parent_field + (1.0 + parent_sppt.astype(jnp.float32)) * (
-        tendency(padded, wind_x, wind_y) + VERTICAL * vertical(parent_field)
+        halo_tendency(parent_field, wind_x, wind_y) + VERTICAL * vertical(parent_field)
     )
     levels, crows, widths = child_storm.shape
     npiece = storm_shift.shape[1]
     band_rows = crows // npiece
-    col_count = lax.axis_size("gy")
     nx, ny = lax.axis_size("gx"), lax.axis_size("gy")
     gathered = lax.all_to_all(
         storm_pieces(child_storm, npiece, devices), ("gx", "gy"), 0, 0, tiled=True
@@ -156,11 +156,10 @@
     divisor = 1.0 + NUDGE * counts[None, :, None]
     factor = 1.0 + child_sppt.astype(jnp.float32)
     for substep in range(SUBSTEPS):
-        padded_child = padded_2(child, (("gx", 1), ("gy", 2)), 1)
         weight = (substep + 1) / 3.0
         target_value = boundary[0] + weight * (boundary[1] - boundary[0])
         child = (
-            child + factor * tendency(padded_child, wind_x, wind_y) + NUDGE * target_value
+            child + factor * halo_tendency(child, wind_x, wind_y) + NUDGE * target_value
         ) / divisor
     return (new_parent, child)
 

time: 261 us -> 265 us (1.015)
  the two profiles are of different devices: /device:TPU:33 before, /device:TPU:7 now
where the time goes in v2:
time: 265 us; the launch traced here: 260 us
  local copies, waits for them, and re-layouts  99.6 us (38%)
  starting transfers between devices  72.8 us (27%)
  waiting for transfers between devices  43.9 us (17%)
  other arithmetic  32 us (12%)
  matrix products  9.63 us (4%)
    ppermute x16, starting transfers between devices, swap(): return lax.ppermute(edge, axis, pairs)  52.3 us
    all_to_all x1, waiting for transfers between devices, shards(): lax.all_to_all(outgoing, ('gx', 'gy'), split_axis=0, concat_axis=0, tiled...  43.9 us
    div x3, other arithmetic, shards(): (child + factor * halo_tendency(child, wind_x, wind_y) + NUDGE * target_v...  16.9 us
    gather x3, local copies, waits for them, and re-layouts, shards(): storm_out = jnp.take_along_axis(gathered, sources[:, :, None], axis=0)  12.6 us
    all_to_all x1, starting transfers between devices, shards(): lax.all_to_all(storm_pieces(child_storm, npiece, devices), ('gx', 'gy'),...  10.4 us
    all_to_all x1, starting transfers between devices, shards(): lax.all_to_all(outgoing, ('gx', 'gy'), split_axis=0, concat_axis=0, tiled...  10.2 us
    unnamed x33, local copies, waits for them, and re-layouts  9 us
    slice x4, local copies, waits for them, and re-layouts, halo_tendency(): north = jnp.concatenate([block[:, 1:, :], after_x[:, None, :]], axis=1)  8.57 us
  transfers between devices with their start and end apart: 18, of which 1 were waited for; matrix products, arithmetic and copies ran while one was open for 27% of the time, Pallas kernels for 0%

profile of v2, /device:TPU:7, one launch (start us, length us, event | category | flops | bytes accessed | tf_op | source)
XLA Modules:
  0.0 259.6 jit_solution(1587300015058982419)
XLA Ops:
  0.6 1.6 fusion.44
  2.4 2.6 collective-permute-start.2
  5.2 3.1 %collective-permute-start.3 = (f32[8,128]{1,0:T(8,128)S(1)}, f32[8,128]{1,0:T(8,128)S(1)}, u32[]{:S(2)}, u32[]{:S(2)}) collective-permute-start(f32[8,128]{1,0:T(8,128)S(1)} %bitcast.148), channel_id=1, source_target_pairs={{0,1},{1,2},{2,3},{3,4},{4,5},{5,6},{6,7},{8,9},{9,10},{10,11},{11... | collective-permute-start | bytes 12296 | tf_op jit(solution)/shard_map/ppermute | solution.py:22
  8.3 2.5 collective-permute-start
  10.8 4.9 %collective-permute-start.1 = (f32[8,512]{1,0:T(8,128)S(1)}, f32[8,512]{1,0:T(8,128)}, u32[]{:S(2)}, u32[]{:S(2)}) collective-permute-start(f32[8,512]{1,0:T(8,128)S(1)} %bitcast.139), channel_id=1, source_target_pairs={{0,8},{8,16},{16,24},{24,32},{32,40},{40,48},{48,56},{56,64},{64,7... | collective-permute-start | bytes 49160 | tf_op jit(solution)/shard_map/ppermute | solution.py:22
  15.7 3.0 %reshape.414 = f32[8,4,16,2,384]{4,3,2,1,0:T(2,128)} reshape(f32[8,128,384]{2,1,0:T(8,128)} %param.11) | data formatting | bytes 3145728 | tf_op jit(solution)/shard_map/reshape | solution.py:51
  18.8 3.1 %copy.238 = f32[8,4,16,2,384]{4,3,1,2,0:T(2,128)} copy(f32[8,4,16,2,384]{4,3,2,1,0:T(2,128)} %reshape.414) | data formatting | bytes 3145728 | tf_op jit(solution)/shard_map/reshape | solution.py:51
  21.9 3.6 %reshape.415 = f32[128,4,768]{2,1,0:T(4,128)} reshape(f32[8,16,4,2,384]{4,3,2,1,0:T(2,128)} %bitcast.130) | data formatting | bytes 3145728 | tf_op jit(solution)/shard_map/reshape | solution.py:52
  25.5 10.4 %all-to-all-start = ((f32[128,4,768]{2,1,0:T(4,128)}), f32[128,4,768]{2,1,0:T(4,128)}, u32[]{:S(2)}, u32[]{:S(2)}) async-start(f32[128,4,768]{2,1,0:T(4,128)} %reshape.415), calls=%async_computation | async-start | bytes 3145728 | tf_op jit(solution)/shard_map/all_to_all | solution.py:104
  35.9 2.5 fusion.41
  38.4 2.8 %fusion.43 = (f32[8,128,511]{2,1,0:T(8,128)}, f32[8,128,511]{2,1,0:T(8,128)}) fusion(f32[8,128,512]{2,1,0:T(8,128)S(1)} %copy-done), kind=kLoop, calls=%fused_computation.135 | loop fusion | bytes 8372224 | tf_op jit(solution)/shard_map/slice | solution.py:35
  41.1 2.5 fusion.46
  47.5 1.4 stack.9
  48.9 4.2 %copy.187 = f32[1,8,512,128]{3,1,2,0:T(8,128)} copy(f32[1,8,512,128]{3,2,1,0:T(8,128)} %stack.9) | data formatting | bytes 4194304 | tf_op jit(solution)/shard_map/stack | solution.py:120
  55.9 7.0 %fusion.4 = f32[8,128,512]{2,1,0:T(8,128)} fusion(f32[8,128,512]{2,1,0:T(8,128)S(1)} %copy-done, f32[1,128,512]{2,1,0:T(8,128)} %get-tuple-element.29, f32[7,128,512]{2,1,0:T(8,128)} %get-tuple-element.31, f32[7,128,512]{2,1,0:T(8,128)} %get-tuple-element.30, f32[1,128,512]{2,1,0:T(8,128)} %get-tuple-element.28, f32[8,128,511]{2,1,0:T(8,128)} %get-tuple-element.25, ...), kind=kLoop, calls=%fused_computation.14 | loop fusion | flops 13107200 | bytes 17039424 | tf_op jit(solution)/shard_map/add | solution.py:97
  62.9 1.6 stack.10
  66.1 2.2 pad_maximum_fusion
  68.4 2.9 %gather_fusion = f32[128,2,8,128]{3,2,1,0:T(8,128)S(1)} fusion(f32[2,8,512,128]{3,1,2,0:T(8,128)} %pad_maximum_fusion, s32[1024]{0:T(1024)S(1)} %pad_clamp_fusion), kind=kCustom, calls=%fused_computation | custom fusion | bytes 2097664 | tf_op jit(solution)/shard_map/jit(_take)/gather | solution.py:121
  72.1 2.3 fusion.12
  74.5 1.9 reshape.413
  76.4 9.7 %gather_fusion.1 = f32[512,768]{1,0:T(8,128)} fusion(f32[128,4,768]{2,1,0:T(4,128)} %all-to-all-done, s32[512]{0:T(512)S(1)} %reshape.426), kind=kCustom, calls=%fused_computation.1 | custom fusion | bytes 3149824 | tf_op jit(solution)/shard_map/jit(take_along_axis)/gather | solution.py:108
  86.2 2.7 %reshape.429 = f32[128,4,768]{2,1,0:T(4,128)} reshape(f32[512,768]{1,0:T(8,128)} %gather_fusion.1) | data formatting | bytes 3145728 | tf_op jit(solution)/shard_map/jit(take_along_axis)/gather | solution.py:108
  88.9 1.8 broadcast_select_fusion
  91.3 3.6 %all_to_all.12 = f32[128,1,7168]{2,1,0:T(1,128)} reshape(f32[128,7168]{1,0:T(8,128)S(1)} %pad_maximum_fusion.1) | data formatting | bytes 7340032 | tf_op jit(solution)/shard_map/all_to_all | solution.py:133
  94.9 10.2 %all-to-all-start.1 = ((f32[128,1,7168]{2,1,0:T(1,128)}), f32[128,1,7168]{2,1,0:T(1,128)}, u32[]{:S(2)}, u32[]{:S(2)}) async-start(f32[128,1,7168]{2,1,0:T(1,128)} %all_to_all.12), calls=%async_computation.1 | async-start | bytes 7340032 | tf_op jit(solution)/shard_map/all_to_all | solution.py:133
  106.3 43.9 %all-to-all-done.1 = f32[128,1,7168]{2,1,0:T(1,128)} async-done(((f32[128,1,7168]{2,1,0:T(1,128)}), f32[128,1,7168]{2,1,0:T(1,128)}, u32[]{:S(2)}, u32[]{:S(2)}) %all-to-all-start.1) | async-done | bytes 3670048 | tf_op jit(solution)/shard_map/all_to_all | solution.py:133
  150.2 2.7 %copy.237 = f32[128,1,7168]{2,0,1:T(8,128)S(1)} copy(f32[128,1,7168]{2,1,0:T(1,128)} %all-to-all-done.1) | data formatting | bytes 7340032
  152.9 1.5 slice.196
  154.5 2.5 reshape_reshape.3
  156.9 2.3 copy.192
  159.8 2.2 fusion.53
  162.0 1.9 fusion.54
  165.0 2.7 %reshape.417 = f32[256,2048]{1,0:T(8,128)} reshape(f32[128,4096]{1,0:T(8,128)} %slice.196) | data formatting | bytes 4194304 | tf_op jit(solution)/shard_map/reshape | solution.py:135
  167.7 2.9 %copy.207 = f32[256,2048]{0,1:T(8,128)} copy(f32[256,2048]{1,0:T(8,128)} %reshape.417) | data formatting | bytes 4194304 | tf_op jit(solution)/shard_map/reshape | solution.py:135
  170.6 2.9 %fusion.13 = f32[128,2,8,128]{3,0,2,1:T(8,128)S(1)} fusion(f32[2,8,128,256]{3,2,1,0:T(8,128)} %bitcast.127, s32[256]{0:T(256)S(1)} %select_n.143), kind=kOutput, calls=%fused_computation.56 | convolution fusion | flops 805339136 | bytes 3146752 | tf_op jit(solution)/shard_map/dot_general | solution.py:146
  173.6 2.0 collective-permute-start.4
  175.5 5.4 %collective-permute-start.5 = (f32[8,384]{1,0:T(8,128)S(1)}, f32[8,384]{1,0:T(8,128)S(1)}, u32[]{:S(2)}, u32[]{:S(2)}) collective-permute-start(f32[8,384]{1,0:T(8,128)S(1)} %get-tuple-element.47), channel_id=1, source_target_pairs={{0,8},{8,16},{16,24},{24,32},{32,40},{40,48},{48,56},{56,64},{64,7... | collective-permute-start | bytes 36872 | tf_op jit(solution)/shard_map/ppermute | solution.py:22
  182.2 3.7 %collective-permute-start.6 = (f32[8,128]{1,0:T(8,128)S(1)}, f32[8,128]{1,0:T(8,128)S(1)}, u32[]{:S(2)}, u32[]{:S(2)}) collective-permute-start(f32[8,128]{1,0:T(8,128)S(1)} %bitcast.156), channel_id=1, source_target_pairs={{1,0},{2,1},{3,2},{4,3},{5,4},{6,5},{7,6},{9,8},{10,9},{11,10},{12... | collective-permute-start | bytes 12296 | tf_op jit(solution)/shard_map/ppermute | solution.py:22
  186.1 2.2 collective-permute-start.7
  188.3 4.4 %convolution_bitcast_fusion = f32[2,8,128,384]{2,3,1,0:T(8,128)} fusion(f32[128,2,8,128]{3,0,2,1:T(8,128)S(1)} %fusion.13, f32[128]{0:T(128)S(1)} %iota_convert_fusion, f32[384]{0:T(512)S(1)} %add_clamp_fusion), kind=kOutput, calls=%fused_computation.15 | convolution fusion | flops 1208156160 | bytes 4196352 | tf_op jit(solution)/shard_map/tald,de->alte/dot_general | solution.py:150
  192.7 1.6 copy.195
  194.3 1.7 copy.197
  196.0 5.5 %add_divide_fusion.2 = f32[8,128,384]{1,2,0:T(8,128)S(1)} fusion(f32[8,128,384]{1,2,0:T(8,128)S(1)} %copy.203, f32[8,128,383]{1,2,0:T(8,128)} %get-tuple-element.49, f32[8,128,1]{1,2,0:T(1,128)S(1)} %bitcast.154, f32[8,128,1]{1,2,0:T(1,128)S(1)} %bitcast.150, f32[8,128,383]{1,2,0:T(8,128)} %get-tuple-element.48, f32[8,127,384]{1,2,0:T(8,128)} %get-tuple-element.45, ...), kind=kLoop, calls=%fused_computation.38 | loop fusion | flops 9437184 | bytes 12780096 | tf_op jit(solution)/shard_map/div | solution.py:161
  201.5 2.2 fusion.50
  203.7 1.3 slice_reduce_fusion.3
  205.0 1.9 collective-permute-start.8
  206.9 5.5 %collective-permute-start.9 = (f32[8,384]{1,0:T(8,128)S(1)}, f32[8,384]{1,0:T(8,128)S(1)}, u32[]{:S(2)}, u32[]{:S(2)}) collective-permute-start(f32[8,384]{1,0:T(8,128)S(1)} %get-tuple-element.17), channel_id=1, source_target_pairs={{0,8},{8,16},{16,24},{24,32},{32,40},{40,48},{48,56},{56,64},{64,7... | collective-permute-start | bytes 36872 | tf_op jit(solution)/shard_map/ppermute | solution.py:22
  212.4 3.0 %collective-permute-start.10 = (f32[8,128]{1,0:T(8,128)S(1)}, f32[8,128]{1,0:T(8,128)S(1)}, u32[]{:S(2)}, u32[]{:S(2)}) collective-permute-start(f32[8,128]{1,0:T(8,128)S(1)} %bitcast.160), channel_id=1, source_target_pairs={{1,0},{2,1},{3,2},{4,3},{5,4},{6,5},{7,6},{9,8},{10,9},{11,10},{12... | collective-permute-start | bytes 12296 | tf_op jit(solution)/shard_map/ppermute | solution.py:22
  215.4 2.6 %collective-permute-start.11 = (f32[8,128]{1,0:T(8,128)S(1)}, f32[8,128]{1,0:T(8,128)S(1)}, u32[]{:S(2)}, u32[]{:S(2)}) collective-permute-start(f32[8,128]{1,0:T(8,128)S(1)} %bitcast.158), channel_id=1, source_target_pairs={{0,1},{1,2},{2,3},{3,4},{4,5},{5,6},{6,7},{8,9},{9,10},{10,11},{11... | collective-permute-start | bytes 12296 | tf_op jit(solution)/shard_map/ppermute | solution.py:22
  218.0 1.9 fusion.51
  219.9 1.7 copy.209
  221.6 1.8 copy.210
  223.3 5.5 %add_divide_fusion.1 = f32[8,128,384]{1,2,0:T(8,128)S(1)} fusion(f32[8,128,384]{1,2,0:T(8,128)S(1)} %add_divide_fusion.2, f32[8,128,383]{1,2,0:T(8,128)} %get-tuple-element.41, f32[8,128,1]{1,2,0:T(1,128)S(1)} %bitcast.155, f32[8,128,1]{1,2,0:T(1,128)S(1)} %bitcast.153, f32[8,128,383]{1,2,0:T(8,128)} %get-tuple-element.40, ...), kind=kLoop, calls=%fused_computation.37 | loop fusion | flops 9437184 | bytes 12780096 | tf_op jit(solution)/shard_map/div | solution.py:161
  228.8 1.7 fusion.47
  230.6 1.3 slice_reduce_fusion.1
  231.9 1.9 collective-permute-start.12
  233.8 5.5 %collective-permute-start.13 = (f32[8,384]{1,0:T(8,128)S(1)}, f32[8,384]{1,0:T(8,128)S(1)}, u32[]{:S(2)}, u32[]{:S(2)}) collective-permute-start(f32[8,384]{1,0:T(8,128)S(1)} %get-tuple-element.15), channel_id=1, source_target_pairs={{0,8},{8,16},{16,24},{24,32},{32,40},{40,48},{48,56},{56,64},{64,7... | collective-permute-start | bytes 36872 | tf_op jit(solution)/shard_map/ppermute | solution.py:22
  239.3 2.3 collective-permute-start.14
  241.6 3.3 %collective-permute-start.15 = (f32[8,128]{1,0:T(8,128)S(1)}, f32[8,128]{1,0:T(8,128)S(1)}, u32[]{:S(2)}, u32[]{:S(2)}) collective-permute-start(f32[8,128]{1,0:T(8,128)S(1)} %bitcast.159), channel_id=1, source_target_pairs={{0,1},{1,2},{2,3},{3,4},{4,5},{5,6},{6,7},{8,9},{9,10},{10,11},{11... | collective-permute-start | bytes 12296 | tf_op jit(solution)/shard_map/ppermute | solution.py:22
  244.9 1.9 fusion.48
  246.8 1.8 copy.213
  248.6 1.7 copy.214
  250.2 5.9 %add_divide_fusion = f32[8,128,384]{1,2,0:T(8,128)} fusion(f32[8,128,384]{1,2,0:T(8,128)S(1)} %add_divide_fusion.1, f32[8,128,383]{1,2,0:T(8,128)} %get-tuple-element.35, f32[8,128,1]{1,2,0:T(1,128)S(1)} %bitcast.152, f32[8,128,1]{1,2,0:T(1,128)S(1)} %bitcast.151, f32[8,128,383]{1,2,0:T(8,128)} %get-tuple-element.34, f32[8,127,384]{1,2,0:T(8,128)} %get-tuple-element.33, ...), kind=kLoop, calls=%fused_computation.36 | loop fusion | flops 9043968 | bytes 12780096 | tf_op jit(solution)/shard_map/div | solution.py:161
  256.2 3.0 %copy.217 = f32[8,128,384]{2,1,0:T(8,128)} copy(f32[8,128,384]{1,2,0:T(8,128)} %add_divide_fusion) | data formatting | bytes 3145728
  (94 shorter events, 14.4 us)
Async XLA Ops:
  0.6 7.6 %copy-start = (f32[8,128,512]{2,1,0:T(8,128)S(1)}, f32[8,128,512]{2,1,0:T(8,128)}, u32[]{:S(2)}) copy-start(f32[8,128,512]{2,1,0:T(8,128)} %param.9) | copy-start | bytes 6291460
  2.4 50.9 %collective-permute-start.2 = (f32[8,128]{1,0:T(8,128)S(1)}, f32[8,128]{1,0:T(8,128)S(1)}, u32[]{:S(2)}, u32[]{:S(2)}) collective-permute-start(f32[8,128]{1,0:T(8,128)S(1)} %bitcast.146), channel_id=1, source_target_pairs={{1,0},{2,1},{3,2},{4,3},{5,4},{6,5},{7,6},{9,8},{10,9},{11,10},{12... | collective-permute-start | bytes 12296 | tf_op jit(solution)/shard_map/ppermute | solution.py:22
  5.2 48.4 %collective-permute-start.3 = (f32[8,128]{1,0:T(8,128)S(1)}, f32[8,128]{1,0:T(8,128)S(1)}, u32[]{:S(2)}, u32[]{:S(2)}) collective-permute-start(f32[8,128]{1,0:T(8,128)S(1)} %bitcast.148), channel_id=1, source_target_pairs={{0,1},{1,2},{2,3},{3,4},{4,5},{5,6},{6,7},{8,9},{9,10},{10,11},{11... | collective-permute-start | bytes 12296 | tf_op jit(solution)/shard_map/ppermute | solution.py:22
  8.3 46.7 %collective-permute-start = (f32[8,512]{1,0:T(8,128)S(1)}, f32[8,512]{1,0:T(8,128)S(1)}, u32[]{:S(2)}, u32[]{:S(2)}) collective-permute-start(f32[8,512]{1,0:T(8,128)S(1)} %bitcast.137), channel_id=1, source_target_pairs={{8,0},{16,8},{24,16},{32,24},{40,32},{48,40},{56,48},{64,56},{72,6... | collective-permute-start | bytes 49160 | tf_op jit(solution)/shard_map/ppermute | solution.py:22
  10.8 44.3 %collective-permute-start.1 = (f32[8,512]{1,0:T(8,128)S(1)}, f32[8,512]{1,0:T(8,128)}, u32[]{:S(2)}, u32[]{:S(2)}) collective-permute-start(f32[8,512]{1,0:T(8,128)S(1)} %bitcast.139), channel_id=1, source_target_pairs={{0,8},{8,16},{16,24},{24,32},{32,40},{40,48},{48,56},{56,64},{64,7... | collective-permute-start | bytes 49160 | tf_op jit(solution)/shard_map/ppermute | solution.py:22
  25.5 51.0 %all-to-all-start = ((f32[128,4,768]{2,1,0:T(4,128)}), f32[128,4,768]{2,1,0:T(4,128)}, u32[]{:S(2)}, u32[]{:S(2)}) async-start(f32[128,4,768]{2,1,0:T(4,128)} %reshape.415), calls=%async_computation | async-start | bytes 3145728 | tf_op jit(solution)/shard_map/all_to_all | solution.py:104
  41.1 3.3 %copy-start.9 = (s32[2,4]{1,0:T(2,128)S(1)}, s32[2,4]{1,0:T(2,128)}, u32[]{:S(2)}) copy-start(s32[2,4]{1,0:T(2,128)} %param.17) | copy-start | bytes 100
  41.1 3.6 %copy-start.10 = (f32[2,8]{1,0:T(2,128)S(1)}, f32[2,8]{1,0:T(2,128)}, u32[]{:S(2)}) copy-start(f32[2,8]{1,0:T(2,128)} %param.13) | copy-start | bytes 196
  41.1 3.6 %copy-start.3 = (bf16[128,512]{1,0:T(8,128)(2,1)S(1)}, bf16[128,512]{1,0:T(8,128)(2,1)}, u32[]{:S(2)}) copy-start(bf16[128,512]{1,0:T(8,128)(2,1)} %param.10) | copy-start | bytes 393220
  41.1 4.4 %copy-start.5 = (s32[16384,1]{0,1:T(1,128)S(1)}, s32[16384,1]{0,1:T(1,128)}, u32[]{:S(2)}) copy-start(s32[16384,1]{0,1:T(1,128)} %param.14) | copy-start | bytes 196612
  53.6 0.6 copy-start.7
  64.5 1.6 copy-start.1
  68.3 2.9 %copy-start.11 = (pred[128]{0:T(512)(128)(4,1)S(1)}, pred[128]{0:T(512)(128)(4,1)}, u32[]{:S(2)}) copy-start(pred[128]{0:T(512)(128)(4,1)} %compare_and_fusion.1) | copy-start | bytes 388
  71.4 0.7 copy-start.8
  94.9 10.7 %copy-start.6 = (s32[16384]{0:T(1024)S(1)}, s32[16384]{0:T(1024)}, u32[]{:S(2)}) copy-start(s32[16384]{0:T(1024)} %param.16) | copy-start | bytes 196612
  94.9 11.1 %copy-start.4 = (bf16[128,384]{1,0:T(8,128)(2,1)S(1)}, bf16[128,384]{1,0:T(8,128)(2,1)}, u32[]{:S(2)}) copy-start(bf16[128,384]{1,0:T(8,128)(2,1)} %param.12) | copy-start | bytes 294916
  94.9 55.2 %all-to-all-start.1 = ((f32[128,1,7168]{2,1,0:T(1,128)}), f32[128,1,7168]{2,1,0:T(1,128)}, u32[]{:S(2)}, u32[]{:S(2)}) async-start(f32[128,1,7168]{2,1,0:T(1,128)} %all_to_all.12), calls=%async_computation.1 | async-start | bytes 7340032 | tf_op jit(solution)/shard_map/all_to_all | solution.py:133
  170.6 15.3 %copy-start.2 = (f32[8,128,1]{2,0,1:T(8,128)S(1)}, f32[8,128,1]{2,0,1:T(8,128)}, u32[]{:S(2)}) copy-start(f32[8,128,1]{2,0,1:T(8,128)} %get-tuple-element.51) | copy-start | bytes 12292
  173.6 19.1 %collective-permute-start.4 = (f32[8,384]{1,0:T(8,128)S(1)}, f32[8,384]{1,0:T(8,128)S(1)}, u32[]{:S(2)}, u32[]{:S(2)}) collective-permute-start(f32[8,384]{1,0:T(8,128)S(1)} %get-tuple-element.46), channel_id=1, source_target_pairs={{8,0},{16,8},{24,16},{32,24},{40,32},{48,40},{56,48},{64,56},{72,6... | collective-permute-start | bytes 36872 | tf_op jit(solution)/shard_map/ppermute | solution.py:22
  175.5 18.8 %collective-permute-start.5 = (f32[8,384]{1,0:T(8,128)S(1)}, f32[8,384]{1,0:T(8,128)S(1)}, u32[]{:S(2)}, u32[]{:S(2)}) collective-permute-start(f32[8,384]{1,0:T(8,128)S(1)} %get-tuple-element.47), channel_id=1, source_target_pairs={{0,8},{8,16},{16,24},{24,32},{32,40},{40,48},{48,56},{56,64},{64,7... | collective-permute-start | bytes 36872 | tf_op jit(solution)/shard_map/ppermute | solution.py:22
  182.2 13.8 %collective-permute-start.6 = (f32[8,128]{1,0:T(8,128)S(1)}, f32[8,128]{1,0:T(8,128)S(1)}, u32[]{:S(2)}, u32[]{:S(2)}) collective-permute-start(f32[8,128]{1,0:T(8,128)S(1)} %bitcast.156), channel_id=1, source_target_pairs={{1,0},{2,1},{3,2},{4,3},{5,4},{6,5},{7,6},{9,8},{10,9},{11,10},{12... | collective-permute-start | bytes 12296 | tf_op jit(solution)/shard_map/ppermute | solution.py:22
  186.1 9.9 %collective-permute-start.7 = (f32[8,128]{1,0:T(8,128)S(1)}, f32[8,128]{1,0:T(8,128)S(1)}, u32[]{:S(2)}, u32[]{:S(2)}) collective-permute-start(f32[8,128]{1,0:T(8,128)S(1)} %bitcast.157), channel_id=1, source_target_pairs={{0,1},{1,2},{2,3},{3,4},{4,5},{5,6},{6,7},{8,9},{9,10},{10,11},{11... | collective-permute-start | bytes 12296 | tf_op jit(solution)/shard_map/ppermute | solution.py:22
  205.0 14.9 %collective-permute-start.8 = (f32[8,384]{1,0:T(8,128)S(1)}, f32[8,384]{1,0:T(8,128)S(1)}, u32[]{:S(2)}, u32[]{:S(2)}) collective-permute-start(f32[8,384]{1,0:T(8,128)S(1)} %get-tuple-element.16), channel_id=1, source_target_pairs={{8,0},{16,8},{24,16},{32,24},{40,32},{48,40},{56,48},{64,56},{72,6... | collective-permute-start | bytes 36872 | tf_op jit(solution)/shard_map/ppermute | solution.py:22
  206.9 14.6 %collective-permute-start.9 = (f32[8,384]{1,0:T(8,128)S(1)}, f32[8,384]{1,0:T(8,128)S(1)}, u32[]{:S(2)}, u32[]{:S(2)}) collective-permute-start(f32[8,384]{1,0:T(8,128)S(1)} %get-tuple-element.17), channel_id=1, source_target_pairs={{0,8},{8,16},{16,24},{24,32},{32,40},{40,48},{48,56},{56,64},{64,7... | collective-permute-start | bytes 36872 | tf_op jit(solution)/shard_map/ppermute | solution.py:22
  212.4 10.9 %collective-permute-start.10 = (f32[8,128]{1,0:T(8,128)S(1)}, f32[8,128]{1,0:T(8,128)S(1)}, u32[]{:S(2)}, u32[]{:S(2)}) collective-permute-start(f32[8,128]{1,0:T(8,128)S(1)} %bitcast.160), channel_id=1, source_target_pairs={{1,0},{2,1},{3,2},{4,3},{5,4},{6,5},{7,6},{9,8},{10,9},{11,10},{12... | collective-permute-start | bytes 12296 | tf_op jit(solution)/shard_map/ppermute | solution.py:22
  215.4 8.0 %collective-permute-start.11 = (f32[8,128]{1,0:T(8,128)S(1)}, f32[8,128]{1,0:T(8,128)S(1)}, u32[]{:S(2)}, u32[]{:S(2)}) collective-permute-start(f32[8,128]{1,0:T(8,128)S(1)} %bitcast.158), channel_id=1, source_target_pairs={{0,1},{1,2},{2,3},{3,4},{4,5},{5,6},{6,7},{8,9},{9,10},{10,11},{11... | collective-permute-start | bytes 12296 | tf_op jit(solution)/shard_map/ppermute | solution.py:22
  231.9 14.9 %collective-permute-start.12 = (f32[8,384]{1,0:T(8,128)S(1)}, f32[8,384]{1,0:T(8,128)S(1)}, u32[]{:S(2)}, u32[]{:S(2)}) collective-permute-start(f32[8,384]{1,0:T(8,128)S(1)} %get-tuple-element.14), channel_id=1, source_target_pairs={{8,0},{16,8},{24,16},{32,24},{40,32},{48,40},{56,48},{64,56},{72,6... | collective-permute-start | bytes 36872 | tf_op jit(solution)/shard_map/ppermute | solution.py:22
  233.8 14.7 %collective-permute-start.13 = (f32[8,384]{1,0:T(8,128)S(1)}, f32[8,384]{1,0:T(8,128)S(1)}, u32[]{:S(2)}, u32[]{:S(2)}) collective-permute-start(f32[8,384]{1,0:T(8,128)S(1)} %get-tuple-element.15), channel_id=1, source_target_pairs={{0,8},{8,16},{16,24},{24,32},{32,40},{40,48},{48,56},{56,64},{64,7... | collective-permute-start | bytes 36872 | tf_op jit(solution)/shard_map/ppermute | solution.py:22
  239.3 10.9 %collective-permute-start.14 = (f32[8,128]{1,0:T(8,128)S(1)}, f32[8,128]{1,0:T(8,128)S(1)}, u32[]{:S(2)}, u32[]{:S(2)}) collective-permute-start(f32[8,128]{1,0:T(8,128)S(1)} %bitcast.161), channel_id=1, source_target_pairs={{1,0},{2,1},{3,2},{4,3},{5,4},{6,5},{7,6},{9,8},{10,9},{11,10},{12... | collective-permute-start | bytes 12296 | tf_op jit(solution)/shard_map/ppermute | solution.py:22
  241.6 8.6 %collective-permute-start.15 = (f32[8,128]{1,0:T(8,128)S(1)}, f32[8,128]{1,0:T(8,128)S(1)}, u32[]{:S(2)}, u32[]{:S(2)}) collective-permute-start(f32[8,128]{1,0:T(8,128)S(1)} %bitcast.159), channel_id=1, source_target_pairs={{0,1},{1,2},{2,3},{3,4},{4,5},{5,6},{6,7},{8,9},{9,10},{10,11},{11... | collective-permute-start | bytes 12296 | tf_op jit(solution)/shard_map/ppermute | solution.py:22

commit v3 on v2

--- a/solution.py
+++ b/solution.py
@@ -44,26 +44,15 @@
     return lax.ppermute(value, axis, pairs)
 
 
-def storm_pieces(child, npiece, devices):
+def storm_rows(child, storm_shift, nx, ny):
     levels, crows, widths = child.shape
-    band_rows = crows // npiece
-    per_level = devices // levels
-    pieces = child.reshape(levels, npiece, per_level, band_rows // per_level, widths)
-    return jnp.transpose(pieces, (0, 2, 1, 3, 4)).reshape(devices, npiece, -1)
-
-
-def storm_unpieces(pieces, levels, crows, widths):
-    devices, npiece = pieces.shape[:2]
-    per_level = devices // levels
-    child = pieces.reshape(levels, per_level, npiece, crows // npiece // per_level, widths)
-    return jnp.transpose(child, (0, 2, 1, 3, 4)).reshape(levels, crows, widths)
-
-
-def storm_sources(storm_shift, nx, ny):
-    dest = jnp.arange(nx * ny)
-    src_x = (dest[:, None] // ny - storm_shift[0][None, :]) % nx
-    src_y = (dest[:, None] % ny - storm_shift[1][None, :]) % ny
-    return src_x * ny + src_y
+    mine = lax.axis_index(("gx", "gy"))
+    gathered = lax.all_to_all(child, ("gx", "gy"), 1, 1, tiled=True)
+    piece = mine // (crows // storm_shift.shape[1])
+    grid = gathered.reshape(levels, nx, ny, widths)
+    grid = jnp.roll(grid, storm_shift[0, piece], axis=1)
+    grid = jnp.roll(grid, storm_shift[1, piece], axis=2)
+    return lax.all_to_all(grid.reshape(levels, crows, widths), ("gx", "gy"), 1, 1, tiled=True)
 
 
 def refine_table(strip):
@@ -101,11 +90,7 @@
     npiece = storm_shift.shape[1]
     band_rows = crows // npiece
     nx, ny = lax.axis_size("gx"), lax.axis_size("gy")
-    gathered = lax.all_to_all(
-        storm_pieces(child_storm, npiece, devices), ("gx", "gy"), 0, 0, tiled=True
-    )
-    sources = storm_sources(storm_shift, nx, ny)
-    storm_out = jnp.take_along_axis(gathered, sources[:, :, None], axis=0)
+    child = storm_rows(child_storm, storm_shift, nx, ny)
     dest_table = strip_dest.reshape(devices, -1)
     row_table = strip_row.reshape(devices, -1)
     target_table = strip_target.reshape(devices, -1)
@@ -126,15 +111,8 @@
         precision=lax.Precision.HIGHEST,
         preferred_element_type=jnp.float32,
     )
-    strip_width = outgoing_strips.shape[1]
-    outgoing = jnp.concatenate(
-        [outgoing_strips.reshape(devices, -1), storm_out.reshape(devices, -1)], axis=1
-    )
-    arrived = lax.all_to_all(outgoing, ("gx", "gy"), split_axis=0, concat_axis=0, tiled=True)
-    strip_part = CAP * strip_width
-    incoming = arrived[:, :strip_part].reshape(devices * CAP, strip_width)
-    child = storm_unpieces(
-        arrived[:, strip_part:].reshape(devices, npiece, -1), levels, crows, widths
+    incoming = lax.all_to_all(
+        outgoing_strips, ("gx", "gy"), split_axis=0, concat_axis=0, tiled=True
     )
     mine = dest_table == my_index
     rank_all = jnp.cumsum(mine.astype(jnp.int32), axis=1) - 1

time: 265 us -> 226 us (0.85)
  the two profiles are of different devices: /device:TPU:7 before, /device:TPU:33 now
where the time goes in v3:
time: 226 us; the launch traced here: 225 us
  starting transfers between devices  76.6 us (34%)
  local copies, waits for them, and re-layouts  75.5 us (33%)
  other arithmetic  30.8 us (14%)
  waiting for transfers between devices  28.6 us (13%)
  matrix products  8.25 us (4%)
  between operations  4.92 us (2%)
    ppermute x16, starting transfers between devices, swap(): return lax.ppermute(edge, axis, pairs)  51.6 us
    all_to_all x1, waiting for transfers between devices, shards(): lax.all_to_all(outgoing_strips, ('gx', 'gy'), split_axis=0, concat_axis=0...  19.5 us
    div x3, other arithmetic, shards(): (child + factor * halo_tendency(child, wind_x, wind_y) + NUDGE * target_v...  16.9 us
    unnamed x34, local copies, waits for them, and re-layouts  12 us
    all_to_all x1, starting transfers between devices, shards(): lax.all_to_all(outgoing_strips, ('gx', 'gy'), split_axis=0, concat_axis=0...  9.77 us
    all_to_all x1, starting transfers between devices, storm_rows(): gathered = lax.all_to_all(child, ('gx', 'gy'), 1, 1, tiled=True)  9.24 us
    all_to_all x1, waiting for transfers between devices, storm_rows(): lax.all_to_all(grid.reshape(levels, crows, widths), ('gx', 'gy'), 1, 1, t...  9.07 us
    slice x4, local copies, waits for them, and re-layouts, halo_tendency(): north = jnp.concatenate([block[:, 1:, :], after_x[:, None, :]], axis=1)  9.01 us
  transfers between devices with their start and end apart: 19, of which 2 were waited for; matrix products, arithmetic and copies ran while one was open for 34% of the time, Pallas kernels for 0%

profile of v3, /device:TPU:33, one launch (start us, length us, event | category | flops | bytes accessed | tf_op | source)
XLA Modules:
  0.0 224.7 jit_solution(2498742965248244502)
XLA Ops:
  0.6 1.6 fusion.38
  2.4 3.8 %collective-permute-start.3 = (f32[8,128]{1,0:T(8,128)S(1)}, f32[8,128]{1,0:T(8,128)S(1)}, u32[]{:S(2)}, u32[]{:S(2)}) collective-permute-start(f32[8,128]{1,0:T(8,128)S(1)} %bitcast.130), channel_id=1, source_target_pairs={{0,1},{1,2},{2,3},{3,4},{4,5},{5,6},{6,7},{8,9},{9,10},{10,11},{11... | collective-permute-start | bytes 12296 | tf_op jit(solution)/shard_map/ppermute | solution.py:22
  6.3 1.9 collective-permute-start.2
  8.3 3.1 %collective-permute-start.1 = (f32[8,512]{1,0:T(8,128)S(1)}, f32[8,512]{1,0:T(8,128)S(1)}, u32[]{:S(2)}, u32[]{:S(2)}) collective-permute-start(f32[8,512]{1,0:T(8,128)S(1)} %bitcast.120), channel_id=1, source_target_pairs={{0,8},{8,16},{16,24},{24,32},{32,40},{40,48},{48,56},{56,64},{64,7... | collective-permute-start | bytes 49160 | tf_op jit(solution)/shard_map/ppermute | solution.py:22
  11.5 4.3 %collective-permute-start = (f32[8,512]{1,0:T(8,128)S(1)}, f32[8,512]{1,0:T(8,128)S(1)}, u32[]{:S(2)}, u32[]{:S(2)}) collective-permute-start(f32[8,512]{1,0:T(8,128)S(1)} %bitcast.122), channel_id=1, source_target_pairs={{8,0},{16,8},{24,16},{32,24},{40,32},{48,40},{56,48},{64,56},{72,6... | collective-permute-start | bytes 49160 | tf_op jit(solution)/shard_map/ppermute | solution.py:22
  15.7 3.5 %copy.138 = f32[8,128,384]{2,0,1:T(8,128)} copy(f32[8,128,384]{2,1,0:T(8,128)} %param.11) | data formatting | bytes 3145728 | tf_op args[2]
  19.2 9.2 %all-to-all-start = ((f32[8,128,384]{2,0,1:T(8,128)}), f32[8,128,384]{2,0,1:T(8,128)}, u32[]{:S(2)}, u32[]{:S(2)}) async-start(f32[8,128,384]{2,0,1:T(8,128)} %copy.138), calls=%async_computation | async-start | bytes 3145728 | tf_op jit(solution)/shard_map/all_to_all | solution.py:50
  29.3 2.5 %fusion.40 = (f32[7,128,512]{2,1,0:T(8,128)}, f32[7,128,512]{2,1,0:T(8,128)}) fusion(f32[8,128,512]{2,1,0:T(8,128)S(1)} %copy-done), kind=kLoop, calls=%fused_computation.104 | loop fusion | bytes 7340032 | tf_op jit(solution)/shard_map/slice | solution.py:67
  31.8 2.8 %fusion.37 = (f32[8,128,511]{2,1,0:T(8,128)}, f32[8,128,511]{2,1,0:T(8,128)}) fusion(f32[8,128,512]{2,1,0:T(8,128)S(1)} %copy-done), kind=kLoop, calls=%fused_computation.101 | loop fusion | bytes 8372224 | tf_op jit(solution)/shard_map/slice | solution.py:35
  34.6 2.5 %fusion.35 = (f32[8,127,512]{2,1,0:T(8,128)}, f32[8,127,512]{2,1,0:T(8,128)}) fusion(f32[8,128,512]{2,1,0:T(8,128)S(1)} %copy-done), kind=kLoop, calls=%fused_computation.99 | loop fusion | bytes 8323072 | tf_op jit(solution)/shard_map/slice | solution.py:33
  39.1 1.2 compare_and_fusion
  40.3 1.4 stack.9
  41.7 4.2 %copy.155 = f32[1,8,512,128]{3,1,2,0:T(8,128)} copy(f32[1,8,512,128]{3,2,1,0:T(8,128)} %stack.9) | data formatting | bytes 4194304 | tf_op jit(solution)/shard_map/stack | solution.py:105
  47.7 7.0 %fusion.4 = f32[8,128,512]{2,1,0:T(8,128)} fusion(f32[8,128,512]{2,1,0:T(8,128)S(1)} %copy-done, f32[1,128,512]{2,1,0:T(8,128)} %get-tuple-element.27, f32[7,128,512]{2,1,0:T(8,128)} %get-tuple-element.29, f32[7,128,512]{2,1,0:T(8,128)} %get-tuple-element.28, f32[1,128,512]{2,1,0:T(8,128)} %get-tuple-element.26, f32[8,128,511]{2,1,0:T(8,128)} %get-tuple-element.23, ...), kind=kLoop, calls=%fused_computation.15 | loop fusion | flops 13107200 | bytes 17039424 | tf_op jit(solution)/shard_map/add | solution.py:86
  54.7 1.6 stack.10
  56.3 1.2 copy.156
  57.9 2.2 pad_maximum_fusion
  60.2 2.9 %gather_fusion = f32[128,2,8,128]{3,2,1,0:T(8,128)S(1)} fusion(f32[2,8,512,128]{3,1,2,0:T(8,128)} %pad_maximum_fusion, s32[1024]{0:T(1024)S(1)} %pad_clamp_fusion), kind=kCustom, calls=%fused_computation | custom fusion | bytes 2097664 | tf_op jit(solution)/shard_map/jit(_take)/gather | solution.py:106
  63.9 1.0 fusion.19
  64.9 3.0 %copy.157 = f32[128,2,2048]{2,1,0:T(2,128)} copy(f32[128,2,2048]{2,0,1:T(8,128)S(1)} %fusion.19) | data formatting | bytes 4194304 | tf_op jit(solution)/shard_map/dot_general | solution.py:108
  67.9 9.8 %all-to-all-start.2 = ((f32[128,2,2048]{2,1,0:T(2,128)}), f32[128,2,2048]{2,1,0:T(2,128)S(1)}, u32[]{:S(2)}, u32[]{:S(2)}) async-start(f32[128,2,2048]{2,1,0:T(2,128)} %copy.157), calls=%async_computation.2 | async-start | bytes 4194304 | tf_op jit(solution)/shard_map/all_to_all | solution.py:114
  82.6 1.7 copy.185
  85.1 2.1 copy.140
  87.1 19.5 %all-to-all-done.2 = f32[128,2,2048]{2,1,0:T(2,128)S(1)} async-done(((f32[128,2,2048]{2,1,0:T(2,128)}), f32[128,2,2048]{2,1,0:T(2,128)S(1)}, u32[]{:S(2)}, u32[]{:S(2)}) %all-to-all-start.2) | async-done | bytes 2097184 | tf_op jit(solution)/shard_map/all_to_all | solution.py:114
  106.6 1.3 copy-done.1
  107.9 6.0 %all-to-all-start.1 = ((f32[8,128,384]{2,0,1:T(8,128)}), f32[8,128,384]{2,0,1:T(8,128)S(1)}, u32[]{:S(2)}, u32[]{:S(2)}) async-start(f32[8,128,384]{2,0,1:T(8,128)} %copy.140), calls=%async_computation.1 | async-start | bytes 3145728 | tf_op jit(solution)/shard_map/all_to_all | solution.py:55
  114.5 3.6 %all_to_all.15 = f32[256,2048]{1,0:T(8,128)} reshape(f32[128,2,2048]{2,1,0:T(2,128)} %copy-done.1) | data formatting | bytes 4194304 | tf_op jit(solution)/shard_map/all_to_all | solution.py:114
  118.1 2.9 %copy.158 = f32[2048,256]{1,0:T(8,128)} copy(f32[2048,256]{0,1:T(8,128)} %bitcast.114) | data formatting | bytes 4194304 | tf_op jit(solution)/shard_map/dot_general | solution.py:124
  121.0 2.9 %fusion.15 = f32[128,2,8,128]{3,0,2,1:T(8,128)S(1)} fusion(f32[2,8,128,256]{3,2,1,0:T(8,128)} %bitcast.113, s32[256]{0:T(256)S(1)} %select_n.83), kind=kOutput, calls=%fused_computation.56 | convolution fusion | flops 805339136 | bytes 3146752 | tf_op jit(solution)/shard_map/dot_general | solution.py:124
  123.9 4.4 %convolution_bitcast_fusion = f32[2,8,128,384]{2,3,1,0:T(8,128)} fusion(f32[128,2,8,128]{3,0,2,1:T(8,128)S(1)} %fusion.15, f32[128]{0:T(128)S(1)} %iota_convert_fusion, f32[384]{0:T(512)S(1)} %add_clamp_fusion), kind=kOutput, calls=%fused_computation.16 | convolution fusion | flops 1208156160 | bytes 4196352 | tf_op jit(solution)/shard_map/tald,de->alte/dot_general | solution.py:128
  128.3 9.1 %all-to-all-done.1 = f32[8,128,384]{2,0,1:T(8,128)S(1)} async-done(((f32[8,128,384]{2,0,1:T(8,128)}), f32[8,128,384]{2,0,1:T(8,128)S(1)}, u32[]{:S(2)}, u32[]{:S(2)}) %all-to-all-start.1) | async-done | bytes 1572896 | tf_op jit(solution)/shard_map/all_to_all | solution.py:55
  137.9 1.9 fusion.48
  139.8 1.2 fusion.49
  140.9 1.2 copy.177
  142.2 1.9 collective-permute-start.7
  144.1 1.2 copy.176
  145.3 2.7 %collective-permute-start.6 = (f32[8,128]{1,0:T(8,128)S(1)}, f32[8,128]{1,0:T(8,128)S(1)}, u32[]{:S(2)}, u32[]{:S(2)}) collective-permute-start(f32[8,128]{1,0:T(8,128)S(1)} %bitcast.141), channel_id=1, source_target_pairs={{1,0},{2,1},{3,2},{4,3},{5,4},{6,5},{7,6},{9,8},{10,9},{11,10},{12... | collective-permute-start | bytes 12296 | tf_op jit(solution)/shard_map/ppermute | solution.py:22
  148.1 2.3 %collective-permute-start.5 = (f32[8,384]{1,0:T(8,128)S(1)}, f32[8,384]{1,0:T(8,128)S(1)}, u32[]{:S(2)}, u32[]{:S(2)}) collective-permute-start(f32[8,384]{1,0:T(8,128)S(1)} %get-tuple-element.45), channel_id=1, source_target_pairs={{0,8},{8,16},{16,24},{24,32},{32,40},{40,48},{48,56},{56,64},{64,7... | collective-permute-start | bytes 36872 | tf_op jit(solution)/shard_map/ppermute | solution.py:22
  150.4 5.4 %collective-permute-start.4 = (f32[8,384]{1,0:T(8,128)S(1)}, f32[8,384]{1,0:T(8,128)S(1)}, u32[]{:S(2)}, u32[]{:S(2)}) collective-permute-start(f32[8,384]{1,0:T(8,128)S(1)} %get-tuple-element.44), channel_id=1, source_target_pairs={{8,0},{16,8},{24,16},{32,24},{40,32},{48,40},{56,48},{64,56},{72,6... | collective-permute-start | bytes 36872 | tf_op jit(solution)/shard_map/ppermute | solution.py:22
  155.7 2.2 fusion.47
  157.9 1.8 copy.145
  159.6 1.7 copy.143
  161.3 5.5 %add_divide_fusion.2 = f32[8,128,384]{1,2,0:T(8,128)S(1)} fusion(f32[8,128,384]{1,2,0:T(8,128)S(1)} %copy.151, f32[8,128,383]{1,2,0:T(8,128)} %get-tuple-element.47, f32[8,128,1]{1,2,0:T(1,128)S(1)} %bitcast.134, f32[8,128,1]{1,2,0:T(1,128)S(1)} %bitcast.137, f32[8,128,383]{1,2,0:T(8,128)} %get-tuple-element.46, f32[8,127,384]{1,2,0:T(8,128)} %get-tuple-element.43, ...), kind=kLoop, calls=%fused_computation.42 | loop fusion | flops 9437184 | bytes 12780096 | tf_op jit(solution)/shard_map/div | solution.py:139
  166.8 1.9 fusion.45
  168.7 1.3 slice_reduce_fusion.3
  170.0 3.4 %collective-permute-start.11 = (f32[8,128]{1,0:T(8,128)S(1)}, f32[8,128]{1,0:T(8,128)S(1)}, u32[]{:S(2)}, u32[]{:S(2)}) collective-permute-start(f32[8,128]{1,0:T(8,128)S(1)} %bitcast.144), channel_id=1, source_target_pairs={{0,1},{1,2},{2,3},{3,4},{4,5},{5,6},{6,7},{8,9},{9,10},{10,11},{11... | collective-permute-start | bytes 12296 | tf_op jit(solution)/shard_map/ppermute | solution.py:22
  173.4 1.9 collective-permute-start.10
  175.4 1.9 collective-permute-start.9
  177.3 5.5 %collective-permute-start.8 = (f32[8,384]{1,0:T(8,128)S(1)}, f32[8,384]{1,0:T(8,128)S(1)}, u32[]{:S(2)}, u32[]{:S(2)}) collective-permute-start(f32[8,384]{1,0:T(8,128)S(1)} %get-tuple-element.14), channel_id=1, source_target_pairs={{8,0},{16,8},{24,16},{32,24},{40,32},{48,40},{56,48},{64,56},{72,6... | collective-permute-start | bytes 36872 | tf_op jit(solution)/shard_map/ppermute | solution.py:22
  182.8 2.2 fusion.44
  184.9 1.8 copy.161
  186.7 1.7 copy.160
  188.4 5.5 %add_divide_fusion.1 = f32[8,128,384]{1,2,0:T(8,128)S(1)} fusion(f32[8,128,384]{1,2,0:T(8,128)S(1)} %add_divide_fusion.2, f32[8,128,383]{1,2,0:T(8,128)} %get-tuple-element.39, f32[8,128,1]{1,2,0:T(1,128)S(1)} %bitcast.138, f32[8,128,1]{1,2,0:T(1,128)S(1)} %bitcast.140, f32[8,128,383]{1,2,0:T(8,128)} %get-tuple-element.38, ...), kind=kLoop, calls=%fused_computation.41 | loop fusion | flops 9437184 | bytes 12780096 | tf_op jit(solution)/shard_map/div | solution.py:139
  193.9 1.4 fusion.42
  195.3 1.3 slice_reduce_fusion.1
  196.6 4.2 %collective-permute-start.15 = (f32[8,128]{1,0:T(8,128)S(1)}, f32[8,128]{1,0:T(8,128)S(1)}, u32[]{:S(2)}, u32[]{:S(2)}) collective-permute-start(f32[8,128]{1,0:T(8,128)S(1)} %bitcast.145), channel_id=1, source_target_pairs={{0,1},{1,2},{2,3},{3,4},{4,5},{5,6},{6,7},{8,9},{9,10},{10,11},{11... | collective-permute-start | bytes 12296 | tf_op jit(solution)/shard_map/ppermute | solution.py:22
  200.8 1.9 collective-permute-start.14
  202.7 1.9 collective-permute-start.13
  204.6 5.5 %collective-permute-start.12 = (f32[8,384]{1,0:T(8,128)S(1)}, f32[8,384]{1,0:T(8,128)S(1)}, u32[]{:S(2)}, u32[]{:S(2)}) collective-permute-start(f32[8,384]{1,0:T(8,128)S(1)} %get-tuple-element.12), channel_id=1, source_target_pairs={{8,0},{16,8},{24,16},{32,24},{40,32},{48,40},{56,48},{64,56},{72,6... | collective-permute-start | bytes 36872 | tf_op jit(solution)/shard_map/ppermute | solution.py:22
  210.1 2.2 fusion.41
  212.3 1.7 copy.165
  214.0 1.8 copy.164
  215.8 5.9 %add_divide_fusion = f32[8,128,384]{1,2,0:T(8,128)} fusion(f32[8,128,384]{1,2,0:T(8,128)S(1)} %add_divide_fusion.1, f32[8,128,383]{1,2,0:T(8,128)} %get-tuple-element.33, f32[8,128,1]{1,2,0:T(1,128)S(1)} %bitcast.135, f32[8,128,1]{1,2,0:T(1,128)S(1)} %bitcast.136, f32[8,128,383]{1,2,0:T(8,128)S(1)} %get-tuple-element.32, ...), kind=kLoop, calls=%fused_computation.40 | loop fusion | flops 9043968 | bytes 12780096 | tf_op jit(solution)/shard_map/div | solution.py:139
  221.7 3.0 %copy.168 = f32[8,128,384]{2,1,0:T(8,128)} copy(f32[8,128,384]{1,2,0:T(8,128)} %add_divide_fusion) | data formatting | bytes 3145728
  (85 shorter events, 9.2 us)
Async XLA Ops:
  0.6 7.6 %copy-start = (f32[8,128,512]{2,1,0:T(8,128)S(1)}, f32[8,128,512]{2,1,0:T(8,128)}, u32[]{:S(2)}) copy-start(f32[8,128,512]{2,1,0:T(8,128)} %param.9) | copy-start | bytes 6291460
  2.4 43.5 %collective-permute-start.3 = (f32[8,128]{1,0:T(8,128)S(1)}, f32[8,128]{1,0:T(8,128)S(1)}, u32[]{:S(2)}, u32[]{:S(2)}) collective-permute-start(f32[8,128]{1,0:T(8,128)S(1)} %bitcast.130), channel_id=1, source_target_pairs={{0,1},{1,2},{2,3},{3,4},{4,5},{5,6},{6,7},{8,9},{9,10},{10,11},{11... | collective-permute-start | bytes 12296 | tf_op jit(solution)/shard_map/ppermute | solution.py:22
  6.3 39.7 %collective-permute-start.2 = (f32[8,128]{1,0:T(8,128)S(1)}, f32[8,128]{1,0:T(8,128)S(1)}, u32[]{:S(2)}, u32[]{:S(2)}) collective-permute-start(f32[8,128]{1,0:T(8,128)S(1)} %bitcast.132), channel_id=1, source_target_pairs={{1,0},{2,1},{3,2},{4,3},{5,4},{6,5},{7,6},{9,8},{10,9},{11,10},{12... | collective-permute-start | bytes 12296 | tf_op jit(solution)/shard_map/ppermute | solution.py:22
  8.3 39.3 %collective-permute-start.1 = (f32[8,512]{1,0:T(8,128)S(1)}, f32[8,512]{1,0:T(8,128)S(1)}, u32[]{:S(2)}, u32[]{:S(2)}) collective-permute-start(f32[8,512]{1,0:T(8,128)S(1)} %bitcast.120), channel_id=1, source_target_pairs={{0,8},{8,16},{16,24},{24,32},{32,40},{40,48},{48,56},{56,64},{64,7... | collective-permute-start | bytes 49160 | tf_op jit(solution)/shard_map/ppermute | solution.py:22
  11.5 36.2 %collective-permute-start = (f32[8,512]{1,0:T(8,128)S(1)}, f32[8,512]{1,0:T(8,128)S(1)}, u32[]{:S(2)}, u32[]{:S(2)}) collective-permute-start(f32[8,512]{1,0:T(8,128)S(1)} %bitcast.122), channel_id=1, source_target_pairs={{8,0},{16,8},{24,16},{32,24},{40,32},{48,40},{56,48},{64,56},{72,6... | collective-permute-start | bytes 49160 | tf_op jit(solution)/shard_map/ppermute | solution.py:22
  19.2 48.7 %all-to-all-start = ((f32[8,128,384]{2,0,1:T(8,128)}), f32[8,128,384]{2,0,1:T(8,128)}, u32[]{:S(2)}, u32[]{:S(2)}) async-start(f32[8,128,384]{2,0,1:T(8,128)} %copy.138), calls=%async_computation | async-start | bytes 3145728 | tf_op jit(solution)/shard_map/all_to_all | solution.py:50
  34.6 2.5 %copy-start.10 = (f32[2,8]{1,0:T(2,128)S(1)}, f32[2,8]{1,0:T(2,128)}, u32[]{:S(2)}) copy-start(f32[2,8]{1,0:T(2,128)} %param.13) | copy-start | bytes 196
  34.6 2.5 %copy-start.3 = (bf16[128,512]{1,0:T(8,128)(2,1)S(1)}, bf16[128,512]{1,0:T(8,128)(2,1)}, u32[]{:S(2)}) copy-start(bf16[128,512]{1,0:T(8,128)(2,1)} %param.10) | copy-start | bytes 393220
  34.6 3.3 %copy-start.5 = (s32[16384,1]{0,1:T(1,128)S(1)}, s32[16384,1]{0,1:T(1,128)}, u32[]{:S(2)}) copy-start(s32[16384,1]{0,1:T(1,128)} %param.14) | copy-start | bytes 196612
  46.1 0.6 copy-start.7
  56.3 1.6 copy-start.2
  60.2 2.9 %copy-start.12 = (pred[128]{0:T(512)(128)(4,1)S(1)}, pred[128]{0:T(512)(128)(4,1)}, u32[]{:S(2)}) copy-start(pred[128]{0:T(512)(128)(4,1)} %compare_and_fusion) | copy-start | bytes 388
  63.3 0.6 copy-start.8
  63.3 0.6 copy-start.9
  67.9 9.8 %copy-start.11 = (s32[2,4]{1,0:T(2,128)S(1)}, s32[2,4]{1,0:T(2,128)}, u32[]{:S(2)}) copy-start(s32[2,4]{1,0:T(2,128)} %param.17) | copy-start | bytes 100
  67.9 14.6 %copy-start.6 = (s32[16384]{0:T(1024)S(1)}, s32[16384]{0:T(1024)}, u32[]{:S(2)}) copy-start(s32[16384]{0:T(1024)} %param.16) | copy-start | bytes 196612
  67.9 38.7 %all-to-all-start.2 = ((f32[128,2,2048]{2,1,0:T(2,128)}), f32[128,2,2048]{2,1,0:T(2,128)S(1)}, u32[]{:S(2)}, u32[]{:S(2)}) async-start(f32[128,2,2048]{2,1,0:T(2,128)} %copy.157), calls=%async_computation.2 | async-start | bytes 4194304 | tf_op jit(solution)/shard_map/all_to_all | solution.py:114
  87.1 27.1 %copy-start.4 = (bf16[128,384]{1,0:T(8,128)(2,1)S(1)}, bf16[128,384]{1,0:T(8,128)(2,1)}, u32[]{:S(2)}) copy-start(bf16[128,384]{1,0:T(8,128)(2,1)} %param.12) | copy-start | bytes 294916
  106.6 1.3 copy-start.1
  107.9 29.4 %all-to-all-start.1 = ((f32[8,128,384]{2,0,1:T(8,128)}), f32[8,128,384]{2,0,1:T(8,128)S(1)}, u32[]{:S(2)}, u32[]{:S(2)}) async-start(f32[8,128,384]{2,0,1:T(8,128)} %copy.140), calls=%async_computation.1 | async-start | bytes 3145728 | tf_op jit(solution)/shard_map/all_to_all | solution.py:55
  142.2 19.1 %collective-permute-start.7 = (f32[8,128]{1,0:T(8,128)S(1)}, f32[8,128]{1,0:T(8,128)S(1)}, u32[]{:S(2)}, u32[]{:S(2)}) collective-permute-start(f32[8,128]{1,0:T(8,128)S(1)} %bitcast.139), channel_id=1, source_target_pairs={{0,1},{1,2},{2,3},{3,4},{4,5},{5,6},{6,7},{8,9},{9,10},{10,11},{11... | collective-permute-start | bytes 12296 | tf_op jit(solution)/shard_map/ppermute | solution.py:22
  145.3 16.0 %collective-permute-start.6 = (f32[8,128]{1,0:T(8,128)S(1)}, f32[8,128]{1,0:T(8,128)S(1)}, u32[]{:S(2)}, u32[]{:S(2)}) collective-permute-start(f32[8,128]{1,0:T(8,128)S(1)} %bitcast.141), channel_id=1, source_target_pairs={{1,0},{2,1},{3,2},{4,3},{5,4},{6,5},{7,6},{9,8},{10,9},{11,10},{12... | collective-permute-start | bytes 12296 | tf_op jit(solution)/shard_map/ppermute | solution.py:22
  148.1 9.8 %collective-permute-start.5 = (f32[8,384]{1,0:T(8,128)S(1)}, f32[8,384]{1,0:T(8,128)S(1)}, u32[]{:S(2)}, u32[]{:S(2)}) collective-permute-start(f32[8,384]{1,0:T(8,128)S(1)} %get-tuple-element.45), channel_id=1, source_target_pairs={{0,8},{8,16},{16,24},{24,32},{32,40},{40,48},{48,56},{56,64},{64,7... | collective-permute-start | bytes 36872 | tf_op jit(solution)/shard_map/ppermute | solution.py:22
  150.4 9.3 %collective-permute-start.4 = (f32[8,384]{1,0:T(8,128)S(1)}, f32[8,384]{1,0:T(8,128)S(1)}, u32[]{:S(2)}, u32[]{:S(2)}) collective-permute-start(f32[8,384]{1,0:T(8,128)S(1)} %get-tuple-element.44), channel_id=1, source_target_pairs={{8,0},{16,8},{24,16},{32,24},{40,32},{48,40},{56,48},{64,56},{72,6... | collective-permute-start | bytes 36872 | tf_op jit(solution)/shard_map/ppermute | solution.py:22
  170.0 18.3 %collective-permute-start.11 = (f32[8,128]{1,0:T(8,128)S(1)}, f32[8,128]{1,0:T(8,128)S(1)}, u32[]{:S(2)}, u32[]{:S(2)}) collective-permute-start(f32[8,128]{1,0:T(8,128)S(1)} %bitcast.144), channel_id=1, source_target_pairs={{0,1},{1,2},{2,3},{3,4},{4,5},{5,6},{6,7},{8,9},{9,10},{10,11},{11... | collective-permute-start | bytes 12296 | tf_op jit(solution)/shard_map/ppermute | solution.py:22
  173.4 14.9 %collective-permute-start.10 = (f32[8,128]{1,0:T(8,128)S(1)}, f32[8,128]{1,0:T(8,128)S(1)}, u32[]{:S(2)}, u32[]{:S(2)}) collective-permute-start(f32[8,128]{1,0:T(8,128)S(1)} %bitcast.142), channel_id=1, source_target_pairs={{1,0},{2,1},{3,2},{4,3},{5,4},{6,5},{7,6},{9,8},{10,9},{11,10},{12... | collective-permute-start | bytes 12296 | tf_op jit(solution)/shard_map/ppermute | solution.py:22
  175.4 9.6 %collective-permute-start.9 = (f32[8,384]{1,0:T(8,128)S(1)}, f32[8,384]{1,0:T(8,128)S(1)}, u32[]{:S(2)}, u32[]{:S(2)}) collective-permute-start(f32[8,384]{1,0:T(8,128)S(1)} %get-tuple-element.15), channel_id=1, source_target_pairs={{0,8},{8,16},{16,24},{24,32},{32,40},{40,48},{48,56},{56,64},{64,7... | collective-permute-start | bytes 36872 | tf_op jit(solution)/shard_map/ppermute | solution.py:22
  177.3 9.4 %collective-permute-start.8 = (f32[8,384]{1,0:T(8,128)S(1)}, f32[8,384]{1,0:T(8,128)S(1)}, u32[]{:S(2)}, u32[]{:S(2)}) collective-permute-start(f32[8,384]{1,0:T(8,128)S(1)} %get-tuple-element.14), channel_id=1, source_target_pairs={{8,0},{16,8},{24,16},{32,24},{40,32},{48,40},{56,48},{64,56},{72,6... | collective-permute-start | bytes 36872 | tf_op jit(solution)/shard_map/ppermute | solution.py:22
  196.6 19.2 %collective-permute-start.15 = (f32[8,128]{1,0:T(8,128)S(1)}, f32[8,128]{1,0:T(8,128)S(1)}, u32[]{:S(2)}, u32[]{:S(2)}) collective-permute-start(f32[8,128]{1,0:T(8,128)S(1)} %bitcast.145), channel_id=1, source_target_pairs={{0,1},{1,2},{2,3},{3,4},{4,5},{5,6},{6,7},{8,9},{9,10},{10,11},{11... | collective-permute-start | bytes 12296 | tf_op jit(solution)/shard_map/ppermute | solution.py:22
  200.8 15.0 %collective-permute-start.14 = (f32[8,128]{1,0:T(8,128)S(1)}, f32[8,128]{1,0:T(8,128)S(1)}, u32[]{:S(2)}, u32[]{:S(2)}) collective-permute-start(f32[8,128]{1,0:T(8,128)S(1)} %bitcast.143), channel_id=1, source_target_pairs={{1,0},{2,1},{3,2},{4,3},{5,4},{6,5},{7,6},{9,8},{10,9},{11,10},{12... | collective-permute-start | bytes 12296 | tf_op jit(solution)/shard_map/ppermute | solution.py:22
  202.7 9.6 %collective-permute-start.13 = (f32[8,384]{1,0:T(8,128)S(1)}, f32[8,384]{1,0:T(8,128)S(1)}, u32[]{:S(2)}, u32[]{:S(2)}) collective-permute-start(f32[8,384]{1,0:T(8,128)S(1)} %get-tuple-element.13), channel_id=1, source_target_pairs={{0,8},{8,16},{16,24},{24,32},{32,40},{40,48},{48,56},{56,64},{64,7... | collective-permute-start | bytes 36872 | tf_op jit(solution)/shard_map/ppermute | solution.py:22
  204.6 9.3 %collective-permute-start.12 = (f32[8,384]{1,0:T(8,128)S(1)}, f32[8,384]{1,0:T(8,128)S(1)}, u32[]{:S(2)}, u32[]{:S(2)}) collective-permute-start(f32[8,384]{1,0:T(8,128)S(1)} %get-tuple-element.12), channel_id=1, source_target_pairs={{8,0},{16,8},{24,16},{32,24},{40,32},{48,40},{56,48},{64,56},{72,6... | collective-permute-start | bytes 36872 | tf_op jit(solution)/shard_map/ppermute | solution.py:22

commit v4 on v3

--- a/solution.py
+++ b/solution.py
@@ -2,6 +2,9 @@
 import jax.numpy as jnp
 from jax import lax
 from jax.sharding import PartitionSpec as P
+from jax.experimental import pallas as pl
+from jax.experimental.pallas import tpu as pltpu
+import functools
 
 SUBSTEPS = 3
 STRIP = 128
@@ -53,6 +56,61 @@
     grid = jnp.roll(grid, storm_shift[0, piece], axis=1)
     grid = jnp.roll(grid, storm_shift[1, piece], axis=2)
     return lax.all_to_all(grid.reshape(levels, crows, widths), ("gx", "gy"), 1, 1, tiled=True)
+
+
+def substep_kernel(weight, wind_ref, child_ref, bx_ref, ax_ref, by_ref, ay_ref, bound_ref,
+                   factor_ref, divisor_ref, out_ref, first_row_ref, last_row_ref, first_col_ref, last_col_ref):
+    levels, rows, cols = child_ref.shape
+    row_id = lax.broadcasted_iota(jnp.int32, (rows, cols), 0)
+    col_id = lax.broadcasted_iota(jnp.int32, (rows, cols), 1)
+    factor = factor_ref[...]
+    divisor = divisor_ref[...]
+    for l in range(levels):
+        c = child_ref[l]
+        north = jnp.where(row_id == rows - 1, ax_ref[l:l + 1, :], pltpu.roll(c, rows - 1, 0))
+        south = jnp.where(row_id == 0, bx_ref[l:l + 1, :], pltpu.roll(c, 1, 0))
+        east = jnp.where(col_id == cols - 1, ay_ref[:, l:l + 1], pltpu.roll(c, cols - 1, 1))
+        west = jnp.where(col_id == 0, by_ref[:, l:l + 1], pltpu.roll(c, 1, 1))
+        laplace = north + south + east + west - 4.0 * c
+        tend = KAPPA * laplace - wind_ref[0, l] * (0.5 * (north - south)) - wind_ref[1, l] * (0.5 * (east - west))
+        b0 = bound_ref[0, l]
+        target = b0 + weight * (bound_ref[1, l] - b0)
+        new = (c + factor * tend + NUDGE * target) / divisor
+        out_ref[l] = new
+        first_row_ref[l:l + 1, :] = new[0:1, :]
+        last_row_ref[l:l + 1, :] = new[rows - 1:rows, :]
+        first_col_ref[:, l:l + 1] = new[:, 0:1]
+        last_col_ref[:, l:l + 1] = new[:, cols - 1:cols]
+
+
+def substep(weight, wind, child, bx, ax, by, ay, bound, factor, divisor):
+    levels, rows, cols = child.shape
+    vmem = pl.BlockSpec(memory_space=pltpu.VMEM)
+    smem = pl.BlockSpec(memory_space=pltpu.SMEM)
+    f32 = jnp.float32
+    return pl.pallas_call(
+        functools.partial(substep_kernel, weight),
+        out_shape=(
+            jax.ShapeDtypeStruct((levels, rows, cols), f32),
+            jax.ShapeDtypeStruct((levels, cols), f32),
+            jax.ShapeDtypeStruct((levels, cols), f32),
+            jax.ShapeDtypeStruct((rows, levels), f32),
+            jax.ShapeDtypeStruct((rows, levels), f32),
+        ),
+        in_specs=[smem] + [vmem] * 8,
+        out_specs=(vmem,) * 5,
+        cost_estimate=pl.CostEstimate(
+            flops=30 * levels * rows * cols, transcendentals=0,
+            bytes_accessed=4 * (4 * levels * rows * cols + 2 * rows * cols)),
+    )(wind, child, bx, ax, by, ay, bound, factor, divisor)
+
+
+def swap_edge(edge, axis, forward):
+    count = lax.axis_size(axis)
+    pairs = [(i, i + 1) for i in range(count - 1)]
+    if not forward:
+        pairs = [(target, source) for source, target in pairs]
+    return lax.ppermute(edge, axis, pairs)
 
 
 def refine_table(strip):
@@ -131,14 +189,19 @@
         refine_table(STRIP),
         precision=lax.Precision.HIGHEST,
     )
-    divisor = 1.0 + NUDGE * counts[None, :, None]
+    divisor = jnp.broadcast_to(1.0 + NUDGE * counts[:, None], (crows, widths))
     factor = 1.0 + child_sppt.astype(jnp.float32)
-    for substep in range(SUBSTEPS):
-        weight = (substep + 1) / 3.0
-        target_value = boundary[0] + weight * (boundary[1] - boundary[0])
-        child = (
-            child + factor * halo_tendency(child, wind_x, wind_y) + NUDGE * target_value
-        ) / divisor
+    edges = (child[:, 0, :], child[:, -1, :], child[:, :, 0].T, child[:, :, -1].T)
+    for substep_index in range(SUBSTEPS):
+        first_row, last_row, first_col, last_col = edges
+        before_x = swap_edge(last_row, "gx", True)
+        after_x = swap_edge(first_row, "gx", False)
+        before_y = swap_edge(last_col, "gy", True)
+        after_y = swap_edge(first_col, "gy", False)
+        weight = (substep_index + 1) / 3.0
+        child, *edges = substep(
+            weight, wind, child, before_x, after_x, before_y, after_y, boundary, factor, divisor
+        )
     return (new_parent, child)
 
 

time: 226 us -> 212 us (0.938)
  local copies, waits for them, and re-layouts: 75.5 us -> 49.3 us
  Pallas kernels: 0 us -> 18 us
  other arithmetic: 30.8 us -> 15.2 us
  waiting for transfers between devices: 28.6 us -> 39.9 us
    ppermute x16 -> x4, starting transfers between devices: 51.6 us -> 13.1 us  [swap(): return lax.ppermute(edge, axis, pairs)]
    ppermute x0 -> x12, starting transfers between devices: none -> 37.1 us  [swap_edge(): return lax.ppermute(edge, axis, pairs)]
    pallas_call x0 -> x3, Pallas kernels: none -> 18 us  [substep(): pl.pallas_call(functools.partial(substep_kernel, weight), out_shape=(jax....]
    div x3 -> x0, other arithmetic: 16.9 us -> none  [shards(): (child + factor * halo_tendency(child, wind_x, wind_y) + NUDGE * target_v...]
    ppermute x0 -> x12, waiting for transfers between devices: none -> 7.5 us  [swap_edge(): return lax.ppermute(edge, axis, pairs)]
    slice x4 -> x1, local copies, waits for them, and re-layouts: 9.01 us -> 2.52 us  [halo_tendency(): north = jnp.concatenate([block[:, 1:, :], after_x[:, None, :]], axis=1)]
    broadcast_in_dim x4 -> x1, local copies, waits for them, and re-layouts: 5.22 us -> 0.02 us  [halo_tendency(): south = jnp.concatenate([before_x[:, None, :], block[:, :-1, :]], axis=1)]
    slice x4 -> x1, local copies, waits for them, and re-layouts: 7.96 us -> 2.77 us  [halo_tendency(): east = jnp.concatenate([block[:, :, 1:], after_y[:, :, None]], axis=2)]
  transfers between devices with their start and end apart: 19 -> 19, of which waited for: 2 -> 4; matrix products, arithmetic and copies ran while one was open for 34% -> 30% of each run, Pallas kernels for 0% -> 0%
where the time goes in v4:
time: 212 us; the launch traced here: 211 us
  starting transfers between devices  75.2 us (35%)
  local copies, waits for them, and re-layouts  49.3 us (23%)
  waiting for transfers between devices  39.9 us (19%)
  Pallas kernels  18 us (8%)
  other arithmetic  15.2 us (7%)
  matrix products  8.24 us (4%)
  between operations  4.89 us (2%)
    ppermute x12, starting transfers between devices, swap_edge(): return lax.ppermute(edge, axis, pairs)  37.1 us
    all_to_all x1, waiting for transfers between devices, shards(): lax.all_to_all(outgoing_strips, ('gx', 'gy'), split_axis=0, concat_axis=0...  19.9 us
    pallas_call x3, Pallas kernels, substep(): pl.pallas_call(functools.partial(substep_kernel, weight), out_shape=(jax....  18 us
    ppermute x4, starting transfers between devices, swap(): return lax.ppermute(edge, axis, pairs)  13.1 us
    all_to_all x1, waiting for transfers between devices, storm_rows(): lax.all_to_all(grid.reshape(levels, crows, widths), ('gx', 'gy'), 1, 1, t...  12.5 us
    all_to_all x1, starting transfers between devices, shards(): lax.all_to_all(outgoing_strips, ('gx', 'gy'), split_axis=0, concat_axis=0...  9.77 us
    unnamed x55, local copies, waits for them, and re-layouts  9.75 us
    all_to_all x1, starting transfers between devices, storm_rows(): gathered = lax.all_to_all(child, ('gx', 'gy'), 1, 1, tiled=True)  9.24 us
  transfers between devices with their start and end apart: 19, of which 4 were waited for; matrix products, arithmetic and copies ran while one was open for 30% of the time, Pallas kernels for 0%

profile of v4, /device:TPU:33, one launch (start us, length us, event | category | flops | bytes accessed | tf_op | source)
XLA Modules:
  0.0 210.8 jit_solution(7150439943445438597)
XLA Ops:
  0.6 1.6 fusion.36
  2.4 3.8 %collective-permute-start.3 = (f32[8,128]{1,0:T(8,128)S(1)}, f32[8,128]{1,0:T(8,128)S(1)}, u32[]{:S(2)}, u32[]{:S(2)}) collective-permute-start(f32[8,128]{1,0:T(8,128)S(1)} %bitcast.77), channel_id=1, source_target_pairs={{0,1},{1,2},{2,3},{3,4},{4,5},{5,6},{6,7},{8,9},{9,10},{10,11},{11... | collective-permute-start | bytes 12296 | tf_op jit(solution)/shard_map/ppermute | solution.py:25
  6.3 1.9 collective-permute-start.2
  8.3 3.1 %collective-permute-start.1 = (f32[8,512]{1,0:T(8,128)S(1)}, f32[8,512]{1,0:T(8,128)S(1)}, u32[]{:S(2)}, u32[]{:S(2)}) collective-permute-start(f32[8,512]{1,0:T(8,128)S(1)} %bitcast.73), channel_id=1, source_target_pairs={{0,8},{8,16},{16,24},{24,32},{32,40},{40,48},{48,56},{56,64},{64,7... | collective-permute-start | bytes 49160 | tf_op jit(solution)/shard_map/ppermute | solution.py:25
  11.5 4.3 %collective-permute-start = (f32[8,512]{1,0:T(8,128)S(1)}, f32[8,512]{1,0:T(8,128)S(1)}, u32[]{:S(2)}, u32[]{:S(2)}) collective-permute-start(f32[8,512]{1,0:T(8,128)S(1)} %bitcast.75), channel_id=1, source_target_pairs={{8,0},{16,8},{24,16},{32,24},{40,32},{48,40},{56,48},{64,56},{72,6... | collective-permute-start | bytes 49160 | tf_op jit(solution)/shard_map/ppermute | solution.py:25
  15.7 3.5 %copy.95 = f32[8,128,384]{2,0,1:T(8,128)} copy(f32[8,128,384]{2,1,0:T(8,128)} %param.11) | data formatting | bytes 3145728 | tf_op args[2]
  19.2 9.2 %all-to-all-start = ((f32[8,128,384]{2,0,1:T(8,128)}), f32[8,128,384]{2,0,1:T(8,128)}, u32[]{:S(2)}, u32[]{:S(2)}) async-start(f32[8,128,384]{2,0,1:T(8,128)} %copy.95), calls=%async_computation | async-start | bytes 3145728 | tf_op jit(solution)/shard_map/all_to_all | solution.py:53
  28.5 0.8 fusion.37
  29.3 2.5 %fusion.38 = (f32[7,128,512]{2,1,0:T(8,128)}, f32[7,128,512]{2,1,0:T(8,128)}) fusion(f32[8,128,512]{2,1,0:T(8,128)S(1)} %copy-done), kind=kLoop, calls=%fused_computation.80 | loop fusion | bytes 7340032 | tf_op jit(solution)/shard_map/slice | solution.py:125
  31.8 2.8 %fusion.35 = (f32[8,128,511]{2,1,0:T(8,128)}, f32[8,128,511]{2,1,0:T(8,128)}) fusion(f32[8,128,512]{2,1,0:T(8,128)S(1)} %copy-done), kind=kLoop, calls=%fused_computation.77 | loop fusion | bytes 8372224 | tf_op jit(solution)/shard_map/slice | solution.py:38
  34.5 2.5 %fusion.33 = (f32[8,127,512]{2,1,0:T(8,128)}, f32[8,127,512]{2,1,0:T(8,128)}) fusion(f32[8,128,512]{2,1,0:T(8,128)S(1)} %copy-done), kind=kLoop, calls=%fused_computation.75 | loop fusion | bytes 8323072 | tf_op jit(solution)/shard_map/slice | solution.py:36
  37.1 0.6 multiply_bitcast_fusion.1
  37.7 0.7 fusion.27
  38.6 0.5 fusion.28
  39.1 0.6 multiply_add_fusion
  39.7 1.2 compare_and_fusion
  40.9 1.4 stack.9
  42.3 4.1 %copy.104 = f32[1,8,512,128]{3,1,2,0:T(8,128)} copy(f32[1,8,512,128]{3,2,1,0:T(8,128)} %stack.9) | data formatting | bytes 4194304 | tf_op jit(solution)/shard_map/stack | solution.py:163
  47.0 7.0 %fusion.4 = f32[8,128,512]{2,1,0:T(8,128)} fusion(f32[8,128,512]{2,1,0:T(8,128)S(1)} %copy-done, f32[1,128,512]{2,1,0:T(8,128)} %get-tuple-element.35, f32[7,128,512]{2,1,0:T(8,128)} %get-tuple-element.37, f32[7,128,512]{2,1,0:T(8,128)} %get-tuple-element.36, f32[1,128,512]{2,1,0:T(8,128)} %get-tuple-element.34, f32[8,128,511]{2,1,0:T(8,128)} %get-tuple-element.31, ...), kind=kLoop, calls=%fused_computation.15 | loop fusion | flops 13107200 | bytes 17039424 | tf_op jit(solution)/shard_map/add | solution.py:144
  54.0 1.6 stack.10
  55.7 1.2 copy.105
  56.9 0.4 copy-done.2
  57.3 2.2 %pad_maximum_fusion = f32[2,8,512,128]{3,1,2,0:T(8,128)} fusion(f32[1,8,512,128]{3,1,2,0:T(8,128)S(1)} %copy.105, f32[1,8,512,128]{3,1,2,0:T(8,128)S(1)} %copy-done.2), kind=kLoop, calls=%fused_computation.1 | loop fusion | flops 1048576 | bytes 8388608 | tf_op jit(solution)/shard_map/stack | solution.py:163
  59.5 2.9 %gather_fusion = f32[128,2,8,128]{3,2,1,0:T(8,128)S(1)} fusion(f32[2,8,512,128]{3,1,2,0:T(8,128)} %pad_maximum_fusion, s32[1024]{0:T(1024)S(1)} %pad_clamp_fusion), kind=kCustom, calls=%fused_computation | custom fusion | bytes 2097664 | tf_op jit(solution)/shard_map/jit(_take)/gather | solution.py:164
  63.1 1.0 fusion.17
  64.1 3.0 %copy.106 = f32[128,2,2048]{2,1,0:T(2,128)} copy(f32[128,2,2048]{2,0,1:T(8,128)S(1)} %fusion.17) | data formatting | bytes 4194304 | tf_op jit(solution)/shard_map/dot_general | solution.py:166
  67.1 9.8 %all-to-all-start.2 = ((f32[128,2,2048]{2,1,0:T(2,128)}), f32[128,2,2048]{2,1,0:T(2,128)S(1)}, u32[]{:S(2)}, u32[]{:S(2)}) async-start(f32[128,2,2048]{2,1,0:T(2,128)} %copy.106), calls=%async_computation.2 | async-start | bytes 4194304 | tf_op jit(solution)/shard_map/all_to_all | solution.py:172
  76.9 0.6 constant_dynamic-slice_fusion.2
  81.4 1.7 copy.96
  83.4 0.4 fusion.5
  83.8 2.1 copy.98
  85.9 19.9 %all-to-all-done.2 = f32[128,2,2048]{2,1,0:T(2,128)S(1)} async-done(((f32[128,2,2048]{2,1,0:T(2,128)}), f32[128,2,2048]{2,1,0:T(2,128)S(1)}, u32[]{:S(2)}, u32[]{:S(2)}) %all-to-all-start.2) | async-done | bytes 2097184 | tf_op jit(solution)/shard_map/all_to_all | solution.py:172
  105.8 1.4 copy-done.1
  107.2 6.0 %all-to-all-start.1 = ((f32[8,128,384]{2,0,1:T(8,128)}), f32[8,128,384]{2,0,1:T(8,128)S(1)}, u32[]{:S(2)}, u32[]{:S(2)}) async-start(f32[8,128,384]{2,0,1:T(8,128)} %bitcast.66), calls=%async_computation.1 | async-start | bytes 3145728 | tf_op jit(solution)/shard_map/all_to_all | solution.py:58
  113.9 0.7 convert_add_fusion.1.factor_ref
  114.6 3.7 %all_to_all.15 = f32[256,2048]{1,0:T(8,128)} reshape(f32[128,2,2048]{2,1,0:T(2,128)} %copy-done.1) | data formatting | bytes 4194304 | tf_op jit(solution)/shard_map/all_to_all | solution.py:172
  118.3 2.9 %copy.107 = f32[2048,256]{1,0:T(8,128)} copy(f32[2048,256]{0,1:T(8,128)} %bitcast.65) | data formatting | bytes 4194304 | tf_op jit(solution)/shard_map/dot_general | solution.py:182
  121.2 2.9 %fusion.13 = f32[128,2,8,128]{3,0,2,1:T(8,128)S(1)} fusion(f32[2,8,128,256]{3,2,1,0:T(8,128)} %bitcast.64, s32[256]{0:T(256)S(1)} %select_n.83), kind=kOutput, calls=%fused_computation.32 | convolution fusion | flops 805339136 | bytes 3146752 | tf_op jit(solution)/shard_map/dot_general | solution.py:182
  124.1 12.5 %all-to-all-done.1 = f32[8,128,384]{2,0,1:T(8,128)S(1)} async-done(((f32[8,128,384]{2,0,1:T(8,128)}), f32[8,128,384]{2,0,1:T(8,128)S(1)}, u32[]{:S(2)}, u32[]{:S(2)}) %all-to-all-start.1) | async-done | bytes 1572896 | tf_op jit(solution)/shard_map/all_to_all | solution.py:58
  136.6 2.5 %collective-permute-start.4 = (f32[8,384]{1,0:T(8,128)S(1)}, f32[8,384]{1,0:T(8,128)S(1)}, u32[]{:S(2)}, u32[]{:S(2)}) collective-permute-start(f32[8,384]{1,0:T(8,128)S(1)} %get-tuple-element.41), channel_id=1, source_target_pairs={{0,8},{8,16},{16,24},{24,32},{32,40},{40,48},{48,56},{56,64},{64,7... | collective-permute-start | bytes 36872 | tf_op jit(solution)/shard_map/ppermute | solution.py:113
  139.0 4.9 %collective-permute-start.5 = (f32[8,384]{1,0:T(8,128)S(1)}, f32[8,384]{1,0:T(8,128)S(1)}, u32[]{:S(2)}, u32[]{:S(2)}) collective-permute-start(f32[8,384]{1,0:T(8,128)S(1)} %get-tuple-element.40), channel_id=1, source_target_pairs={{8,0},{16,8},{24,16},{32,24},{40,32},{48,40},{56,48},{64,56},{72,6... | collective-permute-start | bytes 36872 | tf_op jit(solution)/shard_map/ppermute | solution.py:113
  143.9 1.0 fusion.39
  144.9 1.8 copy.119
  146.8 2.3 %collective-permute-start.6 = (f32[128,8]{1,0:T(8,128)S(1)}, f32[128,8]{1,0:T(8,128)S(1)}, u32[]{:S(2)}, u32[]{:S(2)}) collective-permute-start(f32[128,8]{1,0:T(8,128)S(1)} %bitcast.70), channel_id=1, source_target_pairs={{0,1},{1,2},{2,3},{3,4},{4,5},{5,6},{6,7},{8,9},{9,10},{10,11},{11... | collective-permute-start | bytes 12296 | tf_op jit(solution)/shard_map/ppermute | solution.py:113
  149.1 0.8 copy.120
  149.9 3.0 %collective-permute-start.7 = (f32[128,8]{1,0:T(8,128)S(1)}, f32[128,8]{1,0:T(8,128)S(1)}, u32[]{:S(2)}, u32[]{:S(2)}) collective-permute-start(f32[128,8]{1,0:T(8,128)S(1)} %bitcast.71), channel_id=1, source_target_pairs={{1,0},{2,1},{3,2},{4,3},{5,4},{6,5},{7,6},{9,8},{10,9},{11,10},{12... | collective-permute-start | bytes 12296 | tf_op jit(solution)/shard_map/ppermute | solution.py:113
  152.9 4.4 %convolution_bitcast_fusion.bound_ref = f32[2,8,128,384]{3,2,1,0:T(8,128)} fusion(f32[128,2,8,128]{3,0,2,1:T(8,128)S(1)} %fusion.13, f32[128]{0:T(128)S(1)} %iota_convert_fusion, f32[384]{0:T(512)S(1)} %add_clamp_fusion), kind=kOutput, calls=%fused_computation.16 | convolution fusion | flops 1208156160 | bytes 4196352 | tf_op jit(solution)/shard_map/tald,de->alte/dot_general | solution.py:186
  157.2 1.4 copy.110.child_ref
  158.7 0.8 broadcast_in_dim.69.divisor_ref
  159.5 6.0 %shard_map.104 = (f32[8,128,384]{2,1,0:T(8,128)}, f32[8,384]{1,0:T(8,128)}, f32[8,384]{1,0:T(8,128)}, f32[128,8]{1,0:T(8,128)}, f32[128,8]{1,0:T(8,128)}) custom-call(f32[2,8]{1,0:T(2,128)} %wind_ref.5, f32[8,128,384]{2,1,0:T(8,128)} %copy.110.child_ref, f32[8,384]{1,0:T(8,128)} %copy-done.14, f32[8,384]{1,0:T(8,128)} %copy-done.15, f32[128,8]{1,0:T(8,128)} %copy-done.6, ...), custom_call_target="tpu_custom_call" | custom-call | flops 11796480 | bytes 6684672 | tf_op jit(solution)/shard_map/pallas_call | solution.py:91
  165.5 1.9 collective-permute-start.8
  167.4 5.5 %collective-permute-start.9 = (f32[8,384]{1,0:T(8,128)}, f32[8,384]{1,0:T(8,128)S(1)}, u32[]{:S(2)}, u32[]{:S(2)}) collective-permute-start(f32[8,384]{1,0:T(8,128)} %get-tuple-element.15), channel_id=1, source_target_pairs={{8,0},{16,8},{24,16},{32,24},{40,32},{48,40},{56,48},{64,56},{72,6... | collective-permute-start | bytes 36872 | tf_op jit(solution)/shard_map/ppermute | solution.py:113
  172.9 3.2 %collective-permute-start.10 = (f32[128,8]{1,0:T(8,128)}, f32[128,8]{1,0:T(8,128)S(1)}, u32[]{:S(2)}, u32[]{:S(2)}) collective-permute-start(f32[128,8]{1,0:T(8,128)} %get-tuple-element.16), channel_id=1, source_target_pairs={{0,1},{1,2},{2,3},{3,4},{4,5},{5,6},{6,7},{8,9},{9,10},{10,11},{11... | collective-permute-start | bytes 12296 | tf_op jit(solution)/shard_map/ppermute | solution.py:113
  176.1 2.1 %collective-permute-start.11 = (f32[128,8]{1,0:T(8,128)}, f32[128,8]{1,0:T(8,128)S(1)}, u32[]{:S(2)}, u32[]{:S(2)}) collective-permute-start(f32[128,8]{1,0:T(8,128)} %get-tuple-element.17), channel_id=1, source_target_pairs={{1,0},{2,1},{3,2},{4,3},{5,4},{6,5},{7,6},{9,8},{10,9},{11,10},{12... | collective-permute-start | bytes 12296 | tf_op jit(solution)/shard_map/ppermute | solution.py:113
  178.2 3.6 %collective-permute-done.11.ay_ref = f32[128,8]{1,0:T(8,128)S(1)} collective-permute-done((f32[128,8]{1,0:T(8,128)}, f32[128,8]{1,0:T(8,128)S(1)}, u32[]{:S(2)}, u32[]{:S(2)}) %collective-permute-start.11) | collective-permute-done | bytes 4128 | tf_op jit(solution)/shard_map/ppermute | solution.py:113
  181.9 0.6 copy-done.11
  182.5 6.0 %shard_map.105 = (f32[8,128,384]{2,1,0:T(8,128)}, f32[8,384]{1,0:T(8,128)}, f32[8,384]{1,0:T(8,128)}, f32[128,8]{1,0:T(8,128)}, f32[128,8]{1,0:T(8,128)}) custom-call(f32[2,8]{1,0:T(2,128)} %wind_ref.5, f32[8,128,384]{2,1,0:T(8,128)} %get-tuple-element.13.child_ref, f32[8,384]{1,0:T(8,128)} %copy-done.17, f32[8,384]{1,0:T(8,128)} %copy-done.19, ...), custom_call_target="tpu_custom_call" | custom-call | flops 11796480 | bytes 6684672 | tf_op jit(solution)/shard_map/pallas_call | solution.py:91
  188.5 1.9 collective-permute-start.12
  190.4 5.5 %collective-permute-start.13 = (f32[8,384]{1,0:T(8,128)}, f32[8,384]{1,0:T(8,128)S(1)}, u32[]{:S(2)}, u32[]{:S(2)}) collective-permute-start(f32[8,384]{1,0:T(8,128)} %get-tuple-element.20), channel_id=1, source_target_pairs={{8,0},{16,8},{24,16},{32,24},{40,32},{48,40},{56,48},{64,56},{72,6... | collective-permute-start | bytes 36872 | tf_op jit(solution)/shard_map/ppermute | solution.py:113
  195.9 2.5 %collective-permute-start.14 = (f32[128,8]{1,0:T(8,128)}, f32[128,8]{1,0:T(8,128)S(1)}, u32[]{:S(2)}, u32[]{:S(2)}) collective-permute-start(f32[128,8]{1,0:T(8,128)} %get-tuple-element.21), channel_id=1, source_target_pairs={{0,1},{1,2},{2,3},{3,4},{4,5},{5,6},{6,7},{8,9},{9,10},{10,11},{11... | collective-permute-start | bytes 12296 | tf_op jit(solution)/shard_map/ppermute | solution.py:113
  198.4 1.9 collective-permute-start.15
  200.4 3.8 %collective-permute-done.15.ay_ref = f32[128,8]{1,0:T(8,128)S(1)} collective-permute-done((f32[128,8]{1,0:T(8,128)}, f32[128,8]{1,0:T(8,128)S(1)}, u32[]{:S(2)}, u32[]{:S(2)}) %collective-permute-start.15) | collective-permute-done | bytes 4128 | tf_op jit(solution)/shard_map/ppermute | solution.py:113
  204.2 0.6 copy-done.10
  204.9 6.0 %shard_map.106 = (f32[8,128,384]{2,1,0:T(8,128)}, f32[8,384]{1,0:T(8,128)}, f32[8,384]{1,0:T(8,128)}, f32[128,8]{1,0:T(8,128)}, f32[128,8]{1,0:T(8,128)}) custom-call(f32[2,8]{1,0:T(2,128)} %wind_ref.5, f32[8,128,384]{2,1,0:T(8,128)} %get-tuple-element.18.child_ref, f32[8,384]{1,0:T(8,128)} %copy-done.16, f32[8,384]{1,0:T(8,128)} %copy-done.18, ...), custom_call_target="tpu_custom_call" | custom-call | flops 11796480 | bytes 6684672 | tf_op jit(solution)/shard_map/pallas_call | solution.py:91
  (90 shorter events, 3.2 us)
Async XLA Ops:
  0.6 7.6 %copy-start = (f32[8,128,512]{2,1,0:T(8,128)S(1)}, f32[8,128,512]{2,1,0:T(8,128)}, u32[]{:S(2)}) copy-start(f32[8,128,512]{2,1,0:T(8,128)} %param.9) | copy-start | bytes 6291460
  2.4 44.1 %collective-permute-start.3 = (f32[8,128]{1,0:T(8,128)S(1)}, f32[8,128]{1,0:T(8,128)S(1)}, u32[]{:S(2)}, u32[]{:S(2)}) collective-permute-start(f32[8,128]{1,0:T(8,128)S(1)} %bitcast.77), channel_id=1, source_target_pairs={{0,1},{1,2},{2,3},{3,4},{4,5},{5,6},{6,7},{8,9},{9,10},{10,11},{11... | collective-permute-start | bytes 12296 | tf_op jit(solution)/shard_map/ppermute | solution.py:25
  6.3 40.3 %collective-permute-start.2 = (f32[8,128]{1,0:T(8,128)S(1)}, f32[8,128]{1,0:T(8,128)S(1)}, u32[]{:S(2)}, u32[]{:S(2)}) collective-permute-start(f32[8,128]{1,0:T(8,128)S(1)} %bitcast.79), channel_id=1, source_target_pairs={{1,0},{2,1},{3,2},{4,3},{5,4},{6,5},{7,6},{9,8},{10,9},{11,10},{12... | collective-permute-start | bytes 12296 | tf_op jit(solution)/shard_map/ppermute | solution.py:25
  8.3 38.6 %collective-permute-start.1 = (f32[8,512]{1,0:T(8,128)S(1)}, f32[8,512]{1,0:T(8,128)S(1)}, u32[]{:S(2)}, u32[]{:S(2)}) collective-permute-start(f32[8,512]{1,0:T(8,128)S(1)} %bitcast.73), channel_id=1, source_target_pairs={{0,8},{8,16},{16,24},{24,32},{32,40},{40,48},{48,56},{56,64},{64,7... | collective-permute-start | bytes 49160 | tf_op jit(solution)/shard_map/ppermute | solution.py:25
  11.5 35.5 %collective-permute-start = (f32[8,512]{1,0:T(8,128)S(1)}, f32[8,512]{1,0:T(8,128)S(1)}, u32[]{:S(2)}, u32[]{:S(2)}) collective-permute-start(f32[8,512]{1,0:T(8,128)S(1)} %bitcast.75), channel_id=1, source_target_pairs={{8,0},{16,8},{24,16},{32,24},{40,32},{48,40},{56,48},{64,56},{72,6... | collective-permute-start | bytes 49160 | tf_op jit(solution)/shard_map/ppermute | solution.py:25
  19.2 47.8 %all-to-all-start = ((f32[8,128,384]{2,0,1:T(8,128)}), f32[8,128,384]{2,0,1:T(8,128)}, u32[]{:S(2)}, u32[]{:S(2)}) async-start(f32[8,128,384]{2,0,1:T(8,128)} %copy.95), calls=%async_computation | async-start | bytes 3145728 | tf_op jit(solution)/shard_map/all_to_all | solution.py:53
  34.5 2.5 %copy-start.13 = (f32[2,8]{1,0:T(2,128)S(1)}, f32[2,8]{1,0:T(2,128)}, u32[]{:S(2)}) copy-start(f32[2,8]{1,0:T(2,128)} %wind_ref.5) | copy-start | bytes 196
  34.5 3.1 %copy-start.3 = (bf16[128,512]{1,0:T(8,128)(2,1)S(1)}, bf16[128,512]{1,0:T(8,128)(2,1)}, u32[]{:S(2)}) copy-start(bf16[128,512]{1,0:T(8,128)(2,1)} %param.10) | copy-start | bytes 393220
  34.5 3.9 %copy-start.5 = (s32[16384,1]{0,1:T(1,128)S(1)}, s32[16384,1]{0,1:T(1,128)}, u32[]{:S(2)}) copy-start(s32[16384,1]{0,1:T(1,128)} %param.14) | copy-start | bytes 196612
  55.7 1.6 copy-start.2
  59.5 2.9 %copy-start.23 = (pred[128]{0:T(512)(128)(4,1)S(1)}, pred[128]{0:T(512)(128)(4,1)}, u32[]{:S(2)}) copy-start(pred[128]{0:T(512)(128)(4,1)} %compare_and_fusion) | copy-start | bytes 388
  62.4 0.6 copy-start.20
  62.4 0.7 copy-start.21
  67.1 9.8 %copy-start.22 = (s32[2,4]{1,0:T(2,128)S(1)}, s32[2,4]{1,0:T(2,128)}, u32[]{:S(2)}) copy-start(s32[2,4]{1,0:T(2,128)} %param.17) | copy-start | bytes 100
  67.1 38.7 %all-to-all-start.2 = ((f32[128,2,2048]{2,1,0:T(2,128)}), f32[128,2,2048]{2,1,0:T(2,128)S(1)}, u32[]{:S(2)}, u32[]{:S(2)}) async-start(f32[128,2,2048]{2,1,0:T(2,128)} %copy.106), calls=%async_computation.2 | async-start | bytes 4194304 | tf_op jit(solution)/shard_map/all_to_all | solution.py:172
  85.9 27.5 %copy-start.12 = (s32[16384]{0:T(1024)S(1)}, s32[16384]{0:T(1024)}, u32[]{:S(2)}) copy-start(s32[16384]{0:T(1024)} %param.16) | copy-start | bytes 196612
  85.9 28.1 %copy-start.4 = (bf16[128,384]{1,0:T(8,128)(2,1)S(1)}, bf16[128,384]{1,0:T(8,128)(2,1)}, u32[]{:S(2)}) copy-start(bf16[128,384]{1,0:T(8,128)(2,1)} %param.12) | copy-start | bytes 294916
  105.8 1.4 copy-start.1
  107.2 29.4 %all-to-all-start.1 = ((f32[8,128,384]{2,0,1:T(8,128)}), f32[8,128,384]{2,0,1:T(8,128)S(1)}, u32[]{:S(2)}, u32[]{:S(2)}) async-start(f32[8,128,384]{2,0,1:T(8,128)} %bitcast.66), calls=%async_computation.1 | async-start | bytes 3145728 | tf_op jit(solution)/shard_map/all_to_all | solution.py:58
  136.6 22.1 %collective-permute-start.4 = (f32[8,384]{1,0:T(8,128)S(1)}, f32[8,384]{1,0:T(8,128)S(1)}, u32[]{:S(2)}, u32[]{:S(2)}) collective-permute-start(f32[8,384]{1,0:T(8,128)S(1)} %get-tuple-element.41), channel_id=1, source_target_pairs={{0,8},{8,16},{16,24},{24,32},{32,40},{40,48},{48,56},{56,64},{64,7... | collective-permute-start | bytes 36872 | tf_op jit(solution)/shard_map/ppermute | solution.py:113
  139.0 19.7 %collective-permute-start.5 = (f32[8,384]{1,0:T(8,128)S(1)}, f32[8,384]{1,0:T(8,128)S(1)}, u32[]{:S(2)}, u32[]{:S(2)}) collective-permute-start(f32[8,384]{1,0:T(8,128)S(1)} %get-tuple-element.40), channel_id=1, source_target_pairs={{8,0},{16,8},{24,16},{32,24},{40,32},{48,40},{56,48},{64,56},{72,6... | collective-permute-start | bytes 36872 | tf_op jit(solution)/shard_map/ppermute | solution.py:113
  146.8 11.9 %collective-permute-start.6 = (f32[128,8]{1,0:T(8,128)S(1)}, f32[128,8]{1,0:T(8,128)S(1)}, u32[]{:S(2)}, u32[]{:S(2)}) collective-permute-start(f32[128,8]{1,0:T(8,128)S(1)} %bitcast.70), channel_id=1, source_target_pairs={{0,1},{1,2},{2,3},{3,4},{4,5},{5,6},{6,7},{8,9},{9,10},{10,11},{11... | collective-permute-start | bytes 12296 | tf_op jit(solution)/shard_map/ppermute | solution.py:113
  149.9 8.8 %collective-permute-start.7 = (f32[128,8]{1,0:T(8,128)S(1)}, f32[128,8]{1,0:T(8,128)S(1)}, u32[]{:S(2)}, u32[]{:S(2)}) collective-permute-start(f32[128,8]{1,0:T(8,128)S(1)} %bitcast.71), channel_id=1, source_target_pairs={{1,0},{2,1},{3,2},{4,3},{5,4},{6,5},{7,6},{9,8},{10,9},{11,10},{12... | collective-permute-start | bytes 12296 | tf_op jit(solution)/shard_map/ppermute | solution.py:113
  158.6 0.8 copy-start.6
  158.6 0.8 copy-start.7
  158.7 0.8 copy-start.14
  158.7 0.8 copy-start.15
  165.5 16.4 %collective-permute-start.8 = (f32[8,384]{1,0:T(8,128)}, f32[8,384]{1,0:T(8,128)S(1)}, u32[]{:S(2)}, u32[]{:S(2)}) collective-permute-start(f32[8,384]{1,0:T(8,128)} %get-tuple-element.14), channel_id=1, source_target_pairs={{0,8},{8,16},{16,24},{24,32},{32,40},{40,48},{48,56},{56,64},{64,7... | collective-permute-start | bytes 36872 | tf_op jit(solution)/shard_map/ppermute | solution.py:113
  167.4 14.4 %collective-permute-start.9 = (f32[8,384]{1,0:T(8,128)}, f32[8,384]{1,0:T(8,128)S(1)}, u32[]{:S(2)}, u32[]{:S(2)}) collective-permute-start(f32[8,384]{1,0:T(8,128)} %get-tuple-element.15), channel_id=1, source_target_pairs={{8,0},{16,8},{24,16},{32,24},{40,32},{48,40},{56,48},{64,56},{72,6... | collective-permute-start | bytes 36872 | tf_op jit(solution)/shard_map/ppermute | solution.py:113
  172.9 5.3 %collective-permute-start.10 = (f32[128,8]{1,0:T(8,128)}, f32[128,8]{1,0:T(8,128)S(1)}, u32[]{:S(2)}, u32[]{:S(2)}) collective-permute-start(f32[128,8]{1,0:T(8,128)} %get-tuple-element.16), channel_id=1, source_target_pairs={{0,1},{1,2},{2,3},{3,4},{4,5},{5,6},{6,7},{8,9},{9,10},{10,11},{11... | collective-permute-start | bytes 12296 | tf_op jit(solution)/shard_map/ppermute | solution.py:113
  176.1 5.8 %collective-permute-start.11 = (f32[128,8]{1,0:T(8,128)}, f32[128,8]{1,0:T(8,128)S(1)}, u32[]{:S(2)}, u32[]{:S(2)}) collective-permute-start(f32[128,8]{1,0:T(8,128)} %get-tuple-element.17), channel_id=1, source_target_pairs={{1,0},{2,1},{3,2},{4,3},{5,4},{6,5},{7,6},{9,8},{10,9},{11,10},{12... | collective-permute-start | bytes 12296 | tf_op jit(solution)/shard_map/ppermute | solution.py:113
  178.2 3.7 %copy-start.9 = (f32[128,8]{1,0:T(8,128)}, f32[128,8]{1,0:T(8,128)S(1)}, u32[]{:S(2)}) copy-start(f32[128,8]{1,0:T(8,128)S(1)} %collective-permute-done.10.by_ref) | copy-start | bytes 12292
  181.9 0.6 copy-start.11
  181.9 0.6 copy-start.17
  181.9 0.6 copy-start.19
  188.5 15.7 %collective-permute-start.12 = (f32[8,384]{1,0:T(8,128)}, f32[8,384]{1,0:T(8,128)S(1)}, u32[]{:S(2)}, u32[]{:S(2)}) collective-permute-start(f32[8,384]{1,0:T(8,128)} %get-tuple-element.19), channel_id=1, source_target_pairs={{0,8},{8,16},{16,24},{24,32},{32,40},{40,48},{48,56},{56,64},{64,7... | collective-permute-start | bytes 36872 | tf_op jit(solution)/shard_map/ppermute | solution.py:113
  190.4 13.8 %collective-permute-start.13 = (f32[8,384]{1,0:T(8,128)}, f32[8,384]{1,0:T(8,128)S(1)}, u32[]{:S(2)}, u32[]{:S(2)}) collective-permute-start(f32[8,384]{1,0:T(8,128)} %get-tuple-element.20), channel_id=1, source_target_pairs={{8,0},{16,8},{24,16},{32,24},{40,32},{48,40},{56,48},{64,56},{72,6... | collective-permute-start | bytes 36872 | tf_op jit(solution)/shard_map/ppermute | solution.py:113
  195.9 4.5 %collective-permute-start.14 = (f32[128,8]{1,0:T(8,128)}, f32[128,8]{1,0:T(8,128)S(1)}, u32[]{:S(2)}, u32[]{:S(2)}) collective-permute-start(f32[128,8]{1,0:T(8,128)} %get-tuple-element.21), channel_id=1, source_target_pairs={{0,1},{1,2},{2,3},{3,4},{4,5},{5,6},{6,7},{8,9},{9,10},{10,11},{11... | collective-permute-start | bytes 12296 | tf_op jit(solution)/shard_map/ppermute | solution.py:113
  198.4 5.8 %collective-permute-start.15 = (f32[128,8]{1,0:T(8,128)}, f32[128,8]{1,0:T(8,128)S(1)}, u32[]{:S(2)}, u32[]{:S(2)}) collective-permute-start(f32[128,8]{1,0:T(8,128)} %get-tuple-element.22), channel_id=1, source_target_pairs={{1,0},{2,1},{3,2},{4,3},{5,4},{6,5},{7,6},{9,8},{10,9},{11,10},{12... | collective-permute-start | bytes 12296 | tf_op jit(solution)/shard_map/ppermute | solution.py:113
  200.4 3.9 %copy-start.8 = (f32[128,8]{1,0:T(8,128)}, f32[128,8]{1,0:T(8,128)S(1)}, u32[]{:S(2)}) copy-start(f32[128,8]{1,0:T(8,128)S(1)} %collective-permute-done.14.by_ref) | copy-start | bytes 12292
  204.2 0.6 copy-start.10
  204.2 0.6 copy-start.16
  204.2 0.6 copy-start.18

commit v5 on v4

--- a/solution.py
+++ b/solution.py
@@ -169,6 +169,7 @@
         precision=lax.Precision.HIGHEST,
         preferred_element_type=jnp.float32,
     )
+    child, outgoing_strips = lax.optimization_barrier((child, outgoing_strips))
     incoming = lax.all_to_all(
         outgoing_strips, ("gx", "gy"), split_axis=0, concat_axis=0, tiled=True
     )

time: 212 us -> 203 us (0.958)
  waiting for transfers between devices: 39.9 us -> 7.74 us
  local copies, waits for them, and re-layouts: 49.3 us -> 67.8 us
  starting transfers between devices: 75.2 us -> 82.1 us
    optimization_barrier x0 -> x2, local copies, waits for them, and re-layouts: none -> 23.1 us  [shards(): child, outgoing_strips = lax.optimization_barrier((child, outgoing_strips))]
    all_to_all x1, waiting for transfers between devices: 19.9 us -> 0.01 us  [shards(): lax.all_to_all(outgoing_strips, ('gx', 'gy'), split_axis=0, concat_axis=0...]
    all_to_all x1, waiting for transfers between devices: 12.5 us -> 0.01 us  [storm_rows(): lax.all_to_all(grid.reshape(levels, crows, widths), ('gx', 'gy'), 1, 1, t...]
    dot_general x2 -> x0, local copies, waits for them, and re-layouts: 5.88 us -> none  [the longest x1 2.97 us: shards(): jnp.dot(send_select, strip_values, precision=lax.Precision.HIGHEST, prefe...]
    all_to_all x1, starting transfers between devices: 6 us -> 10.9 us  [storm_rows(): lax.all_to_all(grid.reshape(levels, crows, widths), ('gx', 'gy'), 1, 1, t...]
    all_to_all x1 -> x3, local copies, waits for them, and re-layouts: 3.65 us -> 6.63 us  [shards(): lax.all_to_all(outgoing_strips, ('gx', 'gy'), split_axis=0, concat_axis=0...]
    unnamed x55 -> x51, local copies, waits for them, and re-layouts: 9.75 us -> 7.28 us
  transfers between devices with their start and end apart: 19 -> 19, of which waited for: 4 -> 2; matrix products, arithmetic and copies ran while one was open for 30% -> 38% of each run, Pallas kernels for 0% -> 0%
where the time goes in v5:
time: 203 us; the launch traced here: 202 us
  starting transfers between devices  82.1 us (40%)
  local copies, waits for them, and re-layouts  67.8 us (33%)
  Pallas kernels  17.9 us (9%)
  other arithmetic  14.3 us (7%)
  waiting for transfers between devices  7.74 us (4%)
  matrix products  6.65 us (3%)
  between operations  5.19 us (3%)
    ppermute x12, starting transfers between devices, swap_edge(): return lax.ppermute(edge, axis, pairs)  38.8 us
    optimization_barrier x2, local copies, waits for them, and re-layouts, shards(): child, outgoing_strips = lax.optimization_barrier((child, outgoing_strips))  23.1 us
    pallas_call x3, Pallas kernels, substep(): pl.pallas_call(functools.partial(substep_kernel, weight), out_shape=(jax....  17.9 us
    ppermute x4, starting transfers between devices, swap(): return lax.ppermute(edge, axis, pairs)  11.6 us
    all_to_all x1, starting transfers between devices, storm_rows(): lax.all_to_all(grid.reshape(levels, crows, widths), ('gx', 'gy'), 1, 1, t...  10.9 us
    all_to_all x1, starting transfers between devices, storm_rows(): gathered = lax.all_to_all(child, ('gx', 'gy'), 1, 1, tiled=True)  10.9 us
    all_to_all x1, starting transfers between devices, shards(): lax.all_to_all(outgoing_strips, ('gx', 'gy'), split_axis=0, concat_axis=0...  9.76 us
    another operation x4, local copies, waits for them, and re-layouts, shards(): jnp.stack([parent_field, new_parent]).reshape(2, levels, -1, STRIP)  8.37 us
  transfers between devices with their start and end apart: 19, of which 2 were waited for; matrix products, arithmetic and copies ran while one was open for 38% of the time, Pallas kernels for 0%

profile of v5, /device:TPU:33, one launch (start us, length us, event | category | flops | bytes accessed | tf_op | source)
XLA Modules:
  0.0 201.8 jit_solution(16680697544776533784)
XLA Ops:
  0.6 3.5 %copy.94 = f32[8,128,384]{2,0,1:T(8,128)} copy(f32[8,128,384]{2,1,0:T(8,128)} %param.11) | data formatting | bytes 3145728 | tf_op args[2]
  4.1 10.9 %all-to-all-start = ((f32[8,128,384]{2,0,1:T(8,128)}), f32[8,128,384]{2,0,1:T(8,128)}, u32[]{:S(2)}, u32[]{:S(2)}) async-start(f32[8,128,384]{2,0,1:T(8,128)} %copy.94), calls=%async_computation | async-start | bytes 3145728 | tf_op jit(solution)/shard_map/all_to_all | solution.py:53
  15.3 0.8 copy.116
  16.1 2.3 %collective-permute-start.2 = (f32[8,128]{1,0:T(8,128)}, f32[8,128]{1,0:T(8,128)S(1)}, u32[]{:S(2)}, u32[]{:S(2)}) collective-permute-start(f32[8,128]{1,0:T(8,128)} %bitcast.4), channel_id=1, source_target_pairs={{1,0},{2,1},{3,2},{4,3},{5,4},{6,5},{7,6},{9,8},{10,9},{11,10},{12... | collective-permute-start | bytes 12296 | tf_op jit(solution)/shard_map/ppermute | solution.py:25
  18.5 3.3 %collective-permute-start.3 = (f32[8,128]{1,0:T(8,128)S(1)}, f32[8,128]{1,0:T(8,128)S(1)}, u32[]{:S(2)}, u32[]{:S(2)}) collective-permute-start(f32[8,128]{1,0:T(8,128)S(1)} %bitcast.75), channel_id=1, source_target_pairs={{0,1},{1,2},{2,3},{3,4},{4,5},{5,6},{6,7},{8,9},{9,10},{10,11},{11... | collective-permute-start | bytes 12296 | tf_op jit(solution)/shard_map/ppermute | solution.py:25
  21.8 4.2 %collective-permute-start = (f32[8,512]{1,0:T(8,128)S(1)}, f32[8,512]{1,0:T(8,128)}, u32[]{:S(2)}, u32[]{:S(2)}) collective-permute-start(f32[8,512]{1,0:T(8,128)S(1)} %bitcast.73), channel_id=1, source_target_pairs={{8,0},{16,8},{24,16},{32,24},{40,32},{48,40},{56,48},{64,56},{72,6... | collective-permute-start | bytes 49160 | tf_op jit(solution)/shard_map/ppermute | solution.py:25
  26.0 0.6 copy.120
  26.6 1.9 collective-permute-start.1
  28.6 0.6 constant_dynamic-slice_fusion.2
  33.1 0.6 multiply_bitcast_fusion.1
  33.7 0.7 fusion.25
  34.4 0.7 fusion.27
  35.3 0.7 fusion.26
  36.0 0.8 fusion.35
  36.8 2.4 %fusion.36 = (f32[7,128,512]{2,1,0:T(8,128)}, f32[7,128,512]{2,1,0:T(8,128)}) fusion(f32[8,128,512]{2,1,0:T(8,128)S(1)} %copy-done), kind=kLoop, calls=%fused_computation.80 | loop fusion | bytes 7340032 | tf_op jit(solution)/shard_map/slice | solution.py:125
  39.2 2.5 %fusion.31 = (f32[8,127,512]{2,1,0:T(8,128)}, f32[8,127,512]{2,1,0:T(8,128)}) fusion(f32[8,128,512]{2,1,0:T(8,128)S(1)} %copy-done), kind=kLoop, calls=%fused_computation.75 | loop fusion | bytes 8323072 | tf_op jit(solution)/shard_map/slice | solution.py:36
  41.7 2.8 %fusion.33 = (f32[8,128,511]{2,1,0:T(8,128)}, f32[8,128,511]{2,1,0:T(8,128)}) fusion(f32[8,128,512]{2,1,0:T(8,128)S(1)} %copy-done), kind=kLoop, calls=%fused_computation.77 | loop fusion | bytes 8372224 | tf_op jit(solution)/shard_map/slice | solution.py:38
  44.4 1.7 copy.95
  46.9 2.1 %copy.97 = f32[8,16,8,384]{3,0,2,1:T(8,128)} copy(f32[8,16,8,384]{3,2,1,0:T(8,128)S(1)} %fusion.5) | data formatting | bytes 3145728 | tf_op jit(solution)/shard_map/jit(_roll_dynamic)/dynamic_slice | solution.py:57
  48.9 10.9 %all-to-all-start.1 = ((f32[8,128,384]{2,0,1:T(8,128)}), f32[8,128,384]{2,0,1:T(8,128)}, u32[]{:S(2)}, u32[]{:S(2)}) async-start(f32[8,128,384]{2,0,1:T(8,128)} %bitcast.67), calls=%async_computation.1 | async-start | bytes 3145728 | tf_op jit(solution)/shard_map/all_to_all | solution.py:58
  59.9 0.7 compare_and_fusion
  60.6 1.4 stack.9
  62.0 4.1 %copy.98 = f32[1,8,512,128]{3,1,2,0:T(8,128)} copy(f32[1,8,512,128]{3,2,1,0:T(8,128)} %stack.9) | data formatting | bytes 4194304 | tf_op jit(solution)/shard_map/stack | solution.py:163
  66.4 0.6 copy-done.19
  67.0 0.9 copy.93
  67.9 0.7 copy.87
  68.6 0.7 copy.89
  69.4 7.0 %fusion.4 = f32[8,128,512]{2,1,0:T(8,128)} fusion(f32[8,128,512]{2,1,0:T(8,128)S(1)} %copy-done, f32[1,128,512]{2,1,0:T(8,128)} %get-tuple-element.41, f32[7,128,512]{2,1,0:T(8,128)} %get-tuple-element.43, f32[7,128,512]{2,1,0:T(8,128)} %get-tuple-element.42, f32[1,128,512]{2,1,0:T(8,128)} %get-tuple-element.40, f32[8,128,511]{2,1,0:T(8,128)} %get-tuple-element.37, ...), kind=kLoop, calls=%fused_computation.15 | loop fusion | flops 13107200 | bytes 17039424 | tf_op jit(solution)/shard_map/add | solution.py:144
  76.4 1.6 stack.10
  78.1 1.2 copy.99
  79.6 2.2 %pad_maximum_fusion = f32[2,8,512,128]{3,1,2,0:T(8,128)} fusion(f32[1,8,512,128]{3,1,2,0:T(8,128)S(1)} %copy.99, f32[1,8,512,128]{3,1,2,0:T(8,128)S(1)} %copy-done.1), kind=kLoop, calls=%fused_computation.1 | loop fusion | flops 1048576 | bytes 8388608 | tf_op jit(solution)/shard_map/stack | solution.py:163
  81.9 2.9 %gather_fusion = f32[128,2,8,128]{3,2,1,0:T(8,128)S(1)} fusion(f32[2,8,512,128]{3,1,2,0:T(8,128)} %pad_maximum_fusion, s32[1024]{0:T(1024)S(1)} %pad_clamp_fusion), kind=kCustom, calls=%fused_computation | custom fusion | bytes 2097664 | tf_op jit(solution)/shard_map/jit(_take)/gather | solution.py:164
  85.4 1.0 fusion.13
  86.4 2.2 %all_to_all.16 = f32[128,2,2048]{2,1,0:T(2,128)} reshape(f32[256,2048]{1,0:T(8,128)S(1)} %fusion.13) | data formatting | bytes 4194304 | tf_op jit(solution)/shard_map/all_to_all | solution.py:173
  88.7 9.8 %all-to-all-start.2 = ((f32[128,2,2048]{2,1,0:T(2,128)}), f32[128,2,2048]{2,1,0:T(2,128)S(1)}, u32[]{:S(2)}, u32[]{:S(2)}) async-start(f32[128,2,2048]{2,1,0:T(2,128)} %all_to_all.16), calls=%async_computation.2 | async-start | bytes 4194304 | tf_op jit(solution)/shard_map/all_to_all | solution.py:173
  99.5 0.7 convert_add_fusion.1.factor_ref
  100.2 20.3 %copy.101 = f32[8,128,384]{0,1,2:T(8,128)} copy(f32[8,128,384]{2,0,1:T(8,128)} %all-to-all-done.1) | data formatting | bytes 3145728 | tf_op jit(solution)/shard_map/optimization_barrier | solution.py:172
  120.5 2.9 %copy.109.child_ref = f32[8,128,384]{2,1,0:T(8,128)} copy(f32[8,128,384]{2,0,1:T(8,128)} %all-to-all-done.1) | data formatting | bytes 3145728 | tf_op jit(solution)/shard_map/optimization_barrier | solution.py:172
  123.4 0.9 slice_bitcast_fusion
  124.3 3.4 %collective-permute-start.6 = (f32[128,8]{1,0:T(8,128)S(1)}, f32[128,8]{1,0:T(8,128)S(1)}, u32[]{:S(2)}, u32[]{:S(2)}) collective-permute-start(f32[128,8]{1,0:T(8,128)S(1)} %get-tuple-element.31), channel_id=1, source_target_pairs={{0,1},{1,2},{2,3},{3,4},{4,5},{5,6},{6,7},{8,9},{9,10},{10,11},{11... | collective-permute-start | bytes 12296 | tf_op jit(solution)/shard_map/ppermute | solution.py:113
  127.7 1.9 collective-permute-start.7
  129.6 0.7 slice_bitcast_fusion.2
  130.3 3.1 %collective-permute-start.4 = (f32[8,384]{1,0:T(8,128)S(1)}, f32[8,384]{1,0:T(8,128)S(1)}, u32[]{:S(2)}, u32[]{:S(2)}) collective-permute-start(f32[8,384]{1,0:T(8,128)S(1)} %get-tuple-element.45), channel_id=1, source_target_pairs={{0,8},{8,16},{16,24},{24,32},{32,40},{40,48},{48,56},{56,64},{64,7... | collective-permute-start | bytes 36872 | tf_op jit(solution)/shard_map/ppermute | solution.py:113
  133.5 4.5 %collective-permute-start.5 = (f32[8,384]{1,0:T(8,128)S(1)}, f32[8,384]{1,0:T(8,128)S(1)}, u32[]{:S(2)}, u32[]{:S(2)}) collective-permute-start(f32[8,384]{1,0:T(8,128)S(1)} %get-tuple-element.44), channel_id=1, source_target_pairs={{8,0},{16,8},{24,16},{32,24},{40,32},{48,40},{56,48},{64,56},{72,6... | collective-permute-start | bytes 36872 | tf_op jit(solution)/shard_map/ppermute | solution.py:113
  138.0 2.5 %all_to_all.18 = f32[256,2048]{1,0:T(8,128)} reshape(f32[128,2,2048]{2,1,0:T(2,128)S(1)} %all-to-all-done.2) | data formatting | bytes 4194304 | tf_op jit(solution)/shard_map/all_to_all | solution.py:173
  140.4 1.9 copy.106
  142.4 1.3 fusion.14
  143.7 4.3 %convolution_bitcast_fusion.bound_ref = f32[2,8,128,384]{3,2,1,0:T(8,128)} fusion(f32[128,2,8,128]{3,0,2,1:T(8,128)S(1)} %fusion.14, f32[128]{0:T(128)S(1)} %iota_convert_fusion, f32[384]{0:T(512)S(1)} %add_clamp_fusion), kind=kOutput, calls=%fused_computation.16 | convolution fusion | flops 1208156160 | bytes 4196352 | tf_op jit(solution)/shard_map/tald,de->alte/dot_general | solution.py:187
  148.1 0.8 broadcast_in_dim.69.divisor_ref
  148.8 6.0 %shard_map.104 = (f32[8,128,384]{2,1,0:T(8,128)}, f32[8,384]{1,0:T(8,128)}, f32[8,384]{1,0:T(8,128)}, f32[128,8]{1,0:T(8,128)}, f32[128,8]{1,0:T(8,128)}) custom-call(f32[2,8]{1,0:T(2,128)} %wind_ref.5, f32[8,128,384]{2,1,0:T(8,128)} %copy.109.child_ref, f32[8,384]{1,0:T(8,128)} %copy-done.13, f32[8,384]{1,0:T(8,128)} %copy-done.14, f32[128,8]{1,0:T(8,128)} %copy-done.5, ...), custom_call_target="tpu_custom_call" | custom-call | flops 11796480 | bytes 6684672 | tf_op jit(solution)/shard_map/pallas_call | solution.py:91
  154.8 1.9 collective-permute-start.8
  156.8 5.5 %collective-permute-start.9 = (f32[8,384]{1,0:T(8,128)}, f32[8,384]{1,0:T(8,128)S(1)}, u32[]{:S(2)}, u32[]{:S(2)}) collective-permute-start(f32[8,384]{1,0:T(8,128)} %get-tuple-element.19), channel_id=1, source_target_pairs={{8,0},{16,8},{24,16},{32,24},{40,32},{48,40},{56,48},{64,56},{72,6... | collective-permute-start | bytes 36872 | tf_op jit(solution)/shard_map/ppermute | solution.py:113
  162.2 4.8 %collective-permute-start.10 = (f32[128,8]{1,0:T(8,128)}, f32[128,8]{1,0:T(8,128)S(1)}, u32[]{:S(2)}, u32[]{:S(2)}) collective-permute-start(f32[128,8]{1,0:T(8,128)} %get-tuple-element.20), channel_id=1, source_target_pairs={{0,1},{1,2},{2,3},{3,4},{4,5},{5,6},{6,7},{8,9},{9,10},{10,11},{11... | collective-permute-start | bytes 12296 | tf_op jit(solution)/shard_map/ppermute | solution.py:113
  167.0 1.9 collective-permute-start.11
  169.0 3.8 %collective-permute-done.11.ay_ref = f32[128,8]{1,0:T(8,128)S(1)} collective-permute-done((f32[128,8]{1,0:T(8,128)}, f32[128,8]{1,0:T(8,128)S(1)}, u32[]{:S(2)}, u32[]{:S(2)}) %collective-permute-start.11) | collective-permute-done | bytes 4128 | tf_op jit(solution)/shard_map/ppermute | solution.py:113
  172.8 0.6 copy-done.10
  173.4 6.0 %shard_map.105 = (f32[8,128,384]{2,1,0:T(8,128)}, f32[8,384]{1,0:T(8,128)}, f32[8,384]{1,0:T(8,128)}, f32[128,8]{1,0:T(8,128)}, f32[128,8]{1,0:T(8,128)}) custom-call(f32[2,8]{1,0:T(2,128)} %wind_ref.5, f32[8,128,384]{2,1,0:T(8,128)} %get-tuple-element.17.child_ref, f32[8,384]{1,0:T(8,128)} %copy-done.16, f32[8,384]{1,0:T(8,128)} %copy-done.18, ...), custom_call_target="tpu_custom_call" | custom-call | flops 11796480 | bytes 6684672 | tf_op jit(solution)/shard_map/pallas_call | solution.py:91
  179.4 1.9 collective-permute-start.12
  181.3 5.5 %collective-permute-start.13 = (f32[8,384]{1,0:T(8,128)}, f32[8,384]{1,0:T(8,128)S(1)}, u32[]{:S(2)}, u32[]{:S(2)}) collective-permute-start(f32[8,384]{1,0:T(8,128)} %get-tuple-element.24), channel_id=1, source_target_pairs={{8,0},{16,8},{24,16},{32,24},{40,32},{48,40},{56,48},{64,56},{72,6... | collective-permute-start | bytes 36872 | tf_op jit(solution)/shard_map/ppermute | solution.py:113
  186.8 2.5 %collective-permute-start.14 = (f32[128,8]{1,0:T(8,128)}, f32[128,8]{1,0:T(8,128)S(1)}, u32[]{:S(2)}, u32[]{:S(2)}) collective-permute-start(f32[128,8]{1,0:T(8,128)} %get-tuple-element.25), channel_id=1, source_target_pairs={{0,1},{1,2},{2,3},{3,4},{4,5},{5,6},{6,7},{8,9},{9,10},{10,11},{11... | collective-permute-start | bytes 12296 | tf_op jit(solution)/shard_map/ppermute | solution.py:113
  189.4 1.9 collective-permute-start.15
  191.3 3.8 %collective-permute-done.15.ay_ref = f32[128,8]{1,0:T(8,128)S(1)} collective-permute-done((f32[128,8]{1,0:T(8,128)}, f32[128,8]{1,0:T(8,128)S(1)}, u32[]{:S(2)}, u32[]{:S(2)}) %collective-permute-start.15) | collective-permute-done | bytes 4128 | tf_op jit(solution)/shard_map/ppermute | solution.py:113
  195.2 0.6 copy-done.9
  195.8 6.0 %shard_map.106 = (f32[8,128,384]{2,1,0:T(8,128)}, f32[8,384]{1,0:T(8,128)}, f32[8,384]{1,0:T(8,128)}, f32[128,8]{1,0:T(8,128)}, f32[128,8]{1,0:T(8,128)}) custom-call(f32[2,8]{1,0:T(2,128)} %wind_ref.5, f32[8,128,384]{2,1,0:T(8,128)} %get-tuple-element.22.child_ref, f32[8,384]{1,0:T(8,128)} %copy-done.15, f32[8,384]{1,0:T(8,128)} %copy-done.17, ...), custom_call_target="tpu_custom_call" | custom-call | flops 11796480 | bytes 6684672 | tf_op jit(solution)/shard_map/pallas_call | solution.py:91
  (86 shorter events, 3.7 us)
Async XLA Ops:
  4.1 10.9 %copy-start = (f32[8,128,512]{2,1,0:T(8,128)S(1)}, f32[8,128,512]{2,1,0:T(8,128)}, u32[]{:S(2)}) copy-start(f32[8,128,512]{2,1,0:T(8,128)} %param.9) | copy-start | bytes 6291460
  4.1 40.3 %all-to-all-start = ((f32[8,128,384]{2,0,1:T(8,128)}), f32[8,128,384]{2,0,1:T(8,128)}, u32[]{:S(2)}, u32[]{:S(2)}) async-start(f32[8,128,384]{2,0,1:T(8,128)} %copy.94), calls=%async_computation | async-start | bytes 3145728 | tf_op jit(solution)/shard_map/all_to_all | solution.py:53
  15.0 13.5 %copy-start.22 = (s32[2,4]{1,0:T(2,128)S(1)}, s32[2,4]{1,0:T(2,128)}, u32[]{:S(2)}) copy-start(s32[2,4]{1,0:T(2,128)} %param.17) | copy-start | bytes 100
  15.0 18.0 %copy-start.12 = (f32[2,8]{1,0:T(2,128)S(1)}, f32[2,8]{1,0:T(2,128)}, u32[]{:S(2)}) copy-start(f32[2,8]{1,0:T(2,128)} %wind_ref.5) | copy-start | bytes 196
  15.1 18.6 %copy-start.2 = (bf16[128,512]{1,0:T(8,128)(2,1)S(1)}, bf16[128,512]{1,0:T(8,128)(2,1)}, u32[]{:S(2)}) copy-start(bf16[128,512]{1,0:T(8,128)(2,1)} %param.10) | copy-start | bytes 393220
  16.1 50.1 %collective-permute-start.2 = (f32[8,128]{1,0:T(8,128)}, f32[8,128]{1,0:T(8,128)S(1)}, u32[]{:S(2)}, u32[]{:S(2)}) collective-permute-start(f32[8,128]{1,0:T(8,128)} %bitcast.4), channel_id=1, source_target_pairs={{1,0},{2,1},{3,2},{4,3},{5,4},{6,5},{7,6},{9,8},{10,9},{11,10},{12... | collective-permute-start | bytes 12296 | tf_op jit(solution)/shard_map/ppermute | solution.py:25
  18.5 47.8 %collective-permute-start.3 = (f32[8,128]{1,0:T(8,128)S(1)}, f32[8,128]{1,0:T(8,128)S(1)}, u32[]{:S(2)}, u32[]{:S(2)}) collective-permute-start(f32[8,128]{1,0:T(8,128)S(1)} %bitcast.75), channel_id=1, source_target_pairs={{0,1},{1,2},{2,3},{3,4},{4,5},{5,6},{6,7},{8,9},{9,10},{10,11},{11... | collective-permute-start | bytes 12296 | tf_op jit(solution)/shard_map/ppermute | solution.py:25
  21.8 46.0 %collective-permute-start = (f32[8,512]{1,0:T(8,128)S(1)}, f32[8,512]{1,0:T(8,128)}, u32[]{:S(2)}, u32[]{:S(2)}) collective-permute-start(f32[8,512]{1,0:T(8,128)S(1)} %bitcast.73), channel_id=1, source_target_pairs={{8,0},{16,8},{24,16},{32,24},{40,32},{48,40},{56,48},{64,56},{72,6... | collective-permute-start | bytes 49160 | tf_op jit(solution)/shard_map/ppermute | solution.py:25
  26.6 42.0 %collective-permute-start.1 = (f32[8,512]{1,0:T(8,128)}, f32[8,512]{1,0:T(8,128)}, u32[]{:S(2)}, u32[]{:S(2)}) collective-permute-start(f32[8,512]{1,0:T(8,128)} %bitcast.64), channel_id=1, source_target_pairs={{0,8},{8,16},{16,24},{24,32},{32,40},{40,48},{48,56},{56,64},{64,7... | collective-permute-start | bytes 49160 | tf_op jit(solution)/shard_map/ppermute | solution.py:25
  48.9 37.5 %all-to-all-start.1 = ((f32[8,128,384]{2,0,1:T(8,128)}), f32[8,128,384]{2,0,1:T(8,128)}, u32[]{:S(2)}, u32[]{:S(2)}) async-start(f32[8,128,384]{2,0,1:T(8,128)} %bitcast.67), calls=%async_computation.1 | async-start | bytes 3145728 | tf_op jit(solution)/shard_map/all_to_all | solution.py:58
  62.0 7.4 %copy-start.20 = (f32[8]{0:T(128)S(1)}, f32[8]{0:T(128)}, u32[]{:S(2)}) copy-start(f32[8]{0:T(128)} %get-tuple-element.48) | copy-start | bytes 100
  62.0 7.4 %copy-start.21 = (f32[8]{0:T(128)S(1)}, f32[8]{0:T(128)}, u32[]{:S(2)}) copy-start(f32[8]{0:T(128)} %get-tuple-element.49) | copy-start | bytes 100
  66.4 0.6 copy-start.19
  78.1 1.6 copy-start.1
  88.7 9.8 %copy-start.4 = (s32[16384,1]{0,1:T(1,128)S(1)}, s32[16384,1]{0,1:T(1,128)}, u32[]{:S(2)}) copy-start(s32[16384,1]{0,1:T(1,128)} %param.14) | copy-start | bytes 196612
  88.7 10.3 %copy-start.11 = (s32[16384]{0:T(1024)S(1)}, s32[16384]{0:T(1024)}, u32[]{:S(2)}) copy-start(s32[16384]{0:T(1024)} %param.16) | copy-start | bytes 196612
  88.7 10.8 %copy-start.3 = (bf16[128,384]{1,0:T(8,128)(2,1)S(1)}, bf16[128,384]{1,0:T(8,128)(2,1)}, u32[]{:S(2)}) copy-start(bf16[128,384]{1,0:T(8,128)(2,1)} %param.12) | copy-start | bytes 294916
  88.7 49.3 %all-to-all-start.2 = ((f32[128,2,2048]{2,1,0:T(2,128)}), f32[128,2,2048]{2,1,0:T(2,128)S(1)}, u32[]{:S(2)}, u32[]{:S(2)}) async-start(f32[128,2,2048]{2,1,0:T(2,128)} %all_to_all.16), calls=%async_computation.2 | async-start | bytes 4194304 | tf_op jit(solution)/shard_map/all_to_all | solution.py:173
  124.3 23.7 %collective-permute-start.6 = (f32[128,8]{1,0:T(8,128)S(1)}, f32[128,8]{1,0:T(8,128)S(1)}, u32[]{:S(2)}, u32[]{:S(2)}) collective-permute-start(f32[128,8]{1,0:T(8,128)S(1)} %get-tuple-element.31), channel_id=1, source_target_pairs={{0,1},{1,2},{2,3},{3,4},{4,5},{5,6},{6,7},{8,9},{9,10},{10,11},{11... | collective-permute-start | bytes 12296 | tf_op jit(solution)/shard_map/ppermute | solution.py:113
  127.7 20.3 %collective-permute-start.7 = (f32[128,8]{1,0:T(8,128)S(1)}, f32[128,8]{1,0:T(8,128)S(1)}, u32[]{:S(2)}, u32[]{:S(2)}) collective-permute-start(f32[128,8]{1,0:T(8,128)S(1)} %get-tuple-element.30), channel_id=1, source_target_pairs={{1,0},{2,1},{3,2},{4,3},{5,4},{6,5},{7,6},{9,8},{10,9},{11,10},{12... | collective-permute-start | bytes 12296 | tf_op jit(solution)/shard_map/ppermute | solution.py:113
  130.3 17.7 %collective-permute-start.4 = (f32[8,384]{1,0:T(8,128)S(1)}, f32[8,384]{1,0:T(8,128)S(1)}, u32[]{:S(2)}, u32[]{:S(2)}) collective-permute-start(f32[8,384]{1,0:T(8,128)S(1)} %get-tuple-element.45), channel_id=1, source_target_pairs={{0,8},{8,16},{16,24},{24,32},{32,40},{40,48},{48,56},{56,64},{64,7... | collective-permute-start | bytes 36872 | tf_op jit(solution)/shard_map/ppermute | solution.py:113
  133.5 14.6 %collective-permute-start.5 = (f32[8,384]{1,0:T(8,128)S(1)}, f32[8,384]{1,0:T(8,128)S(1)}, u32[]{:S(2)}, u32[]{:S(2)}) collective-permute-start(f32[8,384]{1,0:T(8,128)S(1)} %get-tuple-element.44), channel_id=1, source_target_pairs={{8,0},{16,8},{24,16},{32,24},{40,32},{48,40},{56,48},{64,56},{72,6... | collective-permute-start | bytes 36872 | tf_op jit(solution)/shard_map/ppermute | solution.py:113
  148.0 0.8 copy-start.5
  148.0 0.8 copy-start.6
  148.0 0.8 copy-start.13
  148.1 0.8 copy-start.14
  154.8 18.0 %collective-permute-start.8 = (f32[8,384]{1,0:T(8,128)}, f32[8,384]{1,0:T(8,128)S(1)}, u32[]{:S(2)}, u32[]{:S(2)}) collective-permute-start(f32[8,384]{1,0:T(8,128)} %get-tuple-element.18), channel_id=1, source_target_pairs={{0,8},{8,16},{16,24},{24,32},{32,40},{40,48},{48,56},{56,64},{64,7... | collective-permute-start | bytes 36872 | tf_op jit(solution)/shard_map/ppermute | solution.py:113
  156.8 16.1 %collective-permute-start.9 = (f32[8,384]{1,0:T(8,128)}, f32[8,384]{1,0:T(8,128)S(1)}, u32[]{:S(2)}, u32[]{:S(2)}) collective-permute-start(f32[8,384]{1,0:T(8,128)} %get-tuple-element.19), channel_id=1, source_target_pairs={{8,0},{16,8},{24,16},{32,24},{40,32},{48,40},{56,48},{64,56},{72,6... | collective-permute-start | bytes 36872 | tf_op jit(solution)/shard_map/ppermute | solution.py:113
  162.2 6.7 %collective-permute-start.10 = (f32[128,8]{1,0:T(8,128)}, f32[128,8]{1,0:T(8,128)S(1)}, u32[]{:S(2)}, u32[]{:S(2)}) collective-permute-start(f32[128,8]{1,0:T(8,128)} %get-tuple-element.20), channel_id=1, source_target_pairs={{0,1},{1,2},{2,3},{3,4},{4,5},{5,6},{6,7},{8,9},{9,10},{10,11},{11... | collective-permute-start | bytes 12296 | tf_op jit(solution)/shard_map/ppermute | solution.py:113
  167.0 5.8 %collective-permute-start.11 = (f32[128,8]{1,0:T(8,128)}, f32[128,8]{1,0:T(8,128)S(1)}, u32[]{:S(2)}, u32[]{:S(2)}) collective-permute-start(f32[128,8]{1,0:T(8,128)} %get-tuple-element.21), channel_id=1, source_target_pairs={{1,0},{2,1},{3,2},{4,3},{5,4},{6,5},{7,6},{9,8},{10,9},{11,10},{12... | collective-permute-start | bytes 12296 | tf_op jit(solution)/shard_map/ppermute | solution.py:113
  168.9 3.9 %copy-start.8 = (f32[128,8]{1,0:T(8,128)}, f32[128,8]{1,0:T(8,128)S(1)}, u32[]{:S(2)}) copy-start(f32[128,8]{1,0:T(8,128)S(1)} %collective-permute-done.10.by_ref) | copy-start | bytes 12292
  172.8 0.6 copy-start.10
  172.8 0.6 copy-start.16
  172.8 0.6 copy-start.18
  179.4 15.7 %collective-permute-start.12 = (f32[8,384]{1,0:T(8,128)}, f32[8,384]{1,0:T(8,128)S(1)}, u32[]{:S(2)}, u32[]{:S(2)}) collective-permute-start(f32[8,384]{1,0:T(8,128)} %get-tuple-element.23), channel_id=1, source_target_pairs={{0,8},{8,16},{16,24},{24,32},{32,40},{40,48},{48,56},{56,64},{64,7... | collective-permute-start | bytes 36872 | tf_op jit(solution)/shard_map/ppermute | solution.py:113
  181.3 13.8 %collective-permute-start.13 = (f32[8,384]{1,0:T(8,128)}, f32[8,384]{1,0:T(8,128)S(1)}, u32[]{:S(2)}, u32[]{:S(2)}) collective-permute-start(f32[8,384]{1,0:T(8,128)} %get-tuple-element.24), channel_id=1, source_target_pairs={{8,0},{16,8},{24,16},{32,24},{40,32},{48,40},{56,48},{64,56},{72,6... | collective-permute-start | bytes 36872 | tf_op jit(solution)/shard_map/ppermute | solution.py:113
  186.8 4.5 %collective-permute-start.14 = (f32[128,8]{1,0:T(8,128)}, f32[128,8]{1,0:T(8,128)S(1)}, u32[]{:S(2)}, u32[]{:S(2)}) collective-permute-start(f32[128,8]{1,0:T(8,128)} %get-tuple-element.25), channel_id=1, source_target_pairs={{0,1},{1,2},{2,3},{3,4},{4,5},{5,6},{6,7},{8,9},{9,10},{10,11},{11... | collective-permute-start | bytes 12296 | tf_op jit(solution)/shard_map/ppermute | solution.py:113
  189.4 5.8 %collective-permute-start.15 = (f32[128,8]{1,0:T(8,128)}, f32[128,8]{1,0:T(8,128)S(1)}, u32[]{:S(2)}, u32[]{:S(2)}) collective-permute-start(f32[128,8]{1,0:T(8,128)} %get-tuple-element.26), channel_id=1, source_target_pairs={{1,0},{2,1},{3,2},{4,3},{5,4},{6,5},{7,6},{9,8},{10,9},{11,10},{12... | collective-permute-start | bytes 12296 | tf_op jit(solution)/shard_map/ppermute | solution.py:113
  191.3 3.9 %copy-start.7 = (f32[128,8]{1,0:T(8,128)}, f32[128,8]{1,0:T(8,128)S(1)}, u32[]{:S(2)}) copy-start(f32[128,8]{1,0:T(8,128)S(1)} %collective-permute-done.14.by_ref) | copy-start | bytes 12292
  195.2 0.6 copy-start.9
  195.2 0.6 copy-start.15
  195.2 0.6 copy-start.17

commit v6 on v4

--- a/solution.py
+++ b/solution.py
@@ -169,6 +169,7 @@
         precision=lax.Precision.HIGHEST,
         preferred_element_type=jnp.float32,
     )
+    _, outgoing_strips = lax.optimization_barrier((child[0, 0, :], outgoing_strips))
     incoming = lax.all_to_all(
         outgoing_strips, ("gx", "gy"), split_axis=0, concat_axis=0, tiled=True
     )

time: 212 us -> 211 us (level)
    dot_general x2 -> x0, local copies, waits for them, and re-layouts: 5.88 us -> none  [the longest x1 2.97 us: shards(): jnp.dot(send_select, strip_values, precision=lax.Precision.HIGHEST, prefe...]
    all_to_all x1 -> x3, local copies, waits for them, and re-layouts: 3.65 us -> 8.83 us  [shards(): lax.all_to_all(outgoing_strips, ('gx', 'gy'), split_axis=0, concat_axis=0...]
    unnamed x55 -> x53, local copies, waits for them, and re-layouts: 9.75 us -> 9.51 us
  transfers between devices with their start and end apart: 19 -> 19, of which waited for: 4 -> 4; matrix products, arithmetic and copies ran while one was open for 30% -> 29% of each run, Pallas kernels for 0% -> 0%
where the time goes in v6:
time: 211 us; the launch traced here: 210 us
  starting transfers between devices  75.2 us (36%)
  local copies, waits for them, and re-layouts  48.7 us (23%)
  waiting for transfers between devices  39.8 us (19%)
  Pallas kernels  18 us (9%)
  other arithmetic  14.7 us (7%)
  matrix products  8.21 us (4%)
  between operations  4.94 us (2%)
    ppermute x12, starting transfers between devices, swap_edge(): return lax.ppermute(edge, axis, pairs)  37.1 us
    all_to_all x1, waiting for transfers between devices, shards(): lax.all_to_all(outgoing_strips, ('gx', 'gy'), split_axis=0, concat_axis=0...  19.8 us
    pallas_call x3, Pallas kernels, substep(): pl.pallas_call(functools.partial(substep_kernel, weight), out_shape=(jax....  18 us
    ppermute x4, starting transfers between devices, swap(): return lax.ppermute(edge, axis, pairs)  13.1 us
    all_to_all x1, waiting for transfers between devices, storm_rows(): lax.all_to_all(grid.reshape(levels, crows, widths), ('gx', 'gy'), 1, 1, t...  12.5 us
    all_to_all x1, starting transfers between devices, shards(): lax.all_to_all(outgoing_strips, ('gx', 'gy'), split_axis=0, concat_axis=0...  9.77 us
    unnamed x53, local copies, waits for them, and re-layouts  9.51 us
    all_to_all x1, starting transfers between devices, storm_rows(): gathered = lax.all_to_all(child, ('gx', 'gy'), 1, 1, tiled=True)  9.24 us
  transfers between devices with their start and end apart: 19, of which 4 were waited for; matrix products, arithmetic and copies ran while one was open for 29% of the time, Pallas kernels for 0%

profile of v6, /device:TPU:33, one launch (start us, length us, event | category | flops | bytes accessed | tf_op | source)
XLA Modules:
  0.0 209.5 jit_solution(10241050287535346415)
XLA Ops:
  0.6 1.6 fusion.34
  2.4 3.8 %collective-permute-start.3 = (f32[8,128]{1,0:T(8,128)S(1)}, f32[8,128]{1,0:T(8,128)S(1)}, u32[]{:S(2)}, u32[]{:S(2)}) collective-permute-start(f32[8,128]{1,0:T(8,128)S(1)} %bitcast.77), channel_id=1, source_target_pairs={{0,1},{1,2},{2,3},{3,4},{4,5},{5,6},{6,7},{8,9},{9,10},{10,11},{11... | collective-permute-start | bytes 12296 | tf_op jit(solution)/shard_map/ppermute | solution.py:25
  6.3 1.9 collective-permute-start.2
  8.3 3.1 %collective-permute-start.1 = (f32[8,512]{1,0:T(8,128)S(1)}, f32[8,512]{1,0:T(8,128)S(1)}, u32[]{:S(2)}, u32[]{:S(2)}) collective-permute-start(f32[8,512]{1,0:T(8,128)S(1)} %bitcast.73), channel_id=1, source_target_pairs={{0,8},{8,16},{16,24},{24,32},{32,40},{40,48},{48,56},{56,64},{64,7... | collective-permute-start | bytes 49160 | tf_op jit(solution)/shard_map/ppermute | solution.py:25
  11.5 4.3 %collective-permute-start = (f32[8,512]{1,0:T(8,128)S(1)}, f32[8,512]{1,0:T(8,128)S(1)}, u32[]{:S(2)}, u32[]{:S(2)}) collective-permute-start(f32[8,512]{1,0:T(8,128)S(1)} %bitcast.75), channel_id=1, source_target_pairs={{8,0},{16,8},{24,16},{32,24},{40,32},{48,40},{56,48},{64,56},{72,6... | collective-permute-start | bytes 49160 | tf_op jit(solution)/shard_map/ppermute | solution.py:25
  15.7 3.5 %copy.94 = f32[8,128,384]{2,0,1:T(8,128)} copy(f32[8,128,384]{2,1,0:T(8,128)} %param.11) | data formatting | bytes 3145728 | tf_op args[2]
  19.2 9.2 %all-to-all-start = ((f32[8,128,384]{2,0,1:T(8,128)}), f32[8,128,384]{2,0,1:T(8,128)}, u32[]{:S(2)}, u32[]{:S(2)}) async-start(f32[8,128,384]{2,0,1:T(8,128)} %copy.94), calls=%async_computation | async-start | bytes 3145728 | tf_op jit(solution)/shard_map/all_to_all | solution.py:53
  28.5 0.9 fusion.35
  29.3 2.5 %fusion.36 = (f32[7,128,512]{2,1,0:T(8,128)}, f32[7,128,512]{2,1,0:T(8,128)}) fusion(f32[8,128,512]{2,1,0:T(8,128)S(1)} %copy-done), kind=kLoop, calls=%fused_computation.78 | loop fusion | bytes 7340032 | tf_op jit(solution)/shard_map/slice | solution.py:125
  31.8 2.8 %fusion.33 = (f32[8,128,511]{2,1,0:T(8,128)}, f32[8,128,511]{2,1,0:T(8,128)}) fusion(f32[8,128,512]{2,1,0:T(8,128)S(1)} %copy-done), kind=kLoop, calls=%fused_computation.75 | loop fusion | bytes 8372224 | tf_op jit(solution)/shard_map/slice | solution.py:38
  34.6 2.5 %fusion.31 = (f32[8,127,512]{2,1,0:T(8,128)}, f32[8,127,512]{2,1,0:T(8,128)}) fusion(f32[8,128,512]{2,1,0:T(8,128)S(1)} %copy-done), kind=kLoop, calls=%fused_computation.73 | loop fusion | bytes 8323072 | tf_op jit(solution)/shard_map/slice | solution.py:36
  37.1 0.5 multiply_bitcast_fusion.1
  37.6 0.7 fusion.25
  38.5 0.6 fusion.26
  39.1 1.3 compare_and_fusion
  40.4 1.4 stack.9
  41.8 4.1 %copy.103 = f32[1,8,512,128]{3,1,2,0:T(8,128)} copy(f32[1,8,512,128]{3,2,1,0:T(8,128)} %stack.9) | data formatting | bytes 4194304 | tf_op jit(solution)/shard_map/stack | solution.py:163
  46.4 7.0 %fusion.4 = f32[8,128,512]{2,1,0:T(8,128)} fusion(f32[8,128,512]{2,1,0:T(8,128)S(1)} %copy-done, f32[1,128,512]{2,1,0:T(8,128)} %get-tuple-element.35, f32[7,128,512]{2,1,0:T(8,128)} %get-tuple-element.37, f32[7,128,512]{2,1,0:T(8,128)} %get-tuple-element.36, f32[1,128,512]{2,1,0:T(8,128)} %get-tuple-element.34, f32[8,128,511]{2,1,0:T(8,128)} %get-tuple-element.31, ...), kind=kLoop, calls=%fused_computation.15 | loop fusion | flops 13107200 | bytes 17039424 | tf_op jit(solution)/shard_map/add | solution.py:144
  53.5 1.6 stack.10
  55.1 1.2 copy.104
  56.4 0.4 copy-done.2
  56.7 2.2 %pad_maximum_fusion = f32[2,8,512,128]{3,1,2,0:T(8,128)} fusion(f32[1,8,512,128]{3,1,2,0:T(8,128)S(1)} %copy.104, f32[1,8,512,128]{3,1,2,0:T(8,128)S(1)} %copy-done.2), kind=kLoop, calls=%fused_computation.1 | loop fusion | flops 1048576 | bytes 8388608 | tf_op jit(solution)/shard_map/stack | solution.py:163
  59.0 2.9 %gather_fusion = f32[128,2,8,128]{3,2,1,0:T(8,128)S(1)} fusion(f32[2,8,512,128]{3,1,2,0:T(8,128)} %pad_maximum_fusion, s32[1024]{0:T(1024)S(1)} %pad_clamp_fusion), kind=kCustom, calls=%fused_computation | custom fusion | bytes 2097664 | tf_op jit(solution)/shard_map/jit(_take)/gather | solution.py:164
  62.1 0.4 copy.105
  62.5 1.0 fusion.17
  63.5 2.3 %all_to_all.16 = f32[128,2,2048]{2,1,0:T(2,128)} reshape(f32[256,2048]{1,0:T(8,128)S(1)} %fusion.17) | data formatting | bytes 4194304 | tf_op jit(solution)/shard_map/all_to_all | solution.py:173
  65.8 9.8 %all-to-all-start.2 = ((f32[128,2,2048]{2,1,0:T(2,128)}), f32[128,2,2048]{2,1,0:T(2,128)S(1)}, u32[]{:S(2)}, u32[]{:S(2)}) async-start(f32[128,2,2048]{2,1,0:T(2,128)} %all_to_all.16), calls=%async_computation.2 | async-start | bytes 4194304 | tf_op jit(solution)/shard_map/all_to_all | solution.py:173
  75.6 0.6 constant_dynamic-slice_fusion.2
  80.2 1.7 copy.95
  82.2 0.4 fusion.5
  82.6 2.1 copy.97
  84.7 19.8 %all-to-all-done.2 = f32[128,2,2048]{2,1,0:T(2,128)S(1)} async-done(((f32[128,2,2048]{2,1,0:T(2,128)}), f32[128,2,2048]{2,1,0:T(2,128)S(1)}, u32[]{:S(2)}, u32[]{:S(2)}) %all-to-all-start.2) | async-done | bytes 2097184 | tf_op jit(solution)/shard_map/all_to_all | solution.py:173
  104.5 1.4 copy-done.1
  105.9 6.0 %all-to-all-start.1 = ((f32[8,128,384]{2,0,1:T(8,128)}), f32[8,128,384]{2,0,1:T(8,128)S(1)}, u32[]{:S(2)}, u32[]{:S(2)}) async-start(f32[8,128,384]{2,0,1:T(8,128)} %bitcast.65), calls=%async_computation.1 | async-start | bytes 3145728 | tf_op jit(solution)/shard_map/all_to_all | solution.py:58
  112.7 0.7 convert_add_fusion.1.factor_ref
  113.4 3.7 %all_to_all.18 = f32[256,2048]{1,0:T(8,128)} reshape(f32[128,2,2048]{2,1,0:T(2,128)} %copy-done.1) | data formatting | bytes 4194304 | tf_op jit(solution)/shard_map/all_to_all | solution.py:173
  117.0 2.9 %copy.106 = f32[256,2048]{0,1:T(8,128)} copy(f32[256,2048]{1,0:T(8,128)} %all_to_all.18) | data formatting | bytes 4194304 | tf_op jit(solution)/shard_map/all_to_all | solution.py:173
  119.9 2.9 %fusion.13 = f32[128,2,8,128]{3,0,2,1:T(8,128)S(1)} fusion(f32[2,8,128,256]{3,2,1,0:T(8,128)} %bitcast.64, s32[256]{0:T(256)S(1)} %select_n.83), kind=kOutput, calls=%fused_computation.33 | convolution fusion | flops 805339136 | bytes 3146752 | tf_op jit(solution)/shard_map/dot_general | solution.py:183
  122.8 12.5 %all-to-all-done.1 = f32[8,128,384]{2,0,1:T(8,128)S(1)} async-done(((f32[8,128,384]{2,0,1:T(8,128)}), f32[8,128,384]{2,0,1:T(8,128)S(1)}, u32[]{:S(2)}, u32[]{:S(2)}) %all-to-all-start.1) | async-done | bytes 1572896 | tf_op jit(solution)/shard_map/all_to_all | solution.py:58
  135.3 2.5 %collective-permute-start.4 = (f32[8,384]{1,0:T(8,128)S(1)}, f32[8,384]{1,0:T(8,128)S(1)}, u32[]{:S(2)}, u32[]{:S(2)}) collective-permute-start(f32[8,384]{1,0:T(8,128)S(1)} %get-tuple-element.41), channel_id=1, source_target_pairs={{0,8},{8,16},{16,24},{24,32},{32,40},{40,48},{48,56},{56,64},{64,7... | collective-permute-start | bytes 36872 | tf_op jit(solution)/shard_map/ppermute | solution.py:113
  137.7 4.9 %collective-permute-start.5 = (f32[8,384]{1,0:T(8,128)S(1)}, f32[8,384]{1,0:T(8,128)S(1)}, u32[]{:S(2)}, u32[]{:S(2)}) collective-permute-start(f32[8,384]{1,0:T(8,128)S(1)} %get-tuple-element.40), channel_id=1, source_target_pairs={{8,0},{16,8},{24,16},{32,24},{40,32},{48,40},{56,48},{64,56},{72,6... | collective-permute-start | bytes 36872 | tf_op jit(solution)/shard_map/ppermute | solution.py:113
  142.7 1.0 fusion.37
  143.7 1.8 copy.118
  145.5 2.3 %collective-permute-start.6 = (f32[128,8]{1,0:T(8,128)S(1)}, f32[128,8]{1,0:T(8,128)S(1)}, u32[]{:S(2)}, u32[]{:S(2)}) collective-permute-start(f32[128,8]{1,0:T(8,128)S(1)} %bitcast.70), channel_id=1, source_target_pairs={{0,1},{1,2},{2,3},{3,4},{4,5},{5,6},{6,7},{8,9},{9,10},{10,11},{11... | collective-permute-start | bytes 12296 | tf_op jit(solution)/shard_map/ppermute | solution.py:113
  147.8 0.8 copy.119
  148.6 3.0 %collective-permute-start.7 = (f32[128,8]{1,0:T(8,128)S(1)}, f32[128,8]{1,0:T(8,128)S(1)}, u32[]{:S(2)}, u32[]{:S(2)}) collective-permute-start(f32[128,8]{1,0:T(8,128)S(1)} %bitcast.71), channel_id=1, source_target_pairs={{1,0},{2,1},{3,2},{4,3},{5,4},{6,5},{7,6},{9,8},{10,9},{11,10},{12... | collective-permute-start | bytes 12296 | tf_op jit(solution)/shard_map/ppermute | solution.py:113
  151.6 4.3 %convolution_bitcast_fusion.bound_ref = f32[2,8,128,384]{3,2,1,0:T(8,128)} fusion(f32[128,2,8,128]{3,0,2,1:T(8,128)S(1)} %fusion.13, f32[128]{0:T(128)S(1)} %iota_convert_fusion, f32[384]{0:T(512)S(1)} %add_clamp_fusion), kind=kOutput, calls=%fused_computation.16 | convolution fusion | flops 1208156160 | bytes 4196352 | tf_op jit(solution)/shard_map/tald,de->alte/dot_general | solution.py:187
  155.9 1.4 copy.109.child_ref
  157.4 0.8 broadcast_in_dim.69.divisor_ref
  158.2 6.0 %shard_map.104 = (f32[8,128,384]{2,1,0:T(8,128)}, f32[8,384]{1,0:T(8,128)}, f32[8,384]{1,0:T(8,128)}, f32[128,8]{1,0:T(8,128)}, f32[128,8]{1,0:T(8,128)}) custom-call(f32[2,8]{1,0:T(2,128)} %wind_ref.5, f32[8,128,384]{2,1,0:T(8,128)} %copy.109.child_ref, f32[8,384]{1,0:T(8,128)} %copy-done.14, f32[8,384]{1,0:T(8,128)} %copy-done.15, f32[128,8]{1,0:T(8,128)} %copy-done.6, ...), custom_call_target="tpu_custom_call" | custom-call | flops 11796480 | bytes 6684672 | tf_op jit(solution)/shard_map/pallas_call | solution.py:91
  164.2 1.9 collective-permute-start.8
  166.1 5.5 %collective-permute-start.9 = (f32[8,384]{1,0:T(8,128)}, f32[8,384]{1,0:T(8,128)S(1)}, u32[]{:S(2)}, u32[]{:S(2)}) collective-permute-start(f32[8,384]{1,0:T(8,128)} %get-tuple-element.15), channel_id=1, source_target_pairs={{8,0},{16,8},{24,16},{32,24},{40,32},{48,40},{56,48},{64,56},{72,6... | collective-permute-start | bytes 36872 | tf_op jit(solution)/shard_map/ppermute | solution.py:113
  171.6 3.2 %collective-permute-start.10 = (f32[128,8]{1,0:T(8,128)}, f32[128,8]{1,0:T(8,128)S(1)}, u32[]{:S(2)}, u32[]{:S(2)}) collective-permute-start(f32[128,8]{1,0:T(8,128)} %get-tuple-element.16), channel_id=1, source_target_pairs={{0,1},{1,2},{2,3},{3,4},{4,5},{5,6},{6,7},{8,9},{9,10},{10,11},{11... | collective-permute-start | bytes 12296 | tf_op jit(solution)/shard_map/ppermute | solution.py:113
  174.8 2.1 %collective-permute-start.11 = (f32[128,8]{1,0:T(8,128)}, f32[128,8]{1,0:T(8,128)S(1)}, u32[]{:S(2)}, u32[]{:S(2)}) collective-permute-start(f32[128,8]{1,0:T(8,128)} %get-tuple-element.17), channel_id=1, source_target_pairs={{1,0},{2,1},{3,2},{4,3},{5,4},{6,5},{7,6},{9,8},{10,9},{11,10},{12... | collective-permute-start | bytes 12296 | tf_op jit(solution)/shard_map/ppermute | solution.py:113
  176.9 3.6 %collective-permute-done.11.ay_ref = f32[128,8]{1,0:T(8,128)S(1)} collective-permute-done((f32[128,8]{1,0:T(8,128)}, f32[128,8]{1,0:T(8,128)S(1)}, u32[]{:S(2)}, u32[]{:S(2)}) %collective-permute-start.11) | collective-permute-done | bytes 4128 | tf_op jit(solution)/shard_map/ppermute | solution.py:113
  180.6 0.6 copy-done.11
  181.2 6.0 %shard_map.105 = (f32[8,128,384]{2,1,0:T(8,128)}, f32[8,384]{1,0:T(8,128)}, f32[8,384]{1,0:T(8,128)}, f32[128,8]{1,0:T(8,128)}, f32[128,8]{1,0:T(8,128)}) custom-call(f32[2,8]{1,0:T(2,128)} %wind_ref.5, f32[8,128,384]{2,1,0:T(8,128)} %get-tuple-element.13.child_ref, f32[8,384]{1,0:T(8,128)} %copy-done.17, f32[8,384]{1,0:T(8,128)} %copy-done.19, ...), custom_call_target="tpu_custom_call" | custom-call | flops 11796480 | bytes 6684672 | tf_op jit(solution)/shard_map/pallas_call | solution.py:91
  187.2 1.9 collective-permute-start.12
  189.1 5.5 %collective-permute-start.13 = (f32[8,384]{1,0:T(8,128)}, f32[8,384]{1,0:T(8,128)S(1)}, u32[]{:S(2)}, u32[]{:S(2)}) collective-permute-start(f32[8,384]{1,0:T(8,128)} %get-tuple-element.20), channel_id=1, source_target_pairs={{8,0},{16,8},{24,16},{32,24},{40,32},{48,40},{56,48},{64,56},{72,6... | collective-permute-start | bytes 36872 | tf_op jit(solution)/shard_map/ppermute | solution.py:113
  194.6 2.5 %collective-permute-start.14 = (f32[128,8]{1,0:T(8,128)}, f32[128,8]{1,0:T(8,128)S(1)}, u32[]{:S(2)}, u32[]{:S(2)}) collective-permute-start(f32[128,8]{1,0:T(8,128)} %get-tuple-element.21), channel_id=1, source_target_pairs={{0,1},{1,2},{2,3},{3,4},{4,5},{5,6},{6,7},{8,9},{9,10},{10,11},{11... | collective-permute-start | bytes 12296 | tf_op jit(solution)/shard_map/ppermute | solution.py:113
  197.1 1.9 collective-permute-start.15
  199.1 3.8 %collective-permute-done.15.ay_ref = f32[128,8]{1,0:T(8,128)S(1)} collective-permute-done((f32[128,8]{1,0:T(8,128)}, f32[128,8]{1,0:T(8,128)S(1)}, u32[]{:S(2)}, u32[]{:S(2)}) %collective-permute-start.15) | collective-permute-done | bytes 4128 | tf_op jit(solution)/shard_map/ppermute | solution.py:113
  203.0 0.6 copy-done.10
  203.6 6.0 %shard_map.106 = (f32[8,128,384]{2,1,0:T(8,128)}, f32[8,384]{1,0:T(8,128)}, f32[8,384]{1,0:T(8,128)}, f32[128,8]{1,0:T(8,128)}, f32[128,8]{1,0:T(8,128)}) custom-call(f32[2,8]{1,0:T(2,128)} %wind_ref.5, f32[8,128,384]{2,1,0:T(8,128)} %get-tuple-element.18.child_ref, f32[8,384]{1,0:T(8,128)} %copy-done.16, f32[8,384]{1,0:T(8,128)} %copy-done.18, ...), custom_call_target="tpu_custom_call" | custom-call | flops 11796480 | bytes 6684672 | tf_op jit(solution)/shard_map/pallas_call | solution.py:91
  (87 shorter events, 2.7 us)
Async XLA Ops:
  0.6 7.6 %copy-start = (f32[8,128,512]{2,1,0:T(8,128)S(1)}, f32[8,128,512]{2,1,0:T(8,128)}, u32[]{:S(2)}) copy-start(f32[8,128,512]{2,1,0:T(8,128)} %param.9) | copy-start | bytes 6291460
  2.4 43.5 %collective-permute-start.3 = (f32[8,128]{1,0:T(8,128)S(1)}, f32[8,128]{1,0:T(8,128)S(1)}, u32[]{:S(2)}, u32[]{:S(2)}) collective-permute-start(f32[8,128]{1,0:T(8,128)S(1)} %bitcast.77), channel_id=1, source_target_pairs={{0,1},{1,2},{2,3},{3,4},{4,5},{5,6},{6,7},{8,9},{9,10},{10,11},{11... | collective-permute-start | bytes 12296 | tf_op jit(solution)/shard_map/ppermute | solution.py:25
  6.3 39.8 %collective-permute-start.2 = (f32[8,128]{1,0:T(8,128)S(1)}, f32[8,128]{1,0:T(8,128)S(1)}, u32[]{:S(2)}, u32[]{:S(2)}) collective-permute-start(f32[8,128]{1,0:T(8,128)S(1)} %bitcast.79), channel_id=1, source_target_pairs={{1,0},{2,1},{3,2},{4,3},{5,4},{6,5},{7,6},{9,8},{10,9},{11,10},{12... | collective-permute-start | bytes 12296 | tf_op jit(solution)/shard_map/ppermute | solution.py:25
  8.3 38.0 %collective-permute-start.1 = (f32[8,512]{1,0:T(8,128)S(1)}, f32[8,512]{1,0:T(8,128)S(1)}, u32[]{:S(2)}, u32[]{:S(2)}) collective-permute-start(f32[8,512]{1,0:T(8,128)S(1)} %bitcast.73), channel_id=1, source_target_pairs={{0,8},{8,16},{16,24},{24,32},{32,40},{40,48},{48,56},{56,64},{64,7... | collective-permute-start | bytes 49160 | tf_op jit(solution)/shard_map/ppermute | solution.py:25
  11.5 34.9 %collective-permute-start = (f32[8,512]{1,0:T(8,128)S(1)}, f32[8,512]{1,0:T(8,128)S(1)}, u32[]{:S(2)}, u32[]{:S(2)}) collective-permute-start(f32[8,512]{1,0:T(8,128)S(1)} %bitcast.75), channel_id=1, source_target_pairs={{8,0},{16,8},{24,16},{32,24},{40,32},{48,40},{56,48},{64,56},{72,6... | collective-permute-start | bytes 49160 | tf_op jit(solution)/shard_map/ppermute | solution.py:25
  19.2 46.6 %all-to-all-start = ((f32[8,128,384]{2,0,1:T(8,128)}), f32[8,128,384]{2,0,1:T(8,128)}, u32[]{:S(2)}, u32[]{:S(2)}) async-start(f32[8,128,384]{2,0,1:T(8,128)} %copy.94), calls=%async_computation | async-start | bytes 3145728 | tf_op jit(solution)/shard_map/all_to_all | solution.py:53
  34.6 2.5 %copy-start.13 = (f32[2,8]{1,0:T(2,128)S(1)}, f32[2,8]{1,0:T(2,128)}, u32[]{:S(2)}) copy-start(f32[2,8]{1,0:T(2,128)} %wind_ref.5) | copy-start | bytes 196
  34.6 3.0 %copy-start.3 = (bf16[128,512]{1,0:T(8,128)(2,1)S(1)}, bf16[128,512]{1,0:T(8,128)(2,1)}, u32[]{:S(2)}) copy-start(bf16[128,512]{1,0:T(8,128)(2,1)} %param.10) | copy-start | bytes 393220
  34.6 3.8 %copy-start.5 = (s32[16384,1]{0,1:T(1,128)S(1)}, s32[16384,1]{0,1:T(1,128)}, u32[]{:S(2)}) copy-start(s32[16384,1]{0,1:T(1,128)} %param.14) | copy-start | bytes 196612
  55.1 1.6 copy-start.2
  59.0 2.9 %copy-start.22 = (pred[128]{0:T(512)(128)(4,1)S(1)}, pred[128]{0:T(512)(128)(4,1)}, u32[]{:S(2)}) copy-start(pred[128]{0:T(512)(128)(4,1)} %compare_and_fusion) | copy-start | bytes 388
  61.8 0.7 copy-start.20
  65.8 9.8 %copy-start.21 = (s32[2,4]{1,0:T(2,128)S(1)}, s32[2,4]{1,0:T(2,128)}, u32[]{:S(2)}) copy-start(s32[2,4]{1,0:T(2,128)} %param.17) | copy-start | bytes 100
  65.8 38.7 %all-to-all-start.2 = ((f32[128,2,2048]{2,1,0:T(2,128)}), f32[128,2,2048]{2,1,0:T(2,128)S(1)}, u32[]{:S(2)}, u32[]{:S(2)}) async-start(f32[128,2,2048]{2,1,0:T(2,128)} %all_to_all.16), calls=%async_computation.2 | async-start | bytes 4194304 | tf_op jit(solution)/shard_map/all_to_all | solution.py:173
  84.7 27.5 %copy-start.12 = (s32[16384]{0:T(1024)S(1)}, s32[16384]{0:T(1024)}, u32[]{:S(2)}) copy-start(s32[16384]{0:T(1024)} %param.16) | copy-start | bytes 196612
  84.7 28.0 %copy-start.4 = (bf16[128,384]{1,0:T(8,128)(2,1)S(1)}, bf16[128,384]{1,0:T(8,128)(2,1)}, u32[]{:S(2)}) copy-start(bf16[128,384]{1,0:T(8,128)(2,1)} %param.12) | copy-start | bytes 294916
  104.5 1.4 copy-start.1
  105.9 29.4 %all-to-all-start.1 = ((f32[8,128,384]{2,0,1:T(8,128)}), f32[8,128,384]{2,0,1:T(8,128)S(1)}, u32[]{:S(2)}, u32[]{:S(2)}) async-start(f32[8,128,384]{2,0,1:T(8,128)} %bitcast.65), calls=%async_computation.1 | async-start | bytes 3145728 | tf_op jit(solution)/shard_map/all_to_all | solution.py:58
  135.3 22.1 %collective-permute-start.4 = (f32[8,384]{1,0:T(8,128)S(1)}, f32[8,384]{1,0:T(8,128)S(1)}, u32[]{:S(2)}, u32[]{:S(2)}) collective-permute-start(f32[8,384]{1,0:T(8,128)S(1)} %get-tuple-element.41), channel_id=1, source_target_pairs={{0,8},{8,16},{16,24},{24,32},{32,40},{40,48},{48,56},{56,64},{64,7... | collective-permute-start | bytes 36872 | tf_op jit(solution)/shard_map/ppermute | solution.py:113
  137.7 19.7 %collective-permute-start.5 = (f32[8,384]{1,0:T(8,128)S(1)}, f32[8,384]{1,0:T(8,128)S(1)}, u32[]{:S(2)}, u32[]{:S(2)}) collective-permute-start(f32[8,384]{1,0:T(8,128)S(1)} %get-tuple-element.40), channel_id=1, source_target_pairs={{8,0},{16,8},{24,16},{32,24},{40,32},{48,40},{56,48},{64,56},{72,6... | collective-permute-start | bytes 36872 | tf_op jit(solution)/shard_map/ppermute | solution.py:113
  145.5 11.8 %collective-permute-start.6 = (f32[128,8]{1,0:T(8,128)S(1)}, f32[128,8]{1,0:T(8,128)S(1)}, u32[]{:S(2)}, u32[]{:S(2)}) collective-permute-start(f32[128,8]{1,0:T(8,128)S(1)} %bitcast.70), channel_id=1, source_target_pairs={{0,1},{1,2},{2,3},{3,4},{4,5},{5,6},{6,7},{8,9},{9,10},{10,11},{11... | collective-permute-start | bytes 12296 | tf_op jit(solution)/shard_map/ppermute | solution.py:113
  148.6 8.8 %collective-permute-start.7 = (f32[128,8]{1,0:T(8,128)S(1)}, f32[128,8]{1,0:T(8,128)S(1)}, u32[]{:S(2)}, u32[]{:S(2)}) collective-permute-start(f32[128,8]{1,0:T(8,128)S(1)} %bitcast.71), channel_id=1, source_target_pairs={{1,0},{2,1},{3,2},{4,3},{5,4},{6,5},{7,6},{9,8},{10,9},{11,10},{12... | collective-permute-start | bytes 12296 | tf_op jit(solution)/shard_map/ppermute | solution.py:113
  157.4 0.8 copy-start.6
  157.4 0.8 copy-start.7
  157.4 0.8 copy-start.14
  157.4 0.8 copy-start.15
  164.2 16.4 %collective-permute-start.8 = (f32[8,384]{1,0:T(8,128)}, f32[8,384]{1,0:T(8,128)S(1)}, u32[]{:S(2)}, u32[]{:S(2)}) collective-permute-start(f32[8,384]{1,0:T(8,128)} %get-tuple-element.14), channel_id=1, source_target_pairs={{0,8},{8,16},{16,24},{24,32},{32,40},{40,48},{48,56},{56,64},{64,7... | collective-permute-start | bytes 36872 | tf_op jit(solution)/shard_map/ppermute | solution.py:113
  166.1 14.4 %collective-permute-start.9 = (f32[8,384]{1,0:T(8,128)}, f32[8,384]{1,0:T(8,128)S(1)}, u32[]{:S(2)}, u32[]{:S(2)}) collective-permute-start(f32[8,384]{1,0:T(8,128)} %get-tuple-element.15), channel_id=1, source_target_pairs={{8,0},{16,8},{24,16},{32,24},{40,32},{48,40},{56,48},{64,56},{72,6... | collective-permute-start | bytes 36872 | tf_op jit(solution)/shard_map/ppermute | solution.py:113
  171.6 5.3 %collective-permute-start.10 = (f32[128,8]{1,0:T(8,128)}, f32[128,8]{1,0:T(8,128)S(1)}, u32[]{:S(2)}, u32[]{:S(2)}) collective-permute-start(f32[128,8]{1,0:T(8,128)} %get-tuple-element.16), channel_id=1, source_target_pairs={{0,1},{1,2},{2,3},{3,4},{4,5},{5,6},{6,7},{8,9},{9,10},{10,11},{11... | collective-permute-start | bytes 12296 | tf_op jit(solution)/shard_map/ppermute | solution.py:113
  174.8 5.8 %collective-permute-start.11 = (f32[128,8]{1,0:T(8,128)}, f32[128,8]{1,0:T(8,128)S(1)}, u32[]{:S(2)}, u32[]{:S(2)}) collective-permute-start(f32[128,8]{1,0:T(8,128)} %get-tuple-element.17), channel_id=1, source_target_pairs={{1,0},{2,1},{3,2},{4,3},{5,4},{6,5},{7,6},{9,8},{10,9},{11,10},{12... | collective-permute-start | bytes 12296 | tf_op jit(solution)/shard_map/ppermute | solution.py:113
  176.9 3.7 %copy-start.9 = (f32[128,8]{1,0:T(8,128)}, f32[128,8]{1,0:T(8,128)S(1)}, u32[]{:S(2)}) copy-start(f32[128,8]{1,0:T(8,128)S(1)} %collective-permute-done.10.by_ref) | copy-start | bytes 12292
  180.6 0.6 copy-start.11
  180.6 0.6 copy-start.17
  180.6 0.6 copy-start.19
  187.2 15.7 %collective-permute-start.12 = (f32[8,384]{1,0:T(8,128)}, f32[8,384]{1,0:T(8,128)S(1)}, u32[]{:S(2)}, u32[]{:S(2)}) collective-permute-start(f32[8,384]{1,0:T(8,128)} %get-tuple-element.19), channel_id=1, source_target_pairs={{0,8},{8,16},{16,24},{24,32},{32,40},{40,48},{48,56},{56,64},{64,7... | collective-permute-start | bytes 36872 | tf_op jit(solution)/shard_map/ppermute | solution.py:113
  189.1 13.8 %collective-permute-start.13 = (f32[8,384]{1,0:T(8,128)}, f32[8,384]{1,0:T(8,128)S(1)}, u32[]{:S(2)}, u32[]{:S(2)}) collective-permute-start(f32[8,384]{1,0:T(8,128)} %get-tuple-element.20), channel_id=1, source_target_pairs={{8,0},{16,8},{24,16},{32,24},{40,32},{48,40},{56,48},{64,56},{72,6... | collective-permute-start | bytes 36872 | tf_op jit(solution)/shard_map/ppermute | solution.py:113
  194.6 4.5 %collective-permute-start.14 = (f32[128,8]{1,0:T(8,128)}, f32[128,8]{1,0:T(8,128)S(1)}, u32[]{:S(2)}, u32[]{:S(2)}) collective-permute-start(f32[128,8]{1,0:T(8,128)} %get-tuple-element.21), channel_id=1, source_target_pairs={{0,1},{1,2},{2,3},{3,4},{4,5},{5,6},{6,7},{8,9},{9,10},{10,11},{11... | collective-permute-start | bytes 12296 | tf_op jit(solution)/shard_map/ppermute | solution.py:113
  197.1 5.8 %collective-permute-start.15 = (f32[128,8]{1,0:T(8,128)}, f32[128,8]{1,0:T(8,128)S(1)}, u32[]{:S(2)}, u32[]{:S(2)}) collective-permute-start(f32[128,8]{1,0:T(8,128)} %get-tuple-element.22), channel_id=1, source_target_pairs={{1,0},{2,1},{3,2},{4,3},{5,4},{6,5},{7,6},{9,8},{10,9},{11,10},{12... | collective-permute-start | bytes 12296 | tf_op jit(solution)/shard_map/ppermute | solution.py:113
  199.1 3.9 %copy-start.8 = (f32[128,8]{1,0:T(8,128)}, f32[128,8]{1,0:T(8,128)S(1)}, u32[]{:S(2)}) copy-start(f32[128,8]{1,0:T(8,128)S(1)} %collective-permute-done.14.by_ref) | copy-start | bytes 12292
  202.9 0.6 copy-start.10
  202.9 0.6 copy-start.16
  203.0 0.6 copy-start.18

commit v7 on v4

--- a/solution.py
+++ b/solution.py
@@ -169,6 +169,7 @@
         precision=lax.Precision.HIGHEST,
         preferred_element_type=jnp.float32,
     )
+    outgoing_strips = outgoing_strips + 0.0 * child[0, 0, 0]
     incoming = lax.all_to_all(
         outgoing_strips, ("gx", "gy"), split_axis=0, concat_axis=0, tiled=True
     )

time: 212 us -> 195 us (0.920)
  waiting for transfers between devices: 39.9 us -> 24.2 us
    all_to_all x1, waiting for transfers between devices: 19.9 us -> 7.05 us  [shards(): lax.all_to_all(outgoing_strips, ('gx', 'gy'), split_axis=0, concat_axis=0...]
    all_to_all x1, waiting for transfers between devices: 12.5 us -> 0.01 us  [storm_rows(): lax.all_to_all(grid.reshape(levels, crows, widths), ('gx', 'gy'), 1, 1, t...]
    all_to_all x1, waiting for transfers between devices: 0.01 us -> 10.5 us  [storm_rows(): gathered = lax.all_to_all(child, ('gx', 'gy'), 1, 1, tiled=True)]
    dot_general x2 -> x0, local copies, waits for them, and re-layouts: 5.88 us -> none  [the longest x1 2.97 us: shards(): jnp.dot(send_select, strip_values, precision=lax.Precision.HIGHEST, prefe...]
    all_to_all x1 -> x3, local copies, waits for them, and re-layouts: 3.65 us -> 6.61 us  [shards(): lax.all_to_all(outgoing_strips, ('gx', 'gy'), split_axis=0, concat_axis=0...]
    unnamed x55 -> x53, local copies, waits for them, and re-layouts: 9.75 us -> 7.12 us
where the time goes in v7:
time: 195 us; the launch traced here: 194 us
  starting transfers between devices  77.1 us (40%)
  local copies, waits for them, and re-layouts  47.7 us (24%)
  waiting for transfers between devices  24.2 us (12%)
  Pallas kernels  18 us (9%)
  other arithmetic  14.7 us (8%)
  matrix products  6.65 us (3%)
  between operations  5.76 us (3%)
    ppermute x12, starting transfers between devices, swap_edge(): return lax.ppermute(edge, axis, pairs)  38 us
    pallas_call x3, Pallas kernels, substep(): pl.pallas_call(functools.partial(substep_kernel, weight), out_shape=(jax....  18 us
    ppermute x4, starting transfers between devices, swap(): return lax.ppermute(edge, axis, pairs)  13.1 us
    all_to_all x1, waiting for transfers between devices, storm_rows(): gathered = lax.all_to_all(child, ('gx', 'gy'), 1, 1, tiled=True)  10.5 us
    all_to_all x1, starting transfers between devices, shards(): lax.all_to_all(outgoing_strips, ('gx', 'gy'), split_axis=0, concat_axis=0...  9.77 us
    all_to_all x1, starting transfers between devices, storm_rows(): gathered = lax.all_to_all(child, ('gx', 'gy'), 1, 1, tiled=True)  9.25 us
    another operation x4, local copies, waits for them, and re-layouts, shards(): jnp.stack([parent_field, new_parent]).reshape(2, levels, -1, STRIP)  8.37 us
    unnamed x53, local copies, waits for them, and re-layouts  7.12 us
  transfers between devices with their start and end apart: 19, of which 4 were waited for; matrix products, arithmetic and copies ran while one was open for 30% of the time, Pallas kernels for 0%

profile of v7, /device:TPU:33, one launch (start us, length us, event | category | flops | bytes accessed | tf_op | source)
XLA Modules:
  0.0 194.1 jit_solution(6677478912859269465)
XLA Ops:
  0.6 1.6 fusion.33
  2.4 3.8 %collective-permute-start.3 = (f32[8,128]{1,0:T(8,128)S(1)}, f32[8,128]{1,0:T(8,128)S(1)}, u32[]{:S(2)}, u32[]{:S(2)}) collective-permute-start(f32[8,128]{1,0:T(8,128)S(1)} %bitcast.78), channel_id=1, source_target_pairs={{0,1},{1,2},{2,3},{3,4},{4,5},{5,6},{6,7},{8,9},{9,10},{10,11},{11... | collective-permute-start | bytes 12296 | tf_op jit(solution)/shard_map/ppermute | solution.py:25
  6.3 1.9 collective-permute-start.2
  8.3 3.1 %collective-permute-start.1 = (f32[8,512]{1,0:T(8,128)S(1)}, f32[8,512]{1,0:T(8,128)S(1)}, u32[]{:S(2)}, u32[]{:S(2)}) collective-permute-start(f32[8,512]{1,0:T(8,128)S(1)} %bitcast.74), channel_id=1, source_target_pairs={{0,8},{8,16},{16,24},{24,32},{32,40},{40,48},{48,56},{56,64},{64,7... | collective-permute-start | bytes 49160 | tf_op jit(solution)/shard_map/ppermute | solution.py:25
  11.5 4.3 %collective-permute-start = (f32[8,512]{1,0:T(8,128)S(1)}, f32[8,512]{1,0:T(8,128)S(1)}, u32[]{:S(2)}, u32[]{:S(2)}) collective-permute-start(f32[8,512]{1,0:T(8,128)S(1)} %bitcast.76), channel_id=1, source_target_pairs={{8,0},{16,8},{24,16},{32,24},{40,32},{48,40},{56,48},{64,56},{72,6... | collective-permute-start | bytes 49160 | tf_op jit(solution)/shard_map/ppermute | solution.py:25
  15.7 3.5 %copy.94 = f32[8,128,384]{2,0,1:T(8,128)} copy(f32[8,128,384]{2,1,0:T(8,128)} %param.11) | data formatting | bytes 3145728 | tf_op args[2]
  19.2 9.2 %all-to-all-start = ((f32[8,128,384]{2,0,1:T(8,128)}), f32[8,128,384]{2,0,1:T(8,128)}, u32[]{:S(2)}, u32[]{:S(2)}) async-start(f32[8,128,384]{2,0,1:T(8,128)} %copy.94), calls=%async_computation | async-start | bytes 3145728 | tf_op jit(solution)/shard_map/all_to_all | solution.py:53
  28.5 0.6 constant_dynamic-slice_fusion.2
  32.9 0.7 fusion.24
  33.8 0.6 fusion.25
  34.4 0.5 multiply_bitcast_fusion.1
  35.0 0.9 fusion.34
  35.8 2.8 %fusion.32 = (f32[8,128,511]{2,1,0:T(8,128)}, f32[8,128,511]{2,1,0:T(8,128)}) fusion(f32[8,128,512]{2,1,0:T(8,128)S(1)} %copy-done), kind=kLoop, calls=%fused_computation.75 | loop fusion | bytes 8372224 | tf_op jit(solution)/shard_map/slice | solution.py:38
  38.6 2.5 %fusion.30 = (f32[8,127,512]{2,1,0:T(8,128)}, f32[8,127,512]{2,1,0:T(8,128)}) fusion(f32[8,128,512]{2,1,0:T(8,128)S(1)} %copy-done), kind=kLoop, calls=%fused_computation.73 | loop fusion | bytes 8323072 | tf_op jit(solution)/shard_map/slice | solution.py:36
  41.1 10.5 %all-to-all-done = f32[8,128,384]{2,0,1:T(8,128)} async-done(((f32[8,128,384]{2,0,1:T(8,128)}), f32[8,128,384]{2,0,1:T(8,128)}, u32[]{:S(2)}, u32[]{:S(2)}) %all-to-all-start) | async-done | bytes 1572896 | tf_op jit(solution)/shard_map/all_to_all | solution.py:53
  51.6 1.7 copy.95
  53.6 0.4 fusion.5
  54.0 2.1 %copy.97 = f32[8,16,8,384]{3,0,2,1:T(8,128)} copy(f32[8,16,8,384]{3,2,1,0:T(8,128)S(1)} %fusion.5) | data formatting | bytes 3145728 | tf_op jit(solution)/shard_map/jit(_roll_dynamic)/dynamic_slice | solution.py:57
  56.1 7.0 %all-to-all-start.1 = ((f32[8,128,384]{2,0,1:T(8,128)}), f32[8,128,384]{2,0,1:T(8,128)}, u32[]{:S(2)}, u32[]{:S(2)}) async-start(f32[8,128,384]{2,0,1:T(8,128)} %bitcast.66), calls=%async_computation.1 | async-start | bytes 3145728 | tf_op jit(solution)/shard_map/all_to_all | solution.py:58
  63.1 2.4 %fusion.35 = (f32[7,128,512]{2,1,0:T(8,128)}, f32[7,128,512]{2,1,0:T(8,128)}) fusion(f32[8,128,512]{2,1,0:T(8,128)S(1)} %copy-done), kind=kLoop, calls=%fused_computation.78 | loop fusion | bytes 7340032 | tf_op jit(solution)/shard_map/slice | solution.py:125
  65.5 1.3 compare_and_fusion
  66.7 1.4 stack.9
  68.1 4.1 %copy.103 = f32[1,8,512,128]{3,1,2,0:T(8,128)} copy(f32[1,8,512,128]{3,2,1,0:T(8,128)} %stack.9) | data formatting | bytes 4194304 | tf_op jit(solution)/shard_map/stack | solution.py:163
  72.8 7.0 %fusion.4 = f32[8,128,512]{2,1,0:T(8,128)} fusion(f32[8,128,512]{2,1,0:T(8,128)S(1)} %copy-done, f32[1,128,512]{2,1,0:T(8,128)} %get-tuple-element.35, f32[7,128,512]{2,1,0:T(8,128)} %get-tuple-element.37, f32[7,128,512]{2,1,0:T(8,128)} %get-tuple-element.36, f32[1,128,512]{2,1,0:T(8,128)} %get-tuple-element.34, f32[8,128,511]{2,1,0:T(8,128)} %get-tuple-element.31, ...), kind=kLoop, calls=%fused_computation.16 | loop fusion | flops 13107200 | bytes 17039424 | tf_op jit(solution)/shard_map/add | solution.py:144
  79.8 1.6 stack.10
  81.5 1.2 copy.104
  83.1 2.2 %pad_maximum_fusion = f32[2,8,512,128]{3,1,2,0:T(8,128)} fusion(f32[1,8,512,128]{3,1,2,0:T(8,128)S(1)} %copy.104, f32[1,8,512,128]{3,1,2,0:T(8,128)S(1)} %copy-done.1), kind=kLoop, calls=%fused_computation.1 | loop fusion | flops 1048576 | bytes 8388608 | tf_op jit(solution)/shard_map/stack | solution.py:163
  85.3 2.9 %gather_fusion = f32[128,2,8,128]{3,2,1,0:T(8,128)S(1)} fusion(f32[2,8,512,128]{3,1,2,0:T(8,128)} %pad_maximum_fusion, s32[1024]{0:T(1024)S(1)} %pad_clamp_fusion), kind=kCustom, calls=%fused_computation | custom fusion | bytes 2097664 | tf_op jit(solution)/shard_map/jit(_take)/gather | solution.py:164
  88.4 0.4 copy.105
  88.9 1.2 slice.82
  90.7 1.0 convolution_add_fusion
  91.7 2.3 %all_to_all.16 = f32[128,2,2048]{2,1,0:T(2,128)} reshape(f32[256,2048]{1,0:T(8,128)S(1)} %convolution_add_fusion) | data formatting | bytes 4194304 | tf_op jit(solution)/shard_map/all_to_all | solution.py:173
  94.0 9.8 %all-to-all-start.2 = ((f32[128,2,2048]{2,1,0:T(2,128)}), f32[128,2,2048]{2,1,0:T(2,128)S(1)}, u32[]{:S(2)}, u32[]{:S(2)}) async-start(f32[128,2,2048]{2,1,0:T(2,128)} %all_to_all.16), calls=%async_computation.2 | async-start | bytes 4194304 | tf_op jit(solution)/shard_map/all_to_all | solution.py:173
  104.8 0.7 convert_add_fusion.1.factor_ref
  105.5 0.7 slice_bitcast_fusion
  106.2 3.1 %collective-permute-start.4 = (f32[8,384]{1,0:T(8,128)S(1)}, f32[8,384]{1,0:T(8,128)S(1)}, u32[]{:S(2)}, u32[]{:S(2)}) collective-permute-start(f32[8,384]{1,0:T(8,128)S(1)} %get-tuple-element.41), channel_id=1, source_target_pairs={{0,8},{8,16},{16,24},{24,32},{32,40},{40,48},{48,56},{56,64},{64,7... | collective-permute-start | bytes 36872 | tf_op jit(solution)/shard_map/ppermute | solution.py:113
  109.4 4.3 %collective-permute-start.5 = (f32[8,384]{1,0:T(8,128)S(1)}, f32[8,384]{1,0:T(8,128)S(1)}, u32[]{:S(2)}, u32[]{:S(2)}) collective-permute-start(f32[8,384]{1,0:T(8,128)S(1)} %get-tuple-element.40), channel_id=1, source_target_pairs={{8,0},{16,8},{24,16},{32,24},{40,32},{48,40},{56,48},{64,56},{72,6... | collective-permute-start | bytes 36872 | tf_op jit(solution)/shard_map/ppermute | solution.py:113
  113.6 1.4 fusion.36
  115.1 0.8 copy.118
  115.9 4.0 %collective-permute-start.6 = (f32[128,8]{1,0:T(8,128)S(1)}, f32[128,8]{1,0:T(8,128)S(1)}, u32[]{:S(2)}, u32[]{:S(2)}) collective-permute-start(f32[128,8]{1,0:T(8,128)S(1)} %bitcast.71), channel_id=1, source_target_pairs={{0,1},{1,2},{2,3},{3,4},{4,5},{5,6},{6,7},{8,9},{9,10},{10,11},{11... | collective-permute-start | bytes 12296 | tf_op jit(solution)/shard_map/ppermute | solution.py:113
  119.9 0.8 copy.119
  120.7 2.1 %collective-permute-start.7 = (f32[128,8]{1,0:T(8,128)S(1)}, f32[128,8]{1,0:T(8,128)S(1)}, u32[]{:S(2)}, u32[]{:S(2)}) collective-permute-start(f32[128,8]{1,0:T(8,128)S(1)} %bitcast.72), channel_id=1, source_target_pairs={{1,0},{2,1},{3,2},{4,3},{5,4},{6,5},{7,6},{9,8},{10,9},{11,10},{12... | collective-permute-start | bytes 12296 | tf_op jit(solution)/shard_map/ppermute | solution.py:113
  122.8 2.9 %copy.109.child_ref = f32[8,128,384]{2,1,0:T(8,128)} copy(f32[8,128,384]{2,0,1:T(8,128)} %all-to-all-done.1) | data formatting | bytes 3145728 | tf_op jit(solution)/shard_map/all_to_all | solution.py:58
  125.7 7.0 %all-to-all-done.2 = f32[128,2,2048]{2,1,0:T(2,128)S(1)} async-done(((f32[128,2,2048]{2,1,0:T(2,128)}), f32[128,2,2048]{2,1,0:T(2,128)S(1)}, u32[]{:S(2)}, u32[]{:S(2)}) %all-to-all-start.2) | async-done | bytes 2097184 | tf_op jit(solution)/shard_map/all_to_all | solution.py:173
  132.7 2.4 %all_to_all.18 = f32[256,2048]{1,0:T(8,128)} reshape(f32[128,2,2048]{2,1,0:T(2,128)S(1)} %all-to-all-done.2) | data formatting | bytes 4194304 | tf_op jit(solution)/shard_map/all_to_all | solution.py:173
  135.2 1.9 copy.106
  137.1 1.3 fusion.13
  138.4 4.3 %convolution_bitcast_fusion.bound_ref = f32[2,8,128,384]{3,2,1,0:T(8,128)} fusion(f32[128,2,8,128]{3,0,2,1:T(8,128)S(1)} %fusion.13, f32[128]{0:T(128)S(1)} %iota_convert_fusion, f32[384]{0:T(512)S(1)} %add_clamp_fusion), kind=kOutput, calls=%fused_computation.17 | convolution fusion | flops 1208156160 | bytes 4196352 | tf_op jit(solution)/shard_map/tald,de->alte/dot_general | solution.py:187
  142.8 0.8 broadcast_in_dim.69.divisor_ref
  143.6 6.0 %shard_map.104 = (f32[8,128,384]{2,1,0:T(8,128)}, f32[8,384]{1,0:T(8,128)}, f32[8,384]{1,0:T(8,128)}, f32[128,8]{1,0:T(8,128)}, f32[128,8]{1,0:T(8,128)}) custom-call(f32[2,8]{1,0:T(2,128)} %wind_ref.5, f32[8,128,384]{2,1,0:T(8,128)} %copy.109.child_ref, f32[8,384]{1,0:T(8,128)} %copy-done.13, f32[8,384]{1,0:T(8,128)} %copy-done.14, f32[128,8]{1,0:T(8,128)} %copy-done.5, ...), custom_call_target="tpu_custom_call" | custom-call | flops 11796480 | bytes 6684672 | tf_op jit(solution)/shard_map/pallas_call | solution.py:91
  149.6 2.5 %collective-permute-start.8 = (f32[8,384]{1,0:T(8,128)}, f32[8,384]{1,0:T(8,128)S(1)}, u32[]{:S(2)}, u32[]{:S(2)}) collective-permute-start(f32[8,384]{1,0:T(8,128)} %get-tuple-element.14), channel_id=1, source_target_pairs={{0,8},{8,16},{16,24},{24,32},{32,40},{40,48},{48,56},{56,64},{64,7... | collective-permute-start | bytes 36872 | tf_op jit(solution)/shard_map/ppermute | solution.py:113
  152.1 4.9 %collective-permute-start.9 = (f32[8,384]{1,0:T(8,128)}, f32[8,384]{1,0:T(8,128)S(1)}, u32[]{:S(2)}, u32[]{:S(2)}) collective-permute-start(f32[8,384]{1,0:T(8,128)} %get-tuple-element.15), channel_id=1, source_target_pairs={{8,0},{16,8},{24,16},{32,24},{40,32},{48,40},{56,48},{64,56},{72,6... | collective-permute-start | bytes 36872 | tf_op jit(solution)/shard_map/ppermute | solution.py:113
  157.0 2.3 %collective-permute-start.10 = (f32[128,8]{1,0:T(8,128)}, f32[128,8]{1,0:T(8,128)S(1)}, u32[]{:S(2)}, u32[]{:S(2)}) collective-permute-start(f32[128,8]{1,0:T(8,128)} %get-tuple-element.16), channel_id=1, source_target_pairs={{0,1},{1,2},{2,3},{3,4},{4,5},{5,6},{6,7},{8,9},{9,10},{10,11},{11... | collective-permute-start | bytes 12296 | tf_op jit(solution)/shard_map/ppermute | solution.py:113
  159.3 2.9 %collective-permute-start.11 = (f32[128,8]{1,0:T(8,128)}, f32[128,8]{1,0:T(8,128)S(1)}, u32[]{:S(2)}, u32[]{:S(2)}) collective-permute-start(f32[128,8]{1,0:T(8,128)} %get-tuple-element.17), channel_id=1, source_target_pairs={{1,0},{2,1},{3,2},{4,3},{5,4},{6,5},{7,6},{9,8},{10,9},{11,10},{12... | collective-permute-start | bytes 12296 | tf_op jit(solution)/shard_map/ppermute | solution.py:113
  162.3 2.8 %collective-permute-done.11.ay_ref = f32[128,8]{1,0:T(8,128)S(1)} collective-permute-done((f32[128,8]{1,0:T(8,128)}, f32[128,8]{1,0:T(8,128)S(1)}, u32[]{:S(2)}, u32[]{:S(2)}) %collective-permute-start.11) | collective-permute-done | bytes 4128 | tf_op jit(solution)/shard_map/ppermute | solution.py:113
  165.2 0.6 copy-done.10
  165.8 6.0 %shard_map.105 = (f32[8,128,384]{2,1,0:T(8,128)}, f32[8,384]{1,0:T(8,128)}, f32[8,384]{1,0:T(8,128)}, f32[128,8]{1,0:T(8,128)}, f32[128,8]{1,0:T(8,128)}) custom-call(f32[2,8]{1,0:T(2,128)} %wind_ref.5, f32[8,128,384]{2,1,0:T(8,128)} %get-tuple-element.13.child_ref, f32[8,384]{1,0:T(8,128)} %copy-done.16, f32[8,384]{1,0:T(8,128)} %copy-done.18, ...), custom_call_target="tpu_custom_call" | custom-call | flops 11796480 | bytes 6684672 | tf_op jit(solution)/shard_map/pallas_call | solution.py:91
  171.8 1.9 collective-permute-start.12
  173.7 5.5 %collective-permute-start.13 = (f32[8,384]{1,0:T(8,128)}, f32[8,384]{1,0:T(8,128)S(1)}, u32[]{:S(2)}, u32[]{:S(2)}) collective-permute-start(f32[8,384]{1,0:T(8,128)} %get-tuple-element.20), channel_id=1, source_target_pairs={{8,0},{16,8},{24,16},{32,24},{40,32},{48,40},{56,48},{64,56},{72,6... | collective-permute-start | bytes 36872 | tf_op jit(solution)/shard_map/ppermute | solution.py:113
  179.2 2.5 %collective-permute-start.14 = (f32[128,8]{1,0:T(8,128)}, f32[128,8]{1,0:T(8,128)S(1)}, u32[]{:S(2)}, u32[]{:S(2)}) collective-permute-start(f32[128,8]{1,0:T(8,128)} %get-tuple-element.21), channel_id=1, source_target_pairs={{0,1},{1,2},{2,3},{3,4},{4,5},{5,6},{6,7},{8,9},{9,10},{10,11},{11... | collective-permute-start | bytes 12296 | tf_op jit(solution)/shard_map/ppermute | solution.py:113
  181.7 1.9 collective-permute-start.15
  183.7 3.8 %collective-permute-done.15.ay_ref = f32[128,8]{1,0:T(8,128)S(1)} collective-permute-done((f32[128,8]{1,0:T(8,128)}, f32[128,8]{1,0:T(8,128)S(1)}, u32[]{:S(2)}, u32[]{:S(2)}) %collective-permute-start.15) | collective-permute-done | bytes 4128 | tf_op jit(solution)/shard_map/ppermute | solution.py:113
  187.5 0.6 copy-done.9
  188.2 6.0 %shard_map.106 = (f32[8,128,384]{2,1,0:T(8,128)}, f32[8,384]{1,0:T(8,128)}, f32[8,384]{1,0:T(8,128)}, f32[128,8]{1,0:T(8,128)}, f32[128,8]{1,0:T(8,128)}) custom-call(f32[2,8]{1,0:T(2,128)} %wind_ref.5, f32[8,128,384]{2,1,0:T(8,128)} %get-tuple-element.18.child_ref, f32[8,384]{1,0:T(8,128)} %copy-done.15, f32[8,384]{1,0:T(8,128)} %copy-done.17, ...), custom_call_target="tpu_custom_call" | custom-call | flops 11796480 | bytes 6684672 | tf_op jit(solution)/shard_map/pallas_call | solution.py:91
  (88 shorter events, 3.1 us)
Async XLA Ops:
  0.6 7.6 %copy-start = (f32[8,128,512]{2,1,0:T(8,128)S(1)}, f32[8,128,512]{2,1,0:T(8,128)}, u32[]{:S(2)}) copy-start(f32[8,128,512]{2,1,0:T(8,128)} %param.9) | copy-start | bytes 6291460
  2.4 69.9 %collective-permute-start.3 = (f32[8,128]{1,0:T(8,128)S(1)}, f32[8,128]{1,0:T(8,128)S(1)}, u32[]{:S(2)}, u32[]{:S(2)}) collective-permute-start(f32[8,128]{1,0:T(8,128)S(1)} %bitcast.78), channel_id=1, source_target_pairs={{0,1},{1,2},{2,3},{3,4},{4,5},{5,6},{6,7},{8,9},{9,10},{10,11},{11... | collective-permute-start | bytes 12296 | tf_op jit(solution)/shard_map/ppermute | solution.py:25
  6.3 66.1 %collective-permute-start.2 = (f32[8,128]{1,0:T(8,128)S(1)}, f32[8,128]{1,0:T(8,128)S(1)}, u32[]{:S(2)}, u32[]{:S(2)}) collective-permute-start(f32[8,128]{1,0:T(8,128)S(1)} %bitcast.80), channel_id=1, source_target_pairs={{1,0},{2,1},{3,2},{4,3},{5,4},{6,5},{7,6},{9,8},{10,9},{11,10},{12... | collective-permute-start | bytes 12296 | tf_op jit(solution)/shard_map/ppermute | solution.py:25
  8.3 64.4 %collective-permute-start.1 = (f32[8,512]{1,0:T(8,128)S(1)}, f32[8,512]{1,0:T(8,128)S(1)}, u32[]{:S(2)}, u32[]{:S(2)}) collective-permute-start(f32[8,512]{1,0:T(8,128)S(1)} %bitcast.74), channel_id=1, source_target_pairs={{0,8},{8,16},{16,24},{24,32},{32,40},{40,48},{48,56},{56,64},{64,7... | collective-permute-start | bytes 49160 | tf_op jit(solution)/shard_map/ppermute | solution.py:25
  11.5 61.3 %collective-permute-start = (f32[8,512]{1,0:T(8,128)S(1)}, f32[8,512]{1,0:T(8,128)S(1)}, u32[]{:S(2)}, u32[]{:S(2)}) collective-permute-start(f32[8,512]{1,0:T(8,128)S(1)} %bitcast.76), channel_id=1, source_target_pairs={{8,0},{16,8},{24,16},{32,24},{40,32},{48,40},{56,48},{64,56},{72,6... | collective-permute-start | bytes 49160 | tf_op jit(solution)/shard_map/ppermute | solution.py:25
  19.2 9.3 %copy-start.21 = (s32[2,4]{1,0:T(2,128)S(1)}, s32[2,4]{1,0:T(2,128)}, u32[]{:S(2)}) copy-start(s32[2,4]{1,0:T(2,128)} %param.17) | copy-start | bytes 100
  19.2 14.4 %copy-start.4 = (s32[16384,1]{0,1:T(1,128)S(1)}, s32[16384,1]{0,1:T(1,128)}, u32[]{:S(2)}) copy-start(s32[16384,1]{0,1:T(1,128)} %param.14) | copy-start | bytes 196612
  19.2 15.2 %copy-start.12 = (f32[2,8]{1,0:T(2,128)S(1)}, f32[2,8]{1,0:T(2,128)}, u32[]{:S(2)}) copy-start(f32[2,8]{1,0:T(2,128)} %wind_ref.5) | copy-start | bytes 196
  19.2 15.7 %copy-start.2 = (bf16[128,512]{1,0:T(8,128)(2,1)S(1)}, bf16[128,512]{1,0:T(8,128)(2,1)}, u32[]{:S(2)}) copy-start(bf16[128,512]{1,0:T(8,128)(2,1)} %param.10) | copy-start | bytes 393220
  19.2 32.3 %all-to-all-start = ((f32[8,128,384]{2,0,1:T(8,128)}), f32[8,128,384]{2,0,1:T(8,128)}, u32[]{:S(2)}, u32[]{:S(2)}) async-start(f32[8,128,384]{2,0,1:T(8,128)} %copy.94), calls=%async_computation | async-start | bytes 3145728 | tf_op jit(solution)/shard_map/all_to_all | solution.py:53
  56.1 32.8 %all-to-all-start.1 = ((f32[8,128,384]{2,0,1:T(8,128)}), f32[8,128,384]{2,0,1:T(8,128)}, u32[]{:S(2)}, u32[]{:S(2)}) async-start(f32[8,128,384]{2,0,1:T(8,128)} %bitcast.66), calls=%async_computation.1 | async-start | bytes 3145728 | tf_op jit(solution)/shard_map/all_to_all | solution.py:58
  68.1 4.7 %copy-start.19 = (f32[8]{0:T(128)S(1)}, f32[8]{0:T(128)}, u32[]{:S(2)}) copy-start(f32[8]{0:T(128)} %get-tuple-element.44) | copy-start | bytes 100
  81.5 1.6 copy-start.1
  85.3 2.9 %copy-start.22 = (pred[128]{0:T(512)(128)(4,1)S(1)}, pred[128]{0:T(512)(128)(4,1)}, u32[]{:S(2)}) copy-start(pred[128]{0:T(512)(128)(4,1)} %compare_and_fusion) | copy-start | bytes 388
  88.2 2.5 %copy-start.20 = (s32[128]{0:T(128)S(1)}, s32[128]{0:T(128)}, u32[]{:S(2)}) copy-start(s32[128]{0:T(128)} %fusion.25) | copy-start | bytes 1540
  94.0 10.3 %copy-start.11 = (s32[16384]{0:T(1024)S(1)}, s32[16384]{0:T(1024)}, u32[]{:S(2)}) copy-start(s32[16384]{0:T(1024)} %param.16) | copy-start | bytes 196612
  94.0 10.8 %copy-start.3 = (bf16[128,384]{1,0:T(8,128)(2,1)S(1)}, bf16[128,384]{1,0:T(8,128)(2,1)}, u32[]{:S(2)}) copy-start(bf16[128,384]{1,0:T(8,128)(2,1)} %param.12) | copy-start | bytes 294916
  94.0 38.7 %all-to-all-start.2 = ((f32[128,2,2048]{2,1,0:T(2,128)}), f32[128,2,2048]{2,1,0:T(2,128)S(1)}, u32[]{:S(2)}, u32[]{:S(2)}) async-start(f32[128,2,2048]{2,1,0:T(2,128)} %all_to_all.16), calls=%async_computation.2 | async-start | bytes 4194304 | tf_op jit(solution)/shard_map/all_to_all | solution.py:173
  106.2 36.5 %collective-permute-start.4 = (f32[8,384]{1,0:T(8,128)S(1)}, f32[8,384]{1,0:T(8,128)S(1)}, u32[]{:S(2)}, u32[]{:S(2)}) collective-permute-start(f32[8,384]{1,0:T(8,128)S(1)} %get-tuple-element.41), channel_id=1, source_target_pairs={{0,8},{8,16},{16,24},{24,32},{32,40},{40,48},{48,56},{56,64},{64,7... | collective-permute-start | bytes 36872 | tf_op jit(solution)/shard_map/ppermute | solution.py:113
  109.4 33.4 %collective-permute-start.5 = (f32[8,384]{1,0:T(8,128)S(1)}, f32[8,384]{1,0:T(8,128)S(1)}, u32[]{:S(2)}, u32[]{:S(2)}) collective-permute-start(f32[8,384]{1,0:T(8,128)S(1)} %get-tuple-element.40), channel_id=1, source_target_pairs={{8,0},{16,8},{24,16},{32,24},{40,32},{48,40},{56,48},{64,56},{72,6... | collective-permute-start | bytes 36872 | tf_op jit(solution)/shard_map/ppermute | solution.py:113
  115.9 26.9 %collective-permute-start.6 = (f32[128,8]{1,0:T(8,128)S(1)}, f32[128,8]{1,0:T(8,128)S(1)}, u32[]{:S(2)}, u32[]{:S(2)}) collective-permute-start(f32[128,8]{1,0:T(8,128)S(1)} %bitcast.71), channel_id=1, source_target_pairs={{0,1},{1,2},{2,3},{3,4},{4,5},{5,6},{6,7},{8,9},{9,10},{10,11},{11... | collective-permute-start | bytes 12296 | tf_op jit(solution)/shard_map/ppermute | solution.py:113
  120.7 22.1 %collective-permute-start.7 = (f32[128,8]{1,0:T(8,128)S(1)}, f32[128,8]{1,0:T(8,128)S(1)}, u32[]{:S(2)}, u32[]{:S(2)}) collective-permute-start(f32[128,8]{1,0:T(8,128)S(1)} %bitcast.72), channel_id=1, source_target_pairs={{1,0},{2,1},{3,2},{4,3},{5,4},{6,5},{7,6},{9,8},{10,9},{11,10},{12... | collective-permute-start | bytes 12296 | tf_op jit(solution)/shard_map/ppermute | solution.py:113
  142.7 0.8 copy-start.5
  142.7 0.8 copy-start.6
  142.8 0.8 copy-start.13
  142.8 0.8 copy-start.14
  149.6 15.5 %collective-permute-start.8 = (f32[8,384]{1,0:T(8,128)}, f32[8,384]{1,0:T(8,128)S(1)}, u32[]{:S(2)}, u32[]{:S(2)}) collective-permute-start(f32[8,384]{1,0:T(8,128)} %get-tuple-element.14), channel_id=1, source_target_pairs={{0,8},{8,16},{16,24},{24,32},{32,40},{40,48},{48,56},{56,64},{64,7... | collective-permute-start | bytes 36872 | tf_op jit(solution)/shard_map/ppermute | solution.py:113
  152.1 13.1 %collective-permute-start.9 = (f32[8,384]{1,0:T(8,128)}, f32[8,384]{1,0:T(8,128)S(1)}, u32[]{:S(2)}, u32[]{:S(2)}) collective-permute-start(f32[8,384]{1,0:T(8,128)} %get-tuple-element.15), channel_id=1, source_target_pairs={{8,0},{16,8},{24,16},{32,24},{40,32},{48,40},{56,48},{64,56},{72,6... | collective-permute-start | bytes 36872 | tf_op jit(solution)/shard_map/ppermute | solution.py:113
  157.0 5.3 %collective-permute-start.10 = (f32[128,8]{1,0:T(8,128)}, f32[128,8]{1,0:T(8,128)S(1)}, u32[]{:S(2)}, u32[]{:S(2)}) collective-permute-start(f32[128,8]{1,0:T(8,128)} %get-tuple-element.16), channel_id=1, source_target_pairs={{0,1},{1,2},{2,3},{3,4},{4,5},{5,6},{6,7},{8,9},{9,10},{10,11},{11... | collective-permute-start | bytes 12296 | tf_op jit(solution)/shard_map/ppermute | solution.py:113
  159.3 5.8 %collective-permute-start.11 = (f32[128,8]{1,0:T(8,128)}, f32[128,8]{1,0:T(8,128)S(1)}, u32[]{:S(2)}, u32[]{:S(2)}) collective-permute-start(f32[128,8]{1,0:T(8,128)} %get-tuple-element.17), channel_id=1, source_target_pairs={{1,0},{2,1},{3,2},{4,3},{5,4},{6,5},{7,6},{9,8},{10,9},{11,10},{12... | collective-permute-start | bytes 12296 | tf_op jit(solution)/shard_map/ppermute | solution.py:113
  162.3 2.9 %copy-start.8 = (f32[128,8]{1,0:T(8,128)}, f32[128,8]{1,0:T(8,128)S(1)}, u32[]{:S(2)}) copy-start(f32[128,8]{1,0:T(8,128)S(1)} %collective-permute-done.10.by_ref) | copy-start | bytes 12292
  165.1 0.6 copy-start.10
  165.1 0.6 copy-start.16
  165.1 0.6 copy-start.18
  171.8 15.7 %collective-permute-start.12 = (f32[8,384]{1,0:T(8,128)}, f32[8,384]{1,0:T(8,128)S(1)}, u32[]{:S(2)}, u32[]{:S(2)}) collective-permute-start(f32[8,384]{1,0:T(8,128)} %get-tuple-element.19), channel_id=1, source_target_pairs={{0,8},{8,16},{16,24},{24,32},{32,40},{40,48},{48,56},{56,64},{64,7... | collective-permute-start | bytes 36872 | tf_op jit(solution)/shard_map/ppermute | solution.py:113
  173.7 13.8 %collective-permute-start.13 = (f32[8,384]{1,0:T(8,128)}, f32[8,384]{1,0:T(8,128)S(1)}, u32[]{:S(2)}, u32[]{:S(2)}) collective-permute-start(f32[8,384]{1,0:T(8,128)} %get-tuple-element.20), channel_id=1, source_target_pairs={{8,0},{16,8},{24,16},{32,24},{40,32},{48,40},{56,48},{64,56},{72,6... | collective-permute-start | bytes 36872 | tf_op jit(solution)/shard_map/ppermute | solution.py:113
  179.2 4.5 %collective-permute-start.14 = (f32[128,8]{1,0:T(8,128)}, f32[128,8]{1,0:T(8,128)S(1)}, u32[]{:S(2)}, u32[]{:S(2)}) collective-permute-start(f32[128,8]{1,0:T(8,128)} %get-tuple-element.21), channel_id=1, source_target_pairs={{0,1},{1,2},{2,3},{3,4},{4,5},{5,6},{6,7},{8,9},{9,10},{10,11},{11... | collective-permute-start | bytes 12296 | tf_op jit(solution)/shard_map/ppermute | solution.py:113
  181.7 5.8 %collective-permute-start.15 = (f32[128,8]{1,0:T(8,128)}, f32[128,8]{1,0:T(8,128)S(1)}, u32[]{:S(2)}, u32[]{:S(2)}) collective-permute-start(f32[128,8]{1,0:T(8,128)} %get-tuple-element.22), channel_id=1, source_target_pairs={{1,0},{2,1},{3,2},{4,3},{5,4},{6,5},{7,6},{9,8},{10,9},{11,10},{12... | collective-permute-start | bytes 12296 | tf_op jit(solution)/shard_map/ppermute | solution.py:113
  183.6 3.9 %copy-start.7 = (f32[128,8]{1,0:T(8,128)}, f32[128,8]{1,0:T(8,128)S(1)}, u32[]{:S(2)}) copy-start(f32[128,8]{1,0:T(8,128)S(1)} %collective-permute-done.14.by_ref) | copy-start | bytes 12292
  187.5 0.6 copy-start.9
  187.5 0.6 copy-start.15
  187.5 0.6 copy-start.17

commit v8 on v4

--- a/solution.py
+++ b/solution.py
@@ -159,19 +159,21 @@
     earlier = jnp.arange(slots)[None, :] < jnp.arange(slots)[:, None]
     rank = jnp.sum((same_owner & earlier).astype(jnp.int32), axis=1)
     slot_index = my_dest * CAP + rank
-    send_select = (jnp.arange(devices * CAP)[:, None] == slot_index[None, :]).astype(jnp.float32)
-    both_states = jnp.stack([parent_field, new_parent]).reshape(2, levels, -1, STRIP)
-    picked = jnp.take(both_states, my_rows, axis=2)
-    strip_values = jnp.moveaxis(picked, 2, 0).reshape(slots, -1)
-    outgoing_strips = jnp.dot(
-        send_select,
-        strip_values,
-        precision=lax.Precision.HIGHEST,
-        preferred_element_type=jnp.float32,
-    )
-    incoming = lax.all_to_all(
-        outgoing_strips, ("gx", "gy"), split_axis=0, concat_axis=0, tiled=True
-    )
+    send_select = jnp.arange(devices * CAP)[:, None] == slot_index[None, :]
+    valid = jnp.any(send_select, axis=1)
+    source = jnp.sum(jnp.where(send_select, jnp.arange(slots)[None, :], 0), axis=1)
+    strip_rows = jnp.take(my_rows, source)
+    per_row = parent_field.shape[2] // STRIP
+    block_row = strip_rows // per_row
+    block_pick = (strip_rows[:, None] % per_row == jnp.arange(per_row)[None, :]) & valid[:, None]
+
+    def pick(state):
+        rows = jnp.take(state, block_row, axis=1).reshape(levels, -1, per_row, STRIP)
+        return jnp.sum(jnp.where(block_pick[None, :, :, None], rows, 0.0), axis=2)
+
+    outgoing = jnp.stack([pick(parent_field), pick(new_parent)])
+    outgoing = jnp.transpose(outgoing, (2, 0, 1, 3)) + 0.0 * child[0, 0, 0]
+    incoming = lax.all_to_all(outgoing, ("gx", "gy"), split_axis=0, concat_axis=0, tiled=True)
     mine = dest_table == my_index
     rank_all = jnp.cumsum(mine.astype(jnp.int32), axis=1) - 1
     slot_ids = jnp.arange(CAP)
@@ -179,13 +181,13 @@
     chosen = jnp.sum(jnp.where(hits, target_table[:, None, :], 0), axis=2)
     target_rows = jnp.where(jnp.any(hits, axis=2), chosen, -1).reshape(-1)
     row_select = (jnp.arange(crows)[:, None] == target_rows[None, :]).astype(jnp.float32)
-    coarse = jnp.dot(
-        row_select, incoming, precision=lax.Precision.HIGHEST, preferred_element_type=jnp.float32
+    coarse = jnp.einsum(
+        "tq,qald->altd", row_select, incoming, precision=lax.Precision.HIGHEST
     )
     counts = jnp.sum(row_select, axis=1)
     boundary = jnp.einsum(
-        "tald,de->alte",
-        coarse.reshape(crows, 2, levels, STRIP),
+        "altd,de->alte",
+        coarse,
         refine_table(STRIP),
         precision=lax.Precision.HIGHEST,
     )

time: 212 us -> 229 us (1.080); the launches traced: 211 us -> 225 us
  waiting for transfers between devices: 39.9 us -> 11.7 us
  other arithmetic: 15.2 us -> 34 us
  local copies, waits for them, and re-layouts: 49.3 us -> 67.6 us
  starting transfers between devices: 75.2 us -> 81.2 us
    reduce_sum x0 -> x2, other arithmetic: none -> 14.9 us  [the longest x1 14.8 us: pick(): return jnp.sum(jnp.where(block_pick[None, :, :, None], rows, 0.0), axis=2)]
    all_to_all x1, waiting for transfers between devices: 12.5 us -> 0.01 us  [storm_rows(): lax.all_to_all(grid.reshape(levels, crows, widths), ('gx', 'gy'), 1, 1, t...]
    all_to_all x1, waiting for transfers between devices: 19.9 us -> 7.74 us  [shards(): lax.all_to_all(outgoing, ('gx', 'gy'), split_axis=0, concat_axis=0, tiled...]
    gather x1 -> x3, local copies, waits for them, and re-layouts: 2.87 us -> 15 us  [the longest x2 13.1 us: pick(): jnp.take(state, block_row, axis=1).reshape(levels, -1, per_row, STRIP)]
    another operation x4 -> x0, local copies, waits for them, and re-layouts: 8.37 us -> none  [shards(): jnp.stack([parent_field, new_parent]).reshape(2, levels, -1, STRIP)]
    unnamed x55 -> x63, local copies, waits for them, and re-layouts: 9.75 us -> 16.4 us
    dot_general x2 -> x0, local copies, waits for them, and re-layouts: 5.88 us -> none  [the longest x1 2.97 us: shards(): jnp.dot(send_select, strip_values, precision=lax.Precision.HIGHEST, prefe...]
    reshape x1, local copies, waits for them, and re-layouts: 0.16 us -> 5.64 us  [pick(): jnp.take(state, block_row, axis=1).reshape(levels, -1, per_row, STRIP)]
  transfers between devices with their start and end apart: 19 -> 19, of which waited for: 4 -> 3; matrix products, arithmetic and copies ran while one was open for 30% -> 42% of each run, Pallas kernels for 0% -> 0%
where the time goes in v8:
time: 229 us; the launch traced here: 225 us
  starting transfers between devices  81.2 us (35%)
  local copies, waits for them, and re-layouts  67.6 us (30%)
  other arithmetic  34 us (15%)
  Pallas kernels  18 us (8%)
  waiting for transfers between devices  11.7 us (5%)
  matrix products  6.45 us (3%)
  between operations  5.69 us (2%)
    ppermute x12, starting transfers between devices, swap_edge(): return lax.ppermute(edge, axis, pairs)  37.4 us
    pallas_call x3, Pallas kernels, substep(): pl.pallas_call(functools.partial(substep_kernel, weight), out_shape=(jax....  18 us
    unnamed x63, local copies, waits for them, and re-layouts  16.4 us
    reduce_sum x1, other arithmetic, pick(): return jnp.sum(jnp.where(block_pick[None, :, :, None], rows, 0.0), axis=2)  14.8 us
    gather x2, local copies, waits for them, and re-layouts, pick(): jnp.take(state, block_row, axis=1).reshape(levels, -1, per_row, STRIP)  13.1 us
    all_to_all x1, starting transfers between devices, storm_rows(): gathered = lax.all_to_all(child, ('gx', 'gy'), 1, 1, tiled=True)  11.8 us
    ppermute x4, starting transfers between devices, swap(): return lax.ppermute(edge, axis, pairs)  11.8 us
    all_to_all x1, starting transfers between devices, storm_rows(): lax.all_to_all(grid.reshape(levels, crows, widths), ('gx', 'gy'), 1, 1, t...  10.2 us
  transfers between devices with their start and end apart: 19, of which 3 were waited for; matrix products, arithmetic and copies ran while one was open for 42% of the time, Pallas kernels for 0%

profile of v8, /device:TPU:33, one launch (start us, length us, event | category | flops | bytes accessed | tf_op | source)
XLA Modules:
  0.0 224.7 jit_solution(3210254424653813803)
XLA Ops:
  0.6 3.0 %copy.125 = f32[8,128,512]{2,0,1:T(8,128)S(1)} copy(f32[8,128,512]{2,1,0:T(8,128)} %param.11) | data formatting | bytes 4194304 | tf_op args[0]
  3.6 1.3 copy-done.1
  4.9 0.6 slice_bitcast_fusion.1
  5.5 3.9 %collective-permute-start = (f32[8,512]{1,0:T(8,128)}, f32[8,512]{1,0:T(8,128)S(1)}, u32[]{:S(2)}, u32[]{:S(2)}) collective-permute-start(f32[8,512]{1,0:T(8,128)} %get-tuple-element.41), channel_id=1, source_target_pairs={{8,0},{16,8},{24,16},{32,24},{40,32},{48,40},{56,48},{64,56},{72,6... | collective-permute-start | bytes 49160 | tf_op jit(solution)/shard_map/ppermute | solution.py:25
  9.5 1.9 collective-permute-start.1
  11.6 0.8 copy.144
  12.4 2.9 %collective-permute-start.2 = (f32[8,128]{1,0:T(8,128)}, f32[8,128]{1,0:T(8,128)S(1)}, u32[]{:S(2)}, u32[]{:S(2)}) collective-permute-start(f32[8,128]{1,0:T(8,128)} %bitcast.4), channel_id=1, source_target_pairs={{1,0},{2,1},{3,2},{4,3},{5,4},{6,5},{7,6},{9,8},{10,9},{11,10},{12... | collective-permute-start | bytes 12296 | tf_op jit(solution)/shard_map/ppermute | solution.py:25
  15.4 3.1 %collective-permute-start.3 = (f32[8,128]{1,0:T(8,128)S(1)}, f32[8,128]{1,0:T(8,128)S(1)}, u32[]{:S(2)}, u32[]{:S(2)}) collective-permute-start(f32[8,128]{1,0:T(8,128)S(1)} %bitcast.80), channel_id=1, source_target_pairs={{0,1},{1,2},{2,3},{3,4},{4,5},{5,6},{6,7},{8,9},{9,10},{10,11},{11... | collective-permute-start | bytes 12296 | tf_op jit(solution)/shard_map/ppermute | solution.py:25
  18.5 3.5 %copy.126 = f32[8,128,384]{2,0,1:T(8,128)} copy(f32[8,128,384]{2,1,0:T(8,128)} %param.13) | data formatting | bytes 3145728 | tf_op args[2]
  22.0 11.8 %all-to-all-start = ((f32[8,128,384]{2,0,1:T(8,128)}), f32[8,128,384]{2,0,1:T(8,128)}, u32[]{:S(2)}, u32[]{:S(2)}) async-start(f32[8,128,384]{2,0,1:T(8,128)} %copy.126), calls=%async_computation | async-start | bytes 3145728 | tf_op jit(solution)/shard_map/all_to_all | solution.py:53
  33.8 4.6 %fusion.38 = (f32[8,127,512]{2,0,1:T(8,128)}, f32[8,127,512]{2,0,1:T(8,128)}) fusion(f32[8,128,512]{2,0,1:T(8,128)} %copy-done.1), kind=kLoop, calls=%fused_computation.94 | loop fusion | bytes 8323072 | tf_op jit(solution)/shard_map/slice | solution.py:36
  38.7 0.7 fusion.32
  39.6 1.9 gather_fusion
  41.7 8.5 %gather_fusion.1 = f32[256,8,512]{2,0,1:T(8,128)} fusion(f32[8,128,512]{2,1,0:T(8,128)S(1)} %copy-done, s32[1024]{0:T(1024)S(1)} %pad_clamp_fusion), kind=kCustom, calls=%fused_computation.clone | custom fusion | bytes 8389632 | tf_op jit(solution)/shard_map/jit(_take)/gather | solution.py:171
  50.4 5.0 %fusion.39 = (f32[8,128,511]{2,0,1:T(8,128)}, f32[8,128,511]{2,0,1:T(8,128)}) fusion(f32[8,128,512]{2,0,1:T(8,128)} %copy-done.1), kind=kLoop, calls=%fused_computation.95 | loop fusion | bytes 8372224 | tf_op jit(solution)/shard_map/slice | solution.py:38
  55.4 2.7 %fusion.42 = (f32[7,128,512]{2,0,1:T(8,128)}, f32[7,128,512]{2,0,1:T(8,128)}) fusion(f32[8,128,512]{2,0,1:T(8,128)S(1)} %copy-done.2), kind=kLoop, calls=%fused_computation.98 | loop fusion | bytes 7340032 | tf_op jit(solution)/shard_map/slice | solution.py:125
  58.0 1.0 copy-done.5
  59.1 2.9 %select_bitcast_fusion.1 = f32[8,256,512]{2,1,0:T(8,128)} fusion(f32[256,8,512]{2,0,1:T(8,128)S(1)} %copy-done.5, pred[256]{0:T(512)(128)(4,1)S(1)} %get-tuple-element.37), kind=kLoop, calls=%fused_computation.6 | loop fusion | flops 1048576 | bytes 8388864 | tf_op jit(solution)/shard_map/jit(_take)/select_n | solution.py:171
  66.7 1.0 copy.121
  67.6 1.0 copy.123
  68.6 5.6 %reshape.170 = f32[8,256,4,128]{3,2,1,0:T(4,128)} reshape(f32[8,256,512]{2,1,0:T(8,128)} %select_bitcast_fusion.1) | data formatting | bytes 8388608 | tf_op jit(solution)/shard_map/reshape | solution.py:171
  75.2 0.9 copy.118
  76.1 1.7 copy.127
  78.6 2.1 copy.129
  80.7 10.2 %all-to-all-start.1 = ((f32[8,128,384]{2,0,1:T(8,128)}), f32[8,128,384]{2,0,1:T(8,128)}, u32[]{:S(2)}, u32[]{:S(2)}) async-start(f32[8,128,384]{2,0,1:T(8,128)} %bitcast.67), calls=%async_computation.1 | async-start | bytes 3145728 | tf_op jit(solution)/shard_map/all_to_all | solution.py:58
  90.8 8.2 %fusion.5 = f32[8,128,512]{2,0,1:T(8,128)} fusion(f32[1,128,512]{2,0,1:T(1,128)} %copy.121, f32[7,128,512]{2,0,1:T(8,128)} %get-tuple-element.50, f32[7,128,512]{2,0,1:T(8,128)} %get-tuple-element.49, f32[1,128,512]{2,0,1:T(1,128)} %copy.123, f32[8,128,511]{2,0,1:T(8,128)} %get-tuple-element.44, f32[8,128,1]{2,0,1:T(8,128)S(1)} %copy.118, ...), kind=kLoop, calls=%fused_computation.21 | loop fusion | flops 13107200 | bytes 17039424 | tf_op jit(solution)/shard_map/add | solution.py:144
  99.1 4.6 %gather_fusion.2 = f32[256,8,512]{2,1,0:T(8,128)} fusion(f32[8,128,512]{2,0,1:T(8,128)} %fusion.5, s32[1024]{0:T(1024)} %copy-done.23), kind=kCustom, calls=%fused_computation.1.clone | custom fusion | bytes 8389632 | tf_op jit(solution)/shard_map/jit(_take)/gather | solution.py:171
  103.6 2.8 %select_bitcast_fusion = f32[8,256,4,128]{3,0,2,1:T(8,128)S(1)} fusion(f32[256,8,512]{2,1,0:T(8,128)} %gather_fusion.2, pred[256]{0:T(512)(128)(4,1)S(1)} %copy-done.25), kind=kLoop, calls=%fused_computation.5 | loop fusion | flops 1048576 | bytes 8388864 | tf_op jit(solution)/shard_map/reshape | solution.py:171
  106.5 0.6 copy-done.4
  107.1 14.8 %select_reduce_fusion = (f32[8,256,128]{2,1,0:T(8,128)S(1)}, f32[8,256,128]{2,1,0:T(8,128)}) fusion(f32[8,256,4,128]{3,2,1,0:T(4,128)S(1)} %copy-done.4, pred[256,4]{1,0:T(8,128)(4,1)S(1)} %fusion.22, f32[8,256,4,128]{3,0,2,1:T(8,128)S(1)} %select_bitcast_fusion), kind=kLoop, calls=%fused_computation.7 | loop fusion | flops 3670016 | bytes 10486784 | tf_op jit(solution)/shard_map/reduce_sum | solution.py:172
  121.9 1.2 slice.94
  123.8 1.4 fusion.6
  125.2 2.5 %copy.133 = f32[256,2,8,128]{3,2,1,0:T(8,128)} copy(f32[256,2,8,128]{3,0,2,1:T(8,128)S(1)} %fusion.6) | data formatting | bytes 4194304 | tf_op jit(solution)/shard_map/add | solution.py:175
  127.7 10.0 %all-to-all-start.2 = ((f32[256,2,8,128]{3,2,1,0:T(8,128)}), f32[256,2,8,128]{3,2,1,0:T(8,128)S(1)}, u32[]{:S(2)}, u32[]{:S(2)}) async-start(f32[256,2,8,128]{3,2,1,0:T(8,128)} %copy.133), calls=%async_computation.2 | async-start | bytes 4194304 | tf_op jit(solution)/shard_map/all_to_all | solution.py:176
  138.8 0.7 convert_add_fusion.1.factor_ref
  139.5 1.4 fusion.43
  140.9 0.8 copy.146
  141.7 3.4 %collective-permute-start.6 = (f32[128,8]{1,0:T(8,128)S(1)}, f32[128,8]{1,0:T(8,128)S(1)}, u32[]{:S(2)}, u32[]{:S(2)}) collective-permute-start(f32[128,8]{1,0:T(8,128)S(1)} %bitcast.73), channel_id=1, source_target_pairs={{0,1},{1,2},{2,3},{3,4},{4,5},{5,6},{6,7},{8,9},{9,10},{10,11},{11... | collective-permute-start | bytes 12296 | tf_op jit(solution)/shard_map/ppermute | solution.py:113
  145.2 0.8 copy.147
  146.0 1.9 collective-permute-start.7
  147.9 0.7 slice_bitcast_fusion.2
  148.6 3.1 %collective-permute-start.4 = (f32[8,384]{1,0:T(8,128)S(1)}, f32[8,384]{1,0:T(8,128)S(1)}, u32[]{:S(2)}, u32[]{:S(2)}) collective-permute-start(f32[8,384]{1,0:T(8,128)S(1)} %get-tuple-element.54), channel_id=1, source_target_pairs={{0,8},{8,16},{16,24},{24,32},{32,40},{40,48},{48,56},{56,64},{64,7... | collective-permute-start | bytes 36872 | tf_op jit(solution)/shard_map/ppermute | solution.py:113
  151.7 4.3 %collective-permute-start.5 = (f32[8,384]{1,0:T(8,128)S(1)}, f32[8,384]{1,0:T(8,128)S(1)}, u32[]{:S(2)}, u32[]{:S(2)}) collective-permute-start(f32[8,384]{1,0:T(8,128)S(1)} %get-tuple-element.53), channel_id=1, source_target_pairs={{8,0},{16,8},{24,16},{32,24},{40,32},{48,40},{56,48},{64,56},{72,6... | collective-permute-start | bytes 36872 | tf_op jit(solution)/shard_map/ppermute | solution.py:113
  156.0 2.9 %copy.139.child_ref = f32[8,128,384]{2,1,0:T(8,128)} copy(f32[8,128,384]{2,0,1:T(8,128)} %all-to-all-done.1) | data formatting | bytes 3145728 | tf_op jit(solution)/shard_map/all_to_all | solution.py:58
  158.9 7.7 %all-to-all-done.2 = f32[256,2,8,128]{3,2,1,0:T(8,128)S(1)} async-done(((f32[256,2,8,128]{3,2,1,0:T(8,128)}), f32[256,2,8,128]{3,2,1,0:T(8,128)S(1)}, u32[]{:S(2)}, u32[]{:S(2)}) %all-to-all-start.2) | async-done | bytes 2097184 | tf_op jit(solution)/shard_map/all_to_all | solution.py:176
  166.6 2.1 fusion.11
  168.7 4.4 %fusion.14.bound_ref = f32[2,8,128,384]{3,2,1,0:T(8,128)} fusion(f32[2,8,128,128]{2,3,1,0:T(8,128)S(1)} %fusion.11, f32[128]{0:T(128)S(1)} %iota_convert_fusion, f32[384]{0:T(512)S(1)} %add_clamp_fusion), kind=kOutput, calls=%fused_computation.30 | convolution fusion | flops 1208156160 | bytes 4196352 | tf_op jit(solution)/shard_map/altd,de->alte/dot_general | solution.py:188
  173.1 0.8 broadcast_in_dim.108.divisor_ref
  173.9 6.0 %shard_map.104 = (f32[8,128,384]{2,1,0:T(8,128)}, f32[8,384]{1,0:T(8,128)}, f32[8,384]{1,0:T(8,128)}, f32[128,8]{1,0:T(8,128)}, f32[128,8]{1,0:T(8,128)}) custom-call(f32[2,8]{1,0:T(2,128)} %wind_ref.5, f32[8,128,384]{2,1,0:T(8,128)} %copy.139.child_ref, f32[8,384]{1,0:T(8,128)} %copy-done.17, f32[8,384]{1,0:T(8,128)} %copy-done.18, f32[128,8]{1,0:T(8,128)} %copy-done.9, ...), custom_call_target="tpu_custom_call" | custom-call | flops 11796480 | bytes 6684672 | tf_op jit(solution)/shard_map/pallas_call | solution.py:91
  179.9 2.5 %collective-permute-start.8 = (f32[8,384]{1,0:T(8,128)}, f32[8,384]{1,0:T(8,128)S(1)}, u32[]{:S(2)}, u32[]{:S(2)}) collective-permute-start(f32[8,384]{1,0:T(8,128)} %get-tuple-element.15), channel_id=1, source_target_pairs={{0,8},{8,16},{16,24},{24,32},{32,40},{40,48},{48,56},{56,64},{64,7... | collective-permute-start | bytes 36872 | tf_op jit(solution)/shard_map/ppermute | solution.py:113
  182.3 4.9 %collective-permute-start.9 = (f32[8,384]{1,0:T(8,128)}, f32[8,384]{1,0:T(8,128)S(1)}, u32[]{:S(2)}, u32[]{:S(2)}) collective-permute-start(f32[8,384]{1,0:T(8,128)} %get-tuple-element.16), channel_id=1, source_target_pairs={{8,0},{16,8},{24,16},{32,24},{40,32},{48,40},{56,48},{64,56},{72,6... | collective-permute-start | bytes 36872 | tf_op jit(solution)/shard_map/ppermute | solution.py:113
  187.3 2.3 %collective-permute-start.10 = (f32[128,8]{1,0:T(8,128)}, f32[128,8]{1,0:T(8,128)S(1)}, u32[]{:S(2)}, u32[]{:S(2)}) collective-permute-start(f32[128,8]{1,0:T(8,128)} %get-tuple-element.17), channel_id=1, source_target_pairs={{0,1},{1,2},{2,3},{3,4},{4,5},{5,6},{6,7},{8,9},{9,10},{10,11},{11... | collective-permute-start | bytes 12296 | tf_op jit(solution)/shard_map/ppermute | solution.py:113
  189.6 2.9 %collective-permute-start.11 = (f32[128,8]{1,0:T(8,128)}, f32[128,8]{1,0:T(8,128)S(1)}, u32[]{:S(2)}, u32[]{:S(2)}) collective-permute-start(f32[128,8]{1,0:T(8,128)} %get-tuple-element.18), channel_id=1, source_target_pairs={{1,0},{2,1},{3,2},{4,3},{5,4},{6,5},{7,6},{9,8},{10,9},{11,10},{12... | collective-permute-start | bytes 12296 | tf_op jit(solution)/shard_map/ppermute | solution.py:113
  192.6 2.8 %collective-permute-done.11.ay_ref = f32[128,8]{1,0:T(8,128)S(1)} collective-permute-done((f32[128,8]{1,0:T(8,128)}, f32[128,8]{1,0:T(8,128)S(1)}, u32[]{:S(2)}, u32[]{:S(2)}) %collective-permute-start.11) | collective-permute-done | bytes 4128 | tf_op jit(solution)/shard_map/ppermute | solution.py:113
  195.4 0.6 copy-done.14
  196.0 6.1 %shard_map.105 = (f32[8,128,384]{2,1,0:T(8,128)}, f32[8,384]{1,0:T(8,128)}, f32[8,384]{1,0:T(8,128)}, f32[128,8]{1,0:T(8,128)}, f32[128,8]{1,0:T(8,128)}) custom-call(f32[2,8]{1,0:T(2,128)} %wind_ref.5, f32[8,128,384]{2,1,0:T(8,128)} %get-tuple-element.14.child_ref, f32[8,384]{1,0:T(8,128)} %copy-done.21, f32[8,384]{1,0:T(8,128)} %copy-done.22, ...), custom_call_target="tpu_custom_call" | custom-call | flops 11796480 | bytes 6684672 | tf_op jit(solution)/shard_map/pallas_call | solution.py:91
  202.1 1.9 collective-permute-start.12
  204.1 5.5 %collective-permute-start.13 = (f32[8,384]{1,0:T(8,128)}, f32[8,384]{1,0:T(8,128)S(1)}, u32[]{:S(2)}, u32[]{:S(2)}) collective-permute-start(f32[8,384]{1,0:T(8,128)} %get-tuple-element.21), channel_id=1, source_target_pairs={{8,0},{16,8},{24,16},{32,24},{40,32},{48,40},{56,48},{64,56},{72,6... | collective-permute-start | bytes 36872 | tf_op jit(solution)/shard_map/ppermute | solution.py:113
  209.5 2.5 %collective-permute-start.14 = (f32[128,8]{1,0:T(8,128)}, f32[128,8]{1,0:T(8,128)S(1)}, u32[]{:S(2)}, u32[]{:S(2)}) collective-permute-start(f32[128,8]{1,0:T(8,128)} %get-tuple-element.22), channel_id=1, source_target_pairs={{0,1},{1,2},{2,3},{3,4},{4,5},{5,6},{6,7},{8,9},{9,10},{10,11},{11... | collective-permute-start | bytes 12296 | tf_op jit(solution)/shard_map/ppermute | solution.py:113
  212.1 2.1 collective-permute-start.15
  214.2 2.5 %copy.140 = f32[8,128,512]{2,1,0:T(8,128)} copy(f32[8,128,512]{2,0,1:T(8,128)S(1)} %copy-done.3) | data formatting | bytes 4194304
  216.8 1.1 collective-permute-done.15.ay_ref
  217.9 0.6 copy-done.12
  218.5 6.0 %shard_map.106 = (f32[8,128,384]{2,1,0:T(8,128)}, f32[8,384]{1,0:T(8,128)}, f32[8,384]{1,0:T(8,128)}, f32[128,8]{1,0:T(8,128)}, f32[128,8]{1,0:T(8,128)}) custom-call(f32[2,8]{1,0:T(2,128)} %wind_ref.5, f32[8,128,384]{2,1,0:T(8,128)} %get-tuple-element.19.child_ref, f32[8,384]{1,0:T(8,128)} %copy-done.19, f32[8,384]{1,0:T(8,128)} %copy-done.20, ...), custom_call_target="tpu_custom_call" | custom-call | flops 11796480 | bytes 6684672 | tf_op jit(solution)/shard_map/pallas_call | solution.py:91
  (100 shorter events, 4.9 us)
Async XLA Ops:
  0.6 10.8 %copy-start = (f32[8,128,512]{2,1,0:T(8,128)S(1)}, f32[8,128,512]{2,1,0:T(8,128)}, u32[]{:S(2)}) copy-start(f32[8,128,512]{2,1,0:T(8,128)} %param.11) | copy-start | bytes 6291460
  3.6 1.3 copy-start.1
  5.5 85.3 %collective-permute-start = (f32[8,512]{1,0:T(8,128)}, f32[8,512]{1,0:T(8,128)S(1)}, u32[]{:S(2)}, u32[]{:S(2)}) collective-permute-start(f32[8,512]{1,0:T(8,128)} %get-tuple-element.41), channel_id=1, source_target_pairs={{8,0},{16,8},{24,16},{32,24},{40,32},{48,40},{56,48},{64,56},{72,6... | collective-permute-start | bytes 49160 | tf_op jit(solution)/shard_map/ppermute | solution.py:25
  9.5 81.4 %collective-permute-start.1 = (f32[8,512]{1,0:T(8,128)S(1)}, f32[8,512]{1,0:T(8,128)S(1)}, u32[]{:S(2)}, u32[]{:S(2)}) collective-permute-start(f32[8,512]{1,0:T(8,128)S(1)} %get-tuple-element.42), channel_id=1, source_target_pairs={{0,8},{8,16},{16,24},{24,32},{32,40},{40,48},{48,56},{56,64},{64,7... | collective-permute-start | bytes 49160 | tf_op jit(solution)/shard_map/ppermute | solution.py:25
  12.4 61.9 %collective-permute-start.2 = (f32[8,128]{1,0:T(8,128)}, f32[8,128]{1,0:T(8,128)S(1)}, u32[]{:S(2)}, u32[]{:S(2)}) collective-permute-start(f32[8,128]{1,0:T(8,128)} %bitcast.4), channel_id=1, source_target_pairs={{1,0},{2,1},{3,2},{4,3},{5,4},{6,5},{7,6},{9,8},{10,9},{11,10},{12... | collective-permute-start | bytes 12296 | tf_op jit(solution)/shard_map/ppermute | solution.py:25
  15.4 59.2 %collective-permute-start.3 = (f32[8,128]{1,0:T(8,128)S(1)}, f32[8,128]{1,0:T(8,128)S(1)}, u32[]{:S(2)}, u32[]{:S(2)}) collective-permute-start(f32[8,128]{1,0:T(8,128)S(1)} %bitcast.80), channel_id=1, source_target_pairs={{0,1},{1,2},{2,3},{3,4},{4,5},{5,6},{6,7},{8,9},{9,10},{10,11},{11... | collective-permute-start | bytes 12296 | tf_op jit(solution)/shard_map/ppermute | solution.py:25
  22.0 54.1 %all-to-all-start = ((f32[8,128,384]{2,0,1:T(8,128)}), f32[8,128,384]{2,0,1:T(8,128)}, u32[]{:S(2)}, u32[]{:S(2)}) async-start(f32[8,128,384]{2,0,1:T(8,128)} %copy.126), calls=%async_computation | async-start | bytes 3145728 | tf_op jit(solution)/shard_map/all_to_all | solution.py:53
  33.8 4.7 %copy-start.8 = (s32[16384,1]{0,1:T(1,128)S(1)}, s32[16384,1]{0,1:T(1,128)}, u32[]{:S(2)}) copy-start(s32[16384,1]{0,1:T(1,128)} %param.16) | copy-start | bytes 196612
  38.5 3.1 %copy-start.6 = (bf16[128,512]{1,0:T(8,128)(2,1)S(1)}, bf16[128,512]{1,0:T(8,128)(2,1)}, u32[]{:S(2)}) copy-start(bf16[128,512]{1,0:T(8,128)(2,1)} %param.12) | copy-start | bytes 393220
  41.5 16.6 %copy-start.24 = (pred[256]{0:T(512)(128)(4,1)}, pred[256]{0:T(512)(128)(4,1)S(1)}, u32[]{:S(2)}) copy-start(pred[256]{0:T(512)(128)(4,1)S(1)} %get-tuple-element.37) | copy-start | bytes 772
  41.6 8.6 %copy-start.23 = (s32[1024]{0:T(1024)}, s32[1024]{0:T(1024)S(1)}, u32[]{:S(2)}) copy-start(s32[1024]{0:T(1024)S(1)} %pad_clamp_fusion) | copy-start | bytes 12292
  50.3 5.0 %copy-start.2 = (f32[8,128,512]{2,0,1:T(8,128)S(1)}, f32[8,128,512]{2,0,1:T(8,128)}, u32[]{:S(2)}) copy-start(f32[8,128,512]{2,0,1:T(8,128)} %copy-done.1) | copy-start | bytes 6291460
  55.4 3.7 %copy-start.5 = (f32[256,8,512]{2,0,1:T(8,128)S(1)}, f32[256,8,512]{2,0,1:T(8,128)}, u32[]{:S(2)}) copy-start(f32[256,8,512]{2,0,1:T(8,128)} %gather_fusion.1) | copy-start | bytes 12582916
  59.1 2.9 %copy-start.16 = (f32[2,8]{1,0:T(2,128)S(1)}, f32[2,8]{1,0:T(2,128)}, u32[]{:S(2)}) copy-start(f32[2,8]{1,0:T(2,128)} %wind_ref.5) | copy-start | bytes 196
  59.1 3.5 %copy-start.27 = (s32[2,4]{1,0:T(2,128)S(1)}, s32[2,4]{1,0:T(2,128)}, u32[]{:S(2)}) copy-start(s32[2,4]{1,0:T(2,128)} %param.19) | copy-start | bytes 100
  74.6 0.6 copy-start.26
  80.7 41.3 %all-to-all-start.1 = ((f32[8,128,384]{2,0,1:T(8,128)}), f32[8,128,384]{2,0,1:T(8,128)}, u32[]{:S(2)}, u32[]{:S(2)}) async-start(f32[8,128,384]{2,0,1:T(8,128)} %bitcast.67), calls=%async_computation.1 | async-start | bytes 3145728 | tf_op jit(solution)/shard_map/all_to_all | solution.py:58
  99.0 4.6 %copy-start.25 = (pred[256]{0:T(512)(128)(4,1)S(1)}, pred[256]{0:T(512)(128)(4,1)}, u32[]{:S(2)}) copy-start(pred[256]{0:T(512)(128)(4,1)} %copy-done.24) | copy-start | bytes 772
  103.6 3.4 %copy-start.4 = (f32[8,256,4,128]{3,2,1,0:T(4,128)S(1)}, f32[8,256,4,128]{3,2,1,0:T(4,128)}, u32[]{:S(2)}) copy-start(f32[8,256,4,128]{3,2,1,0:T(4,128)} %reshape.170) | copy-start | bytes 12582916
  127.7 10.6 %copy-start.15 = (s32[16384]{0:T(1024)S(1)}, s32[16384]{0:T(1024)}, u32[]{:S(2)}) copy-start(s32[16384]{0:T(1024)} %param.18) | copy-start | bytes 196612
  127.7 11.1 %copy-start.7 = (bf16[128,384]{1,0:T(8,128)(2,1)S(1)}, bf16[128,384]{1,0:T(8,128)(2,1)}, u32[]{:S(2)}) copy-start(bf16[128,384]{1,0:T(8,128)(2,1)} %param.14) | copy-start | bytes 294916
  127.7 38.9 %all-to-all-start.2 = ((f32[256,2,8,128]{3,2,1,0:T(8,128)}), f32[256,2,8,128]{3,2,1,0:T(8,128)S(1)}, u32[]{:S(2)}, u32[]{:S(2)}) async-start(f32[256,2,8,128]{3,2,1,0:T(8,128)} %copy.133), calls=%async_computation.2 | async-start | bytes 4194304 | tf_op jit(solution)/shard_map/all_to_all | solution.py:176
  141.7 31.4 %collective-permute-start.6 = (f32[128,8]{1,0:T(8,128)S(1)}, f32[128,8]{1,0:T(8,128)S(1)}, u32[]{:S(2)}, u32[]{:S(2)}) collective-permute-start(f32[128,8]{1,0:T(8,128)S(1)} %bitcast.73), channel_id=1, source_target_pairs={{0,1},{1,2},{2,3},{3,4},{4,5},{5,6},{6,7},{8,9},{9,10},{10,11},{11... | collective-permute-start | bytes 12296 | tf_op jit(solution)/shard_map/ppermute | solution.py:113
  146.0 27.1 %collective-permute-start.7 = (f32[128,8]{1,0:T(8,128)S(1)}, f32[128,8]{1,0:T(8,128)S(1)}, u32[]{:S(2)}, u32[]{:S(2)}) collective-permute-start(f32[128,8]{1,0:T(8,128)S(1)} %bitcast.74), channel_id=1, source_target_pairs={{1,0},{2,1},{3,2},{4,3},{5,4},{6,5},{7,6},{9,8},{10,9},{11,10},{12... | collective-permute-start | bytes 12296 | tf_op jit(solution)/shard_map/ppermute | solution.py:113
  148.6 24.5 %collective-permute-start.4 = (f32[8,384]{1,0:T(8,128)S(1)}, f32[8,384]{1,0:T(8,128)S(1)}, u32[]{:S(2)}, u32[]{:S(2)}) collective-permute-start(f32[8,384]{1,0:T(8,128)S(1)} %get-tuple-element.54), channel_id=1, source_target_pairs={{0,8},{8,16},{16,24},{24,32},{32,40},{40,48},{48,56},{56,64},{64,7... | collective-permute-start | bytes 36872 | tf_op jit(solution)/shard_map/ppermute | solution.py:113
  151.7 21.4 %collective-permute-start.5 = (f32[8,384]{1,0:T(8,128)S(1)}, f32[8,384]{1,0:T(8,128)S(1)}, u32[]{:S(2)}, u32[]{:S(2)}) collective-permute-start(f32[8,384]{1,0:T(8,128)S(1)} %get-tuple-element.53), channel_id=1, source_target_pairs={{8,0},{16,8},{24,16},{32,24},{40,32},{48,40},{56,48},{64,56},{72,6... | collective-permute-start | bytes 36872 | tf_op jit(solution)/shard_map/ppermute | solution.py:113
  173.1 0.8 copy-start.9
  173.1 0.8 copy-start.10
  173.1 0.8 copy-start.17
  173.1 0.8 copy-start.18
  179.9 15.5 %collective-permute-start.8 = (f32[8,384]{1,0:T(8,128)}, f32[8,384]{1,0:T(8,128)S(1)}, u32[]{:S(2)}, u32[]{:S(2)}) collective-permute-start(f32[8,384]{1,0:T(8,128)} %get-tuple-element.15), channel_id=1, source_target_pairs={{0,8},{8,16},{16,24},{24,32},{32,40},{40,48},{48,56},{56,64},{64,7... | collective-permute-start | bytes 36872 | tf_op jit(solution)/shard_map/ppermute | solution.py:113
  182.3 13.1 %collective-permute-start.9 = (f32[8,384]{1,0:T(8,128)}, f32[8,384]{1,0:T(8,128)S(1)}, u32[]{:S(2)}, u32[]{:S(2)}) collective-permute-start(f32[8,384]{1,0:T(8,128)} %get-tuple-element.16), channel_id=1, source_target_pairs={{8,0},{16,8},{24,16},{32,24},{40,32},{48,40},{56,48},{64,56},{72,6... | collective-permute-start | bytes 36872 | tf_op jit(solution)/shard_map/ppermute | solution.py:113
  187.3 5.3 %collective-permute-start.10 = (f32[128,8]{1,0:T(8,128)}, f32[128,8]{1,0:T(8,128)S(1)}, u32[]{:S(2)}, u32[]{:S(2)}) collective-permute-start(f32[128,8]{1,0:T(8,128)} %get-tuple-element.17), channel_id=1, source_target_pairs={{0,1},{1,2},{2,3},{3,4},{4,5},{5,6},{6,7},{8,9},{9,10},{10,11},{11... | collective-permute-start | bytes 12296 | tf_op jit(solution)/shard_map/ppermute | solution.py:113
  189.6 5.8 %collective-permute-start.11 = (f32[128,8]{1,0:T(8,128)}, f32[128,8]{1,0:T(8,128)S(1)}, u32[]{:S(2)}, u32[]{:S(2)}) collective-permute-start(f32[128,8]{1,0:T(8,128)} %get-tuple-element.18), channel_id=1, source_target_pairs={{1,0},{2,1},{3,2},{4,3},{5,4},{6,5},{7,6},{9,8},{10,9},{11,10},{12... | collective-permute-start | bytes 12296 | tf_op jit(solution)/shard_map/ppermute | solution.py:113
  192.6 2.9 %copy-start.13 = (f32[128,8]{1,0:T(8,128)}, f32[128,8]{1,0:T(8,128)S(1)}, u32[]{:S(2)}) copy-start(f32[128,8]{1,0:T(8,128)S(1)} %collective-permute-done.10.by_ref) | copy-start | bytes 12292
  195.4 0.6 copy-start.14
  195.4 0.6 copy-start.21
  195.4 0.6 copy-start.22
  196.0 18.2 %copy-start.3 = (f32[8,128,512]{2,0,1:T(8,128)S(1)}, f32[8,128,512]{2,0,1:T(8,128)}, u32[]{:S(2)}) copy-start(f32[8,128,512]{2,0,1:T(8,128)} %fusion.5) | copy-start | bytes 6291460
  202.1 15.7 %collective-permute-start.12 = (f32[8,384]{1,0:T(8,128)}, f32[8,384]{1,0:T(8,128)S(1)}, u32[]{:S(2)}, u32[]{:S(2)}) collective-permute-start(f32[8,384]{1,0:T(8,128)} %get-tuple-element.20), channel_id=1, source_target_pairs={{0,8},{8,16},{16,24},{24,32},{32,40},{40,48},{48,56},{56,64},{64,7... | collective-permute-start | bytes 36872 | tf_op jit(solution)/shard_map/ppermute | solution.py:113
  204.1 13.8 %collective-permute-start.13 = (f32[8,384]{1,0:T(8,128)}, f32[8,384]{1,0:T(8,128)S(1)}, u32[]{:S(2)}, u32[]{:S(2)}) collective-permute-start(f32[8,384]{1,0:T(8,128)} %get-tuple-element.21), channel_id=1, source_target_pairs={{8,0},{16,8},{24,16},{32,24},{40,32},{48,40},{56,48},{64,56},{72,6... | collective-permute-start | bytes 36872 | tf_op jit(solution)/shard_map/ppermute | solution.py:113
  209.5 7.2 %collective-permute-start.14 = (f32[128,8]{1,0:T(8,128)}, f32[128,8]{1,0:T(8,128)S(1)}, u32[]{:S(2)}, u32[]{:S(2)}) collective-permute-start(f32[128,8]{1,0:T(8,128)} %get-tuple-element.22), channel_id=1, source_target_pairs={{0,1},{1,2},{2,3},{3,4},{4,5},{5,6},{6,7},{8,9},{9,10},{10,11},{11... | collective-permute-start | bytes 12296 | tf_op jit(solution)/shard_map/ppermute | solution.py:113
  212.1 5.8 %collective-permute-start.15 = (f32[128,8]{1,0:T(8,128)}, f32[128,8]{1,0:T(8,128)S(1)}, u32[]{:S(2)}, u32[]{:S(2)}) collective-permute-start(f32[128,8]{1,0:T(8,128)} %get-tuple-element.23), channel_id=1, source_target_pairs={{1,0},{2,1},{3,2},{4,3},{5,4},{6,5},{7,6},{9,8},{10,9},{11,10},{12... | collective-permute-start | bytes 12296 | tf_op jit(solution)/shard_map/ppermute | solution.py:113
  216.8 1.1 copy-start.11
  217.9 0.6 copy-start.12
  217.9 0.6 copy-start.19
  217.9 0.6 copy-start.20

commit v9 on v7

--- a/solution.py
+++ b/solution.py
@@ -166,7 +166,7 @@
     outgoing_strips = jnp.dot(
         send_select,
         strip_values,
-        precision=lax.Precision.HIGHEST,
+        precision=lax.Precision.HIGH,
         preferred_element_type=jnp.float32,
     )
     outgoing_strips = outgoing_strips + 0.0 * child[0, 0, 0]
@@ -181,14 +181,14 @@
     target_rows = jnp.where(jnp.any(hits, axis=2), chosen, -1).reshape(-1)
     row_select = (jnp.arange(crows)[:, None] == target_rows[None, :]).astype(jnp.float32)
     coarse = jnp.dot(
-        row_select, incoming, precision=lax.Precision.HIGHEST, preferred_element_type=jnp.float32
+        row_select, incoming, precision=lax.Precision.HIGH, preferred_element_type=jnp.float32
     )
     counts = jnp.sum(row_select, axis=1)
     boundary = jnp.einsum(
         "tald,de->alte",
         coarse.reshape(crows, 2, levels, STRIP),
         refine_table(STRIP),
-        precision=lax.Precision.HIGHEST,
+        precision=lax.Precision.HIGH,
     )
     divisor = jnp.broadcast_to(1.0 + NUDGE * counts[:, None], (crows, widths))
     factor = 1.0 + child_sppt.astype(jnp.float32)

time: 195 us -> 193 us (0.990)
  matrix products: 6.65 us -> 4.65 us
  transfers between devices with their start and end apart: 19 -> 19, of which waited for: 4 -> 4; matrix products, arithmetic and copies ran while one was open for 30% -> 29% of each run, Pallas kernels for 0% -> 0%
where the time goes in v9:
time: 193 us; the launch traced here: 192 us
  starting transfers between devices  77.1 us (40%)
  local copies, waits for them, and re-layouts  47.7 us (25%)
  waiting for transfers between devices  24.3 us (13%)
  Pallas kernels  18 us (9%)
  other arithmetic  14.7 us (8%)
  between operations  5.76 us (3%)
  matrix products  4.65 us (2%)
    ppermute x12, starting transfers between devices, swap_edge(): return lax.ppermute(edge, axis, pairs)  38 us
    pallas_call x3, Pallas kernels, substep(): pl.pallas_call(functools.partial(substep_kernel, weight), out_shape=(jax....  18 us
    ppermute x4, starting transfers between devices, swap(): return lax.ppermute(edge, axis, pairs)  13.1 us
    all_to_all x1, waiting for transfers between devices, storm_rows(): gathered = lax.all_to_all(child, ('gx', 'gy'), 1, 1, tiled=True)  10.5 us
    all_to_all x1, starting transfers between devices, shards(): lax.all_to_all(outgoing_strips, ('gx', 'gy'), split_axis=0, concat_axis=0...  9.76 us
    all_to_all x1, starting transfers between devices, storm_rows(): gathered = lax.all_to_all(child, ('gx', 'gy'), 1, 1, tiled=True)  9.25 us
    another operation x4, local copies, waits for them, and re-layouts, shards(): jnp.stack([parent_field, new_parent]).reshape(2, levels, -1, STRIP)  8.37 us
    unnamed x53, local copies, waits for them, and re-layouts  7.12 us
  transfers between devices with their start and end apart: 19, of which 4 were waited for; matrix products, arithmetic and copies ran while one was open for 29% of the time, Pallas kernels for 0%

profile of v9, /device:TPU:33, one launch (start us, length us, event | category | flops | bytes accessed | tf_op | source)
XLA Modules:
  0.0 192.1 jit_solution(18273616026950041754)
XLA Ops:
  0.6 1.6 fusion.33
  2.4 3.8 %collective-permute-start.3 = (f32[8,128]{1,0:T(8,128)S(1)}, f32[8,128]{1,0:T(8,128)S(1)}, u32[]{:S(2)}, u32[]{:S(2)}) collective-permute-start(f32[8,128]{1,0:T(8,128)S(1)} %bitcast.78), channel_id=1, source_target_pairs={{0,1},{1,2},{2,3},{3,4},{4,5},{5,6},{6,7},{8,9},{9,10},{10,11},{11... | collective-permute-start | bytes 12296 | tf_op jit(solution)/shard_map/ppermute | solution.py:25
  6.3 1.9 %collective-permute-start.2 = (f32[8,128]{1,0:T(8,128)S(1)}, f32[8,128]{1,0:T(8,128)S(1)}, u32[]{:S(2)}, u32[]{:S(2)}) collective-permute-start(f32[8,128]{1,0:T(8,128)S(1)} %bitcast.80), channel_id=1, source_target_pairs={{1,0},{2,1},{3,2},{4,3},{5,4},{6,5},{7,6},{9,8},{10,9},{11,10},{12... | collective-permute-start | bytes 12296 | tf_op jit(solution)/shard_map/ppermute | solution.py:25
  8.3 3.1 %collective-permute-start.1 = (f32[8,512]{1,0:T(8,128)S(1)}, f32[8,512]{1,0:T(8,128)S(1)}, u32[]{:S(2)}, u32[]{:S(2)}) collective-permute-start(f32[8,512]{1,0:T(8,128)S(1)} %bitcast.74), channel_id=1, source_target_pairs={{0,8},{8,16},{16,24},{24,32},{32,40},{40,48},{48,56},{56,64},{64,7... | collective-permute-start | bytes 49160 | tf_op jit(solution)/shard_map/ppermute | solution.py:25
  11.5 4.3 %collective-permute-start = (f32[8,512]{1,0:T(8,128)S(1)}, f32[8,512]{1,0:T(8,128)S(1)}, u32[]{:S(2)}, u32[]{:S(2)}) collective-permute-start(f32[8,512]{1,0:T(8,128)S(1)} %bitcast.76), channel_id=1, source_target_pairs={{8,0},{16,8},{24,16},{32,24},{40,32},{48,40},{56,48},{64,56},{72,6... | collective-permute-start | bytes 49160 | tf_op jit(solution)/shard_map/ppermute | solution.py:25
  15.7 3.5 %copy.94 = f32[8,128,384]{2,0,1:T(8,128)} copy(f32[8,128,384]{2,1,0:T(8,128)} %param.11) | data formatting | bytes 3145728 | tf_op args[2]
  19.2 9.2 %all-to-all-start = ((f32[8,128,384]{2,0,1:T(8,128)}), f32[8,128,384]{2,0,1:T(8,128)}, u32[]{:S(2)}, u32[]{:S(2)}) async-start(f32[8,128,384]{2,0,1:T(8,128)} %copy.94), calls=%async_computation | async-start | bytes 3145728 | tf_op jit(solution)/shard_map/all_to_all | solution.py:53
  28.5 0.6 constant_dynamic-slice_fusion.2
  32.9 0.7 fusion.24
  33.8 0.6 fusion.25
  34.4 0.5 multiply_bitcast_fusion.1
  35.0 0.9 fusion.34
  35.8 2.8 %fusion.32 = (f32[8,128,511]{2,1,0:T(8,128)}, f32[8,128,511]{2,1,0:T(8,128)}) fusion(f32[8,128,512]{2,1,0:T(8,128)S(1)} %copy-done), kind=kLoop, calls=%fused_computation.75 | loop fusion | bytes 8372224 | tf_op jit(solution)/shard_map/slice | solution.py:38
  38.6 2.5 %fusion.30 = (f32[8,127,512]{2,1,0:T(8,128)}, f32[8,127,512]{2,1,0:T(8,128)}) fusion(f32[8,128,512]{2,1,0:T(8,128)S(1)} %copy-done), kind=kLoop, calls=%fused_computation.73 | loop fusion | bytes 8323072 | tf_op jit(solution)/shard_map/slice | solution.py:36
  41.1 10.5 %all-to-all-done = f32[8,128,384]{2,0,1:T(8,128)} async-done(((f32[8,128,384]{2,0,1:T(8,128)}), f32[8,128,384]{2,0,1:T(8,128)}, u32[]{:S(2)}, u32[]{:S(2)}) %all-to-all-start) | async-done | bytes 1572896 | tf_op jit(solution)/shard_map/all_to_all | solution.py:53
  51.6 1.7 copy.95
  53.6 0.4 fusion.5
  54.0 2.1 %copy.97 = f32[8,16,8,384]{3,0,2,1:T(8,128)} copy(f32[8,16,8,384]{3,2,1,0:T(8,128)S(1)} %fusion.5) | data formatting | bytes 3145728 | tf_op jit(solution)/shard_map/jit(_roll_dynamic)/dynamic_slice | solution.py:57
  56.1 7.0 %all-to-all-start.1 = ((f32[8,128,384]{2,0,1:T(8,128)}), f32[8,128,384]{2,0,1:T(8,128)}, u32[]{:S(2)}, u32[]{:S(2)}) async-start(f32[8,128,384]{2,0,1:T(8,128)} %bitcast.66), calls=%async_computation.1 | async-start | bytes 3145728 | tf_op jit(solution)/shard_map/all_to_all | solution.py:58
  63.1 2.4 %fusion.35 = (f32[7,128,512]{2,1,0:T(8,128)}, f32[7,128,512]{2,1,0:T(8,128)}) fusion(f32[8,128,512]{2,1,0:T(8,128)S(1)} %copy-done), kind=kLoop, calls=%fused_computation.78 | loop fusion | bytes 7340032 | tf_op jit(solution)/shard_map/slice | solution.py:125
  65.5 1.3 compare_and_fusion
  66.7 1.4 stack.9
  68.1 4.1 %copy.103 = f32[1,8,512,128]{3,1,2,0:T(8,128)} copy(f32[1,8,512,128]{3,2,1,0:T(8,128)} %stack.9) | data formatting | bytes 4194304 | tf_op jit(solution)/shard_map/stack | solution.py:163
  72.8 7.0 %fusion.4 = f32[8,128,512]{2,1,0:T(8,128)} fusion(f32[8,128,512]{2,1,0:T(8,128)S(1)} %copy-done, f32[1,128,512]{2,1,0:T(8,128)} %get-tuple-element.35, f32[7,128,512]{2,1,0:T(8,128)} %get-tuple-element.37, f32[7,128,512]{2,1,0:T(8,128)} %get-tuple-element.36, f32[1,128,512]{2,1,0:T(8,128)} %get-tuple-element.34, f32[8,128,511]{2,1,0:T(8,128)} %get-tuple-element.31, ...), kind=kLoop, calls=%fused_computation.16 | loop fusion | flops 13107200 | bytes 17039424 | tf_op jit(solution)/shard_map/add | solution.py:144
  79.8 1.6 stack.10
  81.5 1.2 copy.104
  83.1 2.2 %pad_maximum_fusion = f32[2,8,512,128]{3,1,2,0:T(8,128)} fusion(f32[1,8,512,128]{3,1,2,0:T(8,128)S(1)} %copy.104, f32[1,8,512,128]{3,1,2,0:T(8,128)S(1)} %copy-done.1), kind=kLoop, calls=%fused_computation.1 | loop fusion | flops 1048576 | bytes 8388608 | tf_op jit(solution)/shard_map/stack | solution.py:163
  85.3 2.9 %gather_fusion = f32[128,2,8,128]{3,2,1,0:T(8,128)S(1)} fusion(f32[2,8,512,128]{3,1,2,0:T(8,128)} %pad_maximum_fusion, s32[1024]{0:T(1024)S(1)} %pad_clamp_fusion), kind=kCustom, calls=%fused_computation | custom fusion | bytes 2097664 | tf_op jit(solution)/shard_map/jit(_take)/gather | solution.py:164
  88.4 0.4 copy.105
  88.9 1.2 slice.82
  90.7 0.7 convolution_add_fusion
  91.4 2.3 %all_to_all.16 = f32[128,2,2048]{2,1,0:T(2,128)} reshape(f32[256,2048]{1,0:T(8,128)S(1)} %convolution_add_fusion) | data formatting | bytes 4194304 | tf_op jit(solution)/shard_map/all_to_all | solution.py:173
  93.7 9.8 %all-to-all-start.2 = ((f32[128,2,2048]{2,1,0:T(2,128)}), f32[128,2,2048]{2,1,0:T(2,128)S(1)}, u32[]{:S(2)}, u32[]{:S(2)}) async-start(f32[128,2,2048]{2,1,0:T(2,128)} %all_to_all.16), calls=%async_computation.2 | async-start | bytes 4194304 | tf_op jit(solution)/shard_map/all_to_all | solution.py:173
  104.5 0.7 convert_add_fusion.1.factor_ref
  105.2 0.7 slice_bitcast_fusion
  106.0 3.1 %collective-permute-start.4 = (f32[8,384]{1,0:T(8,128)S(1)}, f32[8,384]{1,0:T(8,128)S(1)}, u32[]{:S(2)}, u32[]{:S(2)}) collective-permute-start(f32[8,384]{1,0:T(8,128)S(1)} %get-tuple-element.41), channel_id=1, source_target_pairs={{0,8},{8,16},{16,24},{24,32},{32,40},{40,48},{48,56},{56,64},{64,7... | collective-permute-start | bytes 36872 | tf_op jit(solution)/shard_map/ppermute | solution.py:113
  109.1 4.3 %collective-permute-start.5 = (f32[8,384]{1,0:T(8,128)S(1)}, f32[8,384]{1,0:T(8,128)S(1)}, u32[]{:S(2)}, u32[]{:S(2)}) collective-permute-start(f32[8,384]{1,0:T(8,128)S(1)} %get-tuple-element.40), channel_id=1, source_target_pairs={{8,0},{16,8},{24,16},{32,24},{40,32},{48,40},{56,48},{64,56},{72,6... | collective-permute-start | bytes 36872 | tf_op jit(solution)/shard_map/ppermute | solution.py:113
  113.3 1.4 fusion.36
  114.8 0.8 copy.118
  115.6 4.0 %collective-permute-start.6 = (f32[128,8]{1,0:T(8,128)S(1)}, f32[128,8]{1,0:T(8,128)S(1)}, u32[]{:S(2)}, u32[]{:S(2)}) collective-permute-start(f32[128,8]{1,0:T(8,128)S(1)} %bitcast.71), channel_id=1, source_target_pairs={{0,1},{1,2},{2,3},{3,4},{4,5},{5,6},{6,7},{8,9},{9,10},{10,11},{11... | collective-permute-start | bytes 12296 | tf_op jit(solution)/shard_map/ppermute | solution.py:113
  119.6 0.8 copy.119
  120.4 2.1 %collective-permute-start.7 = (f32[128,8]{1,0:T(8,128)S(1)}, f32[128,8]{1,0:T(8,128)S(1)}, u32[]{:S(2)}, u32[]{:S(2)}) collective-permute-start(f32[128,8]{1,0:T(8,128)S(1)} %bitcast.72), channel_id=1, source_target_pairs={{1,0},{2,1},{3,2},{4,3},{5,4},{6,5},{7,6},{9,8},{10,9},{11,10},{12... | collective-permute-start | bytes 12296 | tf_op jit(solution)/shard_map/ppermute | solution.py:113
  122.5 2.9 %copy.109.child_ref = f32[8,128,384]{2,1,0:T(8,128)} copy(f32[8,128,384]{2,0,1:T(8,128)} %all-to-all-done.1) | data formatting | bytes 3145728 | tf_op jit(solution)/shard_map/all_to_all | solution.py:58
  125.4 7.0 %all-to-all-done.2 = f32[128,2,2048]{2,1,0:T(2,128)S(1)} async-done(((f32[128,2,2048]{2,1,0:T(2,128)}), f32[128,2,2048]{2,1,0:T(2,128)S(1)}, u32[]{:S(2)}, u32[]{:S(2)}) %all-to-all-start.2) | async-done | bytes 2097184 | tf_op jit(solution)/shard_map/all_to_all | solution.py:173
  132.4 2.4 %all_to_all.18 = f32[256,2048]{1,0:T(8,128)} reshape(f32[128,2,2048]{2,1,0:T(2,128)S(1)} %all-to-all-done.2) | data formatting | bytes 4194304 | tf_op jit(solution)/shard_map/all_to_all | solution.py:173
  134.9 1.9 copy.106
  136.8 0.8 fusion.13
  137.6 3.1 %convolution_bitcast_fusion.bound_ref = f32[2,8,128,384]{3,2,1,0:T(8,128)} fusion(f32[128,2,8,128]{3,0,2,1:T(8,128)S(1)} %fusion.13, f32[128]{0:T(128)S(1)} %iota_convert_fusion, f32[384]{0:T(512)S(1)} %add_clamp_fusion), kind=kOutput, calls=%fused_computation.17 | convolution fusion | flops 604176384 | bytes 4196352 | tf_op jit(solution)/shard_map/tald,de->alte/dot_general | solution.py:187
  140.8 0.8 broadcast_in_dim.69.divisor_ref
  141.6 6.0 %shard_map.104 = (f32[8,128,384]{2,1,0:T(8,128)}, f32[8,384]{1,0:T(8,128)}, f32[8,384]{1,0:T(8,128)}, f32[128,8]{1,0:T(8,128)}, f32[128,8]{1,0:T(8,128)}) custom-call(f32[2,8]{1,0:T(2,128)} %wind_ref.5, f32[8,128,384]{2,1,0:T(8,128)} %copy.109.child_ref, f32[8,384]{1,0:T(8,128)} %copy-done.13, f32[8,384]{1,0:T(8,128)} %copy-done.14, f32[128,8]{1,0:T(8,128)} %copy-done.5, ...), custom_call_target="tpu_custom_call" | custom-call | flops 11796480 | bytes 6684672 | tf_op jit(solution)/shard_map/pallas_call | solution.py:91
  147.6 2.5 %collective-permute-start.8 = (f32[8,384]{1,0:T(8,128)}, f32[8,384]{1,0:T(8,128)S(1)}, u32[]{:S(2)}, u32[]{:S(2)}) collective-permute-start(f32[8,384]{1,0:T(8,128)} %get-tuple-element.14), channel_id=1, source_target_pairs={{0,8},{8,16},{16,24},{24,32},{32,40},{40,48},{48,56},{56,64},{64,7... | collective-permute-start | bytes 36872 | tf_op jit(solution)/shard_map/ppermute | solution.py:113
  150.1 4.9 %collective-permute-start.9 = (f32[8,384]{1,0:T(8,128)}, f32[8,384]{1,0:T(8,128)S(1)}, u32[]{:S(2)}, u32[]{:S(2)}) collective-permute-start(f32[8,384]{1,0:T(8,128)} %get-tuple-element.15), channel_id=1, source_target_pairs={{8,0},{16,8},{24,16},{32,24},{40,32},{48,40},{56,48},{64,56},{72,6... | collective-permute-start | bytes 36872 | tf_op jit(solution)/shard_map/ppermute | solution.py:113
  155.0 2.3 %collective-permute-start.10 = (f32[128,8]{1,0:T(8,128)}, f32[128,8]{1,0:T(8,128)S(1)}, u32[]{:S(2)}, u32[]{:S(2)}) collective-permute-start(f32[128,8]{1,0:T(8,128)} %get-tuple-element.16), channel_id=1, source_target_pairs={{0,1},{1,2},{2,3},{3,4},{4,5},{5,6},{6,7},{8,9},{9,10},{10,11},{11... | collective-permute-start | bytes 12296 | tf_op jit(solution)/shard_map/ppermute | solution.py:113
  157.3 2.9 %collective-permute-start.11 = (f32[128,8]{1,0:T(8,128)}, f32[128,8]{1,0:T(8,128)S(1)}, u32[]{:S(2)}, u32[]{:S(2)}) collective-permute-start(f32[128,8]{1,0:T(8,128)} %get-tuple-element.17), channel_id=1, source_target_pairs={{1,0},{2,1},{3,2},{4,3},{5,4},{6,5},{7,6},{9,8},{10,9},{11,10},{12... | collective-permute-start | bytes 12296 | tf_op jit(solution)/shard_map/ppermute | solution.py:113
  160.3 2.8 %collective-permute-done.11.ay_ref = f32[128,8]{1,0:T(8,128)S(1)} collective-permute-done((f32[128,8]{1,0:T(8,128)}, f32[128,8]{1,0:T(8,128)S(1)}, u32[]{:S(2)}, u32[]{:S(2)}) %collective-permute-start.11) | collective-permute-done | bytes 4128 | tf_op jit(solution)/shard_map/ppermute | solution.py:113
  163.2 0.6 copy-done.10
  163.8 6.0 %shard_map.105 = (f32[8,128,384]{2,1,0:T(8,128)}, f32[8,384]{1,0:T(8,128)}, f32[8,384]{1,0:T(8,128)}, f32[128,8]{1,0:T(8,128)}, f32[128,8]{1,0:T(8,128)}) custom-call(f32[2,8]{1,0:T(2,128)} %wind_ref.5, f32[8,128,384]{2,1,0:T(8,128)} %get-tuple-element.13.child_ref, f32[8,384]{1,0:T(8,128)} %copy-done.16, f32[8,384]{1,0:T(8,128)} %copy-done.18, ...), custom_call_target="tpu_custom_call" | custom-call | flops 11796480 | bytes 6684672 | tf_op jit(solution)/shard_map/pallas_call | solution.py:91
  169.8 1.9 collective-permute-start.12
  171.7 5.5 %collective-permute-start.13 = (f32[8,384]{1,0:T(8,128)}, f32[8,384]{1,0:T(8,128)S(1)}, u32[]{:S(2)}, u32[]{:S(2)}) collective-permute-start(f32[8,384]{1,0:T(8,128)} %get-tuple-element.20), channel_id=1, source_target_pairs={{8,0},{16,8},{24,16},{32,24},{40,32},{48,40},{56,48},{64,56},{72,6... | collective-permute-start | bytes 36872 | tf_op jit(solution)/shard_map/ppermute | solution.py:113
  177.2 2.5 %collective-permute-start.14 = (f32[128,8]{1,0:T(8,128)}, f32[128,8]{1,0:T(8,128)S(1)}, u32[]{:S(2)}, u32[]{:S(2)}) collective-permute-start(f32[128,8]{1,0:T(8,128)} %get-tuple-element.21), channel_id=1, source_target_pairs={{0,1},{1,2},{2,3},{3,4},{4,5},{5,6},{6,7},{8,9},{9,10},{10,11},{11... | collective-permute-start | bytes 12296 | tf_op jit(solution)/shard_map/ppermute | solution.py:113
  179.7 1.9 collective-permute-start.15
  181.7 3.8 %collective-permute-done.15.ay_ref = f32[128,8]{1,0:T(8,128)S(1)} collective-permute-done((f32[128,8]{1,0:T(8,128)}, f32[128,8]{1,0:T(8,128)S(1)}, u32[]{:S(2)}, u32[]{:S(2)}) %collective-permute-start.15) | collective-permute-done | bytes 4128 | tf_op jit(solution)/shard_map/ppermute | solution.py:113
  185.5 0.6 copy-done.9
  186.2 6.0 %shard_map.106 = (f32[8,128,384]{2,1,0:T(8,128)}, f32[8,384]{1,0:T(8,128)}, f32[8,384]{1,0:T(8,128)}, f32[128,8]{1,0:T(8,128)}, f32[128,8]{1,0:T(8,128)}) custom-call(f32[2,8]{1,0:T(2,128)} %wind_ref.5, f32[8,128,384]{2,1,0:T(8,128)} %get-tuple-element.18.child_ref, f32[8,384]{1,0:T(8,128)} %copy-done.15, f32[8,384]{1,0:T(8,128)} %copy-done.17, ...), custom_call_target="tpu_custom_call" | custom-call | flops 11796480 | bytes 6684672 | tf_op jit(solution)/shard_map/pallas_call | solution.py:91
  (88 shorter events, 3.1 us)
Async XLA Ops:
  0.6 7.6 %copy-start = (f32[8,128,512]{2,1,0:T(8,128)S(1)}, f32[8,128,512]{2,1,0:T(8,128)}, u32[]{:S(2)}) copy-start(f32[8,128,512]{2,1,0:T(8,128)} %param.9) | copy-start | bytes 6291460
  2.4 69.9 %collective-permute-start.3 = (f32[8,128]{1,0:T(8,128)S(1)}, f32[8,128]{1,0:T(8,128)S(1)}, u32[]{:S(2)}, u32[]{:S(2)}) collective-permute-start(f32[8,128]{1,0:T(8,128)S(1)} %bitcast.78), channel_id=1, source_target_pairs={{0,1},{1,2},{2,3},{3,4},{4,5},{5,6},{6,7},{8,9},{9,10},{10,11},{11... | collective-permute-start | bytes 12296 | tf_op jit(solution)/shard_map/ppermute | solution.py:25
  6.3 66.1 %collective-permute-start.2 = (f32[8,128]{1,0:T(8,128)S(1)}, f32[8,128]{1,0:T(8,128)S(1)}, u32[]{:S(2)}, u32[]{:S(2)}) collective-permute-start(f32[8,128]{1,0:T(8,128)S(1)} %bitcast.80), channel_id=1, source_target_pairs={{1,0},{2,1},{3,2},{4,3},{5,4},{6,5},{7,6},{9,8},{10,9},{11,10},{12... | collective-permute-start | bytes 12296 | tf_op jit(solution)/shard_map/ppermute | solution.py:25
  8.3 64.4 %collective-permute-start.1 = (f32[8,512]{1,0:T(8,128)S(1)}, f32[8,512]{1,0:T(8,128)S(1)}, u32[]{:S(2)}, u32[]{:S(2)}) collective-permute-start(f32[8,512]{1,0:T(8,128)S(1)} %bitcast.74), channel_id=1, source_target_pairs={{0,8},{8,16},{16,24},{24,32},{32,40},{40,48},{48,56},{56,64},{64,7... | collective-permute-start | bytes 49160 | tf_op jit(solution)/shard_map/ppermute | solution.py:25
  11.5 61.3 %collective-permute-start = (f32[8,512]{1,0:T(8,128)S(1)}, f32[8,512]{1,0:T(8,128)S(1)}, u32[]{:S(2)}, u32[]{:S(2)}) collective-permute-start(f32[8,512]{1,0:T(8,128)S(1)} %bitcast.76), channel_id=1, source_target_pairs={{8,0},{16,8},{24,16},{32,24},{40,32},{48,40},{56,48},{64,56},{72,6... | collective-permute-start | bytes 49160 | tf_op jit(solution)/shard_map/ppermute | solution.py:25
  19.2 9.3 %copy-start.21 = (s32[2,4]{1,0:T(2,128)S(1)}, s32[2,4]{1,0:T(2,128)}, u32[]{:S(2)}) copy-start(s32[2,4]{1,0:T(2,128)} %param.17) | copy-start | bytes 100
  19.2 14.4 %copy-start.4 = (s32[16384,1]{0,1:T(1,128)S(1)}, s32[16384,1]{0,1:T(1,128)}, u32[]{:S(2)}) copy-start(s32[16384,1]{0,1:T(1,128)} %param.14) | copy-start | bytes 196612
  19.2 15.2 %copy-start.12 = (f32[2,8]{1,0:T(2,128)S(1)}, f32[2,8]{1,0:T(2,128)}, u32[]{:S(2)}) copy-start(f32[2,8]{1,0:T(2,128)} %wind_ref.5) | copy-start | bytes 196
  19.2 15.7 %copy-start.2 = (bf16[128,512]{1,0:T(8,128)(2,1)S(1)}, bf16[128,512]{1,0:T(8,128)(2,1)}, u32[]{:S(2)}) copy-start(bf16[128,512]{1,0:T(8,128)(2,1)} %param.10) | copy-start | bytes 393220
  19.2 32.3 %all-to-all-start = ((f32[8,128,384]{2,0,1:T(8,128)}), f32[8,128,384]{2,0,1:T(8,128)}, u32[]{:S(2)}, u32[]{:S(2)}) async-start(f32[8,128,384]{2,0,1:T(8,128)} %copy.94), calls=%async_computation | async-start | bytes 3145728 | tf_op jit(solution)/shard_map/all_to_all | solution.py:53
  56.1 32.8 %all-to-all-start.1 = ((f32[8,128,384]{2,0,1:T(8,128)}), f32[8,128,384]{2,0,1:T(8,128)}, u32[]{:S(2)}, u32[]{:S(2)}) async-start(f32[8,128,384]{2,0,1:T(8,128)} %bitcast.66), calls=%async_computation.1 | async-start | bytes 3145728 | tf_op jit(solution)/shard_map/all_to_all | solution.py:58
  68.1 4.7 %copy-start.19 = (f32[8]{0:T(128)S(1)}, f32[8]{0:T(128)}, u32[]{:S(2)}) copy-start(f32[8]{0:T(128)} %get-tuple-element.44) | copy-start | bytes 100
  81.5 1.6 copy-start.1
  85.3 2.9 %copy-start.22 = (pred[128]{0:T(512)(128)(4,1)S(1)}, pred[128]{0:T(512)(128)(4,1)}, u32[]{:S(2)}) copy-start(pred[128]{0:T(512)(128)(4,1)} %compare_and_fusion) | copy-start | bytes 388
  88.2 2.5 %copy-start.20 = (s32[128]{0:T(128)S(1)}, s32[128]{0:T(128)}, u32[]{:S(2)}) copy-start(s32[128]{0:T(128)} %fusion.25) | copy-start | bytes 1540
  93.7 10.3 %copy-start.11 = (s32[16384]{0:T(1024)S(1)}, s32[16384]{0:T(1024)}, u32[]{:S(2)}) copy-start(s32[16384]{0:T(1024)} %param.16) | copy-start | bytes 196612
  93.7 10.8 %copy-start.3 = (bf16[128,384]{1,0:T(8,128)(2,1)S(1)}, bf16[128,384]{1,0:T(8,128)(2,1)}, u32[]{:S(2)}) copy-start(bf16[128,384]{1,0:T(8,128)(2,1)} %param.12) | copy-start | bytes 294916
  93.7 38.7 %all-to-all-start.2 = ((f32[128,2,2048]{2,1,0:T(2,128)}), f32[128,2,2048]{2,1,0:T(2,128)S(1)}, u32[]{:S(2)}, u32[]{:S(2)}) async-start(f32[128,2,2048]{2,1,0:T(2,128)} %all_to_all.16), calls=%async_computation.2 | async-start | bytes 4194304 | tf_op jit(solution)/shard_map/all_to_all | solution.py:173
  106.0 34.8 %collective-permute-start.4 = (f32[8,384]{1,0:T(8,128)S(1)}, f32[8,384]{1,0:T(8,128)S(1)}, u32[]{:S(2)}, u32[]{:S(2)}) collective-permute-start(f32[8,384]{1,0:T(8,128)S(1)} %get-tuple-element.41), channel_id=1, source_target_pairs={{0,8},{8,16},{16,24},{24,32},{32,40},{40,48},{48,56},{56,64},{64,7... | collective-permute-start | bytes 36872 | tf_op jit(solution)/shard_map/ppermute | solution.py:113
  109.1 31.7 %collective-permute-start.5 = (f32[8,384]{1,0:T(8,128)S(1)}, f32[8,384]{1,0:T(8,128)S(1)}, u32[]{:S(2)}, u32[]{:S(2)}) collective-permute-start(f32[8,384]{1,0:T(8,128)S(1)} %get-tuple-element.40), channel_id=1, source_target_pairs={{8,0},{16,8},{24,16},{32,24},{40,32},{48,40},{56,48},{64,56},{72,6... | collective-permute-start | bytes 36872 | tf_op jit(solution)/shard_map/ppermute | solution.py:113
  115.6 25.2 %collective-permute-start.6 = (f32[128,8]{1,0:T(8,128)S(1)}, f32[128,8]{1,0:T(8,128)S(1)}, u32[]{:S(2)}, u32[]{:S(2)}) collective-permute-start(f32[128,8]{1,0:T(8,128)S(1)} %bitcast.71), channel_id=1, source_target_pairs={{0,1},{1,2},{2,3},{3,4},{4,5},{5,6},{6,7},{8,9},{9,10},{10,11},{11... | collective-permute-start | bytes 12296 | tf_op jit(solution)/shard_map/ppermute | solution.py:113
  120.4 20.4 %collective-permute-start.7 = (f32[128,8]{1,0:T(8,128)S(1)}, f32[128,8]{1,0:T(8,128)S(1)}, u32[]{:S(2)}, u32[]{:S(2)}) collective-permute-start(f32[128,8]{1,0:T(8,128)S(1)} %bitcast.72), channel_id=1, source_target_pairs={{1,0},{2,1},{3,2},{4,3},{5,4},{6,5},{7,6},{9,8},{10,9},{11,10},{12... | collective-permute-start | bytes 12296 | tf_op jit(solution)/shard_map/ppermute | solution.py:113
  140.7 0.8 copy-start.5
  140.7 0.8 copy-start.6
  140.8 0.8 copy-start.13
  140.8 0.8 copy-start.14
  147.6 15.6 %collective-permute-start.8 = (f32[8,384]{1,0:T(8,128)}, f32[8,384]{1,0:T(8,128)S(1)}, u32[]{:S(2)}, u32[]{:S(2)}) collective-permute-start(f32[8,384]{1,0:T(8,128)} %get-tuple-element.14), channel_id=1, source_target_pairs={{0,8},{8,16},{16,24},{24,32},{32,40},{40,48},{48,56},{56,64},{64,7... | collective-permute-start | bytes 36872 | tf_op jit(solution)/shard_map/ppermute | solution.py:113
  150.1 13.1 %collective-permute-start.9 = (f32[8,384]{1,0:T(8,128)}, f32[8,384]{1,0:T(8,128)S(1)}, u32[]{:S(2)}, u32[]{:S(2)}) collective-permute-start(f32[8,384]{1,0:T(8,128)} %get-tuple-element.15), channel_id=1, source_target_pairs={{8,0},{16,8},{24,16},{32,24},{40,32},{48,40},{56,48},{64,56},{72,6... | collective-permute-start | bytes 36872 | tf_op jit(solution)/shard_map/ppermute | solution.py:113
  155.0 5.3 %collective-permute-start.10 = (f32[128,8]{1,0:T(8,128)}, f32[128,8]{1,0:T(8,128)S(1)}, u32[]{:S(2)}, u32[]{:S(2)}) collective-permute-start(f32[128,8]{1,0:T(8,128)} %get-tuple-element.16), channel_id=1, source_target_pairs={{0,1},{1,2},{2,3},{3,4},{4,5},{5,6},{6,7},{8,9},{9,10},{10,11},{11... | collective-permute-start | bytes 12296 | tf_op jit(solution)/shard_map/ppermute | solution.py:113
  157.3 5.8 %collective-permute-start.11 = (f32[128,8]{1,0:T(8,128)}, f32[128,8]{1,0:T(8,128)S(1)}, u32[]{:S(2)}, u32[]{:S(2)}) collective-permute-start(f32[128,8]{1,0:T(8,128)} %get-tuple-element.17), channel_id=1, source_target_pairs={{1,0},{2,1},{3,2},{4,3},{5,4},{6,5},{7,6},{9,8},{10,9},{11,10},{12... | collective-permute-start | bytes 12296 | tf_op jit(solution)/shard_map/ppermute | solution.py:113
  160.3 2.9 %copy-start.8 = (f32[128,8]{1,0:T(8,128)}, f32[128,8]{1,0:T(8,128)S(1)}, u32[]{:S(2)}) copy-start(f32[128,8]{1,0:T(8,128)S(1)} %collective-permute-done.10.by_ref) | copy-start | bytes 12292
  163.1 0.6 copy-start.10
  163.1 0.6 copy-start.16
  163.2 0.6 copy-start.18
  169.8 15.7 %collective-permute-start.12 = (f32[8,384]{1,0:T(8,128)}, f32[8,384]{1,0:T(8,128)S(1)}, u32[]{:S(2)}, u32[]{:S(2)}) collective-permute-start(f32[8,384]{1,0:T(8,128)} %get-tuple-element.19), channel_id=1, source_target_pairs={{0,8},{8,16},{16,24},{24,32},{32,40},{40,48},{48,56},{56,64},{64,7... | collective-permute-start | bytes 36872 | tf_op jit(solution)/shard_map/ppermute | solution.py:113
  171.7 13.8 %collective-permute-start.13 = (f32[8,384]{1,0:T(8,128)}, f32[8,384]{1,0:T(8,128)S(1)}, u32[]{:S(2)}, u32[]{:S(2)}) collective-permute-start(f32[8,384]{1,0:T(8,128)} %get-tuple-element.20), channel_id=1, source_target_pairs={{8,0},{16,8},{24,16},{32,24},{40,32},{48,40},{56,48},{64,56},{72,6... | collective-permute-start | bytes 36872 | tf_op jit(solution)/shard_map/ppermute | solution.py:113
  177.2 4.5 %collective-permute-start.14 = (f32[128,8]{1,0:T(8,128)}, f32[128,8]{1,0:T(8,128)S(1)}, u32[]{:S(2)}, u32[]{:S(2)}) collective-permute-start(f32[128,8]{1,0:T(8,128)} %get-tuple-element.21), channel_id=1, source_target_pairs={{0,1},{1,2},{2,3},{3,4},{4,5},{5,6},{6,7},{8,9},{9,10},{10,11},{11... | collective-permute-start | bytes 12296 | tf_op jit(solution)/shard_map/ppermute | solution.py:113
  179.7 5.8 %collective-permute-start.15 = (f32[128,8]{1,0:T(8,128)}, f32[128,8]{1,0:T(8,128)S(1)}, u32[]{:S(2)}, u32[]{:S(2)}) collective-permute-start(f32[128,8]{1,0:T(8,128)} %get-tuple-element.22), channel_id=1, source_target_pairs={{1,0},{2,1},{3,2},{4,3},{5,4},{6,5},{7,6},{9,8},{10,9},{11,10},{12... | collective-permute-start | bytes 12296 | tf_op jit(solution)/shard_map/ppermute | solution.py:113
  181.7 3.9 %copy-start.7 = (f32[128,8]{1,0:T(8,128)}, f32[128,8]{1,0:T(8,128)S(1)}, u32[]{:S(2)}) copy-start(f32[128,8]{1,0:T(8,128)S(1)} %collective-permute-done.14.by_ref) | copy-start | bytes 12292
  185.5 0.6 copy-start.9
  185.5 0.6 copy-start.15
  185.5 0.6 copy-start.17

commit v10 on v9

--- a/solution.py
+++ b/solution.py
@@ -60,45 +60,65 @@
 
 def substep_kernel(weight, wind_ref, child_ref, bx_ref, ax_ref, by_ref, ay_ref, bound_ref,
                    factor_ref, divisor_ref, out_ref, first_row_ref, last_row_ref, first_col_ref, last_col_ref):
-    levels, rows, cols = child_ref.shape
+    l = pl.program_id(0)
+    _, rows, cols = child_ref.shape
+    levels = bx_ref.shape[0]
     row_id = lax.broadcasted_iota(jnp.int32, (rows, cols), 0)
     col_id = lax.broadcasted_iota(jnp.int32, (rows, cols), 1)
-    factor = factor_ref[...]
-    divisor = divisor_ref[...]
-    for l in range(levels):
-        c = child_ref[l]
-        north = jnp.where(row_id == rows - 1, ax_ref[l:l + 1, :], pltpu.roll(c, rows - 1, 0))
-        south = jnp.where(row_id == 0, bx_ref[l:l + 1, :], pltpu.roll(c, 1, 0))
-        east = jnp.where(col_id == cols - 1, ay_ref[:, l:l + 1], pltpu.roll(c, cols - 1, 1))
-        west = jnp.where(col_id == 0, by_ref[:, l:l + 1], pltpu.roll(c, 1, 1))
-        laplace = north + south + east + west - 4.0 * c
-        tend = KAPPA * laplace - wind_ref[0, l] * (0.5 * (north - south)) - wind_ref[1, l] * (0.5 * (east - west))
-        b0 = bound_ref[0, l]
-        target = b0 + weight * (bound_ref[1, l] - b0)
-        new = (c + factor * tend + NUDGE * target) / divisor
-        out_ref[l] = new
-        first_row_ref[l:l + 1, :] = new[0:1, :]
-        last_row_ref[l:l + 1, :] = new[rows - 1:rows, :]
-        first_col_ref[:, l:l + 1] = new[:, 0:1]
-        last_col_ref[:, l:l + 1] = new[:, cols - 1:cols]
+    level_id = lax.broadcasted_iota(jnp.int32, (rows, levels), 1)
+    by_col = jnp.sum(jnp.where(level_id == l, by_ref[...].T, 0.0), axis=1, keepdims=True)
+    ay_col = jnp.sum(jnp.where(level_id == l, ay_ref[...].T, 0.0), axis=1, keepdims=True)
+    c = child_ref[0]
+    north = jnp.where(row_id == rows - 1, ax_ref[pl.ds(l, 1), :], pltpu.roll(c, rows - 1, 0))
+    south = jnp.where(row_id == 0, bx_ref[pl.ds(l, 1), :], pltpu.roll(c, 1, 0))
+    east = jnp.where(col_id == cols - 1, ay_col, pltpu.roll(c, cols - 1, 1))
+    west = jnp.where(col_id == 0, by_col, pltpu.roll(c, 1, 1))
+    laplace = north + south + east + west - 4.0 * c
+    tend = KAPPA * laplace - wind_ref[0, l] * (0.5 * (north - south)) - wind_ref[1, l] * (0.5 * (east - west))
+    b0 = bound_ref[0, 0]
+    target = b0 + weight * (bound_ref[1, 0] - b0)
+    new = (c + factor_ref[...] * tend + NUDGE * target) / divisor_ref[...]
+    out_ref[0] = new
+    first_row_ref[pl.ds(l, 1), :] = new[0:1, :]
+    last_row_ref[pl.ds(l, 1), :] = new[rows - 1:rows, :]
+    first_col_ref[pl.ds(l, 1), :] = new[:, 0:rows].T[0:1, :]
+    last_col_ref[pl.ds(l, 1), :] = new[:, cols - rows:cols].T[rows - 1:rows, :]
 
 
 def substep(weight, wind, child, bx, ax, by, ay, bound, factor, divisor):
     levels, rows, cols = child.shape
-    vmem = pl.BlockSpec(memory_space=pltpu.VMEM)
-    smem = pl.BlockSpec(memory_space=pltpu.SMEM)
     f32 = jnp.float32
+    whole = lambda shape: pl.BlockSpec(shape, lambda l: (0,) * len(shape))
+    level_block = pl.BlockSpec((1, rows, cols), lambda l: (l, 0, 0))
     return pl.pallas_call(
         functools.partial(substep_kernel, weight),
+        grid=(levels,),
         out_shape=(
             jax.ShapeDtypeStruct((levels, rows, cols), f32),
             jax.ShapeDtypeStruct((levels, cols), f32),
             jax.ShapeDtypeStruct((levels, cols), f32),
-            jax.ShapeDtypeStruct((rows, levels), f32),
-            jax.ShapeDtypeStruct((rows, levels), f32),
+            jax.ShapeDtypeStruct((levels, rows), f32),
+            jax.ShapeDtypeStruct((levels, rows), f32),
         ),
-        in_specs=[smem] + [vmem] * 8,
-        out_specs=(vmem,) * 5,
+        in_specs=[
+            pl.BlockSpec(memory_space=pltpu.SMEM),
+            level_block,
+            whole((levels, cols)),
+            whole((levels, cols)),
+            whole((levels, rows)),
+            whole((levels, rows)),
+            pl.BlockSpec((2, 1, rows, cols), lambda l: (0, l, 0, 0)),
+            whole((rows, cols)),
+            whole((rows, cols)),
+        ],
+        out_specs=(
+            level_block,
+            whole((levels, cols)),
+            whole((levels, cols)),
+            whole((levels, rows)),
+            whole((levels, rows)),
+        ),
+        compiler_params=pltpu.CompilerParams(dimension_semantics=("arbitrary",)),
         cost_estimate=pl.CostEstimate(
             flops=30 * levels * rows * cols, transcendentals=0,
             bytes_accessed=4 * (4 * levels * rows * cols + 2 * rows * cols)),
@@ -192,7 +212,7 @@
     )
     divisor = jnp.broadcast_to(1.0 + NUDGE * counts[:, None], (crows, widths))
     factor = 1.0 + child_sppt.astype(jnp.float32)
-    edges = (child[:, 0, :], child[:, -1, :], child[:, :, 0].T, child[:, :, -1].T)
+    edges = (child[:, 0, :], child[:, -1, :], child[:, :, 0], child[:, :, -1])
     for substep_index in range(SUBSTEPS):
         first_row, last_row, first_col, last_col = edges
         before_x = swap_edge(last_row, "gx", True)

time: 193 us -> 198 us (1.026)
  Pallas kernels: 18 us -> 23 us
    pallas_call x3, Pallas kernels: 18 us -> 23 us  [substep(): pl.pallas_call(functools.partial(substep_kernel, weight), grid=(levels,),...]
    dynamic_slice x1 -> x0, local copies, waits for them, and re-layouts: 2.06 us -> none  [storm_rows(): grid = jnp.roll(grid, storm_shift[1, piece], axis=2)]
  transfers between devices with their start and end apart: 19 -> 19, of which waited for: 4 -> 4; matrix products, arithmetic and copies ran while one was open for 29% -> 28% of each run, Pallas kernels for 0% -> 0%
where the time goes in v10:
time: 198 us; the launch traced here: 196 us
  starting transfers between devices  77.1 us (39%)
  local copies, waits for them, and re-layouts  46.5 us (23%)
  waiting for transfers between devices  24.1 us (12%)
  Pallas kernels  23 us (12%)
  other arithmetic  14.7 us (7%)
  between operations  5.94 us (3%)
  matrix products  4.65 us (2%)
    ppermute x12, starting transfers between devices, swap_edge(): return lax.ppermute(edge, axis, pairs)  38 us
    pallas_call x3, Pallas kernels, substep(): pl.pallas_call(functools.partial(substep_kernel, weight), grid=(levels,),...  23 us
    ppermute x4, starting transfers between devices, swap(): return lax.ppermute(edge, axis, pairs)  13.1 us
    all_to_all x1, waiting for transfers between devices, storm_rows(): gathered = lax.all_to_all(child, ('gx', 'gy'), 1, 1, tiled=True)  10.4 us
    all_to_all x1, starting transfers between devices, shards(): lax.all_to_all(outgoing_strips, ('gx', 'gy'), split_axis=0, concat_axis=0...  9.76 us
    all_to_all x1, starting transfers between devices, storm_rows(): gathered = lax.all_to_all(child, ('gx', 'gy'), 1, 1, tiled=True)  9.25 us
    another operation x4, local copies, waits for them, and re-layouts, shards(): jnp.stack([parent_field, new_parent]).reshape(2, levels, -1, STRIP)  8.37 us
    all_to_all x1, waiting for transfers between devices, shards(): lax.all_to_all(outgoing_strips, ('gx', 'gy'), split_axis=0, concat_axis=0...  8.24 us
  transfers between devices with their start and end apart: 19, of which 4 were waited for; matrix products, arithmetic and copies ran while one was open for 28% of the time, Pallas kernels for 0%

profile of v10, /device:TPU:33, one launch (start us, length us, event | category | flops | bytes accessed | tf_op | source)
XLA Modules:
  0.0 196.1 jit_solution(9885858949649751273)
XLA Ops:
  0.6 1.6 fusion.34
  2.4 3.8 %collective-permute-start.3 = (f32[8,128]{1,0:T(8,128)S(1)}, f32[8,128]{1,0:T(8,128)S(1)}, u32[]{:S(2)}, u32[]{:S(2)}) collective-permute-start(f32[8,128]{1,0:T(8,128)S(1)} %bitcast.75), channel_id=1, source_target_pairs={{0,1},{1,2},{2,3},{3,4},{4,5},{5,6},{6,7},{8,9},{9,10},{10,11},{11... | collective-permute-start | bytes 12296 | tf_op jit(solution)/shard_map/ppermute | solution.py:25
  6.3 1.9 collective-permute-start.2
  8.3 3.1 %collective-permute-start.1 = (f32[8,512]{1,0:T(8,128)S(1)}, f32[8,512]{1,0:T(8,128)S(1)}, u32[]{:S(2)}, u32[]{:S(2)}) collective-permute-start(f32[8,512]{1,0:T(8,128)S(1)} %bitcast.71), channel_id=1, source_target_pairs={{0,8},{8,16},{16,24},{24,32},{32,40},{40,48},{48,56},{56,64},{64,7... | collective-permute-start | bytes 49160 | tf_op jit(solution)/shard_map/ppermute | solution.py:25
  11.5 4.3 %collective-permute-start = (f32[8,512]{1,0:T(8,128)S(1)}, f32[8,512]{1,0:T(8,128)S(1)}, u32[]{:S(2)}, u32[]{:S(2)}) collective-permute-start(f32[8,512]{1,0:T(8,128)S(1)} %bitcast.73), channel_id=1, source_target_pairs={{8,0},{16,8},{24,16},{32,24},{40,32},{48,40},{56,48},{64,56},{72,6... | collective-permute-start | bytes 49160 | tf_op jit(solution)/shard_map/ppermute | solution.py:25
  15.7 3.5 %copy.115 = f32[8,128,384]{2,0,1:T(8,128)} copy(f32[8,128,384]{2,1,0:T(8,128)} %param.11) | data formatting | bytes 3145728 | tf_op args[2]
  19.2 9.2 %all-to-all-start = ((f32[8,128,384]{2,0,1:T(8,128)}), f32[8,128,384]{2,0,1:T(8,128)}, u32[]{:S(2)}, u32[]{:S(2)}) async-start(f32[8,128,384]{2,0,1:T(8,128)} %copy.115), calls=%async_computation | async-start | bytes 3145728 | tf_op jit(solution)/shard_map/all_to_all | solution.py:53
  28.5 0.6 constant_dynamic-slice_fusion.2
  32.9 0.7 fusion.25
  33.8 0.6 fusion.26
  34.4 0.5 multiply_bitcast_fusion.1
  35.0 0.9 fusion.35
  35.8 2.8 %fusion.33 = (f32[8,128,511]{2,1,0:T(8,128)}, f32[8,128,511]{2,1,0:T(8,128)}) fusion(f32[8,128,512]{2,1,0:T(8,128)S(1)} %copy-done), kind=kLoop, calls=%fused_computation.77 | loop fusion | bytes 8372224 | tf_op jit(solution)/shard_map/slice | solution.py:38
  38.6 2.5 %fusion.31 = (f32[8,127,512]{2,1,0:T(8,128)}, f32[8,127,512]{2,1,0:T(8,128)}) fusion(f32[8,128,512]{2,1,0:T(8,128)S(1)} %copy-done), kind=kLoop, calls=%fused_computation.75 | loop fusion | bytes 8323072 | tf_op jit(solution)/shard_map/slice | solution.py:36
  41.1 10.4 %all-to-all-done = f32[8,128,384]{2,0,1:T(8,128)} async-done(((f32[8,128,384]{2,0,1:T(8,128)}), f32[8,128,384]{2,0,1:T(8,128)}, u32[]{:S(2)}, u32[]{:S(2)}) %all-to-all-start) | async-done | bytes 1572896 | tf_op jit(solution)/shard_map/all_to_all | solution.py:53
  51.6 1.7 copy.143
  53.3 0.3 fusion.7
  53.6 0.4 fusion.6
  54.0 2.1 %copy.117 = f32[8,128,384]{2,0,1:T(8,128)} copy(f32[8,128,384]{2,1,0:T(8,128)S(1)} %fusion.6) | data formatting | bytes 3145728 | tf_op jit(solution)/shard_map/reshape | solution.py:58
  56.1 7.0 %all-to-all-start.1 = ((f32[8,128,384]{2,0,1:T(8,128)}), f32[8,128,384]{2,0,1:T(8,128)}, u32[]{:S(2)}, u32[]{:S(2)}) async-start(f32[8,128,384]{2,0,1:T(8,128)} %copy.117), calls=%async_computation.1 | async-start | bytes 3145728 | tf_op jit(solution)/shard_map/all_to_all | solution.py:58
  63.1 2.5 %fusion.36 = (f32[7,128,512]{2,1,0:T(8,128)}, f32[7,128,512]{2,1,0:T(8,128)}) fusion(f32[8,128,512]{2,1,0:T(8,128)S(1)} %copy-done), kind=kLoop, calls=%fused_computation.80 | loop fusion | bytes 7340032 | tf_op jit(solution)/shard_map/slice | solution.py:145
  65.5 1.3 compare_and_fusion
  66.8 1.4 stack.9
  68.2 4.1 %copy.123 = f32[1,8,512,128]{3,1,2,0:T(8,128)} copy(f32[1,8,512,128]{3,2,1,0:T(8,128)} %stack.9) | data formatting | bytes 4194304 | tf_op jit(solution)/shard_map/stack | solution.py:183
  72.9 7.0 %fusion.4 = f32[8,128,512]{2,1,0:T(8,128)} fusion(f32[8,128,512]{2,1,0:T(8,128)S(1)} %copy-done, f32[1,128,512]{2,1,0:T(8,128)} %get-tuple-element.35, f32[7,128,512]{2,1,0:T(8,128)} %get-tuple-element.37, f32[7,128,512]{2,1,0:T(8,128)} %get-tuple-element.36, f32[1,128,512]{2,1,0:T(8,128)} %get-tuple-element.34, f32[8,128,511]{2,1,0:T(8,128)} %get-tuple-element.31, ...), kind=kLoop, calls=%fused_computation.16 | loop fusion | flops 13107200 | bytes 17039424 | tf_op jit(solution)/shard_map/add | solution.py:164
  79.9 1.6 stack.10
  81.6 1.2 copy.124
  82.8 0.4 copy-done.1
  83.2 2.2 %pad_maximum_fusion = f32[2,8,512,128]{3,1,2,0:T(8,128)} fusion(f32[1,8,512,128]{3,1,2,0:T(8,128)S(1)} %copy.124, f32[1,8,512,128]{3,1,2,0:T(8,128)S(1)} %copy-done.1), kind=kLoop, calls=%fused_computation.1 | loop fusion | flops 1048576 | bytes 8388608 | tf_op jit(solution)/shard_map/stack | solution.py:183
  85.4 2.9 %gather_fusion = f32[128,2,8,128]{3,2,1,0:T(8,128)S(1)} fusion(f32[2,8,512,128]{3,1,2,0:T(8,128)} %pad_maximum_fusion, s32[1024]{0:T(1024)S(1)} %pad_clamp_fusion), kind=kCustom, calls=%fused_computation | custom fusion | bytes 2097664 | tf_op jit(solution)/shard_map/jit(_take)/gather | solution.py:184
  88.5 0.4 copy.125
  88.9 1.2 slice.82
  90.8 0.7 convolution_add_fusion
  91.5 2.3 %all_to_all.16 = f32[128,2,2048]{2,1,0:T(2,128)} reshape(f32[256,2048]{1,0:T(8,128)S(1)} %convolution_add_fusion) | data formatting | bytes 4194304 | tf_op jit(solution)/shard_map/all_to_all | solution.py:193
  93.8 9.8 %all-to-all-start.2 = ((f32[128,2,2048]{2,1,0:T(2,128)}), f32[128,2,2048]{2,1,0:T(2,128)S(1)}, u32[]{:S(2)}, u32[]{:S(2)}) async-start(f32[128,2,2048]{2,1,0:T(2,128)} %all_to_all.16), calls=%async_computation.2 | async-start | bytes 4194304 | tf_op jit(solution)/shard_map/all_to_all | solution.py:193
  104.6 0.7 convert_add_fusion.1.factor_ref
  105.3 0.7 slice_bitcast_fusion
  106.0 3.1 %collective-permute-start.4 = (f32[8,384]{1,0:T(8,128)S(1)}, f32[8,384]{1,0:T(8,128)S(1)}, u32[]{:S(2)}, u32[]{:S(2)}) collective-permute-start(f32[8,384]{1,0:T(8,128)S(1)} %get-tuple-element.41), channel_id=1, source_target_pairs={{0,8},{8,16},{16,24},{24,32},{32,40},{40,48},{48,56},{56,64},{64,7... | collective-permute-start | bytes 36872 | tf_op jit(solution)/shard_map/ppermute | solution.py:133
  109.1 4.3 %collective-permute-start.5 = (f32[8,384]{1,0:T(8,128)S(1)}, f32[8,384]{1,0:T(8,128)S(1)}, u32[]{:S(2)}, u32[]{:S(2)}) collective-permute-start(f32[8,384]{1,0:T(8,128)S(1)} %get-tuple-element.40), channel_id=1, source_target_pairs={{8,0},{16,8},{24,16},{32,24},{40,32},{48,40},{56,48},{64,56},{72,6... | collective-permute-start | bytes 36872 | tf_op jit(solution)/shard_map/ppermute | solution.py:133
  113.4 1.4 fusion.37
  115.1 4.0 %collective-permute-start.6 = (f32[8,128]{1,0:T(8,128)S(1)}, f32[8,128]{1,0:T(8,128)S(1)}, u32[]{:S(2)}, u32[]{:S(2)}) collective-permute-start(f32[8,128]{1,0:T(8,128)S(1)} %bitcast.79), channel_id=1, source_target_pairs={{0,1},{1,2},{2,3},{3,4},{4,5},{5,6},{6,7},{8,9},{9,10},{10,11},{11... | collective-permute-start | bytes 12296 | tf_op jit(solution)/shard_map/ppermute | solution.py:133
  119.3 2.2 %collective-permute-start.7 = (f32[8,128]{1,0:T(8,128)S(1)}, f32[8,128]{1,0:T(8,128)S(1)}, u32[]{:S(2)}, u32[]{:S(2)}) collective-permute-start(f32[8,128]{1,0:T(8,128)S(1)} %bitcast.80), channel_id=1, source_target_pairs={{1,0},{2,1},{3,2},{4,3},{5,4},{6,5},{7,6},{9,8},{10,9},{11,10},{12... | collective-permute-start | bytes 12296 | tf_op jit(solution)/shard_map/ppermute | solution.py:133
  121.4 2.9 %copy.129.child_ref = f32[8,128,384]{2,1,0:T(8,128)} copy(f32[8,128,384]{2,0,1:T(8,128)} %all-to-all-done.1) | data formatting | bytes 3145728 | tf_op jit(solution)/shard_map/all_to_all | solution.py:58
  124.3 8.2 %all-to-all-done.2 = f32[128,2,2048]{2,1,0:T(2,128)S(1)} async-done(((f32[128,2,2048]{2,1,0:T(2,128)}), f32[128,2,2048]{2,1,0:T(2,128)S(1)}, u32[]{:S(2)}, u32[]{:S(2)}) %all-to-all-start.2) | async-done | bytes 2097184 | tf_op jit(solution)/shard_map/all_to_all | solution.py:193
  132.5 2.4 %all_to_all.18 = f32[256,2048]{1,0:T(8,128)} reshape(f32[128,2,2048]{2,1,0:T(2,128)S(1)} %all-to-all-done.2) | data formatting | bytes 4194304 | tf_op jit(solution)/shard_map/all_to_all | solution.py:193
  135.0 1.9 copy.126
  136.9 0.8 fusion.14
  137.7 3.1 %convolution_bitcast_fusion.bound_ref = f32[2,8,128,384]{3,2,1,0:T(8,128)} fusion(f32[128,2,8,128]{3,0,2,1:T(8,128)S(1)} %fusion.14, f32[128]{0:T(128)S(1)} %iota_convert_fusion, f32[384]{0:T(512)S(1)} %add_clamp_fusion), kind=kOutput, calls=%fused_computation.17 | convolution fusion | flops 604176384 | bytes 4196352 | tf_op jit(solution)/shard_map/tald,de->alte/dot_general | solution.py:207
  140.9 0.8 broadcast_in_dim.69.divisor_ref
  141.7 7.7 %shard_map.104 = (f32[8,128,384]{2,1,0:T(8,128)}, f32[8,384]{1,0:T(8,128)}, f32[8,384]{1,0:T(8,128)}, f32[8,128]{1,0:T(8,128)}, f32[8,128]{1,0:T(8,128)}) custom-call(f32[2,8]{1,0:T(2,128)} %wind_ref.5, f32[8,128,384]{2,1,0:T(8,128)} %copy.129.child_ref, f32[8,384]{1,0:T(8,128)} %copy-done.7, f32[8,384]{1,0:T(8,128)} %copy-done.8, f32[8,128]{1,0:T(8,128)} %copy-done.13, ...), custom_call_target="tpu_custom_call" | custom-call | flops 11796480 | bytes 6684672 | tf_op jit(solution)/shard_map/pallas_call | solution.py:93
  149.4 2.5 %collective-permute-start.8 = (f32[8,384]{1,0:T(8,128)}, f32[8,384]{1,0:T(8,128)S(1)}, u32[]{:S(2)}, u32[]{:S(2)}) collective-permute-start(f32[8,384]{1,0:T(8,128)} %get-tuple-element.14), channel_id=1, source_target_pairs={{0,8},{8,16},{16,24},{24,32},{32,40},{40,48},{48,56},{56,64},{64,7... | collective-permute-start | bytes 36872 | tf_op jit(solution)/shard_map/ppermute | solution.py:133
  151.9 4.9 %collective-permute-start.9 = (f32[8,384]{1,0:T(8,128)}, f32[8,384]{1,0:T(8,128)S(1)}, u32[]{:S(2)}, u32[]{:S(2)}) collective-permute-start(f32[8,384]{1,0:T(8,128)} %get-tuple-element.15), channel_id=1, source_target_pairs={{8,0},{16,8},{24,16},{32,24},{40,32},{48,40},{56,48},{64,56},{72,6... | collective-permute-start | bytes 36872 | tf_op jit(solution)/shard_map/ppermute | solution.py:133
  156.8 2.3 %collective-permute-start.10 = (f32[8,128]{1,0:T(8,128)}, f32[8,128]{1,0:T(8,128)S(1)}, u32[]{:S(2)}, u32[]{:S(2)}) collective-permute-start(f32[8,128]{1,0:T(8,128)} %get-tuple-element.16), channel_id=1, source_target_pairs={{0,1},{1,2},{2,3},{3,4},{4,5},{5,6},{6,7},{8,9},{9,10},{10,11},{11... | collective-permute-start | bytes 12296 | tf_op jit(solution)/shard_map/ppermute | solution.py:133
  159.1 2.9 %collective-permute-start.11 = (f32[8,128]{1,0:T(8,128)}, f32[8,128]{1,0:T(8,128)S(1)}, u32[]{:S(2)}, u32[]{:S(2)}) collective-permute-start(f32[8,128]{1,0:T(8,128)} %get-tuple-element.17), channel_id=1, source_target_pairs={{1,0},{2,1},{3,2},{4,3},{5,4},{6,5},{7,6},{9,8},{10,9},{11,10},{12... | collective-permute-start | bytes 12296 | tf_op jit(solution)/shard_map/ppermute | solution.py:133
  162.1 2.2 %collective-permute-done.11.ay_ref = f32[8,128]{1,0:T(8,128)S(1)} collective-permute-done((f32[8,128]{1,0:T(8,128)}, f32[8,128]{1,0:T(8,128)S(1)}, u32[]{:S(2)}, u32[]{:S(2)}) %collective-permute-start.11) | collective-permute-done | bytes 4128 | tf_op jit(solution)/shard_map/ppermute | solution.py:133
  164.3 0.5 copy-done.18
  164.9 7.7 %shard_map.105 = (f32[8,128,384]{2,1,0:T(8,128)}, f32[8,384]{1,0:T(8,128)}, f32[8,384]{1,0:T(8,128)}, f32[8,128]{1,0:T(8,128)}, f32[8,128]{1,0:T(8,128)}) custom-call(f32[2,8]{1,0:T(2,128)} %wind_ref.5, f32[8,128,384]{2,1,0:T(8,128)} %get-tuple-element.13.child_ref, f32[8,384]{1,0:T(8,128)} %copy-done.10, f32[8,384]{1,0:T(8,128)} %copy-done.12, ...), custom_call_target="tpu_custom_call" | custom-call | flops 11796480 | bytes 6684672 | tf_op jit(solution)/shard_map/pallas_call | solution.py:93
  172.6 1.9 collective-permute-start.12
  174.5 5.5 %collective-permute-start.13 = (f32[8,384]{1,0:T(8,128)}, f32[8,384]{1,0:T(8,128)S(1)}, u32[]{:S(2)}, u32[]{:S(2)}) collective-permute-start(f32[8,384]{1,0:T(8,128)} %get-tuple-element.20), channel_id=1, source_target_pairs={{8,0},{16,8},{24,16},{32,24},{40,32},{48,40},{56,48},{64,56},{72,6... | collective-permute-start | bytes 36872 | tf_op jit(solution)/shard_map/ppermute | solution.py:133
  180.0 2.5 %collective-permute-start.14 = (f32[8,128]{1,0:T(8,128)}, f32[8,128]{1,0:T(8,128)S(1)}, u32[]{:S(2)}, u32[]{:S(2)}) collective-permute-start(f32[8,128]{1,0:T(8,128)} %get-tuple-element.21), channel_id=1, source_target_pairs={{0,1},{1,2},{2,3},{3,4},{4,5},{5,6},{6,7},{8,9},{9,10},{10,11},{11... | collective-permute-start | bytes 12296 | tf_op jit(solution)/shard_map/ppermute | solution.py:133
  182.5 1.9 collective-permute-start.15
  184.5 3.2 %collective-permute-done.15.ay_ref = f32[8,128]{1,0:T(8,128)S(1)} collective-permute-done((f32[8,128]{1,0:T(8,128)}, f32[8,128]{1,0:T(8,128)S(1)}, u32[]{:S(2)}, u32[]{:S(2)}) %collective-permute-start.15) | collective-permute-done | bytes 4128 | tf_op jit(solution)/shard_map/ppermute | solution.py:133
  187.7 0.6 copy-done.17
  188.2 7.6 %shard_map.106 = (f32[8,128,384]{2,1,0:T(8,128)}, f32[8,384]{1,0:T(8,128)}, f32[8,384]{1,0:T(8,128)}, f32[8,128]{1,0:T(8,128)}, f32[8,128]{1,0:T(8,128)}) custom-call(f32[2,8]{1,0:T(2,128)} %wind_ref.5, f32[8,128,384]{2,1,0:T(8,128)} %get-tuple-element.18.child_ref, f32[8,384]{1,0:T(8,128)} %copy-done.9, f32[8,384]{1,0:T(8,128)} %copy-done.11, ...), custom_call_target="tpu_custom_call" | custom-call | flops 11796480 | bytes 6684672 | tf_op jit(solution)/shard_map/pallas_call | solution.py:93
  (88 shorter events, 2.8 us)
Async XLA Ops:
  0.6 7.6 %copy-start = (f32[8,128,512]{2,1,0:T(8,128)S(1)}, f32[8,128,512]{2,1,0:T(8,128)}, u32[]{:S(2)}) copy-start(f32[8,128,512]{2,1,0:T(8,128)} %param.9) | copy-start | bytes 6291460
  2.4 69.9 %collective-permute-start.3 = (f32[8,128]{1,0:T(8,128)S(1)}, f32[8,128]{1,0:T(8,128)S(1)}, u32[]{:S(2)}, u32[]{:S(2)}) collective-permute-start(f32[8,128]{1,0:T(8,128)S(1)} %bitcast.75), channel_id=1, source_target_pairs={{0,1},{1,2},{2,3},{3,4},{4,5},{5,6},{6,7},{8,9},{9,10},{10,11},{11... | collective-permute-start | bytes 12296 | tf_op jit(solution)/shard_map/ppermute | solution.py:25
  6.3 66.2 %collective-permute-start.2 = (f32[8,128]{1,0:T(8,128)S(1)}, f32[8,128]{1,0:T(8,128)S(1)}, u32[]{:S(2)}, u32[]{:S(2)}) collective-permute-start(f32[8,128]{1,0:T(8,128)S(1)} %bitcast.77), channel_id=1, source_target_pairs={{1,0},{2,1},{3,2},{4,3},{5,4},{6,5},{7,6},{9,8},{10,9},{11,10},{12... | collective-permute-start | bytes 12296 | tf_op jit(solution)/shard_map/ppermute | solution.py:25
  8.3 64.5 %collective-permute-start.1 = (f32[8,512]{1,0:T(8,128)S(1)}, f32[8,512]{1,0:T(8,128)S(1)}, u32[]{:S(2)}, u32[]{:S(2)}) collective-permute-start(f32[8,512]{1,0:T(8,128)S(1)} %bitcast.71), channel_id=1, source_target_pairs={{0,8},{8,16},{16,24},{24,32},{32,40},{40,48},{48,56},{56,64},{64,7... | collective-permute-start | bytes 49160 | tf_op jit(solution)/shard_map/ppermute | solution.py:25
  11.5 61.4 %collective-permute-start = (f32[8,512]{1,0:T(8,128)S(1)}, f32[8,512]{1,0:T(8,128)S(1)}, u32[]{:S(2)}, u32[]{:S(2)}) collective-permute-start(f32[8,512]{1,0:T(8,128)S(1)} %bitcast.73), channel_id=1, source_target_pairs={{8,0},{16,8},{24,16},{32,24},{40,32},{48,40},{56,48},{64,56},{72,6... | collective-permute-start | bytes 49160 | tf_op jit(solution)/shard_map/ppermute | solution.py:25
  19.2 9.3 %copy-start.21 = (s32[2,4]{1,0:T(2,128)S(1)}, s32[2,4]{1,0:T(2,128)}, u32[]{:S(2)}) copy-start(s32[2,4]{1,0:T(2,128)} %param.17) | copy-start | bytes 100
  19.2 14.4 %copy-start.4 = (s32[16384,1]{0,1:T(1,128)S(1)}, s32[16384,1]{0,1:T(1,128)}, u32[]{:S(2)}) copy-start(s32[16384,1]{0,1:T(1,128)} %param.14) | copy-start | bytes 196612
  19.2 15.2 %copy-start.6 = (f32[2,8]{1,0:T(2,128)S(1)}, f32[2,8]{1,0:T(2,128)}, u32[]{:S(2)}) copy-start(f32[2,8]{1,0:T(2,128)} %wind_ref.5) | copy-start | bytes 196
  19.2 15.7 %copy-start.2 = (bf16[128,512]{1,0:T(8,128)(2,1)S(1)}, bf16[128,512]{1,0:T(8,128)(2,1)}, u32[]{:S(2)}) copy-start(bf16[128,512]{1,0:T(8,128)(2,1)} %param.10) | copy-start | bytes 393220
  19.2 32.3 %all-to-all-start = ((f32[8,128,384]{2,0,1:T(8,128)}), f32[8,128,384]{2,0,1:T(8,128)}, u32[]{:S(2)}, u32[]{:S(2)}) async-start(f32[8,128,384]{2,0,1:T(8,128)} %copy.115), calls=%async_computation | async-start | bytes 3145728 | tf_op jit(solution)/shard_map/all_to_all | solution.py:53
  56.1 32.8 %all-to-all-start.1 = ((f32[8,128,384]{2,0,1:T(8,128)}), f32[8,128,384]{2,0,1:T(8,128)}, u32[]{:S(2)}, u32[]{:S(2)}) async-start(f32[8,128,384]{2,0,1:T(8,128)} %copy.117), calls=%async_computation.1 | async-start | bytes 3145728 | tf_op jit(solution)/shard_map/all_to_all | solution.py:58
  68.2 4.7 %copy-start.19 = (f32[8]{0:T(128)S(1)}, f32[8]{0:T(128)}, u32[]{:S(2)}) copy-start(f32[8]{0:T(128)} %get-tuple-element.44) | copy-start | bytes 100
  81.6 1.6 copy-start.1
  85.4 2.9 %copy-start.22 = (pred[128]{0:T(512)(128)(4,1)S(1)}, pred[128]{0:T(512)(128)(4,1)}, u32[]{:S(2)}) copy-start(pred[128]{0:T(512)(128)(4,1)} %compare_and_fusion) | copy-start | bytes 388
  88.3 2.5 %copy-start.20 = (s32[128]{0:T(128)S(1)}, s32[128]{0:T(128)}, u32[]{:S(2)}) copy-start(s32[128]{0:T(128)} %fusion.26) | copy-start | bytes 1540
  93.8 10.3 %copy-start.5 = (s32[16384]{0:T(1024)S(1)}, s32[16384]{0:T(1024)}, u32[]{:S(2)}) copy-start(s32[16384]{0:T(1024)} %param.16) | copy-start | bytes 196612
  93.8 10.8 %copy-start.3 = (bf16[128,384]{1,0:T(8,128)(2,1)S(1)}, bf16[128,384]{1,0:T(8,128)(2,1)}, u32[]{:S(2)}) copy-start(bf16[128,384]{1,0:T(8,128)(2,1)} %param.12) | copy-start | bytes 294916
  93.8 38.7 %all-to-all-start.2 = ((f32[128,2,2048]{2,1,0:T(2,128)}), f32[128,2,2048]{2,1,0:T(2,128)S(1)}, u32[]{:S(2)}, u32[]{:S(2)}) async-start(f32[128,2,2048]{2,1,0:T(2,128)} %all_to_all.16), calls=%async_computation.2 | async-start | bytes 4194304 | tf_op jit(solution)/shard_map/all_to_all | solution.py:193
  106.0 34.8 %collective-permute-start.4 = (f32[8,384]{1,0:T(8,128)S(1)}, f32[8,384]{1,0:T(8,128)S(1)}, u32[]{:S(2)}, u32[]{:S(2)}) collective-permute-start(f32[8,384]{1,0:T(8,128)S(1)} %get-tuple-element.41), channel_id=1, source_target_pairs={{0,8},{8,16},{16,24},{24,32},{32,40},{40,48},{48,56},{56,64},{64,7... | collective-permute-start | bytes 36872 | tf_op jit(solution)/shard_map/ppermute | solution.py:133
  109.1 31.7 %collective-permute-start.5 = (f32[8,384]{1,0:T(8,128)S(1)}, f32[8,384]{1,0:T(8,128)S(1)}, u32[]{:S(2)}, u32[]{:S(2)}) collective-permute-start(f32[8,384]{1,0:T(8,128)S(1)} %get-tuple-element.40), channel_id=1, source_target_pairs={{8,0},{16,8},{24,16},{32,24},{40,32},{48,40},{56,48},{64,56},{72,6... | collective-permute-start | bytes 36872 | tf_op jit(solution)/shard_map/ppermute | solution.py:133
  115.1 25.8 %collective-permute-start.6 = (f32[8,128]{1,0:T(8,128)S(1)}, f32[8,128]{1,0:T(8,128)S(1)}, u32[]{:S(2)}, u32[]{:S(2)}) collective-permute-start(f32[8,128]{1,0:T(8,128)S(1)} %bitcast.79), channel_id=1, source_target_pairs={{0,1},{1,2},{2,3},{3,4},{4,5},{5,6},{6,7},{8,9},{9,10},{10,11},{11... | collective-permute-start | bytes 12296 | tf_op jit(solution)/shard_map/ppermute | solution.py:133
  119.3 21.6 %collective-permute-start.7 = (f32[8,128]{1,0:T(8,128)S(1)}, f32[8,128]{1,0:T(8,128)S(1)}, u32[]{:S(2)}, u32[]{:S(2)}) collective-permute-start(f32[8,128]{1,0:T(8,128)S(1)} %bitcast.80), channel_id=1, source_target_pairs={{1,0},{2,1},{3,2},{4,3},{5,4},{6,5},{7,6},{9,8},{10,9},{11,10},{12... | collective-permute-start | bytes 12296 | tf_op jit(solution)/shard_map/ppermute | solution.py:133
  140.8 0.8 copy-start.13
  140.8 0.8 copy-start.14
  140.9 0.8 copy-start.7
  140.9 0.8 copy-start.8
  149.4 14.9 %collective-permute-start.8 = (f32[8,384]{1,0:T(8,128)}, f32[8,384]{1,0:T(8,128)S(1)}, u32[]{:S(2)}, u32[]{:S(2)}) collective-permute-start(f32[8,384]{1,0:T(8,128)} %get-tuple-element.14), channel_id=1, source_target_pairs={{0,8},{8,16},{16,24},{24,32},{32,40},{40,48},{48,56},{56,64},{64,7... | collective-permute-start | bytes 36872 | tf_op jit(solution)/shard_map/ppermute | solution.py:133
  151.9 12.4 %collective-permute-start.9 = (f32[8,384]{1,0:T(8,128)}, f32[8,384]{1,0:T(8,128)S(1)}, u32[]{:S(2)}, u32[]{:S(2)}) collective-permute-start(f32[8,384]{1,0:T(8,128)} %get-tuple-element.15), channel_id=1, source_target_pairs={{8,0},{16,8},{24,16},{32,24},{40,32},{48,40},{56,48},{64,56},{72,6... | collective-permute-start | bytes 36872 | tf_op jit(solution)/shard_map/ppermute | solution.py:133
  156.8 5.3 %collective-permute-start.10 = (f32[8,128]{1,0:T(8,128)}, f32[8,128]{1,0:T(8,128)S(1)}, u32[]{:S(2)}, u32[]{:S(2)}) collective-permute-start(f32[8,128]{1,0:T(8,128)} %get-tuple-element.16), channel_id=1, source_target_pairs={{0,1},{1,2},{2,3},{3,4},{4,5},{5,6},{6,7},{8,9},{9,10},{10,11},{11... | collective-permute-start | bytes 12296 | tf_op jit(solution)/shard_map/ppermute | solution.py:133
  159.1 5.1 %collective-permute-start.11 = (f32[8,128]{1,0:T(8,128)}, f32[8,128]{1,0:T(8,128)S(1)}, u32[]{:S(2)}, u32[]{:S(2)}) collective-permute-start(f32[8,128]{1,0:T(8,128)} %get-tuple-element.17), channel_id=1, source_target_pairs={{1,0},{2,1},{3,2},{4,3},{5,4},{6,5},{7,6},{9,8},{10,9},{11,10},{12... | collective-permute-start | bytes 12296 | tf_op jit(solution)/shard_map/ppermute | solution.py:133
  162.1 2.2 %copy-start.16 = (f32[8,128]{1,0:T(8,128)}, f32[8,128]{1,0:T(8,128)S(1)}, u32[]{:S(2)}) copy-start(f32[8,128]{1,0:T(8,128)S(1)} %collective-permute-done.10.by_ref) | copy-start | bytes 12292
  164.3 0.6 copy-start.18
  164.3 0.6 copy-start.10
  164.3 0.6 copy-start.12
  172.6 15.1 %collective-permute-start.12 = (f32[8,384]{1,0:T(8,128)}, f32[8,384]{1,0:T(8,128)S(1)}, u32[]{:S(2)}, u32[]{:S(2)}) collective-permute-start(f32[8,384]{1,0:T(8,128)} %get-tuple-element.19), channel_id=1, source_target_pairs={{0,8},{8,16},{16,24},{24,32},{32,40},{40,48},{48,56},{56,64},{64,7... | collective-permute-start | bytes 36872 | tf_op jit(solution)/shard_map/ppermute | solution.py:133
  174.5 13.1 %collective-permute-start.13 = (f32[8,384]{1,0:T(8,128)}, f32[8,384]{1,0:T(8,128)S(1)}, u32[]{:S(2)}, u32[]{:S(2)}) collective-permute-start(f32[8,384]{1,0:T(8,128)} %get-tuple-element.20), channel_id=1, source_target_pairs={{8,0},{16,8},{24,16},{32,24},{40,32},{48,40},{56,48},{64,56},{72,6... | collective-permute-start | bytes 36872 | tf_op jit(solution)/shard_map/ppermute | solution.py:133
  180.0 4.4 %collective-permute-start.14 = (f32[8,128]{1,0:T(8,128)}, f32[8,128]{1,0:T(8,128)S(1)}, u32[]{:S(2)}, u32[]{:S(2)}) collective-permute-start(f32[8,128]{1,0:T(8,128)} %get-tuple-element.21), channel_id=1, source_target_pairs={{0,1},{1,2},{2,3},{3,4},{4,5},{5,6},{6,7},{8,9},{9,10},{10,11},{11... | collective-permute-start | bytes 12296 | tf_op jit(solution)/shard_map/ppermute | solution.py:133
  182.5 5.1 %collective-permute-start.15 = (f32[8,128]{1,0:T(8,128)}, f32[8,128]{1,0:T(8,128)S(1)}, u32[]{:S(2)}, u32[]{:S(2)}) collective-permute-start(f32[8,128]{1,0:T(8,128)} %get-tuple-element.22), channel_id=1, source_target_pairs={{1,0},{2,1},{3,2},{4,3},{5,4},{6,5},{7,6},{9,8},{10,9},{11,10},{12... | collective-permute-start | bytes 12296 | tf_op jit(solution)/shard_map/ppermute | solution.py:133
  184.4 3.2 %copy-start.15 = (f32[8,128]{1,0:T(8,128)}, f32[8,128]{1,0:T(8,128)S(1)}, u32[]{:S(2)}) copy-start(f32[8,128]{1,0:T(8,128)S(1)} %collective-permute-done.14.by_ref) | copy-start | bytes 12292
  187.6 0.6 copy-start.17
  187.6 0.6 copy-start.9
  187.7 0.6 copy-start.11

commit v11 on v9

--- a/solution.py
+++ b/solution.py
@@ -163,11 +163,11 @@
     both_states = jnp.stack([parent_field, new_parent]).reshape(2, levels, -1, STRIP)
     picked = jnp.take(both_states, my_rows, axis=2)
     strip_values = jnp.moveaxis(picked, 2, 0).reshape(slots, -1)
-    outgoing_strips = jnp.dot(
-        send_select,
+    outgoing_strips = jnp.einsum(
+        "dsj,jk->dsk",
+        send_select.reshape(devices, CAP, slots),
         strip_values,
         precision=lax.Precision.HIGH,
-        preferred_element_type=jnp.float32,
     )
     outgoing_strips = outgoing_strips + 0.0 * child[0, 0, 0]
     incoming = lax.all_to_all(
@@ -180,8 +180,11 @@
     chosen = jnp.sum(jnp.where(hits, target_table[:, None, :], 0), axis=2)
     target_rows = jnp.where(jnp.any(hits, axis=2), chosen, -1).reshape(-1)
     row_select = (jnp.arange(crows)[:, None] == target_rows[None, :]).astype(jnp.float32)
-    coarse = jnp.dot(
-        row_select, incoming, precision=lax.Precision.HIGH, preferred_element_type=jnp.float32
+    coarse = jnp.einsum(
+        "tqs,qsk->tk",
+        row_select.reshape(crows, devices, CAP),
+        incoming,
+        precision=lax.Precision.HIGH,
     )
     counts = jnp.sum(row_select, axis=1)
     boundary = jnp.einsum(

time: 193 us -> 194 us (level)
    all_to_all x3 -> x1, local copies, waits for them, and re-layouts: 6.61 us -> 2.43 us  [shards(): lax.all_to_all(outgoing_strips, ('gx', 'gy'), split_axis=0, concat_axis=0...]
    add x0 -> x1, local copies, waits for them, and re-layouts: none -> 2.97 us  [shards(): outgoing_strips = outgoing_strips + 0.0 * child[0, 0, 0]]
    unnamed x53 -> x55, local copies, waits for them, and re-layouts: 7.12 us -> 7.11 us
  transfers between devices with their start and end apart: 19 -> 19, of which waited for: 4 -> 4; matrix products, arithmetic and copies ran while one was open for 29% -> 31% of each run, Pallas kernels for 0% -> 0%
where the time goes in v11:
time: 194 us; the launch traced here: 192 us
  starting transfers between devices  77.1 us (40%)
  local copies, waits for them, and re-layouts  46.4 us (24%)
  waiting for transfers between devices  23.4 us (12%)
  Pallas kernels  18 us (9%)
  other arithmetic  15.2 us (8%)
  matrix products  6.3 us (3%)
  between operations  5.94 us (3%)
    ppermute x12, starting transfers between devices, swap_edge(): return lax.ppermute(edge, axis, pairs)  38 us
    pallas_call x3, Pallas kernels, substep(): pl.pallas_call(functools.partial(substep_kernel, weight), out_shape=(jax....  18 us
    ppermute x4, starting transfers between devices, swap(): return lax.ppermute(edge, axis, pairs)  13.1 us
    all_to_all x1, starting transfers between devices, shards(): lax.all_to_all(outgoing_strips, ('gx', 'gy'), split_axis=0, concat_axis=0...  9.76 us
    all_to_all x1, waiting for transfers between devices, storm_rows(): gathered = lax.all_to_all(child, ('gx', 'gy'), 1, 1, tiled=True)  9.65 us
    all_to_all x1, starting transfers between devices, storm_rows(): gathered = lax.all_to_all(child, ('gx', 'gy'), 1, 1, tiled=True)  9.25 us
    another operation x4, local copies, waits for them, and re-layouts, shards(): jnp.stack([parent_field, new_parent]).reshape(2, levels, -1, STRIP)  8.37 us
    unnamed x55, local copies, waits for them, and re-layouts  7.11 us
  transfers between devices with their start and end apart: 19, of which 4 were waited for; matrix products, arithmetic and copies ran while one was open for 31% of the time, Pallas kernels for 0%

profile of v11, /device:TPU:33, one launch (start us, length us, event | category | flops | bytes accessed | tf_op | source)
XLA Modules:
  0.0 192.3 jit_solution(17181139007848170310)
XLA Ops:
  0.6 1.6 fusion.34
  2.4 3.8 %collective-permute-start.3 = (f32[8,128]{1,0:T(8,128)S(1)}, f32[8,128]{1,0:T(8,128)S(1)}, u32[]{:S(2)}, u32[]{:S(2)}) collective-permute-start(f32[8,128]{1,0:T(8,128)S(1)} %bitcast.87), channel_id=1, source_target_pairs={{0,1},{1,2},{2,3},{3,4},{4,5},{5,6},{6,7},{8,9},{9,10},{10,11},{11... | collective-permute-start | bytes 12296 | tf_op jit(solution)/shard_map/ppermute | solution.py:25
  6.3 1.9 collective-permute-start.2
  8.3 3.1 %collective-permute-start.1 = (f32[8,512]{1,0:T(8,128)S(1)}, f32[8,512]{1,0:T(8,128)S(1)}, u32[]{:S(2)}, u32[]{:S(2)}) collective-permute-start(f32[8,512]{1,0:T(8,128)S(1)} %bitcast.83), channel_id=1, source_target_pairs={{0,8},{8,16},{16,24},{24,32},{32,40},{40,48},{48,56},{56,64},{64,7... | collective-permute-start | bytes 49160 | tf_op jit(solution)/shard_map/ppermute | solution.py:25
  11.5 4.3 %collective-permute-start = (f32[8,512]{1,0:T(8,128)S(1)}, f32[8,512]{1,0:T(8,128)S(1)}, u32[]{:S(2)}, u32[]{:S(2)}) collective-permute-start(f32[8,512]{1,0:T(8,128)S(1)} %bitcast.85), channel_id=1, source_target_pairs={{8,0},{16,8},{24,16},{32,24},{40,32},{48,40},{56,48},{64,56},{72,6... | collective-permute-start | bytes 49160 | tf_op jit(solution)/shard_map/ppermute | solution.py:25
  15.7 3.5 %copy.119 = f32[8,128,384]{2,0,1:T(8,128)} copy(f32[8,128,384]{2,1,0:T(8,128)} %param.11) | data formatting | bytes 3145728 | tf_op args[2]
  19.2 9.2 %all-to-all-start = ((f32[8,128,384]{2,0,1:T(8,128)}), f32[8,128,384]{2,0,1:T(8,128)}, u32[]{:S(2)}, u32[]{:S(2)}) async-start(f32[8,128,384]{2,0,1:T(8,128)} %copy.119), calls=%async_computation | async-start | bytes 3145728 | tf_op jit(solution)/shard_map/all_to_all | solution.py:53
  28.5 0.7 constant_dynamic-slice_fusion.2
  33.2 0.7 fusion.25
  34.1 0.5 fusion.26
  34.6 0.6 multiply_add_fusion
  35.2 0.6 multiply_bitcast_fusion.1
  35.8 0.8 fusion.35
  36.6 2.8 %fusion.33 = (f32[8,128,511]{2,1,0:T(8,128)}, f32[8,128,511]{2,1,0:T(8,128)}) fusion(f32[8,128,512]{2,1,0:T(8,128)S(1)} %copy-done), kind=kLoop, calls=%fused_computation.78 | loop fusion | bytes 8372224 | tf_op jit(solution)/shard_map/slice | solution.py:38
  39.4 2.5 %fusion.31 = (f32[8,127,512]{2,1,0:T(8,128)}, f32[8,127,512]{2,1,0:T(8,128)}) fusion(f32[8,128,512]{2,1,0:T(8,128)S(1)} %copy-done), kind=kLoop, calls=%fused_computation.76 | loop fusion | bytes 8323072 | tf_op jit(solution)/shard_map/slice | solution.py:36
  41.9 9.7 %all-to-all-done = f32[8,128,384]{2,0,1:T(8,128)} async-done(((f32[8,128,384]{2,0,1:T(8,128)}), f32[8,128,384]{2,0,1:T(8,128)}, u32[]{:S(2)}, u32[]{:S(2)}) %all-to-all-start) | async-done | bytes 1572896 | tf_op jit(solution)/shard_map/all_to_all | solution.py:53
  51.6 1.7 copy.120
  53.6 0.4 fusion.5
  54.0 2.1 %copy.122 = f32[8,16,8,384]{3,0,2,1:T(8,128)} copy(f32[8,16,8,384]{3,2,1,0:T(8,128)S(1)} %fusion.5) | data formatting | bytes 3145728 | tf_op jit(solution)/shard_map/jit(_roll_dynamic)/dynamic_slice | solution.py:57
  56.1 7.0 %all-to-all-start.1 = ((f32[8,128,384]{2,0,1:T(8,128)}), f32[8,128,384]{2,0,1:T(8,128)}, u32[]{:S(2)}, u32[]{:S(2)}) async-start(f32[8,128,384]{2,0,1:T(8,128)} %bitcast.76), calls=%async_computation.1 | async-start | bytes 3145728 | tf_op jit(solution)/shard_map/all_to_all | solution.py:58
  63.1 2.5 %fusion.36 = (f32[7,128,512]{2,1,0:T(8,128)}, f32[7,128,512]{2,1,0:T(8,128)}) fusion(f32[8,128,512]{2,1,0:T(8,128)S(1)} %copy-done), kind=kLoop, calls=%fused_computation.81 | loop fusion | bytes 7340032 | tf_op jit(solution)/shard_map/slice | solution.py:125
  65.5 1.2 compare_and_fusion
  66.8 1.4 stack.9
  68.2 4.1 %copy.127 = f32[1,8,512,128]{3,1,2,0:T(8,128)} copy(f32[1,8,512,128]{3,2,1,0:T(8,128)} %stack.9) | data formatting | bytes 4194304 | tf_op jit(solution)/shard_map/stack | solution.py:163
  72.8 7.0 %fusion.4 = f32[8,128,512]{2,1,0:T(8,128)} fusion(f32[8,128,512]{2,1,0:T(8,128)S(1)} %copy-done, f32[1,128,512]{2,1,0:T(8,128)} %get-tuple-element.35, f32[7,128,512]{2,1,0:T(8,128)} %get-tuple-element.37, f32[7,128,512]{2,1,0:T(8,128)} %get-tuple-element.36, f32[1,128,512]{2,1,0:T(8,128)} %get-tuple-element.34, f32[8,128,511]{2,1,0:T(8,128)} %get-tuple-element.31, ...), kind=kLoop, calls=%fused_computation.16 | loop fusion | flops 13107200 | bytes 17039424 | tf_op jit(solution)/shard_map/add | solution.py:144
  79.9 1.6 stack.10
  81.5 1.2 copy.128
  82.8 0.4 copy-done.1
  83.1 2.2 %pad_maximum_fusion = f32[2,8,512,128]{3,1,2,0:T(8,128)} fusion(f32[1,8,512,128]{3,1,2,0:T(8,128)S(1)} %copy.128, f32[1,8,512,128]{3,1,2,0:T(8,128)S(1)} %copy-done.1), kind=kLoop, calls=%fused_computation.1 | loop fusion | flops 1048576 | bytes 8388608 | tf_op jit(solution)/shard_map/stack | solution.py:163
  85.4 2.9 %gather_fusion = f32[128,2,8,128]{3,2,1,0:T(8,128)S(1)} fusion(f32[2,8,512,128]{3,1,2,0:T(8,128)} %pad_maximum_fusion, s32[1024]{0:T(1024)S(1)} %pad_clamp_fusion), kind=kCustom, calls=%fused_computation | custom fusion | bytes 2097664 | tf_op jit(solution)/shard_map/jit(_take)/gather | solution.py:164
  88.7 1.2 slice.82
  90.5 0.8 convolution_add_fusion
  91.3 3.0 %copy.129 = f32[128,2,2048]{2,1,0:T(2,128)} copy(f32[128,2,2048]{2,0,1:T(8,128)S(1)} %convolution_add_fusion) | data formatting | bytes 4194304 | tf_op jit(solution)/shard_map/add | solution.py:172
  94.3 9.8 %all-to-all-start.2 = ((f32[128,2,2048]{2,1,0:T(2,128)}), f32[128,2,2048]{2,1,0:T(2,128)S(1)}, u32[]{:S(2)}, u32[]{:S(2)}) async-start(f32[128,2,2048]{2,1,0:T(2,128)} %copy.129), calls=%async_computation.2 | async-start | bytes 4194304 | tf_op jit(solution)/shard_map/all_to_all | solution.py:173
  105.1 0.7 convert_add_fusion.1.factor_ref
  105.8 0.7 slice_bitcast_fusion
  106.5 3.1 %collective-permute-start.4 = (f32[8,384]{1,0:T(8,128)S(1)}, f32[8,384]{1,0:T(8,128)S(1)}, u32[]{:S(2)}, u32[]{:S(2)}) collective-permute-start(f32[8,384]{1,0:T(8,128)S(1)} %get-tuple-element.41), channel_id=1, source_target_pairs={{0,8},{8,16},{16,24},{24,32},{32,40},{40,48},{48,56},{56,64},{64,7... | collective-permute-start | bytes 36872 | tf_op jit(solution)/shard_map/ppermute | solution.py:113
  109.6 4.3 %collective-permute-start.5 = (f32[8,384]{1,0:T(8,128)S(1)}, f32[8,384]{1,0:T(8,128)S(1)}, u32[]{:S(2)}, u32[]{:S(2)}) collective-permute-start(f32[8,384]{1,0:T(8,128)S(1)} %get-tuple-element.40), channel_id=1, source_target_pairs={{8,0},{16,8},{24,16},{32,24},{40,32},{48,40},{56,48},{64,56},{72,6... | collective-permute-start | bytes 36872 | tf_op jit(solution)/shard_map/ppermute | solution.py:113
  113.9 1.4 fusion.37
  115.3 0.8 copy.145
  116.1 4.0 %collective-permute-start.6 = (f32[128,8]{1,0:T(8,128)S(1)}, f32[128,8]{1,0:T(8,128)S(1)}, u32[]{:S(2)}, u32[]{:S(2)}) collective-permute-start(f32[128,8]{1,0:T(8,128)S(1)} %bitcast.80), channel_id=1, source_target_pairs={{0,1},{1,2},{2,3},{3,4},{4,5},{5,6},{6,7},{8,9},{9,10},{10,11},{11... | collective-permute-start | bytes 12296 | tf_op jit(solution)/shard_map/ppermute | solution.py:113
  120.1 0.8 copy.146
  120.9 2.1 %collective-permute-start.7 = (f32[128,8]{1,0:T(8,128)S(1)}, f32[128,8]{1,0:T(8,128)S(1)}, u32[]{:S(2)}, u32[]{:S(2)}) collective-permute-start(f32[128,8]{1,0:T(8,128)S(1)} %bitcast.81), channel_id=1, source_target_pairs={{1,0},{2,1},{3,2},{4,3},{5,4},{6,5},{7,6},{9,8},{10,9},{11,10},{12... | collective-permute-start | bytes 12296 | tf_op jit(solution)/shard_map/ppermute | solution.py:113
  123.1 2.9 %copy.135.child_ref = f32[8,128,384]{2,1,0:T(8,128)} copy(f32[8,128,384]{2,0,1:T(8,128)} %all-to-all-done.1) | data formatting | bytes 3145728 | tf_op jit(solution)/shard_map/all_to_all | solution.py:58
  125.9 7.1 %all-to-all-done.2 = f32[128,2,2048]{2,1,0:T(2,128)S(1)} async-done(((f32[128,2,2048]{2,1,0:T(2,128)}), f32[128,2,2048]{2,1,0:T(2,128)S(1)}, u32[]{:S(2)}, u32[]{:S(2)}) %all-to-all-start.2) | async-done | bytes 2097184 | tf_op jit(solution)/shard_map/all_to_all | solution.py:173
  133.0 2.4 %copy.130 = f32[128,2,2048]{0,2,1:T(8,128)} copy(f32[128,2,2048]{2,1,0:T(2,128)S(1)} %all-to-all-done.2) | data formatting | bytes 4194304 | tf_op jit(solution)/shard_map/all_to_all | solution.py:173
  135.4 2.4 %convolution_bitcast_fusion.1 = f32[128,2,8,128]{3,0,2,1:T(8,128)S(1)} fusion(f32[2,8,128,128,2]{3,2,1,0,4:T(8,128)} %bitcast.75, s32[128,2]{0,1:T(2,128)S(1)} %broadcast_select_fusion.1), kind=kOutput, calls=%fused_computation.20 | convolution fusion | flops 402685952 | bytes 3146752 | tf_op jit(solution)/shard_map/tqs,qsk->tk/dot_general | solution.py:183
  137.9 3.1 %convolution_bitcast_fusion.bound_ref = f32[2,8,128,384]{3,2,1,0:T(8,128)} fusion(f32[128,2,8,128]{3,0,2,1:T(8,128)S(1)} %convolution_bitcast_fusion.1, f32[128]{0:T(128)S(1)} %iota_convert_fusion, f32[384]{0:T(512)S(1)} %add_clamp_fusion), kind=kOutput, calls=%fused_computation.17 | convolution fusion | flops 604176384 | bytes 4196352 | tf_op jit(solution)/shard_map/tald,de->alte/dot_general | solution.py:190
  141.0 0.8 broadcast_in_dim.69.divisor_ref
  141.8 6.0 %shard_map.104 = (f32[8,128,384]{2,1,0:T(8,128)}, f32[8,384]{1,0:T(8,128)}, f32[8,384]{1,0:T(8,128)}, f32[128,8]{1,0:T(8,128)}, f32[128,8]{1,0:T(8,128)}) custom-call(f32[2,8]{1,0:T(2,128)} %wind_ref.5, f32[8,128,384]{2,1,0:T(8,128)} %copy.135.child_ref, f32[8,384]{1,0:T(8,128)} %copy-done.13, f32[8,384]{1,0:T(8,128)} %copy-done.14, f32[128,8]{1,0:T(8,128)} %copy-done.5, ...), custom_call_target="tpu_custom_call" | custom-call | flops 11796480 | bytes 6684672 | tf_op jit(solution)/shard_map/pallas_call | solution.py:91
  147.8 2.5 %collective-permute-start.8 = (f32[8,384]{1,0:T(8,128)}, f32[8,384]{1,0:T(8,128)S(1)}, u32[]{:S(2)}, u32[]{:S(2)}) collective-permute-start(f32[8,384]{1,0:T(8,128)} %get-tuple-element.14), channel_id=1, source_target_pairs={{0,8},{8,16},{16,24},{24,32},{32,40},{40,48},{48,56},{56,64},{64,7... | collective-permute-start | bytes 36872 | tf_op jit(solution)/shard_map/ppermute | solution.py:113
  150.3 4.9 %collective-permute-start.9 = (f32[8,384]{1,0:T(8,128)}, f32[8,384]{1,0:T(8,128)S(1)}, u32[]{:S(2)}, u32[]{:S(2)}) collective-permute-start(f32[8,384]{1,0:T(8,128)} %get-tuple-element.15), channel_id=1, source_target_pairs={{8,0},{16,8},{24,16},{32,24},{40,32},{48,40},{56,48},{64,56},{72,6... | collective-permute-start | bytes 36872 | tf_op jit(solution)/shard_map/ppermute | solution.py:113
  155.2 2.3 %collective-permute-start.10 = (f32[128,8]{1,0:T(8,128)}, f32[128,8]{1,0:T(8,128)S(1)}, u32[]{:S(2)}, u32[]{:S(2)}) collective-permute-start(f32[128,8]{1,0:T(8,128)} %get-tuple-element.16), channel_id=1, source_target_pairs={{0,1},{1,2},{2,3},{3,4},{4,5},{5,6},{6,7},{8,9},{9,10},{10,11},{11... | collective-permute-start | bytes 12296 | tf_op jit(solution)/shard_map/ppermute | solution.py:113
  157.6 2.9 %collective-permute-start.11 = (f32[128,8]{1,0:T(8,128)}, f32[128,8]{1,0:T(8,128)S(1)}, u32[]{:S(2)}, u32[]{:S(2)}) collective-permute-start(f32[128,8]{1,0:T(8,128)} %get-tuple-element.17), channel_id=1, source_target_pairs={{1,0},{2,1},{3,2},{4,3},{5,4},{6,5},{7,6},{9,8},{10,9},{11,10},{12... | collective-permute-start | bytes 12296 | tf_op jit(solution)/shard_map/ppermute | solution.py:113
  160.5 2.8 %collective-permute-done.11.ay_ref = f32[128,8]{1,0:T(8,128)S(1)} collective-permute-done((f32[128,8]{1,0:T(8,128)}, f32[128,8]{1,0:T(8,128)S(1)}, u32[]{:S(2)}, u32[]{:S(2)}) %collective-permute-start.11) | collective-permute-done | bytes 4128 | tf_op jit(solution)/shard_map/ppermute | solution.py:113
  163.4 0.6 copy-done.10
  164.0 6.0 %shard_map.105 = (f32[8,128,384]{2,1,0:T(8,128)}, f32[8,384]{1,0:T(8,128)}, f32[8,384]{1,0:T(8,128)}, f32[128,8]{1,0:T(8,128)}, f32[128,8]{1,0:T(8,128)}) custom-call(f32[2,8]{1,0:T(2,128)} %wind_ref.5, f32[8,128,384]{2,1,0:T(8,128)} %get-tuple-element.13.child_ref, f32[8,384]{1,0:T(8,128)} %copy-done.16, f32[8,384]{1,0:T(8,128)} %copy-done.18, ...), custom_call_target="tpu_custom_call" | custom-call | flops 11796480 | bytes 6684672 | tf_op jit(solution)/shard_map/pallas_call | solution.py:91
  170.0 1.9 collective-permute-start.12
  171.9 5.5 %collective-permute-start.13 = (f32[8,384]{1,0:T(8,128)}, f32[8,384]{1,0:T(8,128)S(1)}, u32[]{:S(2)}, u32[]{:S(2)}) collective-permute-start(f32[8,384]{1,0:T(8,128)} %get-tuple-element.20), channel_id=1, source_target_pairs={{8,0},{16,8},{24,16},{32,24},{40,32},{48,40},{56,48},{64,56},{72,6... | collective-permute-start | bytes 36872 | tf_op jit(solution)/shard_map/ppermute | solution.py:113
  177.4 2.5 %collective-permute-start.14 = (f32[128,8]{1,0:T(8,128)}, f32[128,8]{1,0:T(8,128)S(1)}, u32[]{:S(2)}, u32[]{:S(2)}) collective-permute-start(f32[128,8]{1,0:T(8,128)} %get-tuple-element.21), channel_id=1, source_target_pairs={{0,1},{1,2},{2,3},{3,4},{4,5},{5,6},{6,7},{8,9},{9,10},{10,11},{11... | collective-permute-start | bytes 12296 | tf_op jit(solution)/shard_map/ppermute | solution.py:113
  179.9 1.9 collective-permute-start.15
  181.9 3.8 %collective-permute-done.15.ay_ref = f32[128,8]{1,0:T(8,128)S(1)} collective-permute-done((f32[128,8]{1,0:T(8,128)}, f32[128,8]{1,0:T(8,128)S(1)}, u32[]{:S(2)}, u32[]{:S(2)}) %collective-permute-start.15) | collective-permute-done | bytes 4128 | tf_op jit(solution)/shard_map/ppermute | solution.py:113
  185.8 0.6 copy-done.9
  186.4 6.0 %shard_map.106 = (f32[8,128,384]{2,1,0:T(8,128)}, f32[8,384]{1,0:T(8,128)}, f32[8,384]{1,0:T(8,128)}, f32[128,8]{1,0:T(8,128)}, f32[128,8]{1,0:T(8,128)}) custom-call(f32[2,8]{1,0:T(2,128)} %wind_ref.5, f32[8,128,384]{2,1,0:T(8,128)} %get-tuple-element.18.child_ref, f32[8,384]{1,0:T(8,128)} %copy-done.15, f32[8,384]{1,0:T(8,128)} %copy-done.17, ...), custom_call_target="tpu_custom_call" | custom-call | flops 11796480 | bytes 6684672 | tf_op jit(solution)/shard_map/pallas_call | solution.py:91
  (90 shorter events, 2.9 us)
Async XLA Ops:
  0.6 7.6 %copy-start = (f32[8,128,512]{2,1,0:T(8,128)S(1)}, f32[8,128,512]{2,1,0:T(8,128)}, u32[]{:S(2)}) copy-start(f32[8,128,512]{2,1,0:T(8,128)} %param.9) | copy-start | bytes 6291460
  2.4 69.9 %collective-permute-start.3 = (f32[8,128]{1,0:T(8,128)S(1)}, f32[8,128]{1,0:T(8,128)S(1)}, u32[]{:S(2)}, u32[]{:S(2)}) collective-permute-start(f32[8,128]{1,0:T(8,128)S(1)} %bitcast.87), channel_id=1, source_target_pairs={{0,1},{1,2},{2,3},{3,4},{4,5},{5,6},{6,7},{8,9},{9,10},{10,11},{11... | collective-permute-start | bytes 12296 | tf_op jit(solution)/shard_map/ppermute | solution.py:25
  6.3 66.2 %collective-permute-start.2 = (f32[8,128]{1,0:T(8,128)S(1)}, f32[8,128]{1,0:T(8,128)S(1)}, u32[]{:S(2)}, u32[]{:S(2)}) collective-permute-start(f32[8,128]{1,0:T(8,128)S(1)} %bitcast.89), channel_id=1, source_target_pairs={{1,0},{2,1},{3,2},{4,3},{5,4},{6,5},{7,6},{9,8},{10,9},{11,10},{12... | collective-permute-start | bytes 12296 | tf_op jit(solution)/shard_map/ppermute | solution.py:25
  8.3 64.4 %collective-permute-start.1 = (f32[8,512]{1,0:T(8,128)S(1)}, f32[8,512]{1,0:T(8,128)S(1)}, u32[]{:S(2)}, u32[]{:S(2)}) collective-permute-start(f32[8,512]{1,0:T(8,128)S(1)} %bitcast.83), channel_id=1, source_target_pairs={{0,8},{8,16},{16,24},{24,32},{32,40},{40,48},{48,56},{56,64},{64,7... | collective-permute-start | bytes 49160 | tf_op jit(solution)/shard_map/ppermute | solution.py:25
  11.5 61.3 %collective-permute-start = (f32[8,512]{1,0:T(8,128)S(1)}, f32[8,512]{1,0:T(8,128)S(1)}, u32[]{:S(2)}, u32[]{:S(2)}) collective-permute-start(f32[8,512]{1,0:T(8,128)S(1)} %bitcast.85), channel_id=1, source_target_pairs={{8,0},{16,8},{24,16},{32,24},{40,32},{48,40},{56,48},{64,56},{72,6... | collective-permute-start | bytes 49160 | tf_op jit(solution)/shard_map/ppermute | solution.py:25
  19.2 9.3 %copy-start.22 = (s32[2,4]{1,0:T(2,128)S(1)}, s32[2,4]{1,0:T(2,128)}, u32[]{:S(2)}) copy-start(s32[2,4]{1,0:T(2,128)} %param.17) | copy-start | bytes 100
  19.2 14.7 %copy-start.4 = (s32[16384,1]{0,1:T(1,128)S(1)}, s32[16384,1]{0,1:T(1,128)}, u32[]{:S(2)}) copy-start(s32[16384,1]{0,1:T(1,128)} %param.14) | copy-start | bytes 196612
  19.2 15.9 %copy-start.12 = (f32[2,8]{1,0:T(2,128)S(1)}, f32[2,8]{1,0:T(2,128)}, u32[]{:S(2)}) copy-start(f32[2,8]{1,0:T(2,128)} %wind_ref.5) | copy-start | bytes 196
  19.2 16.5 %copy-start.2 = (bf16[128,512]{1,0:T(8,128)(2,1)S(1)}, bf16[128,512]{1,0:T(8,128)(2,1)}, u32[]{:S(2)}) copy-start(bf16[128,512]{1,0:T(8,128)(2,1)} %param.10) | copy-start | bytes 393220
  19.2 32.3 %all-to-all-start = ((f32[8,128,384]{2,0,1:T(8,128)}), f32[8,128,384]{2,0,1:T(8,128)}, u32[]{:S(2)}, u32[]{:S(2)}) async-start(f32[8,128,384]{2,0,1:T(8,128)} %copy.119), calls=%async_computation | async-start | bytes 3145728 | tf_op jit(solution)/shard_map/all_to_all | solution.py:53
  56.1 32.6 %all-to-all-start.1 = ((f32[8,128,384]{2,0,1:T(8,128)}), f32[8,128,384]{2,0,1:T(8,128)}, u32[]{:S(2)}, u32[]{:S(2)}) async-start(f32[8,128,384]{2,0,1:T(8,128)} %bitcast.76), calls=%async_computation.1 | async-start | bytes 3145728 | tf_op jit(solution)/shard_map/all_to_all | solution.py:58
  68.1 4.7 %copy-start.19 = (f32[8]{0:T(128)S(1)}, f32[8]{0:T(128)}, u32[]{:S(2)}) copy-start(f32[8]{0:T(128)} %get-tuple-element.44) | copy-start | bytes 100
  81.5 1.6 copy-start.1
  85.4 2.9 %copy-start.23 = (pred[128]{0:T(512)(128)(4,1)S(1)}, pred[128]{0:T(512)(128)(4,1)}, u32[]{:S(2)}) copy-start(pred[128]{0:T(512)(128)(4,1)} %compare_and_fusion) | copy-start | bytes 388
  88.2 2.2 %copy-start.20 = (s32[128]{0:T(128)S(1)}, s32[128]{0:T(128)}, u32[]{:S(2)}) copy-start(s32[128]{0:T(128)} %fusion.26) | copy-start | bytes 1540
  88.3 2.2 %copy-start.21 = (s32[128,2]{0,1:T(2,128)S(1)}, s32[128,2]{0,1:T(2,128)}, u32[]{:S(2)}) copy-start(s32[128,2]{0,1:T(2,128)} %multiply_add_fusion) | copy-start | bytes 3076
  94.2 10.3 %copy-start.11 = (s32[16384]{0:T(1024)S(1)}, s32[16384]{0:T(1024)}, u32[]{:S(2)}) copy-start(s32[16384]{0:T(1024)} %param.16) | copy-start | bytes 196612
  94.3 10.8 %copy-start.3 = (bf16[128,384]{1,0:T(8,128)(2,1)S(1)}, bf16[128,384]{1,0:T(8,128)(2,1)}, u32[]{:S(2)}) copy-start(bf16[128,384]{1,0:T(8,128)(2,1)} %param.12) | copy-start | bytes 294916
  94.3 38.7 %all-to-all-start.2 = ((f32[128,2,2048]{2,1,0:T(2,128)}), f32[128,2,2048]{2,1,0:T(2,128)S(1)}, u32[]{:S(2)}, u32[]{:S(2)}) async-start(f32[128,2,2048]{2,1,0:T(2,128)} %copy.129), calls=%async_computation.2 | async-start | bytes 4194304 | tf_op jit(solution)/shard_map/all_to_all | solution.py:173
  106.5 34.5 %collective-permute-start.4 = (f32[8,384]{1,0:T(8,128)S(1)}, f32[8,384]{1,0:T(8,128)S(1)}, u32[]{:S(2)}, u32[]{:S(2)}) collective-permute-start(f32[8,384]{1,0:T(8,128)S(1)} %get-tuple-element.41), channel_id=1, source_target_pairs={{0,8},{8,16},{16,24},{24,32},{32,40},{40,48},{48,56},{56,64},{64,7... | collective-permute-start | bytes 36872 | tf_op jit(solution)/shard_map/ppermute | solution.py:113
  109.6 31.4 %collective-permute-start.5 = (f32[8,384]{1,0:T(8,128)S(1)}, f32[8,384]{1,0:T(8,128)S(1)}, u32[]{:S(2)}, u32[]{:S(2)}) collective-permute-start(f32[8,384]{1,0:T(8,128)S(1)} %get-tuple-element.40), channel_id=1, source_target_pairs={{8,0},{16,8},{24,16},{32,24},{40,32},{48,40},{56,48},{64,56},{72,6... | collective-permute-start | bytes 36872 | tf_op jit(solution)/shard_map/ppermute | solution.py:113
  116.1 24.9 %collective-permute-start.6 = (f32[128,8]{1,0:T(8,128)S(1)}, f32[128,8]{1,0:T(8,128)S(1)}, u32[]{:S(2)}, u32[]{:S(2)}) collective-permute-start(f32[128,8]{1,0:T(8,128)S(1)} %bitcast.80), channel_id=1, source_target_pairs={{0,1},{1,2},{2,3},{3,4},{4,5},{5,6},{6,7},{8,9},{9,10},{10,11},{11... | collective-permute-start | bytes 12296 | tf_op jit(solution)/shard_map/ppermute | solution.py:113
  120.9 20.0 %collective-permute-start.7 = (f32[128,8]{1,0:T(8,128)S(1)}, f32[128,8]{1,0:T(8,128)S(1)}, u32[]{:S(2)}, u32[]{:S(2)}) collective-permute-start(f32[128,8]{1,0:T(8,128)S(1)} %bitcast.81), channel_id=1, source_target_pairs={{1,0},{2,1},{3,2},{4,3},{5,4},{6,5},{7,6},{9,8},{10,9},{11,10},{12... | collective-permute-start | bytes 12296 | tf_op jit(solution)/shard_map/ppermute | solution.py:113
  141.0 0.8 copy-start.5
  141.0 0.8 copy-start.6
  141.0 0.8 copy-start.13
  141.0 0.8 copy-start.14
  147.8 15.5 %collective-permute-start.8 = (f32[8,384]{1,0:T(8,128)}, f32[8,384]{1,0:T(8,128)S(1)}, u32[]{:S(2)}, u32[]{:S(2)}) collective-permute-start(f32[8,384]{1,0:T(8,128)} %get-tuple-element.14), channel_id=1, source_target_pairs={{0,8},{8,16},{16,24},{24,32},{32,40},{40,48},{48,56},{56,64},{64,7... | collective-permute-start | bytes 36872 | tf_op jit(solution)/shard_map/ppermute | solution.py:113
  150.3 13.1 %collective-permute-start.9 = (f32[8,384]{1,0:T(8,128)}, f32[8,384]{1,0:T(8,128)S(1)}, u32[]{:S(2)}, u32[]{:S(2)}) collective-permute-start(f32[8,384]{1,0:T(8,128)} %get-tuple-element.15), channel_id=1, source_target_pairs={{8,0},{16,8},{24,16},{32,24},{40,32},{48,40},{56,48},{64,56},{72,6... | collective-permute-start | bytes 36872 | tf_op jit(solution)/shard_map/ppermute | solution.py:113
  155.2 5.3 %collective-permute-start.10 = (f32[128,8]{1,0:T(8,128)}, f32[128,8]{1,0:T(8,128)S(1)}, u32[]{:S(2)}, u32[]{:S(2)}) collective-permute-start(f32[128,8]{1,0:T(8,128)} %get-tuple-element.16), channel_id=1, source_target_pairs={{0,1},{1,2},{2,3},{3,4},{4,5},{5,6},{6,7},{8,9},{9,10},{10,11},{11... | collective-permute-start | bytes 12296 | tf_op jit(solution)/shard_map/ppermute | solution.py:113
  157.6 5.8 %collective-permute-start.11 = (f32[128,8]{1,0:T(8,128)}, f32[128,8]{1,0:T(8,128)S(1)}, u32[]{:S(2)}, u32[]{:S(2)}) collective-permute-start(f32[128,8]{1,0:T(8,128)} %get-tuple-element.17), channel_id=1, source_target_pairs={{1,0},{2,1},{3,2},{4,3},{5,4},{6,5},{7,6},{9,8},{10,9},{11,10},{12... | collective-permute-start | bytes 12296 | tf_op jit(solution)/shard_map/ppermute | solution.py:113
  160.5 2.9 %copy-start.8 = (f32[128,8]{1,0:T(8,128)}, f32[128,8]{1,0:T(8,128)S(1)}, u32[]{:S(2)}) copy-start(f32[128,8]{1,0:T(8,128)S(1)} %collective-permute-done.10.by_ref) | copy-start | bytes 12292
  163.4 0.6 copy-start.10
  163.4 0.6 copy-start.16
  163.4 0.6 copy-start.18
  170.0 15.7 %collective-permute-start.12 = (f32[8,384]{1,0:T(8,128)}, f32[8,384]{1,0:T(8,128)S(1)}, u32[]{:S(2)}, u32[]{:S(2)}) collective-permute-start(f32[8,384]{1,0:T(8,128)} %get-tuple-element.19), channel_id=1, source_target_pairs={{0,8},{8,16},{16,24},{24,32},{32,40},{40,48},{48,56},{56,64},{64,7... | collective-permute-start | bytes 36872 | tf_op jit(solution)/shard_map/ppermute | solution.py:113
  171.9 13.8 %collective-permute-start.13 = (f32[8,384]{1,0:T(8,128)}, f32[8,384]{1,0:T(8,128)S(1)}, u32[]{:S(2)}, u32[]{:S(2)}) collective-permute-start(f32[8,384]{1,0:T(8,128)} %get-tuple-element.20), channel_id=1, source_target_pairs={{8,0},{16,8},{24,16},{32,24},{40,32},{48,40},{56,48},{64,56},{72,6... | collective-permute-start | bytes 36872 | tf_op jit(solution)/shard_map/ppermute | solution.py:113
  177.4 4.5 %collective-permute-start.14 = (f32[128,8]{1,0:T(8,128)}, f32[128,8]{1,0:T(8,128)S(1)}, u32[]{:S(2)}, u32[]{:S(2)}) collective-permute-start(f32[128,8]{1,0:T(8,128)} %get-tuple-element.21), channel_id=1, source_target_pairs={{0,1},{1,2},{2,3},{3,4},{4,5},{5,6},{6,7},{8,9},{9,10},{10,11},{11... | collective-permute-start | bytes 12296 | tf_op jit(solution)/shard_map/ppermute | solution.py:113
  179.9 5.8 %collective-permute-start.15 = (f32[128,8]{1,0:T(8,128)}, f32[128,8]{1,0:T(8,128)S(1)}, u32[]{:S(2)}, u32[]{:S(2)}) collective-permute-start(f32[128,8]{1,0:T(8,128)} %get-tuple-element.22), channel_id=1, source_target_pairs={{1,0},{2,1},{3,2},{4,3},{5,4},{6,5},{7,6},{9,8},{10,9},{11,10},{12... | collective-permute-start | bytes 12296 | tf_op jit(solution)/shard_map/ppermute | solution.py:113
  181.9 3.9 %copy-start.7 = (f32[128,8]{1,0:T(8,128)}, f32[128,8]{1,0:T(8,128)S(1)}, u32[]{:S(2)}) copy-start(f32[128,8]{1,0:T(8,128)S(1)} %collective-permute-done.14.by_ref) | copy-start | bytes 12292
  185.7 0.6 copy-start.9
  185.7 0.6 copy-start.15
  185.7 0.6 copy-start.17

commit v12 on v11

--- a/solution.py
+++ b/solution.py
@@ -31,20 +31,14 @@
     return before_x, after_x, before_y, after_y
 
 
-def halo_tendency(block, wind_x, wind_y):
-    before_x, after_x, before_y, after_y = edge_halos(block)
+def halo_tendency(block, wind_x, wind_y, halos):
+    before_x, after_x, before_y, after_y = halos
     north = jnp.concatenate([block[:, 1:, :], after_x[:, None, :]], axis=1)
     south = jnp.concatenate([before_x[:, None, :], block[:, :-1, :]], axis=1)
     east = jnp.concatenate([block[:, :, 1:], after_y[:, :, None]], axis=2)
     west = jnp.concatenate([before_y[:, :, None], block[:, :, :-1]], axis=2)
     laplace = north + south + east + west - 4.0 * block
     return KAPPA * laplace - wind_x * (0.5 * (north - south)) - wind_y * (0.5 * (east - west))
-
-
-def from_behind(value, axis, steps):
-    count = lax.axis_size(axis)
-    pairs = [(source, (source + steps) % count) for source in range(count)]
-    return lax.ppermute(value, axis, pairs)
 
 
 def storm_rows(child, storm_shift, nx, ny):
@@ -141,12 +135,11 @@
     my_index = lax.axis_index(("gx", "gy"))
     wind_x = wind[0][:, None, None]
     wind_y = wind[1][:, None, None]
+    parent_halos = edge_halos(parent_field)
     new_parent = parent_field + (1.0 + parent_sppt.astype(jnp.float32)) * (
-        halo_tendency(parent_field, wind_x, wind_y) + VERTICAL * vertical(parent_field)
+        halo_tendency(parent_field, wind_x, wind_y, parent_halos) + VERTICAL * vertical(parent_field)
     )
     levels, crows, widths = child_storm.shape
-    npiece = storm_shift.shape[1]
-    band_rows = crows // npiece
     nx, ny = lax.axis_size("gx"), lax.axis_size("gy")
     child = storm_rows(child_storm, storm_shift, nx, ny)
     dest_table = strip_dest.reshape(devices, -1)
@@ -221,6 +214,7 @@
         P(),
         P(),
     )
+
     return jax.shard_map(
         shards,
         mesh=mesh,

time: 194 us -> 194 us (level)
  no operation moved by 1% of the time
where the time goes in v12:
time: 194 us; the launch traced here: 192 us
  starting transfers between devices  77.1 us (40%)
  local copies, waits for them, and re-layouts  46.4 us (24%)
  waiting for transfers between devices  23.4 us (12%)
  Pallas kernels  18 us (9%)
  other arithmetic  15.2 us (8%)
  matrix products  6.3 us (3%)
  between operations  5.94 us (3%)
    ppermute x12, starting transfers between devices, swap_edge(): return lax.ppermute(edge, axis, pairs)  38 us
    pallas_call x3, Pallas kernels, substep(): pl.pallas_call(functools.partial(substep_kernel, weight), out_shape=(jax....  18 us
    ppermute x4, starting transfers between devices, swap(): return lax.ppermute(edge, axis, pairs)  13.1 us
    all_to_all x1, starting transfers between devices, shards(): lax.all_to_all(outgoing_strips, ('gx', 'gy'), split_axis=0, concat_axis=0...  9.76 us
    all_to_all x1, waiting for transfers between devices, storm_rows(): gathered = lax.all_to_all(child, ('gx', 'gy'), 1, 1, tiled=True)  9.65 us
    all_to_all x1, starting transfers between devices, storm_rows(): gathered = lax.all_to_all(child, ('gx', 'gy'), 1, 1, tiled=True)  9.25 us
    another operation x4, local copies, waits for them, and re-layouts, shards(): jnp.stack([parent_field, new_parent]).reshape(2, levels, -1, STRIP)  8.37 us
    unnamed x55, local copies, waits for them, and re-layouts  7.11 us
  transfers between devices with their start and end apart: 19, of which 4 were waited for; matrix products, arithmetic and copies ran while one was open for 31% of the time, Pallas kernels for 0%

profile of v12, /device:TPU:33, one launch (start us, length us, event | category | flops | bytes accessed | tf_op | source)
XLA Modules:
  0.0 192.3 jit_solution(17181139007848170310)
XLA Ops:
  0.6 1.6 fusion.34
  2.4 3.8 %collective-permute-start.3 = (f32[8,128]{1,0:T(8,128)S(1)}, f32[8,128]{1,0:T(8,128)S(1)}, u32[]{:S(2)}, u32[]{:S(2)}) collective-permute-start(f32[8,128]{1,0:T(8,128)S(1)} %bitcast.87), channel_id=1, source_target_pairs={{0,1},{1,2},{2,3},{3,4},{4,5},{5,6},{6,7},{8,9},{9,10},{10,11},{11... | collective-permute-start | bytes 12296 | tf_op jit(solution)/shard_map/ppermute | solution.py:25
  6.3 1.9 collective-permute-start.2
  8.3 3.1 %collective-permute-start.1 = (f32[8,512]{1,0:T(8,128)S(1)}, f32[8,512]{1,0:T(8,128)S(1)}, u32[]{:S(2)}, u32[]{:S(2)}) collective-permute-start(f32[8,512]{1,0:T(8,128)S(1)} %bitcast.83), channel_id=1, source_target_pairs={{0,8},{8,16},{16,24},{24,32},{32,40},{40,48},{48,56},{56,64},{64,7... | collective-permute-start | bytes 49160 | tf_op jit(solution)/shard_map/ppermute | solution.py:25
  11.5 4.3 %collective-permute-start = (f32[8,512]{1,0:T(8,128)S(1)}, f32[8,512]{1,0:T(8,128)S(1)}, u32[]{:S(2)}, u32[]{:S(2)}) collective-permute-start(f32[8,512]{1,0:T(8,128)S(1)} %bitcast.85), channel_id=1, source_target_pairs={{8,0},{16,8},{24,16},{32,24},{40,32},{48,40},{56,48},{64,56},{72,6... | collective-permute-start | bytes 49160 | tf_op jit(solution)/shard_map/ppermute | solution.py:25
  15.7 3.5 %copy.119 = f32[8,128,384]{2,0,1:T(8,128)} copy(f32[8,128,384]{2,1,0:T(8,128)} %param.11) | data formatting | bytes 3145728 | tf_op args[2]
  19.2 9.2 %all-to-all-start = ((f32[8,128,384]{2,0,1:T(8,128)}), f32[8,128,384]{2,0,1:T(8,128)}, u32[]{:S(2)}, u32[]{:S(2)}) async-start(f32[8,128,384]{2,0,1:T(8,128)} %copy.119), calls=%async_computation | async-start | bytes 3145728 | tf_op jit(solution)/shard_map/all_to_all | solution.py:47
  28.5 0.7 constant_dynamic-slice_fusion.2
  33.2 0.7 fusion.25
  34.1 0.5 fusion.26
  34.6 0.6 multiply_add_fusion
  35.2 0.6 multiply_bitcast_fusion.1
  35.8 0.8 fusion.35
  36.6 2.8 %fusion.33 = (f32[8,128,511]{2,1,0:T(8,128)}, f32[8,128,511]{2,1,0:T(8,128)}) fusion(f32[8,128,512]{2,1,0:T(8,128)S(1)} %copy-done), kind=kLoop, calls=%fused_computation.78 | loop fusion | bytes 8372224 | tf_op jit(solution)/shard_map/slice | solution.py:38
  39.4 2.5 %fusion.31 = (f32[8,127,512]{2,1,0:T(8,128)}, f32[8,127,512]{2,1,0:T(8,128)}) fusion(f32[8,128,512]{2,1,0:T(8,128)S(1)} %copy-done), kind=kLoop, calls=%fused_computation.76 | loop fusion | bytes 8323072 | tf_op jit(solution)/shard_map/slice | solution.py:36
  41.9 9.7 %all-to-all-done = f32[8,128,384]{2,0,1:T(8,128)} async-done(((f32[8,128,384]{2,0,1:T(8,128)}), f32[8,128,384]{2,0,1:T(8,128)}, u32[]{:S(2)}, u32[]{:S(2)}) %all-to-all-start) | async-done | bytes 1572896 | tf_op jit(solution)/shard_map/all_to_all | solution.py:47
  51.6 1.7 copy.120
  53.6 0.4 fusion.5
  54.0 2.1 %copy.122 = f32[8,16,8,384]{3,0,2,1:T(8,128)} copy(f32[8,16,8,384]{3,2,1,0:T(8,128)S(1)} %fusion.5) | data formatting | bytes 3145728 | tf_op jit(solution)/shard_map/jit(_roll_dynamic)/dynamic_slice | solution.py:51
  56.1 7.0 %all-to-all-start.1 = ((f32[8,128,384]{2,0,1:T(8,128)}), f32[8,128,384]{2,0,1:T(8,128)}, u32[]{:S(2)}, u32[]{:S(2)}) async-start(f32[8,128,384]{2,0,1:T(8,128)} %bitcast.76), calls=%async_computation.1 | async-start | bytes 3145728 | tf_op jit(solution)/shard_map/all_to_all | solution.py:52
  63.1 2.5 %fusion.36 = (f32[7,128,512]{2,1,0:T(8,128)}, f32[7,128,512]{2,1,0:T(8,128)}) fusion(f32[8,128,512]{2,1,0:T(8,128)S(1)} %copy-done), kind=kLoop, calls=%fused_computation.81 | loop fusion | bytes 7340032 | tf_op jit(solution)/shard_map/slice | solution.py:119
  65.5 1.2 compare_and_fusion
  66.8 1.4 stack.9
  68.2 4.1 %copy.127 = f32[1,8,512,128]{3,1,2,0:T(8,128)} copy(f32[1,8,512,128]{3,2,1,0:T(8,128)} %stack.9) | data formatting | bytes 4194304 | tf_op jit(solution)/shard_map/stack | solution.py:156
  72.8 7.0 %fusion.4 = f32[8,128,512]{2,1,0:T(8,128)} fusion(f32[8,128,512]{2,1,0:T(8,128)S(1)} %copy-done, f32[1,128,512]{2,1,0:T(8,128)} %get-tuple-element.35, f32[7,128,512]{2,1,0:T(8,128)} %get-tuple-element.37, f32[7,128,512]{2,1,0:T(8,128)} %get-tuple-element.36, f32[1,128,512]{2,1,0:T(8,128)} %get-tuple-element.34, f32[8,128,511]{2,1,0:T(8,128)} %get-tuple-element.31, ...), kind=kLoop, calls=%fused_computation.16 | loop fusion | flops 13107200 | bytes 17039424 | tf_op jit(solution)/shard_map/add | solution.py:139
  79.9 1.6 stack.10
  81.5 1.2 copy.128
  82.8 0.4 copy-done.1
  83.1 2.2 %pad_maximum_fusion = f32[2,8,512,128]{3,1,2,0:T(8,128)} fusion(f32[1,8,512,128]{3,1,2,0:T(8,128)S(1)} %copy.128, f32[1,8,512,128]{3,1,2,0:T(8,128)S(1)} %copy-done.1), kind=kLoop, calls=%fused_computation.1 | loop fusion | flops 1048576 | bytes 8388608 | tf_op jit(solution)/shard_map/stack | solution.py:156
  85.4 2.9 %gather_fusion = f32[128,2,8,128]{3,2,1,0:T(8,128)S(1)} fusion(f32[2,8,512,128]{3,1,2,0:T(8,128)} %pad_maximum_fusion, s32[1024]{0:T(1024)S(1)} %pad_clamp_fusion), kind=kCustom, calls=%fused_computation | custom fusion | bytes 2097664 | tf_op jit(solution)/shard_map/jit(_take)/gather | solution.py:157
  88.7 1.2 slice.82
  90.5 0.8 convolution_add_fusion
  91.3 3.0 %copy.129 = f32[128,2,2048]{2,1,0:T(2,128)} copy(f32[128,2,2048]{2,0,1:T(8,128)S(1)} %convolution_add_fusion) | data formatting | bytes 4194304 | tf_op jit(solution)/shard_map/add | solution.py:165
  94.3 9.8 %all-to-all-start.2 = ((f32[128,2,2048]{2,1,0:T(2,128)}), f32[128,2,2048]{2,1,0:T(2,128)S(1)}, u32[]{:S(2)}, u32[]{:S(2)}) async-start(f32[128,2,2048]{2,1,0:T(2,128)} %copy.129), calls=%async_computation.2 | async-start | bytes 4194304 | tf_op jit(solution)/shard_map/all_to_all | solution.py:166
  105.1 0.7 convert_add_fusion.1.factor_ref
  105.8 0.7 slice_bitcast_fusion
  106.5 3.1 %collective-permute-start.4 = (f32[8,384]{1,0:T(8,128)S(1)}, f32[8,384]{1,0:T(8,128)S(1)}, u32[]{:S(2)}, u32[]{:S(2)}) collective-permute-start(f32[8,384]{1,0:T(8,128)S(1)} %get-tuple-element.41), channel_id=1, source_target_pairs={{0,8},{8,16},{16,24},{24,32},{32,40},{40,48},{48,56},{56,64},{64,7... | collective-permute-start | bytes 36872 | tf_op jit(solution)/shard_map/ppermute | solution.py:107
  109.6 4.3 %collective-permute-start.5 = (f32[8,384]{1,0:T(8,128)S(1)}, f32[8,384]{1,0:T(8,128)S(1)}, u32[]{:S(2)}, u32[]{:S(2)}) collective-permute-start(f32[8,384]{1,0:T(8,128)S(1)} %get-tuple-element.40), channel_id=1, source_target_pairs={{8,0},{16,8},{24,16},{32,24},{40,32},{48,40},{56,48},{64,56},{72,6... | collective-permute-start | bytes 36872 | tf_op jit(solution)/shard_map/ppermute | solution.py:107
  113.9 1.4 fusion.37
  115.3 0.8 copy.145
  116.1 4.0 %collective-permute-start.6 = (f32[128,8]{1,0:T(8,128)S(1)}, f32[128,8]{1,0:T(8,128)S(1)}, u32[]{:S(2)}, u32[]{:S(2)}) collective-permute-start(f32[128,8]{1,0:T(8,128)S(1)} %bitcast.80), channel_id=1, source_target_pairs={{0,1},{1,2},{2,3},{3,4},{4,5},{5,6},{6,7},{8,9},{9,10},{10,11},{11... | collective-permute-start | bytes 12296 | tf_op jit(solution)/shard_map/ppermute | solution.py:107
  120.1 0.8 copy.146
  120.9 2.1 %collective-permute-start.7 = (f32[128,8]{1,0:T(8,128)S(1)}, f32[128,8]{1,0:T(8,128)S(1)}, u32[]{:S(2)}, u32[]{:S(2)}) collective-permute-start(f32[128,8]{1,0:T(8,128)S(1)} %bitcast.81), channel_id=1, source_target_pairs={{1,0},{2,1},{3,2},{4,3},{5,4},{6,5},{7,6},{9,8},{10,9},{11,10},{12... | collective-permute-start | bytes 12296 | tf_op jit(solution)/shard_map/ppermute | solution.py:107
  123.1 2.9 %copy.135.child_ref = f32[8,128,384]{2,1,0:T(8,128)} copy(f32[8,128,384]{2,0,1:T(8,128)} %all-to-all-done.1) | data formatting | bytes 3145728 | tf_op jit(solution)/shard_map/all_to_all | solution.py:52
  125.9 7.1 %all-to-all-done.2 = f32[128,2,2048]{2,1,0:T(2,128)S(1)} async-done(((f32[128,2,2048]{2,1,0:T(2,128)}), f32[128,2,2048]{2,1,0:T(2,128)S(1)}, u32[]{:S(2)}, u32[]{:S(2)}) %all-to-all-start.2) | async-done | bytes 2097184 | tf_op jit(solution)/shard_map/all_to_all | solution.py:166
  133.0 2.4 %copy.130 = f32[128,2,2048]{0,2,1:T(8,128)} copy(f32[128,2,2048]{2,1,0:T(2,128)S(1)} %all-to-all-done.2) | data formatting | bytes 4194304 | tf_op jit(solution)/shard_map/all_to_all | solution.py:166
  135.4 2.4 %convolution_bitcast_fusion.1 = f32[128,2,8,128]{3,0,2,1:T(8,128)S(1)} fusion(f32[2,8,128,128,2]{3,2,1,0,4:T(8,128)} %bitcast.75, s32[128,2]{0,1:T(2,128)S(1)} %broadcast_select_fusion.1), kind=kOutput, calls=%fused_computation.20 | convolution fusion | flops 402685952 | bytes 3146752 | tf_op jit(solution)/shard_map/tqs,qsk->tk/dot_general | solution.py:176
  137.9 3.1 %convolution_bitcast_fusion.bound_ref = f32[2,8,128,384]{3,2,1,0:T(8,128)} fusion(f32[128,2,8,128]{3,0,2,1:T(8,128)S(1)} %convolution_bitcast_fusion.1, f32[128]{0:T(128)S(1)} %iota_convert_fusion, f32[384]{0:T(512)S(1)} %add_clamp_fusion), kind=kOutput, calls=%fused_computation.17 | convolution fusion | flops 604176384 | bytes 4196352 | tf_op jit(solution)/shard_map/tald,de->alte/dot_general | solution.py:183
  141.0 0.8 broadcast_in_dim.69.divisor_ref
  141.8 6.0 %shard_map.104 = (f32[8,128,384]{2,1,0:T(8,128)}, f32[8,384]{1,0:T(8,128)}, f32[8,384]{1,0:T(8,128)}, f32[128,8]{1,0:T(8,128)}, f32[128,8]{1,0:T(8,128)}) custom-call(f32[2,8]{1,0:T(2,128)} %wind_ref.5, f32[8,128,384]{2,1,0:T(8,128)} %copy.135.child_ref, f32[8,384]{1,0:T(8,128)} %copy-done.13, f32[8,384]{1,0:T(8,128)} %copy-done.14, f32[128,8]{1,0:T(8,128)} %copy-done.5, ...), custom_call_target="tpu_custom_call" | custom-call | flops 11796480 | bytes 6684672 | tf_op jit(solution)/shard_map/pallas_call | solution.py:85
  147.8 2.5 %collective-permute-start.8 = (f32[8,384]{1,0:T(8,128)}, f32[8,384]{1,0:T(8,128)S(1)}, u32[]{:S(2)}, u32[]{:S(2)}) collective-permute-start(f32[8,384]{1,0:T(8,128)} %get-tuple-element.14), channel_id=1, source_target_pairs={{0,8},{8,16},{16,24},{24,32},{32,40},{40,48},{48,56},{56,64},{64,7... | collective-permute-start | bytes 36872 | tf_op jit(solution)/shard_map/ppermute | solution.py:107
  150.3 4.9 %collective-permute-start.9 = (f32[8,384]{1,0:T(8,128)}, f32[8,384]{1,0:T(8,128)S(1)}, u32[]{:S(2)}, u32[]{:S(2)}) collective-permute-start(f32[8,384]{1,0:T(8,128)} %get-tuple-element.15), channel_id=1, source_target_pairs={{8,0},{16,8},{24,16},{32,24},{40,32},{48,40},{56,48},{64,56},{72,6... | collective-permute-start | bytes 36872 | tf_op jit(solution)/shard_map/ppermute | solution.py:107
  155.2 2.3 %collective-permute-start.10 = (f32[128,8]{1,0:T(8,128)}, f32[128,8]{1,0:T(8,128)S(1)}, u32[]{:S(2)}, u32[]{:S(2)}) collective-permute-start(f32[128,8]{1,0:T(8,128)} %get-tuple-element.16), channel_id=1, source_target_pairs={{0,1},{1,2},{2,3},{3,4},{4,5},{5,6},{6,7},{8,9},{9,10},{10,11},{11... | collective-permute-start | bytes 12296 | tf_op jit(solution)/shard_map/ppermute | solution.py:107
  157.6 2.9 %collective-permute-start.11 = (f32[128,8]{1,0:T(8,128)}, f32[128,8]{1,0:T(8,128)S(1)}, u32[]{:S(2)}, u32[]{:S(2)}) collective-permute-start(f32[128,8]{1,0:T(8,128)} %get-tuple-element.17), channel_id=1, source_target_pairs={{1,0},{2,1},{3,2},{4,3},{5,4},{6,5},{7,6},{9,8},{10,9},{11,10},{12... | collective-permute-start | bytes 12296 | tf_op jit(solution)/shard_map/ppermute | solution.py:107
  160.5 2.8 %collective-permute-done.11.ay_ref = f32[128,8]{1,0:T(8,128)S(1)} collective-permute-done((f32[128,8]{1,0:T(8,128)}, f32[128,8]{1,0:T(8,128)S(1)}, u32[]{:S(2)}, u32[]{:S(2)}) %collective-permute-start.11) | collective-permute-done | bytes 4128 | tf_op jit(solution)/shard_map/ppermute | solution.py:107
  163.4 0.6 copy-done.10
  164.0 6.0 %shard_map.105 = (f32[8,128,384]{2,1,0:T(8,128)}, f32[8,384]{1,0:T(8,128)}, f32[8,384]{1,0:T(8,128)}, f32[128,8]{1,0:T(8,128)}, f32[128,8]{1,0:T(8,128)}) custom-call(f32[2,8]{1,0:T(2,128)} %wind_ref.5, f32[8,128,384]{2,1,0:T(8,128)} %get-tuple-element.13.child_ref, f32[8,384]{1,0:T(8,128)} %copy-done.16, f32[8,384]{1,0:T(8,128)} %copy-done.18, ...), custom_call_target="tpu_custom_call" | custom-call | flops 11796480 | bytes 6684672 | tf_op jit(solution)/shard_map/pallas_call | solution.py:85
  170.0 1.9 collective-permute-start.12
  171.9 5.5 %collective-permute-start.13 = (f32[8,384]{1,0:T(8,128)}, f32[8,384]{1,0:T(8,128)S(1)}, u32[]{:S(2)}, u32[]{:S(2)}) collective-permute-start(f32[8,384]{1,0:T(8,128)} %get-tuple-element.20), channel_id=1, source_target_pairs={{8,0},{16,8},{24,16},{32,24},{40,32},{48,40},{56,48},{64,56},{72,6... | collective-permute-start | bytes 36872 | tf_op jit(solution)/shard_map/ppermute | solution.py:107
  177.4 2.5 %collective-permute-start.14 = (f32[128,8]{1,0:T(8,128)}, f32[128,8]{1,0:T(8,128)S(1)}, u32[]{:S(2)}, u32[]{:S(2)}) collective-permute-start(f32[128,8]{1,0:T(8,128)} %get-tuple-element.21), channel_id=1, source_target_pairs={{0,1},{1,2},{2,3},{3,4},{4,5},{5,6},{6,7},{8,9},{9,10},{10,11},{11... | collective-permute-start | bytes 12296 | tf_op jit(solution)/shard_map/ppermute | solution.py:107
  179.9 1.9 collective-permute-start.15
  181.9 3.8 %collective-permute-done.15.ay_ref = f32[128,8]{1,0:T(8,128)S(1)} collective-permute-done((f32[128,8]{1,0:T(8,128)}, f32[128,8]{1,0:T(8,128)S(1)}, u32[]{:S(2)}, u32[]{:S(2)}) %collective-permute-start.15) | collective-permute-done | bytes 4128 | tf_op jit(solution)/shard_map/ppermute | solution.py:107
  185.8 0.6 copy-done.9
  186.4 6.0 %shard_map.106 = (f32[8,128,384]{2,1,0:T(8,128)}, f32[8,384]{1,0:T(8,128)}, f32[8,384]{1,0:T(8,128)}, f32[128,8]{1,0:T(8,128)}, f32[128,8]{1,0:T(8,128)}) custom-call(f32[2,8]{1,0:T(2,128)} %wind_ref.5, f32[8,128,384]{2,1,0:T(8,128)} %get-tuple-element.18.child_ref, f32[8,384]{1,0:T(8,128)} %copy-done.15, f32[8,384]{1,0:T(8,128)} %copy-done.17, ...), custom_call_target="tpu_custom_call" | custom-call | flops 11796480 | bytes 6684672 | tf_op jit(solution)/shard_map/pallas_call | solution.py:85
  (90 shorter events, 2.9 us)
Async XLA Ops:
  0.6 7.6 %copy-start = (f32[8,128,512]{2,1,0:T(8,128)S(1)}, f32[8,128,512]{2,1,0:T(8,128)}, u32[]{:S(2)}) copy-start(f32[8,128,512]{2,1,0:T(8,128)} %param.9) | copy-start | bytes 6291460
  2.4 69.9 %collective-permute-start.3 = (f32[8,128]{1,0:T(8,128)S(1)}, f32[8,128]{1,0:T(8,128)S(1)}, u32[]{:S(2)}, u32[]{:S(2)}) collective-permute-start(f32[8,128]{1,0:T(8,128)S(1)} %bitcast.87), channel_id=1, source_target_pairs={{0,1},{1,2},{2,3},{3,4},{4,5},{5,6},{6,7},{8,9},{9,10},{10,11},{11... | collective-permute-start | bytes 12296 | tf_op jit(solution)/shard_map/ppermute | solution.py:25
  6.3 66.2 %collective-permute-start.2 = (f32[8,128]{1,0:T(8,128)S(1)}, f32[8,128]{1,0:T(8,128)S(1)}, u32[]{:S(2)}, u32[]{:S(2)}) collective-permute-start(f32[8,128]{1,0:T(8,128)S(1)} %bitcast.89), channel_id=1, source_target_pairs={{1,0},{2,1},{3,2},{4,3},{5,4},{6,5},{7,6},{9,8},{10,9},{11,10},{12... | collective-permute-start | bytes 12296 | tf_op jit(solution)/shard_map/ppermute | solution.py:25
  8.3 64.4 %collective-permute-start.1 = (f32[8,512]{1,0:T(8,128)S(1)}, f32[8,512]{1,0:T(8,128)S(1)}, u32[]{:S(2)}, u32[]{:S(2)}) collective-permute-start(f32[8,512]{1,0:T(8,128)S(1)} %bitcast.83), channel_id=1, source_target_pairs={{0,8},{8,16},{16,24},{24,32},{32,40},{40,48},{48,56},{56,64},{64,7... | collective-permute-start | bytes 49160 | tf_op jit(solution)/shard_map/ppermute | solution.py:25
  11.5 61.3 %collective-permute-start = (f32[8,512]{1,0:T(8,128)S(1)}, f32[8,512]{1,0:T(8,128)S(1)}, u32[]{:S(2)}, u32[]{:S(2)}) collective-permute-start(f32[8,512]{1,0:T(8,128)S(1)} %bitcast.85), channel_id=1, source_target_pairs={{8,0},{16,8},{24,16},{32,24},{40,32},{48,40},{56,48},{64,56},{72,6... | collective-permute-start | bytes 49160 | tf_op jit(solution)/shard_map/ppermute | solution.py:25
  19.2 9.3 %copy-start.22 = (s32[2,4]{1,0:T(2,128)S(1)}, s32[2,4]{1,0:T(2,128)}, u32[]{:S(2)}) copy-start(s32[2,4]{1,0:T(2,128)} %param.17) | copy-start | bytes 100
  19.2 14.7 %copy-start.4 = (s32[16384,1]{0,1:T(1,128)S(1)}, s32[16384,1]{0,1:T(1,128)}, u32[]{:S(2)}) copy-start(s32[16384,1]{0,1:T(1,128)} %param.14) | copy-start | bytes 196612
  19.2 15.9 %copy-start.12 = (f32[2,8]{1,0:T(2,128)S(1)}, f32[2,8]{1,0:T(2,128)}, u32[]{:S(2)}) copy-start(f32[2,8]{1,0:T(2,128)} %wind_ref.5) | copy-start | bytes 196
  19.2 16.5 %copy-start.2 = (bf16[128,512]{1,0:T(8,128)(2,1)S(1)}, bf16[128,512]{1,0:T(8,128)(2,1)}, u32[]{:S(2)}) copy-start(bf16[128,512]{1,0:T(8,128)(2,1)} %param.10) | copy-start | bytes 393220
  19.2 32.3 %all-to-all-start = ((f32[8,128,384]{2,0,1:T(8,128)}), f32[8,128,384]{2,0,1:T(8,128)}, u32[]{:S(2)}, u32[]{:S(2)}) async-start(f32[8,128,384]{2,0,1:T(8,128)} %copy.119), calls=%async_computation | async-start | bytes 3145728 | tf_op jit(solution)/shard_map/all_to_all | solution.py:47
  56.1 32.6 %all-to-all-start.1 = ((f32[8,128,384]{2,0,1:T(8,128)}), f32[8,128,384]{2,0,1:T(8,128)}, u32[]{:S(2)}, u32[]{:S(2)}) async-start(f32[8,128,384]{2,0,1:T(8,128)} %bitcast.76), calls=%async_computation.1 | async-start | bytes 3145728 | tf_op jit(solution)/shard_map/all_to_all | solution.py:52
  68.1 4.7 %copy-start.19 = (f32[8]{0:T(128)S(1)}, f32[8]{0:T(128)}, u32[]{:S(2)}) copy-start(f32[8]{0:T(128)} %get-tuple-element.44) | copy-start | bytes 100
  81.5 1.6 copy-start.1
  85.4 2.9 %copy-start.23 = (pred[128]{0:T(512)(128)(4,1)S(1)}, pred[128]{0:T(512)(128)(4,1)}, u32[]{:S(2)}) copy-start(pred[128]{0:T(512)(128)(4,1)} %compare_and_fusion) | copy-start | bytes 388
  88.2 2.2 %copy-start.20 = (s32[128]{0:T(128)S(1)}, s32[128]{0:T(128)}, u32[]{:S(2)}) copy-start(s32[128]{0:T(128)} %fusion.26) | copy-start | bytes 1540
  88.3 2.2 %copy-start.21 = (s32[128,2]{0,1:T(2,128)S(1)}, s32[128,2]{0,1:T(2,128)}, u32[]{:S(2)}) copy-start(s32[128,2]{0,1:T(2,128)} %multiply_add_fusion) | copy-start | bytes 3076
  94.2 10.3 %copy-start.11 = (s32[16384]{0:T(1024)S(1)}, s32[16384]{0:T(1024)}, u32[]{:S(2)}) copy-start(s32[16384]{0:T(1024)} %param.16) | copy-start | bytes 196612
  94.3 10.8 %copy-start.3 = (bf16[128,384]{1,0:T(8,128)(2,1)S(1)}, bf16[128,384]{1,0:T(8,128)(2,1)}, u32[]{:S(2)}) copy-start(bf16[128,384]{1,0:T(8,128)(2,1)} %param.12) | copy-start | bytes 294916
  94.3 38.7 %all-to-all-start.2 = ((f32[128,2,2048]{2,1,0:T(2,128)}), f32[128,2,2048]{2,1,0:T(2,128)S(1)}, u32[]{:S(2)}, u32[]{:S(2)}) async-start(f32[128,2,2048]{2,1,0:T(2,128)} %copy.129), calls=%async_computation.2 | async-start | bytes 4194304 | tf_op jit(solution)/shard_map/all_to_all | solution.py:166
  106.5 34.5 %collective-permute-start.4 = (f32[8,384]{1,0:T(8,128)S(1)}, f32[8,384]{1,0:T(8,128)S(1)}, u32[]{:S(2)}, u32[]{:S(2)}) collective-permute-start(f32[8,384]{1,0:T(8,128)S(1)} %get-tuple-element.41), channel_id=1, source_target_pairs={{0,8},{8,16},{16,24},{24,32},{32,40},{40,48},{48,56},{56,64},{64,7... | collective-permute-start | bytes 36872 | tf_op jit(solution)/shard_map/ppermute | solution.py:107
  109.6 31.4 %collective-permute-start.5 = (f32[8,384]{1,0:T(8,128)S(1)}, f32[8,384]{1,0:T(8,128)S(1)}, u32[]{:S(2)}, u32[]{:S(2)}) collective-permute-start(f32[8,384]{1,0:T(8,128)S(1)} %get-tuple-element.40), channel_id=1, source_target_pairs={{8,0},{16,8},{24,16},{32,24},{40,32},{48,40},{56,48},{64,56},{72,6... | collective-permute-start | bytes 36872 | tf_op jit(solution)/shard_map/ppermute | solution.py:107
  116.1 24.9 %collective-permute-start.6 = (f32[128,8]{1,0:T(8,128)S(1)}, f32[128,8]{1,0:T(8,128)S(1)}, u32[]{:S(2)}, u32[]{:S(2)}) collective-permute-start(f32[128,8]{1,0:T(8,128)S(1)} %bitcast.80), channel_id=1, source_target_pairs={{0,1},{1,2},{2,3},{3,4},{4,5},{5,6},{6,7},{8,9},{9,10},{10,11},{11... | collective-permute-start | bytes 12296 | tf_op jit(solution)/shard_map/ppermute | solution.py:107
  120.9 20.0 %collective-permute-start.7 = (f32[128,8]{1,0:T(8,128)S(1)}, f32[128,8]{1,0:T(8,128)S(1)}, u32[]{:S(2)}, u32[]{:S(2)}) collective-permute-start(f32[128,8]{1,0:T(8,128)S(1)} %bitcast.81), channel_id=1, source_target_pairs={{1,0},{2,1},{3,2},{4,3},{5,4},{6,5},{7,6},{9,8},{10,9},{11,10},{12... | collective-permute-start | bytes 12296 | tf_op jit(solution)/shard_map/ppermute | solution.py:107
  141.0 0.8 copy-start.5
  141.0 0.8 copy-start.6
  141.0 0.8 copy-start.13
  141.0 0.8 copy-start.14
  147.8 15.5 %collective-permute-start.8 = (f32[8,384]{1,0:T(8,128)}, f32[8,384]{1,0:T(8,128)S(1)}, u32[]{:S(2)}, u32[]{:S(2)}) collective-permute-start(f32[8,384]{1,0:T(8,128)} %get-tuple-element.14), channel_id=1, source_target_pairs={{0,8},{8,16},{16,24},{24,32},{32,40},{40,48},{48,56},{56,64},{64,7... | collective-permute-start | bytes 36872 | tf_op jit(solution)/shard_map/ppermute | solution.py:107
  150.3 13.1 %collective-permute-start.9 = (f32[8,384]{1,0:T(8,128)}, f32[8,384]{1,0:T(8,128)S(1)}, u32[]{:S(2)}, u32[]{:S(2)}) collective-permute-start(f32[8,384]{1,0:T(8,128)} %get-tuple-element.15), channel_id=1, source_target_pairs={{8,0},{16,8},{24,16},{32,24},{40,32},{48,40},{56,48},{64,56},{72,6... | collective-permute-start | bytes 36872 | tf_op jit(solution)/shard_map/ppermute | solution.py:107
  155.2 5.3 %collective-permute-start.10 = (f32[128,8]{1,0:T(8,128)}, f32[128,8]{1,0:T(8,128)S(1)}, u32[]{:S(2)}, u32[]{:S(2)}) collective-permute-start(f32[128,8]{1,0:T(8,128)} %get-tuple-element.16), channel_id=1, source_target_pairs={{0,1},{1,2},{2,3},{3,4},{4,5},{5,6},{6,7},{8,9},{9,10},{10,11},{11... | collective-permute-start | bytes 12296 | tf_op jit(solution)/shard_map/ppermute | solution.py:107
  157.6 5.8 %collective-permute-start.11 = (f32[128,8]{1,0:T(8,128)}, f32[128,8]{1,0:T(8,128)S(1)}, u32[]{:S(2)}, u32[]{:S(2)}) collective-permute-start(f32[128,8]{1,0:T(8,128)} %get-tuple-element.17), channel_id=1, source_target_pairs={{1,0},{2,1},{3,2},{4,3},{5,4},{6,5},{7,6},{9,8},{10,9},{11,10},{12... | collective-permute-start | bytes 12296 | tf_op jit(solution)/shard_map/ppermute | solution.py:107
  160.5 2.9 %copy-start.8 = (f32[128,8]{1,0:T(8,128)}, f32[128,8]{1,0:T(8,128)S(1)}, u32[]{:S(2)}) copy-start(f32[128,8]{1,0:T(8,128)S(1)} %collective-permute-done.10.by_ref) | copy-start | bytes 12292
  163.4 0.6 copy-start.10
  163.4 0.6 copy-start.16
  163.4 0.6 copy-start.18
  170.0 15.7 %collective-permute-start.12 = (f32[8,384]{1,0:T(8,128)}, f32[8,384]{1,0:T(8,128)S(1)}, u32[]{:S(2)}, u32[]{:S(2)}) collective-permute-start(f32[8,384]{1,0:T(8,128)} %get-tuple-element.19), channel_id=1, source_target_pairs={{0,8},{8,16},{16,24},{24,32},{32,40},{40,48},{48,56},{56,64},{64,7... | collective-permute-start | bytes 36872 | tf_op jit(solution)/shard_map/ppermute | solution.py:107
  171.9 13.8 %collective-permute-start.13 = (f32[8,384]{1,0:T(8,128)}, f32[8,384]{1,0:T(8,128)S(1)}, u32[]{:S(2)}, u32[]{:S(2)}) collective-permute-start(f32[8,384]{1,0:T(8,128)} %get-tuple-element.20), channel_id=1, source_target_pairs={{8,0},{16,8},{24,16},{32,24},{40,32},{48,40},{56,48},{64,56},{72,6... | collective-permute-start | bytes 36872 | tf_op jit(solution)/shard_map/ppermute | solution.py:107
  177.4 4.5 %collective-permute-start.14 = (f32[128,8]{1,0:T(8,128)}, f32[128,8]{1,0:T(8,128)S(1)}, u32[]{:S(2)}, u32[]{:S(2)}) collective-permute-start(f32[128,8]{1,0:T(8,128)} %get-tuple-element.21), channel_id=1, source_target_pairs={{0,1},{1,2},{2,3},{3,4},{4,5},{5,6},{6,7},{8,9},{9,10},{10,11},{11... | collective-permute-start | bytes 12296 | tf_op jit(solution)/shard_map/ppermute | solution.py:107
  179.9 5.8 %collective-permute-start.15 = (f32[128,8]{1,0:T(8,128)}, f32[128,8]{1,0:T(8,128)S(1)}, u32[]{:S(2)}, u32[]{:S(2)}) collective-permute-start(f32[128,8]{1,0:T(8,128)} %get-tuple-element.22), channel_id=1, source_target_pairs={{1,0},{2,1},{3,2},{4,3},{5,4},{6,5},{7,6},{9,8},{10,9},{11,10},{12... | collective-permute-start | bytes 12296 | tf_op jit(solution)/shard_map/ppermute | solution.py:107
  181.9 3.9 %copy-start.7 = (f32[128,8]{1,0:T(8,128)}, f32[128,8]{1,0:T(8,128)S(1)}, u32[]{:S(2)}) copy-start(f32[128,8]{1,0:T(8,128)S(1)} %collective-permute-done.14.by_ref) | copy-start | bytes 12292
  185.7 0.6 copy-start.9
  185.7 0.6 copy-start.15
  185.7 0.6 copy-start.17

commit v13 on v12

--- a/solution.py
+++ b/solution.py
@@ -43,13 +43,18 @@
 
 def storm_rows(child, storm_shift, nx, ny):
     levels, crows, widths = child.shape
+    devices = nx * ny
+    per_level = devices // levels
+    piece_rows = crows // per_level
     mine = lax.axis_index(("gx", "gy"))
-    gathered = lax.all_to_all(child, ("gx", "gy"), 1, 1, tiled=True)
-    piece = mine // (crows // storm_shift.shape[1])
-    grid = gathered.reshape(levels, nx, ny, widths)
-    grid = jnp.roll(grid, storm_shift[0, piece], axis=1)
-    grid = jnp.roll(grid, storm_shift[1, piece], axis=2)
-    return lax.all_to_all(grid.reshape(levels, crows, widths), ("gx", "gy"), 1, 1, tiled=True)
+    pieces = child.reshape(devices, piece_rows, widths)
+    gathered = lax.all_to_all(pieces, ("gx", "gy"), 0, 0, tiled=True)
+    piece = (mine % per_level) * piece_rows // (crows // storm_shift.shape[1])
+    grid = gathered.reshape(nx, ny, piece_rows, widths)
+    grid = jnp.roll(grid, storm_shift[0, piece], axis=0)
+    grid = jnp.roll(grid, storm_shift[1, piece], axis=1)
+    back = lax.all_to_all(grid.reshape(devices, piece_rows, widths), ("gx", "gy"), 0, 0, tiled=True)
+    return back.reshape(levels, crows, widths)
 
 
 def substep_kernel(weight, wind_ref, child_ref, bx_ref, ax_ref, by_ref, ay_ref, bound_ref,

time: 194 us -> 189 us (0.974)
  local copies, waits for them, and re-layouts: 46.4 us -> 36.4 us
  waiting for transfers between devices: 23.4 us -> 26.1 us
  other arithmetic: 15.2 us -> 17.6 us
    unnamed x55 -> x56, local copies, waits for them, and re-layouts: 7.11 us -> 3.72 us
    all_to_all x1 -> x0, local copies, waits for them, and re-layouts: 2.86 us -> none  [storm_rows(): lax.all_to_all(grid.reshape(levels, crows, widths), ('gx', 'gy'), 1, 1, t...]
    all_to_all x1, waiting for transfers between devices: 7.05 us -> 9.56 us  [shards(): lax.all_to_all(outgoing_strips, ('gx', 'gy'), split_axis=0, concat_axis=0...]
    concatenate x2, other arithmetic: 0.73 us -> 3.1 us  [the longest x1 1.71 us: storm_rows(): grid = jnp.roll(grid, storm_shift[0, piece], axis=0)]
    dynamic_slice x2 -> x1, local copies, waits for them, and re-layouts: 2.71 us -> 0.59 us  [storm_rows(): grid = jnp.roll(grid, storm_shift[0, piece], axis=0)]
  transfers between devices with their start and end apart: 19 -> 19, of which waited for: 4 -> 4; matrix products, arithmetic and copies ran while one was open for 31% -> 27% of each run, Pallas kernels for 0% -> 0%
where the time goes in v13:
time: 189 us; the launch traced here: 187 us
  starting transfers between devices  77.2 us (41%)
  local copies, waits for them, and re-layouts  36.4 us (19%)
  waiting for transfers between devices  26.1 us (14%)
  Pallas kernels  17.9 us (9%)
  other arithmetic  17.6 us (9%)
  matrix products  6.3 us (3%)
  between operations  5.9 us (3%)
    ppermute x12, starting transfers between devices, swap_edge(): return lax.ppermute(edge, axis, pairs)  38 us
    pallas_call x3, Pallas kernels, substep(): pl.pallas_call(functools.partial(substep_kernel, weight), out_shape=(jax....  17.9 us
    ppermute x4, starting transfers between devices, swap(): return lax.ppermute(edge, axis, pairs)  13.2 us
    all_to_all x1, waiting for transfers between devices, storm_rows(): gathered = lax.all_to_all(pieces, ('gx', 'gy'), 0, 0, tiled=True)  9.83 us
    all_to_all x1, starting transfers between devices, shards(): lax.all_to_all(outgoing_strips, ('gx', 'gy'), split_axis=0, concat_axis=0...  9.76 us
    all_to_all x1, waiting for transfers between devices, shards(): lax.all_to_all(outgoing_strips, ('gx', 'gy'), split_axis=0, concat_axis=0...  9.56 us
    all_to_all x1, starting transfers between devices, storm_rows(): gathered = lax.all_to_all(pieces, ('gx', 'gy'), 0, 0, tiled=True)  9.25 us
    another operation x4, local copies, waits for them, and re-layouts, shards(): jnp.stack([parent_field, new_parent]).reshape(2, levels, -1, STRIP)  8.37 us
  transfers between devices with their start and end apart: 19, of which 4 were waited for; matrix products, arithmetic and copies ran while one was open for 27% of the time, Pallas kernels for 0%

profile of v13, /device:TPU:33, one launch (start us, length us, event | category | flops | bytes accessed | tf_op | source)
XLA Modules:
  0.0 187.4 jit_solution(4561752136686553747)
XLA Ops:
  0.6 1.6 fusion.34
  2.4 3.9 %collective-permute-start.3 = (f32[8,128]{1,0:T(8,128)S(1)}, f32[8,128]{1,0:T(8,128)S(1)}, u32[]{:S(2)}, u32[]{:S(2)}) collective-permute-start(f32[8,128]{1,0:T(8,128)S(1)} %bitcast.94), channel_id=1, source_target_pairs={{0,1},{1,2},{2,3},{3,4},{4,5},{5,6},{6,7},{8,9},{9,10},{10,11},{11... | collective-permute-start | bytes 12296 | tf_op jit(solution)/shard_map/ppermute | solution.py:25
  6.5 1.9 %collective-permute-start.2 = (f32[8,128]{1,0:T(8,128)S(1)}, f32[8,128]{1,0:T(8,128)S(1)}, u32[]{:S(2)}, u32[]{:S(2)}) collective-permute-start(f32[8,128]{1,0:T(8,128)S(1)} %bitcast.96), channel_id=1, source_target_pairs={{1,0},{2,1},{3,2},{4,3},{5,4},{6,5},{7,6},{9,8},{10,9},{11,10},{12... | collective-permute-start | bytes 12296 | tf_op jit(solution)/shard_map/ppermute | solution.py:25
  8.5 3.1 %collective-permute-start.1 = (f32[8,512]{1,0:T(8,128)S(1)}, f32[8,512]{1,0:T(8,128)S(1)}, u32[]{:S(2)}, u32[]{:S(2)}) collective-permute-start(f32[8,512]{1,0:T(8,128)S(1)} %bitcast.88), channel_id=1, source_target_pairs={{0,8},{8,16},{16,24},{24,32},{32,40},{40,48},{48,56},{56,64},{64,7... | collective-permute-start | bytes 49160 | tf_op jit(solution)/shard_map/ppermute | solution.py:25
  11.6 4.3 %collective-permute-start = (f32[8,512]{1,0:T(8,128)S(1)}, f32[8,512]{1,0:T(8,128)S(1)}, u32[]{:S(2)}, u32[]{:S(2)}) collective-permute-start(f32[8,512]{1,0:T(8,128)S(1)} %bitcast.90), channel_id=1, source_target_pairs={{8,0},{16,8},{24,16},{32,24},{40,32},{48,40},{56,48},{64,56},{72,6... | collective-permute-start | bytes 49160 | tf_op jit(solution)/shard_map/ppermute | solution.py:25
  15.9 9.2 %all-to-all-start = ((f32[128,8,384]{2,1,0:T(8,128)}), f32[128,8,384]{2,1,0:T(8,128)}, u32[]{:S(2)}, u32[]{:S(2)}) async-start(f32[128,8,384]{2,1,0:T(8,128)} %bitcast.81), calls=%async_computation | async-start | bytes 3145728 | tf_op jit(solution)/shard_map/all_to_all | solution.py:51
  25.2 0.6 constant_dynamic-slice_fusion.2
  29.7 0.7 fusion.25
  30.6 0.5 fusion.26
  31.1 0.6 multiply_add_fusion
  31.7 0.6 multiply_bitcast_fusion.1
  32.3 0.8 fusion.35
  33.2 2.8 %fusion.33 = (f32[8,128,511]{2,1,0:T(8,128)}, f32[8,128,511]{2,1,0:T(8,128)}) fusion(f32[8,128,512]{2,1,0:T(8,128)S(1)} %copy-done), kind=kLoop, calls=%fused_computation.78 | loop fusion | bytes 8372224 | tf_op jit(solution)/shard_map/slice | solution.py:38
  35.9 2.5 %fusion.31 = (f32[8,127,512]{2,1,0:T(8,128)}, f32[8,127,512]{2,1,0:T(8,128)}) fusion(f32[8,128,512]{2,1,0:T(8,128)S(1)} %copy-done), kind=kLoop, calls=%fused_computation.76 | loop fusion | bytes 8323072 | tf_op jit(solution)/shard_map/slice | solution.py:36
  38.4 9.8 %all-to-all-done = f32[128,8,384]{2,1,0:T(8,128)} async-done(((f32[128,8,384]{2,1,0:T(8,128)}), f32[128,8,384]{2,1,0:T(8,128)}, u32[]{:S(2)}, u32[]{:S(2)}) %all-to-all-start) | async-done | bytes 1572896 | tf_op jit(solution)/shard_map/all_to_all | solution.py:51
  48.2 1.7 fusion.6
  50.0 1.4 fusion.5
  51.3 7.0 %all-to-all-start.1 = ((f32[128,8,384]{2,1,0:T(8,128)}), f32[128,8,384]{2,1,0:T(8,128)}, u32[]{:S(2)}, u32[]{:S(2)}) async-start(f32[128,8,384]{2,1,0:T(8,128)} %bitcast.80), calls=%async_computation.1 | async-start | bytes 3145728 | tf_op jit(solution)/shard_map/all_to_all | solution.py:56
  58.3 2.4 %fusion.36 = (f32[7,128,512]{2,1,0:T(8,128)}, f32[7,128,512]{2,1,0:T(8,128)}) fusion(f32[8,128,512]{2,1,0:T(8,128)S(1)} %copy-done), kind=kLoop, calls=%fused_computation.81 | loop fusion | bytes 7340032 | tf_op jit(solution)/shard_map/slice | solution.py:124
  60.7 1.2 compare_and_fusion
  61.9 1.4 stack.9
  63.3 4.1 %copy.115 = f32[1,8,512,128]{3,1,2,0:T(8,128)} copy(f32[1,8,512,128]{3,2,1,0:T(8,128)} %stack.9) | data formatting | bytes 4194304 | tf_op jit(solution)/shard_map/stack | solution.py:161
  67.5 0.2 copy.108
  67.7 0.2 copy.106
  68.0 7.0 %fusion.4 = f32[8,128,512]{2,1,0:T(8,128)} fusion(f32[8,128,512]{2,1,0:T(8,128)S(1)} %copy-done, f32[1,128,512]{2,1,0:T(8,128)} %get-tuple-element.35, f32[7,128,512]{2,1,0:T(8,128)} %get-tuple-element.37, f32[7,128,512]{2,1,0:T(8,128)} %get-tuple-element.36, f32[1,128,512]{2,1,0:T(8,128)} %get-tuple-element.34, f32[8,128,511]{2,1,0:T(8,128)} %get-tuple-element.31, ...), kind=kLoop, calls=%fused_computation.16 | loop fusion | flops 13107200 | bytes 17039424 | tf_op jit(solution)/shard_map/add | solution.py:144
  75.1 1.6 stack.10
  76.7 1.2 copy.116
  77.9 0.4 copy-done.1
  78.3 2.2 %pad_maximum_fusion = f32[2,8,512,128]{3,1,2,0:T(8,128)} fusion(f32[1,8,512,128]{3,1,2,0:T(8,128)S(1)} %copy.116, f32[1,8,512,128]{3,1,2,0:T(8,128)S(1)} %copy-done.1), kind=kLoop, calls=%fused_computation.1 | loop fusion | flops 1048576 | bytes 8388608 | tf_op jit(solution)/shard_map/stack | solution.py:161
  80.5 2.9 %gather_fusion = f32[128,2,8,128]{3,2,1,0:T(8,128)S(1)} fusion(f32[2,8,512,128]{3,1,2,0:T(8,128)} %pad_maximum_fusion, s32[1024]{0:T(1024)S(1)} %pad_clamp_fusion), kind=kCustom, calls=%fused_computation | custom fusion | bytes 2097664 | tf_op jit(solution)/shard_map/jit(_take)/gather | solution.py:162
  83.4 0.2 broadcast_select_fusion
  83.8 1.2 slice.82
  85.7 0.8 convolution_add_fusion
  86.5 3.0 %copy.117 = f32[128,2,2048]{2,1,0:T(2,128)} copy(f32[128,2,2048]{2,0,1:T(8,128)S(1)} %convolution_add_fusion) | data formatting | bytes 4194304 | tf_op jit(solution)/shard_map/add | solution.py:170
  89.4 9.8 %all-to-all-start.2 = ((f32[128,2,2048]{2,1,0:T(2,128)}), f32[128,2,2048]{2,1,0:T(2,128)S(1)}, u32[]{:S(2)}, u32[]{:S(2)}) async-start(f32[128,2,2048]{2,1,0:T(2,128)} %copy.117), calls=%async_computation.2 | async-start | bytes 4194304 | tf_op jit(solution)/shard_map/all_to_all | solution.py:171
  100.3 0.7 convert_add_fusion.1.factor_ref
  101.0 1.0 fusion.38
  101.9 3.1 %collective-permute-start.4 = (f32[8,384]{1,0:T(8,128)S(1)}, f32[8,384]{1,0:T(8,128)S(1)}, u32[]{:S(2)}, u32[]{:S(2)}) collective-permute-start(f32[8,384]{1,0:T(8,128)S(1)} %bitcast.92), channel_id=1, source_target_pairs={{0,8},{8,16},{16,24},{24,32},{32,40},{40,48},{48,56},{56,64},{64,7... | collective-permute-start | bytes 36872 | tf_op jit(solution)/shard_map/ppermute | solution.py:112
  105.1 4.3 %collective-permute-start.5 = (f32[8,384]{1,0:T(8,128)S(1)}, f32[8,384]{1,0:T(8,128)S(1)}, u32[]{:S(2)}, u32[]{:S(2)}) collective-permute-start(f32[8,384]{1,0:T(8,128)S(1)} %bitcast.93), channel_id=1, source_target_pairs={{8,0},{16,8},{24,16},{32,24},{40,32},{48,40},{56,48},{64,56},{72,6... | collective-permute-start | bytes 36872 | tf_op jit(solution)/shard_map/ppermute | solution.py:112
  109.4 1.4 fusion.37
  110.8 0.8 copy.134
  111.6 4.0 %collective-permute-start.6 = (f32[128,8]{1,0:T(8,128)S(1)}, f32[128,8]{1,0:T(8,128)S(1)}, u32[]{:S(2)}, u32[]{:S(2)}) collective-permute-start(f32[128,8]{1,0:T(8,128)S(1)} %bitcast.85), channel_id=1, source_target_pairs={{0,1},{1,2},{2,3},{3,4},{4,5},{5,6},{6,7},{8,9},{9,10},{10,11},{11... | collective-permute-start | bytes 12296 | tf_op jit(solution)/shard_map/ppermute | solution.py:112
  115.6 0.8 copy.135
  116.5 2.1 %collective-permute-start.7 = (f32[128,8]{1,0:T(8,128)S(1)}, f32[128,8]{1,0:T(8,128)S(1)}, u32[]{:S(2)}, u32[]{:S(2)}) collective-permute-start(f32[128,8]{1,0:T(8,128)S(1)} %bitcast.86), channel_id=1, source_target_pairs={{1,0},{2,1},{3,2},{4,3},{5,4},{6,5},{7,6},{9,8},{10,9},{11,10},{12... | collective-permute-start | bytes 12296 | tf_op jit(solution)/shard_map/ppermute | solution.py:112
  118.6 9.6 %all-to-all-done.2 = f32[128,2,2048]{2,1,0:T(2,128)S(1)} async-done(((f32[128,2,2048]{2,1,0:T(2,128)}), f32[128,2,2048]{2,1,0:T(2,128)S(1)}, u32[]{:S(2)}, u32[]{:S(2)}) %all-to-all-start.2) | async-done | bytes 2097184 | tf_op jit(solution)/shard_map/all_to_all | solution.py:171
  128.2 2.4 %copy.118 = f32[128,2,2048]{0,2,1:T(8,128)} copy(f32[128,2,2048]{2,1,0:T(2,128)S(1)} %all-to-all-done.2) | data formatting | bytes 4194304 | tf_op jit(solution)/shard_map/all_to_all | solution.py:171
  130.6 2.4 %convolution_bitcast_fusion.1 = f32[128,2,8,128]{3,0,2,1:T(8,128)S(1)} fusion(f32[2,8,128,128,2]{3,2,1,0,4:T(8,128)} %bitcast.79, s32[128,2]{0,1:T(2,128)S(1)} %broadcast_select_fusion.1), kind=kOutput, calls=%fused_computation.20 | convolution fusion | flops 402685952 | bytes 3146752 | tf_op jit(solution)/shard_map/tqs,qsk->tk/dot_general | solution.py:181
  133.0 3.1 %convolution_bitcast_fusion.bound_ref = f32[2,8,128,384]{3,2,1,0:T(8,128)} fusion(f32[128,2,8,128]{3,0,2,1:T(8,128)S(1)} %convolution_bitcast_fusion.1, f32[128]{0:T(128)S(1)} %iota_convert_fusion, f32[384]{0:T(512)S(1)} %add_clamp_fusion), kind=kOutput, calls=%fused_computation.17 | convolution fusion | flops 604176384 | bytes 4196352 | tf_op jit(solution)/shard_map/tald,de->alte/dot_general | solution.py:188
  136.2 0.8 broadcast_in_dim.69.divisor_ref
  137.0 6.0 %shard_map.104 = (f32[8,128,384]{2,1,0:T(8,128)}, f32[8,384]{1,0:T(8,128)}, f32[8,384]{1,0:T(8,128)}, f32[128,8]{1,0:T(8,128)}, f32[128,8]{1,0:T(8,128)}) custom-call(f32[2,8]{1,0:T(2,128)} %wind_ref.5, f32[8,128,384]{2,1,0:T(8,128)} %bitcast.15.child_ref, f32[8,384]{1,0:T(8,128)} %copy-done.13, f32[8,384]{1,0:T(8,128)} %copy-done.14, f32[128,8]{1,0:T(8,128)} %copy-done.5, ...), custom_call_target="tpu_custom_call" | custom-call | flops 11796480 | bytes 6684672 | tf_op jit(solution)/shard_map/pallas_call | solution.py:90
  142.9 2.5 %collective-permute-start.8 = (f32[8,384]{1,0:T(8,128)}, f32[8,384]{1,0:T(8,128)S(1)}, u32[]{:S(2)}, u32[]{:S(2)}) collective-permute-start(f32[8,384]{1,0:T(8,128)} %get-tuple-element.14), channel_id=1, source_target_pairs={{0,8},{8,16},{16,24},{24,32},{32,40},{40,48},{48,56},{56,64},{64,7... | collective-permute-start | bytes 36872 | tf_op jit(solution)/shard_map/ppermute | solution.py:112
  145.4 4.9 %collective-permute-start.9 = (f32[8,384]{1,0:T(8,128)}, f32[8,384]{1,0:T(8,128)S(1)}, u32[]{:S(2)}, u32[]{:S(2)}) collective-permute-start(f32[8,384]{1,0:T(8,128)} %get-tuple-element.15), channel_id=1, source_target_pairs={{8,0},{16,8},{24,16},{32,24},{40,32},{48,40},{56,48},{64,56},{72,6... | collective-permute-start | bytes 36872 | tf_op jit(solution)/shard_map/ppermute | solution.py:112
  150.3 2.3 %collective-permute-start.10 = (f32[128,8]{1,0:T(8,128)}, f32[128,8]{1,0:T(8,128)S(1)}, u32[]{:S(2)}, u32[]{:S(2)}) collective-permute-start(f32[128,8]{1,0:T(8,128)} %get-tuple-element.16), channel_id=1, source_target_pairs={{0,1},{1,2},{2,3},{3,4},{4,5},{5,6},{6,7},{8,9},{9,10},{10,11},{11... | collective-permute-start | bytes 12296 | tf_op jit(solution)/shard_map/ppermute | solution.py:112
  152.7 2.9 %collective-permute-start.11 = (f32[128,8]{1,0:T(8,128)}, f32[128,8]{1,0:T(8,128)S(1)}, u32[]{:S(2)}, u32[]{:S(2)}) collective-permute-start(f32[128,8]{1,0:T(8,128)} %get-tuple-element.17), channel_id=1, source_target_pairs={{1,0},{2,1},{3,2},{4,3},{5,4},{6,5},{7,6},{9,8},{10,9},{11,10},{12... | collective-permute-start | bytes 12296 | tf_op jit(solution)/shard_map/ppermute | solution.py:112
  155.6 2.8 %collective-permute-done.11.ay_ref = f32[128,8]{1,0:T(8,128)S(1)} collective-permute-done((f32[128,8]{1,0:T(8,128)}, f32[128,8]{1,0:T(8,128)S(1)}, u32[]{:S(2)}, u32[]{:S(2)}) %collective-permute-start.11) | collective-permute-done | bytes 4128 | tf_op jit(solution)/shard_map/ppermute | solution.py:112
  158.5 0.6 copy-done.10
  159.1 6.0 %shard_map.105 = (f32[8,128,384]{2,1,0:T(8,128)}, f32[8,384]{1,0:T(8,128)}, f32[8,384]{1,0:T(8,128)}, f32[128,8]{1,0:T(8,128)}, f32[128,8]{1,0:T(8,128)}) custom-call(f32[2,8]{1,0:T(2,128)} %wind_ref.5, f32[8,128,384]{2,1,0:T(8,128)} %get-tuple-element.13.child_ref, f32[8,384]{1,0:T(8,128)} %copy-done.16, f32[8,384]{1,0:T(8,128)} %copy-done.18, ...), custom_call_target="tpu_custom_call" | custom-call | flops 11796480 | bytes 6684672 | tf_op jit(solution)/shard_map/pallas_call | solution.py:90
  165.1 1.9 %collective-permute-start.12 = (f32[8,384]{1,0:T(8,128)}, f32[8,384]{1,0:T(8,128)S(1)}, u32[]{:S(2)}, u32[]{:S(2)}) collective-permute-start(f32[8,384]{1,0:T(8,128)} %get-tuple-element.19), channel_id=1, source_target_pairs={{0,8},{8,16},{16,24},{24,32},{32,40},{40,48},{48,56},{56,64},{64,7... | collective-permute-start | bytes 36872 | tf_op jit(solution)/shard_map/ppermute | solution.py:112
  167.0 5.5 %collective-permute-start.13 = (f32[8,384]{1,0:T(8,128)}, f32[8,384]{1,0:T(8,128)S(1)}, u32[]{:S(2)}, u32[]{:S(2)}) collective-permute-start(f32[8,384]{1,0:T(8,128)} %get-tuple-element.20), channel_id=1, source_target_pairs={{8,0},{16,8},{24,16},{32,24},{40,32},{48,40},{56,48},{64,56},{72,6... | collective-permute-start | bytes 36872 | tf_op jit(solution)/shard_map/ppermute | solution.py:112
  172.5 2.5 %collective-permute-start.14 = (f32[128,8]{1,0:T(8,128)}, f32[128,8]{1,0:T(8,128)S(1)}, u32[]{:S(2)}, u32[]{:S(2)}) collective-permute-start(f32[128,8]{1,0:T(8,128)} %get-tuple-element.21), channel_id=1, source_target_pairs={{0,1},{1,2},{2,3},{3,4},{4,5},{5,6},{6,7},{8,9},{9,10},{10,11},{11... | collective-permute-start | bytes 12296 | tf_op jit(solution)/shard_map/ppermute | solution.py:112
  175.0 1.9 %collective-permute-start.15 = (f32[128,8]{1,0:T(8,128)}, f32[128,8]{1,0:T(8,128)S(1)}, u32[]{:S(2)}, u32[]{:S(2)}) collective-permute-start(f32[128,8]{1,0:T(8,128)} %get-tuple-element.22), channel_id=1, source_target_pairs={{1,0},{2,1},{3,2},{4,3},{5,4},{6,5},{7,6},{9,8},{10,9},{11,10},{12... | collective-permute-start | bytes 12296 | tf_op jit(solution)/shard_map/ppermute | solution.py:112
  177.0 3.8 %collective-permute-done.15.ay_ref = f32[128,8]{1,0:T(8,128)S(1)} collective-permute-done((f32[128,8]{1,0:T(8,128)}, f32[128,8]{1,0:T(8,128)S(1)}, u32[]{:S(2)}, u32[]{:S(2)}) %collective-permute-start.15) | collective-permute-done | bytes 4128 | tf_op jit(solution)/shard_map/ppermute | solution.py:112
  180.9 0.6 copy-done.9
  181.5 6.0 %shard_map.106 = (f32[8,128,384]{2,1,0:T(8,128)}, f32[8,384]{1,0:T(8,128)}, f32[8,384]{1,0:T(8,128)}, f32[128,8]{1,0:T(8,128)}, f32[128,8]{1,0:T(8,128)}) custom-call(f32[2,8]{1,0:T(2,128)} %wind_ref.5, f32[8,128,384]{2,1,0:T(8,128)} %get-tuple-element.18.child_ref, f32[8,384]{1,0:T(8,128)} %copy-done.15, f32[8,384]{1,0:T(8,128)} %copy-done.17, ...), custom_call_target="tpu_custom_call" | custom-call | flops 11796480 | bytes 6684672 | tf_op jit(solution)/shard_map/pallas_call | solution.py:90
  (88 shorter events, 1.9 us)
Async XLA Ops:
  0.6 7.8 %copy-start = (f32[8,128,512]{2,1,0:T(8,128)S(1)}, f32[8,128,512]{2,1,0:T(8,128)}, u32[]{:S(2)}) copy-start(f32[8,128,512]{2,1,0:T(8,128)} %param.9) | copy-start | bytes 6291460
  2.2 23.0 %copy-start.22 = (s32[2,4]{1,0:T(2,128)S(1)}, s32[2,4]{1,0:T(2,128)}, u32[]{:S(2)}) copy-start(s32[2,4]{1,0:T(2,128)} %param.17) | copy-start | bytes 100
  2.4 28.0 %copy-start.4 = (s32[16384,1]{0,1:T(1,128)S(1)}, s32[16384,1]{0,1:T(1,128)}, u32[]{:S(2)}) copy-start(s32[16384,1]{0,1:T(1,128)} %param.14) | copy-start | bytes 196612
  2.4 29.3 %copy-start.12 = (f32[2,8]{1,0:T(2,128)S(1)}, f32[2,8]{1,0:T(2,128)}, u32[]{:S(2)}) copy-start(f32[2,8]{1,0:T(2,128)} %wind_ref.5) | copy-start | bytes 196
  2.4 29.9 %copy-start.2 = (bf16[128,512]{1,0:T(8,128)(2,1)S(1)}, bf16[128,512]{1,0:T(8,128)(2,1)}, u32[]{:S(2)}) copy-start(bf16[128,512]{1,0:T(8,128)(2,1)} %param.10) | copy-start | bytes 393220
  2.4 65.1 %collective-permute-start.3 = (f32[8,128]{1,0:T(8,128)S(1)}, f32[8,128]{1,0:T(8,128)S(1)}, u32[]{:S(2)}, u32[]{:S(2)}) collective-permute-start(f32[8,128]{1,0:T(8,128)S(1)} %bitcast.94), channel_id=1, source_target_pairs={{0,1},{1,2},{2,3},{3,4},{4,5},{5,6},{6,7},{8,9},{9,10},{10,11},{11... | collective-permute-start | bytes 12296 | tf_op jit(solution)/shard_map/ppermute | solution.py:25
  6.5 61.2 %collective-permute-start.2 = (f32[8,128]{1,0:T(8,128)S(1)}, f32[8,128]{1,0:T(8,128)S(1)}, u32[]{:S(2)}, u32[]{:S(2)}) collective-permute-start(f32[8,128]{1,0:T(8,128)S(1)} %bitcast.96), channel_id=1, source_target_pairs={{1,0},{2,1},{3,2},{4,3},{5,4},{6,5},{7,6},{9,8},{10,9},{11,10},{12... | collective-permute-start | bytes 12296 | tf_op jit(solution)/shard_map/ppermute | solution.py:25
  8.5 59.5 %collective-permute-start.1 = (f32[8,512]{1,0:T(8,128)S(1)}, f32[8,512]{1,0:T(8,128)S(1)}, u32[]{:S(2)}, u32[]{:S(2)}) collective-permute-start(f32[8,512]{1,0:T(8,128)S(1)} %bitcast.88), channel_id=1, source_target_pairs={{0,8},{8,16},{16,24},{24,32},{32,40},{40,48},{48,56},{56,64},{64,7... | collective-permute-start | bytes 49160 | tf_op jit(solution)/shard_map/ppermute | solution.py:25
  11.6 56.4 %collective-permute-start = (f32[8,512]{1,0:T(8,128)S(1)}, f32[8,512]{1,0:T(8,128)S(1)}, u32[]{:S(2)}, u32[]{:S(2)}) collective-permute-start(f32[8,512]{1,0:T(8,128)S(1)} %bitcast.90), channel_id=1, source_target_pairs={{8,0},{16,8},{24,16},{32,24},{40,32},{48,40},{56,48},{64,56},{72,6... | collective-permute-start | bytes 49160 | tf_op jit(solution)/shard_map/ppermute | solution.py:25
  15.9 32.3 %all-to-all-start = ((f32[128,8,384]{2,1,0:T(8,128)}), f32[128,8,384]{2,1,0:T(8,128)}, u32[]{:S(2)}, u32[]{:S(2)}) async-start(f32[128,8,384]{2,1,0:T(8,128)} %bitcast.81), calls=%async_computation | async-start | bytes 3145728 | tf_op jit(solution)/shard_map/all_to_all | solution.py:51
  51.3 32.5 %all-to-all-start.1 = ((f32[128,8,384]{2,1,0:T(8,128)}), f32[128,8,384]{2,1,0:T(8,128)}, u32[]{:S(2)}, u32[]{:S(2)}) async-start(f32[128,8,384]{2,1,0:T(8,128)} %bitcast.80), calls=%async_computation.1 | async-start | bytes 3145728 | tf_op jit(solution)/shard_map/all_to_all | solution.py:56
  63.3 4.7 %copy-start.19 = (f32[8]{0:T(128)S(1)}, f32[8]{0:T(128)}, u32[]{:S(2)}) copy-start(f32[8]{0:T(128)} %get-tuple-element.44) | copy-start | bytes 100
  76.7 1.6 copy-start.1
  80.5 2.9 %copy-start.23 = (pred[128]{0:T(512)(128)(4,1)S(1)}, pred[128]{0:T(512)(128)(4,1)}, u32[]{:S(2)}) copy-start(pred[128]{0:T(512)(128)(4,1)} %compare_and_fusion) | copy-start | bytes 388
  83.4 2.2 %copy-start.20 = (s32[128]{0:T(128)S(1)}, s32[128]{0:T(128)}, u32[]{:S(2)}) copy-start(s32[128]{0:T(128)} %fusion.26) | copy-start | bytes 1540
  83.4 2.2 %copy-start.21 = (s32[128,2]{0,1:T(2,128)S(1)}, s32[128,2]{0,1:T(2,128)}, u32[]{:S(2)}) copy-start(s32[128,2]{0,1:T(2,128)} %multiply_add_fusion) | copy-start | bytes 3076
  89.4 10.3 %copy-start.11 = (s32[16384]{0:T(1024)S(1)}, s32[16384]{0:T(1024)}, u32[]{:S(2)}) copy-start(s32[16384]{0:T(1024)} %param.16) | copy-start | bytes 196612
  89.4 10.8 %copy-start.3 = (bf16[128,384]{1,0:T(8,128)(2,1)S(1)}, bf16[128,384]{1,0:T(8,128)(2,1)}, u32[]{:S(2)}) copy-start(bf16[128,384]{1,0:T(8,128)(2,1)} %param.12) | copy-start | bytes 294916
  89.4 38.7 %all-to-all-start.2 = ((f32[128,2,2048]{2,1,0:T(2,128)}), f32[128,2,2048]{2,1,0:T(2,128)S(1)}, u32[]{:S(2)}, u32[]{:S(2)}) async-start(f32[128,2,2048]{2,1,0:T(2,128)} %copy.117), calls=%async_computation.2 | async-start | bytes 4194304 | tf_op jit(solution)/shard_map/all_to_all | solution.py:171
  101.9 34.2 %collective-permute-start.4 = (f32[8,384]{1,0:T(8,128)S(1)}, f32[8,384]{1,0:T(8,128)S(1)}, u32[]{:S(2)}, u32[]{:S(2)}) collective-permute-start(f32[8,384]{1,0:T(8,128)S(1)} %bitcast.92), channel_id=1, source_target_pairs={{0,8},{8,16},{16,24},{24,32},{32,40},{40,48},{48,56},{56,64},{64,7... | collective-permute-start | bytes 36872 | tf_op jit(solution)/shard_map/ppermute | solution.py:112
  105.1 31.1 %collective-permute-start.5 = (f32[8,384]{1,0:T(8,128)S(1)}, f32[8,384]{1,0:T(8,128)S(1)}, u32[]{:S(2)}, u32[]{:S(2)}) collective-permute-start(f32[8,384]{1,0:T(8,128)S(1)} %bitcast.93), channel_id=1, source_target_pairs={{8,0},{16,8},{24,16},{32,24},{40,32},{48,40},{56,48},{64,56},{72,6... | collective-permute-start | bytes 36872 | tf_op jit(solution)/shard_map/ppermute | solution.py:112
  111.6 24.5 %collective-permute-start.6 = (f32[128,8]{1,0:T(8,128)S(1)}, f32[128,8]{1,0:T(8,128)S(1)}, u32[]{:S(2)}, u32[]{:S(2)}) collective-permute-start(f32[128,8]{1,0:T(8,128)S(1)} %bitcast.85), channel_id=1, source_target_pairs={{0,1},{1,2},{2,3},{3,4},{4,5},{5,6},{6,7},{8,9},{9,10},{10,11},{11... | collective-permute-start | bytes 12296 | tf_op jit(solution)/shard_map/ppermute | solution.py:112
  116.5 19.7 %collective-permute-start.7 = (f32[128,8]{1,0:T(8,128)S(1)}, f32[128,8]{1,0:T(8,128)S(1)}, u32[]{:S(2)}, u32[]{:S(2)}) collective-permute-start(f32[128,8]{1,0:T(8,128)S(1)} %bitcast.86), channel_id=1, source_target_pairs={{1,0},{2,1},{3,2},{4,3},{5,4},{6,5},{7,6},{9,8},{10,9},{11,10},{12... | collective-permute-start | bytes 12296 | tf_op jit(solution)/shard_map/ppermute | solution.py:112
  136.1 0.8 copy-start.5
  136.1 0.8 copy-start.6
  136.2 0.8 copy-start.13
  136.2 0.8 copy-start.14
  142.9 15.6 %collective-permute-start.8 = (f32[8,384]{1,0:T(8,128)}, f32[8,384]{1,0:T(8,128)S(1)}, u32[]{:S(2)}, u32[]{:S(2)}) collective-permute-start(f32[8,384]{1,0:T(8,128)} %get-tuple-element.14), channel_id=1, source_target_pairs={{0,8},{8,16},{16,24},{24,32},{32,40},{40,48},{48,56},{56,64},{64,7... | collective-permute-start | bytes 36872 | tf_op jit(solution)/shard_map/ppermute | solution.py:112
  145.4 13.1 %collective-permute-start.9 = (f32[8,384]{1,0:T(8,128)}, f32[8,384]{1,0:T(8,128)S(1)}, u32[]{:S(2)}, u32[]{:S(2)}) collective-permute-start(f32[8,384]{1,0:T(8,128)} %get-tuple-element.15), channel_id=1, source_target_pairs={{8,0},{16,8},{24,16},{32,24},{40,32},{48,40},{56,48},{64,56},{72,6... | collective-permute-start | bytes 36872 | tf_op jit(solution)/shard_map/ppermute | solution.py:112
  150.3 5.3 %collective-permute-start.10 = (f32[128,8]{1,0:T(8,128)}, f32[128,8]{1,0:T(8,128)S(1)}, u32[]{:S(2)}, u32[]{:S(2)}) collective-permute-start(f32[128,8]{1,0:T(8,128)} %get-tuple-element.16), channel_id=1, source_target_pairs={{0,1},{1,2},{2,3},{3,4},{4,5},{5,6},{6,7},{8,9},{9,10},{10,11},{11... | collective-permute-start | bytes 12296 | tf_op jit(solution)/shard_map/ppermute | solution.py:112
  152.7 5.8 %collective-permute-start.11 = (f32[128,8]{1,0:T(8,128)}, f32[128,8]{1,0:T(8,128)S(1)}, u32[]{:S(2)}, u32[]{:S(2)}) collective-permute-start(f32[128,8]{1,0:T(8,128)} %get-tuple-element.17), channel_id=1, source_target_pairs={{1,0},{2,1},{3,2},{4,3},{5,4},{6,5},{7,6},{9,8},{10,9},{11,10},{12... | collective-permute-start | bytes 12296 | tf_op jit(solution)/shard_map/ppermute | solution.py:112
  155.6 2.9 %copy-start.8 = (f32[128,8]{1,0:T(8,128)}, f32[128,8]{1,0:T(8,128)S(1)}, u32[]{:S(2)}) copy-start(f32[128,8]{1,0:T(8,128)S(1)} %collective-permute-done.10.by_ref) | copy-start | bytes 12292
  158.5 0.6 copy-start.10
  158.5 0.6 copy-start.16
  158.5 0.6 copy-start.18
  165.1 15.7 %collective-permute-start.12 = (f32[8,384]{1,0:T(8,128)}, f32[8,384]{1,0:T(8,128)S(1)}, u32[]{:S(2)}, u32[]{:S(2)}) collective-permute-start(f32[8,384]{1,0:T(8,128)} %get-tuple-element.19), channel_id=1, source_target_pairs={{0,8},{8,16},{16,24},{24,32},{32,40},{40,48},{48,56},{56,64},{64,7... | collective-permute-start | bytes 36872 | tf_op jit(solution)/shard_map/ppermute | solution.py:112
  167.0 13.8 %collective-permute-start.13 = (f32[8,384]{1,0:T(8,128)}, f32[8,384]{1,0:T(8,128)S(1)}, u32[]{:S(2)}, u32[]{:S(2)}) collective-permute-start(f32[8,384]{1,0:T(8,128)} %get-tuple-element.20), channel_id=1, source_target_pairs={{8,0},{16,8},{24,16},{32,24},{40,32},{48,40},{56,48},{64,56},{72,6... | collective-permute-start | bytes 36872 | tf_op jit(solution)/shard_map/ppermute | solution.py:112
  172.5 4.5 %collective-permute-start.14 = (f32[128,8]{1,0:T(8,128)}, f32[128,8]{1,0:T(8,128)S(1)}, u32[]{:S(2)}, u32[]{:S(2)}) collective-permute-start(f32[128,8]{1,0:T(8,128)} %get-tuple-element.21), channel_id=1, source_target_pairs={{0,1},{1,2},{2,3},{3,4},{4,5},{5,6},{6,7},{8,9},{9,10},{10,11},{11... | collective-permute-start | bytes 12296 | tf_op jit(solution)/shard_map/ppermute | solution.py:112
  175.0 5.8 %collective-permute-start.15 = (f32[128,8]{1,0:T(8,128)}, f32[128,8]{1,0:T(8,128)S(1)}, u32[]{:S(2)}, u32[]{:S(2)}) collective-permute-start(f32[128,8]{1,0:T(8,128)} %get-tuple-element.22), channel_id=1, source_target_pairs={{1,0},{2,1},{3,2},{4,3},{5,4},{6,5},{7,6},{9,8},{10,9},{11,10},{12... | collective-permute-start | bytes 12296 | tf_op jit(solution)/shard_map/ppermute | solution.py:112
  177.0 3.9 %copy-start.7 = (f32[128,8]{1,0:T(8,128)}, f32[128,8]{1,0:T(8,128)S(1)}, u32[]{:S(2)}) copy-start(f32[128,8]{1,0:T(8,128)S(1)} %collective-permute-done.14.by_ref) | copy-start | bytes 12292
  180.8 0.6 copy-start.9
  180.8 0.6 copy-start.15
  180.9 0.6 copy-start.17

commit v14 on v13

--- a/solution.py
+++ b/solution.py
@@ -160,11 +160,10 @@
     send_select = (jnp.arange(devices * CAP)[:, None] == slot_index[None, :]).astype(jnp.float32)
     both_states = jnp.stack([parent_field, new_parent]).reshape(2, levels, -1, STRIP)
     picked = jnp.take(both_states, my_rows, axis=2)
-    strip_values = jnp.moveaxis(picked, 2, 0).reshape(slots, -1)
     outgoing_strips = jnp.einsum(
-        "dsj,jk->dsk",
+        "dsj,aljk->dsalk",
         send_select.reshape(devices, CAP, slots),
-        strip_values,
+        picked,
         precision=lax.Precision.HIGH,
     )
     outgoing_strips = outgoing_strips + 0.0 * child[0, 0, 0]
@@ -179,15 +178,15 @@
     target_rows = jnp.where(jnp.any(hits, axis=2), chosen, -1).reshape(-1)
     row_select = (jnp.arange(crows)[:, None] == target_rows[None, :]).astype(jnp.float32)
     coarse = jnp.einsum(
-        "tqs,qsk->tk",
+        "tqs,qsald->altd",
         row_select.reshape(crows, devices, CAP),
         incoming,
         precision=lax.Precision.HIGH,
     )
     counts = jnp.sum(row_select, axis=1)
     boundary = jnp.einsum(
-        "tald,de->alte",
-        coarse.reshape(crows, 2, levels, STRIP),
+        "altd,de->alte",
+        coarse,
         refine_table(STRIP),
         precision=lax.Precision.HIGH,
     )

time: 189 us -> 185 us (0.979)
  local copies, waits for them, and re-layouts: 36.4 us -> 33.4 us
    all_to_all x1 -> x0, local copies, waits for them, and re-layouts: 2.43 us -> none  [shards(): lax.all_to_all(outgoing_strips, ('gx', 'gy'), split_axis=0, concat_axis=0...]
  transfers between devices with their start and end apart: 19 -> 19, of which waited for: 4 -> 4; matrix products, arithmetic and copies ran while one was open for 27% -> 26% of each run, Pallas kernels for 0% -> 0%
where the time goes in v14:
time: 185 us; the launch traced here: 184 us
  starting transfers between devices  77 us (42%)
  local copies, waits for them, and re-layouts  33.4 us (18%)
  waiting for transfers between devices  26.3 us (14%)
  Pallas kernels  17.9 us (10%)
  other arithmetic  17.6 us (10%)
  matrix products  6.07 us (3%)
  between operations  5.87 us (3%)
    ppermute x12, starting transfers between devices, swap_edge(): return lax.ppermute(edge, axis, pairs)  37.8 us
    pallas_call x3, Pallas kernels, substep(): pl.pallas_call(functools.partial(substep_kernel, weight), out_shape=(jax....  17.9 us
    ppermute x4, starting transfers between devices, swap(): return lax.ppermute(edge, axis, pairs)  13.2 us
    all_to_all x1, waiting for transfers between devices, storm_rows(): gathered = lax.all_to_all(pieces, ('gx', 'gy'), 0, 0, tiled=True)  9.83 us
    all_to_all x1, waiting for transfers between devices, shards(): lax.all_to_all(outgoing_strips, ('gx', 'gy'), split_axis=0, concat_axis=0...  9.78 us
    all_to_all x1, starting transfers between devices, shards(): lax.all_to_all(outgoing_strips, ('gx', 'gy'), split_axis=0, concat_axis=0...  9.75 us
    all_to_all x1, starting transfers between devices, storm_rows(): gathered = lax.all_to_all(pieces, ('gx', 'gy'), 0, 0, tiled=True)  9.25 us
    another operation x4, local copies, waits for them, and re-layouts, shards(): jnp.stack([parent_field, new_parent]).reshape(2, levels, -1, STRIP)  8.37 us
  transfers between devices with their start and end apart: 19, of which 4 were waited for; matrix products, arithmetic and copies ran while one was open for 26% of the time, Pallas kernels for 0%

profile of v14, /device:TPU:33, one launch (start us, length us, event | category | flops | bytes accessed | tf_op | source)
XLA Modules:
  0.0 184.2 jit_solution(1523621446573217123)
XLA Ops:
  0.6 1.6 fusion.44
  2.2 0.2 copy.104
  2.4 3.9 %collective-permute-start.3 = (f32[8,128]{1,0:T(8,128)S(1)}, f32[8,128]{1,0:T(8,128)S(1)}, u32[]{:S(2)}, u32[]{:S(2)}) collective-permute-start(f32[8,128]{1,0:T(8,128)S(1)} %bitcast.89), channel_id=1, source_target_pairs={{0,1},{1,2},{2,3},{3,4},{4,5},{5,6},{6,7},{8,9},{9,10},{10,11},{11... | collective-permute-start | bytes 12296 | tf_op jit(solution)/shard_map/ppermute | solution.py:25
  6.5 1.9 %collective-permute-start.2 = (f32[8,128]{1,0:T(8,128)S(1)}, f32[8,128]{1,0:T(8,128)S(1)}, u32[]{:S(2)}, u32[]{:S(2)}) collective-permute-start(f32[8,128]{1,0:T(8,128)S(1)} %bitcast.91), channel_id=1, source_target_pairs={{1,0},{2,1},{3,2},{4,3},{5,4},{6,5},{7,6},{9,8},{10,9},{11,10},{12... | collective-permute-start | bytes 12296 | tf_op jit(solution)/shard_map/ppermute | solution.py:25
  8.5 3.1 %collective-permute-start.1 = (f32[8,512]{1,0:T(8,128)S(1)}, f32[8,512]{1,0:T(8,128)S(1)}, u32[]{:S(2)}, u32[]{:S(2)}) collective-permute-start(f32[8,512]{1,0:T(8,128)S(1)} %bitcast.83), channel_id=1, source_target_pairs={{0,8},{8,16},{16,24},{24,32},{32,40},{40,48},{48,56},{56,64},{64,7... | collective-permute-start | bytes 49160 | tf_op jit(solution)/shard_map/ppermute | solution.py:25
  11.6 4.3 %collective-permute-start = (f32[8,512]{1,0:T(8,128)S(1)}, f32[8,512]{1,0:T(8,128)S(1)}, u32[]{:S(2)}, u32[]{:S(2)}) collective-permute-start(f32[8,512]{1,0:T(8,128)S(1)} %bitcast.85), channel_id=1, source_target_pairs={{8,0},{16,8},{24,16},{32,24},{40,32},{48,40},{56,48},{64,56},{72,6... | collective-permute-start | bytes 49160 | tf_op jit(solution)/shard_map/ppermute | solution.py:25
  15.9 9.2 %all-to-all-start = ((f32[128,8,384]{2,1,0:T(8,128)}), f32[128,8,384]{2,1,0:T(8,128)}, u32[]{:S(2)}, u32[]{:S(2)}) async-start(f32[128,8,384]{2,1,0:T(8,128)} %bitcast.76), calls=%async_computation | async-start | bytes 3145728 | tf_op jit(solution)/shard_map/all_to_all | solution.py:51
  25.2 0.6 constant_dynamic-slice_fusion.2
  29.7 0.7 fusion.35
  30.6 0.5 fusion.36
  31.1 0.6 multiply_add_fusion
  31.7 0.6 multiply_bitcast_fusion.1
  32.3 0.8 fusion.45
  33.2 2.8 %fusion.43 = (f32[8,128,511]{2,1,0:T(8,128)}, f32[8,128,511]{2,1,0:T(8,128)}) fusion(f32[8,128,512]{2,1,0:T(8,128)S(1)} %copy-done), kind=kLoop, calls=%fused_computation.84 | loop fusion | bytes 8372224 | tf_op jit(solution)/shard_map/slice | solution.py:38
  35.9 2.5 %fusion.41 = (f32[8,127,512]{2,1,0:T(8,128)}, f32[8,127,512]{2,1,0:T(8,128)}) fusion(f32[8,128,512]{2,1,0:T(8,128)S(1)} %copy-done), kind=kLoop, calls=%fused_computation.82 | loop fusion | bytes 8323072 | tf_op jit(solution)/shard_map/slice | solution.py:36
  38.4 9.8 %all-to-all-done = f32[128,8,384]{2,1,0:T(8,128)} async-done(((f32[128,8,384]{2,1,0:T(8,128)}), f32[128,8,384]{2,1,0:T(8,128)}, u32[]{:S(2)}, u32[]{:S(2)}) %all-to-all-start) | async-done | bytes 1572896 | tf_op jit(solution)/shard_map/all_to_all | solution.py:51
  48.2 1.7 fusion.8
  50.0 1.4 fusion.7
  51.3 7.0 %all-to-all-start.1 = ((f32[128,8,384]{2,1,0:T(8,128)}), f32[128,8,384]{2,1,0:T(8,128)}, u32[]{:S(2)}, u32[]{:S(2)}) async-start(f32[128,8,384]{2,1,0:T(8,128)} %bitcast.75), calls=%async_computation.1 | async-start | bytes 3145728 | tf_op jit(solution)/shard_map/all_to_all | solution.py:56
  58.3 2.4 %fusion.46 = (f32[7,128,512]{2,1,0:T(8,128)}, f32[7,128,512]{2,1,0:T(8,128)}) fusion(f32[8,128,512]{2,1,0:T(8,128)S(1)} %copy-done), kind=kLoop, calls=%fused_computation.87 | loop fusion | bytes 7340032 | tf_op jit(solution)/shard_map/slice | solution.py:124
  60.7 1.2 compare_and_fusion
  61.9 1.4 stack.9
  63.3 4.1 %copy.87 = f32[1,8,512,128]{3,1,2,0:T(8,128)} copy(f32[1,8,512,128]{3,2,1,0:T(8,128)} %stack.9) | data formatting | bytes 4194304 | tf_op jit(solution)/shard_map/stack | solution.py:161
  67.5 0.2 copy.82
  67.7 0.2 copy.80
  68.0 7.0 %fusion.4 = f32[8,128,512]{2,1,0:T(8,128)} fusion(f32[8,128,512]{2,1,0:T(8,128)S(1)} %copy-done, f32[1,128,512]{2,1,0:T(8,128)} %get-tuple-element.35, f32[7,128,512]{2,1,0:T(8,128)} %get-tuple-element.37, f32[7,128,512]{2,1,0:T(8,128)} %get-tuple-element.36, f32[1,128,512]{2,1,0:T(8,128)} %get-tuple-element.34, f32[8,128,511]{2,1,0:T(8,128)} %get-tuple-element.31, ...), kind=kLoop, calls=%fused_computation.15 | loop fusion | flops 13107200 | bytes 17039424 | tf_op jit(solution)/shard_map/add | solution.py:144
  75.1 1.6 stack.10
  76.7 1.2 copy.88
  77.9 0.4 copy-done.1
  78.3 2.2 %pad_maximum_fusion = f32[2,8,512,128]{3,1,2,0:T(8,128)} fusion(f32[1,8,512,128]{3,1,2,0:T(8,128)S(1)} %copy.88, f32[1,8,512,128]{3,1,2,0:T(8,128)S(1)} %copy-done.1), kind=kLoop, calls=%fused_computation.1 | loop fusion | flops 1048576 | bytes 8388608 | tf_op jit(solution)/shard_map/stack | solution.py:161
  80.5 2.9 %gather_fusion = f32[128,2,8,128]{3,2,1,0:T(8,128)S(1)} fusion(f32[2,8,512,128]{3,1,2,0:T(8,128)} %pad_maximum_fusion, s32[1024]{0:T(1024)S(1)} %pad_clamp_fusion), kind=kCustom, calls=%fused_computation | custom fusion | bytes 2097664 | tf_op jit(solution)/shard_map/jit(_take)/gather | solution.py:162
  83.4 0.2 select_bitcast_fusion
  83.6 1.2 slice.82
  85.5 0.9 convolution_add_fusion
  86.4 2.6 %copy.90 = f32[128,2,2,8,128]{4,3,2,1,0:T(8,128)} copy(f32[128,2,2,8,128]{4,0,3,2,1:T(8,128)S(1)} %convolution_add_fusion) | data formatting | bytes 4194304 | tf_op jit(solution)/shard_map/add | solution.py:169
  89.0 9.8 %all-to-all-start.2 = ((f32[128,2,2,8,128]{4,3,2,1,0:T(8,128)}), f32[128,2,2,8,128]{4,3,2,1,0:T(8,128)S(1)}, u32[]{:S(2)}, u32[]{:S(2)}) async-start(f32[128,2,2,8,128]{4,3,2,1,0:T(8,128)} %copy.90), calls=%async_computation.2 | async-start | bytes 4194304 | tf_op jit(solution)/shard_map/all_to_all | solution.py:170
  99.8 0.7 convert_add_fusion.1.factor_ref
  100.6 1.0 fusion.48
  101.5 3.1 %collective-permute-start.4 = (f32[8,384]{1,0:T(8,128)S(1)}, f32[8,384]{1,0:T(8,128)S(1)}, u32[]{:S(2)}, u32[]{:S(2)}) collective-permute-start(f32[8,384]{1,0:T(8,128)S(1)} %bitcast.87), channel_id=1, source_target_pairs={{0,8},{8,16},{16,24},{24,32},{32,40},{40,48},{48,56},{56,64},{64,7... | collective-permute-start | bytes 36872 | tf_op jit(solution)/shard_map/ppermute | solution.py:112
  104.7 4.3 %collective-permute-start.5 = (f32[8,384]{1,0:T(8,128)S(1)}, f32[8,384]{1,0:T(8,128)S(1)}, u32[]{:S(2)}, u32[]{:S(2)}) collective-permute-start(f32[8,384]{1,0:T(8,128)S(1)} %bitcast.88), channel_id=1, source_target_pairs={{8,0},{16,8},{24,16},{32,24},{40,32},{48,40},{56,48},{64,56},{72,6... | collective-permute-start | bytes 36872 | tf_op jit(solution)/shard_map/ppermute | solution.py:112
  108.9 1.4 fusion.47
  110.4 0.8 copy.107
  111.2 4.0 %collective-permute-start.6 = (f32[128,8]{1,0:T(8,128)S(1)}, f32[128,8]{1,0:T(8,128)S(1)}, u32[]{:S(2)}, u32[]{:S(2)}) collective-permute-start(f32[128,8]{1,0:T(8,128)S(1)} %bitcast.80), channel_id=1, source_target_pairs={{0,1},{1,2},{2,3},{3,4},{4,5},{5,6},{6,7},{8,9},{9,10},{10,11},{11... | collective-permute-start | bytes 12296 | tf_op jit(solution)/shard_map/ppermute | solution.py:112
  115.2 0.8 copy.108
  116.0 1.9 %collective-permute-start.7 = (f32[128,8]{1,0:T(8,128)S(1)}, f32[128,8]{1,0:T(8,128)S(1)}, u32[]{:S(2)}, u32[]{:S(2)}) collective-permute-start(f32[128,8]{1,0:T(8,128)S(1)} %bitcast.81), channel_id=1, source_target_pairs={{1,0},{2,1},{3,2},{4,3},{5,4},{6,5},{7,6},{9,8},{10,9},{11,10},{12... | collective-permute-start | bytes 12296 | tf_op jit(solution)/shard_map/ppermute | solution.py:112
  118.0 9.8 %all-to-all-done.2 = f32[128,2,2,8,128]{4,3,2,1,0:T(8,128)S(1)} async-done(((f32[128,2,2,8,128]{4,3,2,1,0:T(8,128)}), f32[128,2,2,8,128]{4,3,2,1,0:T(8,128)S(1)}, u32[]{:S(2)}, u32[]{:S(2)}) %all-to-all-start.2) | async-done | bytes 2097184 | tf_op jit(solution)/shard_map/all_to_all | solution.py:170
  127.7 2.0 %fusion.9 = f32[2,8,128,128]{2,3,0,1:T(8,128)S(1)} fusion(f32[128,2,2,8,128]{4,3,2,1,0:T(8,128)S(1)} %all-to-all-done.2, s32[128,2]{0,1:T(2,128)S(1)} %broadcast_select_fusion), kind=kOutput, calls=%fused_computation.21 | convolution fusion | flops 402685952 | bytes 3146752 | tf_op jit(solution)/shard_map/tqs,qsald->altd/dot_general | solution.py:180
  129.8 3.1 %fusion.12.bound_ref = f32[2,8,128,384]{3,2,1,0:T(8,128)} fusion(f32[2,8,128,128]{2,3,0,1:T(8,128)S(1)} %fusion.9, f32[128]{0:T(128)S(1)} %iota_convert_fusion, f32[384]{0:T(512)S(1)} %add_clamp_fusion), kind=kOutput, calls=%fused_computation.22 | convolution fusion | flops 604176384 | bytes 4196352 | tf_op jit(solution)/shard_map/altd,de->alte/dot_general | solution.py:187
  132.9 0.8 broadcast_in_dim.69.divisor_ref
  133.7 6.0 %shard_map.104 = (f32[8,128,384]{2,1,0:T(8,128)}, f32[8,384]{1,0:T(8,128)}, f32[8,384]{1,0:T(8,128)}, f32[128,8]{1,0:T(8,128)}, f32[128,8]{1,0:T(8,128)}) custom-call(f32[2,8]{1,0:T(2,128)} %wind_ref.5, f32[8,128,384]{2,1,0:T(8,128)} %bitcast.15.child_ref, f32[8,384]{1,0:T(8,128)} %copy-done.13, f32[8,384]{1,0:T(8,128)} %copy-done.14, f32[128,8]{1,0:T(8,128)} %copy-done.5, ...), custom_call_target="tpu_custom_call" | custom-call | flops 11796480 | bytes 6684672 | tf_op jit(solution)/shard_map/pallas_call | solution.py:90
  139.7 2.5 %collective-permute-start.8 = (f32[8,384]{1,0:T(8,128)}, f32[8,384]{1,0:T(8,128)S(1)}, u32[]{:S(2)}, u32[]{:S(2)}) collective-permute-start(f32[8,384]{1,0:T(8,128)} %get-tuple-element.14), channel_id=1, source_target_pairs={{0,8},{8,16},{16,24},{24,32},{32,40},{40,48},{48,56},{56,64},{64,7... | collective-permute-start | bytes 36872 | tf_op jit(solution)/shard_map/ppermute | solution.py:112
  142.2 4.9 %collective-permute-start.9 = (f32[8,384]{1,0:T(8,128)}, f32[8,384]{1,0:T(8,128)S(1)}, u32[]{:S(2)}, u32[]{:S(2)}) collective-permute-start(f32[8,384]{1,0:T(8,128)} %get-tuple-element.15), channel_id=1, source_target_pairs={{8,0},{16,8},{24,16},{32,24},{40,32},{48,40},{56,48},{64,56},{72,6... | collective-permute-start | bytes 36872 | tf_op jit(solution)/shard_map/ppermute | solution.py:112
  147.1 2.3 %collective-permute-start.10 = (f32[128,8]{1,0:T(8,128)}, f32[128,8]{1,0:T(8,128)S(1)}, u32[]{:S(2)}, u32[]{:S(2)}) collective-permute-start(f32[128,8]{1,0:T(8,128)} %get-tuple-element.16), channel_id=1, source_target_pairs={{0,1},{1,2},{2,3},{3,4},{4,5},{5,6},{6,7},{8,9},{9,10},{10,11},{11... | collective-permute-start | bytes 12296 | tf_op jit(solution)/shard_map/ppermute | solution.py:112
  149.4 2.9 %collective-permute-start.11 = (f32[128,8]{1,0:T(8,128)}, f32[128,8]{1,0:T(8,128)S(1)}, u32[]{:S(2)}, u32[]{:S(2)}) collective-permute-start(f32[128,8]{1,0:T(8,128)} %get-tuple-element.17), channel_id=1, source_target_pairs={{1,0},{2,1},{3,2},{4,3},{5,4},{6,5},{7,6},{9,8},{10,9},{11,10},{12... | collective-permute-start | bytes 12296 | tf_op jit(solution)/shard_map/ppermute | solution.py:112
  152.4 2.8 %collective-permute-done.11.ay_ref = f32[128,8]{1,0:T(8,128)S(1)} collective-permute-done((f32[128,8]{1,0:T(8,128)}, f32[128,8]{1,0:T(8,128)S(1)}, u32[]{:S(2)}, u32[]{:S(2)}) %collective-permute-start.11) | collective-permute-done | bytes 4128 | tf_op jit(solution)/shard_map/ppermute | solution.py:112
  155.3 0.6 copy-done.10
  155.9 6.0 %shard_map.105 = (f32[8,128,384]{2,1,0:T(8,128)}, f32[8,384]{1,0:T(8,128)}, f32[8,384]{1,0:T(8,128)}, f32[128,8]{1,0:T(8,128)}, f32[128,8]{1,0:T(8,128)}) custom-call(f32[2,8]{1,0:T(2,128)} %wind_ref.5, f32[8,128,384]{2,1,0:T(8,128)} %get-tuple-element.13.child_ref, f32[8,384]{1,0:T(8,128)} %copy-done.16, f32[8,384]{1,0:T(8,128)} %copy-done.18, ...), custom_call_target="tpu_custom_call" | custom-call | flops 11796480 | bytes 6684672 | tf_op jit(solution)/shard_map/pallas_call | solution.py:90
  161.9 1.9 %collective-permute-start.12 = (f32[8,384]{1,0:T(8,128)}, f32[8,384]{1,0:T(8,128)S(1)}, u32[]{:S(2)}, u32[]{:S(2)}) collective-permute-start(f32[8,384]{1,0:T(8,128)} %get-tuple-element.19), channel_id=1, source_target_pairs={{0,8},{8,16},{16,24},{24,32},{32,40},{40,48},{48,56},{56,64},{64,7... | collective-permute-start | bytes 36872 | tf_op jit(solution)/shard_map/ppermute | solution.py:112
  163.8 5.5 %collective-permute-start.13 = (f32[8,384]{1,0:T(8,128)}, f32[8,384]{1,0:T(8,128)S(1)}, u32[]{:S(2)}, u32[]{:S(2)}) collective-permute-start(f32[8,384]{1,0:T(8,128)} %get-tuple-element.20), channel_id=1, source_target_pairs={{8,0},{16,8},{24,16},{32,24},{40,32},{48,40},{56,48},{64,56},{72,6... | collective-permute-start | bytes 36872 | tf_op jit(solution)/shard_map/ppermute | solution.py:112
  169.3 2.5 %collective-permute-start.14 = (f32[128,8]{1,0:T(8,128)}, f32[128,8]{1,0:T(8,128)S(1)}, u32[]{:S(2)}, u32[]{:S(2)}) collective-permute-start(f32[128,8]{1,0:T(8,128)} %get-tuple-element.21), channel_id=1, source_target_pairs={{0,1},{1,2},{2,3},{3,4},{4,5},{5,6},{6,7},{8,9},{9,10},{10,11},{11... | collective-permute-start | bytes 12296 | tf_op jit(solution)/shard_map/ppermute | solution.py:112
  171.8 1.9 %collective-permute-start.15 = (f32[128,8]{1,0:T(8,128)}, f32[128,8]{1,0:T(8,128)S(1)}, u32[]{:S(2)}, u32[]{:S(2)}) collective-permute-start(f32[128,8]{1,0:T(8,128)} %get-tuple-element.22), channel_id=1, source_target_pairs={{1,0},{2,1},{3,2},{4,3},{5,4},{6,5},{7,6},{9,8},{10,9},{11,10},{12... | collective-permute-start | bytes 12296 | tf_op jit(solution)/shard_map/ppermute | solution.py:112
  173.7 3.8 %collective-permute-done.15.ay_ref = f32[128,8]{1,0:T(8,128)S(1)} collective-permute-done((f32[128,8]{1,0:T(8,128)}, f32[128,8]{1,0:T(8,128)S(1)}, u32[]{:S(2)}, u32[]{:S(2)}) %collective-permute-start.15) | collective-permute-done | bytes 4128 | tf_op jit(solution)/shard_map/ppermute | solution.py:112
  177.6 0.6 copy-done.9
  178.2 6.0 %shard_map.106 = (f32[8,128,384]{2,1,0:T(8,128)}, f32[8,384]{1,0:T(8,128)}, f32[8,384]{1,0:T(8,128)}, f32[128,8]{1,0:T(8,128)}, f32[128,8]{1,0:T(8,128)}) custom-call(f32[2,8]{1,0:T(2,128)} %wind_ref.5, f32[8,128,384]{2,1,0:T(8,128)} %get-tuple-element.18.child_ref, f32[8,384]{1,0:T(8,128)} %copy-done.15, f32[8,384]{1,0:T(8,128)} %copy-done.17, ...), custom_call_target="tpu_custom_call" | custom-call | flops 11796480 | bytes 6684672 | tf_op jit(solution)/shard_map/pallas_call | solution.py:90
  (86 shorter events, 1.6 us)
Async XLA Ops:
  0.6 7.8 %copy-start = (f32[8,128,512]{2,1,0:T(8,128)S(1)}, f32[8,128,512]{2,1,0:T(8,128)}, u32[]{:S(2)}) copy-start(f32[8,128,512]{2,1,0:T(8,128)} %param.9) | copy-start | bytes 6291460
  2.2 23.0 %copy-start.22 = (s32[2,4]{1,0:T(2,128)S(1)}, s32[2,4]{1,0:T(2,128)}, u32[]{:S(2)}) copy-start(s32[2,4]{1,0:T(2,128)} %param.17) | copy-start | bytes 100
  2.4 28.0 %copy-start.4 = (s32[16384,1]{0,1:T(1,128)S(1)}, s32[16384,1]{0,1:T(1,128)}, u32[]{:S(2)}) copy-start(s32[16384,1]{0,1:T(1,128)} %param.14) | copy-start | bytes 196612
  2.4 29.3 %copy-start.12 = (f32[2,8]{1,0:T(2,128)S(1)}, f32[2,8]{1,0:T(2,128)}, u32[]{:S(2)}) copy-start(f32[2,8]{1,0:T(2,128)} %wind_ref.5) | copy-start | bytes 196
  2.4 29.9 %copy-start.2 = (bf16[128,512]{1,0:T(8,128)(2,1)S(1)}, bf16[128,512]{1,0:T(8,128)(2,1)}, u32[]{:S(2)}) copy-start(bf16[128,512]{1,0:T(8,128)(2,1)} %param.10) | copy-start | bytes 393220
  2.4 65.0 %collective-permute-start.3 = (f32[8,128]{1,0:T(8,128)S(1)}, f32[8,128]{1,0:T(8,128)S(1)}, u32[]{:S(2)}, u32[]{:S(2)}) collective-permute-start(f32[8,128]{1,0:T(8,128)S(1)} %bitcast.89), channel_id=1, source_target_pairs={{0,1},{1,2},{2,3},{3,4},{4,5},{5,6},{6,7},{8,9},{9,10},{10,11},{11... | collective-permute-start | bytes 12296 | tf_op jit(solution)/shard_map/ppermute | solution.py:25
  6.5 61.2 %collective-permute-start.2 = (f32[8,128]{1,0:T(8,128)S(1)}, f32[8,128]{1,0:T(8,128)S(1)}, u32[]{:S(2)}, u32[]{:S(2)}) collective-permute-start(f32[8,128]{1,0:T(8,128)S(1)} %bitcast.91), channel_id=1, source_target_pairs={{1,0},{2,1},{3,2},{4,3},{5,4},{6,5},{7,6},{9,8},{10,9},{11,10},{12... | collective-permute-start | bytes 12296 | tf_op jit(solution)/shard_map/ppermute | solution.py:25
  8.5 59.4 %collective-permute-start.1 = (f32[8,512]{1,0:T(8,128)S(1)}, f32[8,512]{1,0:T(8,128)S(1)}, u32[]{:S(2)}, u32[]{:S(2)}) collective-permute-start(f32[8,512]{1,0:T(8,128)S(1)} %bitcast.83), channel_id=1, source_target_pairs={{0,8},{8,16},{16,24},{24,32},{32,40},{40,48},{48,56},{56,64},{64,7... | collective-permute-start | bytes 49160 | tf_op jit(solution)/shard_map/ppermute | solution.py:25
  11.6 56.3 %collective-permute-start = (f32[8,512]{1,0:T(8,128)S(1)}, f32[8,512]{1,0:T(8,128)S(1)}, u32[]{:S(2)}, u32[]{:S(2)}) collective-permute-start(f32[8,512]{1,0:T(8,128)S(1)} %bitcast.85), channel_id=1, source_target_pairs={{8,0},{16,8},{24,16},{32,24},{40,32},{48,40},{56,48},{64,56},{72,6... | collective-permute-start | bytes 49160 | tf_op jit(solution)/shard_map/ppermute | solution.py:25
  15.9 32.3 %all-to-all-start = ((f32[128,8,384]{2,1,0:T(8,128)}), f32[128,8,384]{2,1,0:T(8,128)}, u32[]{:S(2)}, u32[]{:S(2)}) async-start(f32[128,8,384]{2,1,0:T(8,128)} %bitcast.76), calls=%async_computation | async-start | bytes 3145728 | tf_op jit(solution)/shard_map/all_to_all | solution.py:51
  51.3 32.3 %all-to-all-start.1 = ((f32[128,8,384]{2,1,0:T(8,128)}), f32[128,8,384]{2,1,0:T(8,128)}, u32[]{:S(2)}, u32[]{:S(2)}) async-start(f32[128,8,384]{2,1,0:T(8,128)} %bitcast.75), calls=%async_computation.1 | async-start | bytes 3145728 | tf_op jit(solution)/shard_map/all_to_all | solution.py:56
  63.3 4.7 %copy-start.19 = (f32[8]{0:T(128)S(1)}, f32[8]{0:T(128)}, u32[]{:S(2)}) copy-start(f32[8]{0:T(128)} %get-tuple-element.44) | copy-start | bytes 100
  76.7 1.6 copy-start.1
  80.5 2.9 %copy-start.23 = (pred[128]{0:T(512)(128)(4,1)S(1)}, pred[128]{0:T(512)(128)(4,1)}, u32[]{:S(2)}) copy-start(pred[128]{0:T(512)(128)(4,1)} %compare_and_fusion) | copy-start | bytes 388
  80.5 5.0 %copy-start.20 = (s32[128]{0:T(128)S(1)}, s32[128]{0:T(128)}, u32[]{:S(2)}) copy-start(s32[128]{0:T(128)} %fusion.36) | copy-start | bytes 1540
  80.5 5.0 %copy-start.21 = (s32[128,2]{0,1:T(2,128)S(1)}, s32[128,2]{0,1:T(2,128)}, u32[]{:S(2)}) copy-start(s32[128,2]{0,1:T(2,128)} %multiply_add_fusion) | copy-start | bytes 3076
  89.0 10.3 %copy-start.11 = (s32[16384]{0:T(1024)S(1)}, s32[16384]{0:T(1024)}, u32[]{:S(2)}) copy-start(s32[16384]{0:T(1024)} %param.16) | copy-start | bytes 196612
  89.0 10.8 %copy-start.3 = (bf16[128,384]{1,0:T(8,128)(2,1)S(1)}, bf16[128,384]{1,0:T(8,128)(2,1)}, u32[]{:S(2)}) copy-start(bf16[128,384]{1,0:T(8,128)(2,1)} %param.12) | copy-start | bytes 294916
  89.0 38.7 %all-to-all-start.2 = ((f32[128,2,2,8,128]{4,3,2,1,0:T(8,128)}), f32[128,2,2,8,128]{4,3,2,1,0:T(8,128)S(1)}, u32[]{:S(2)}, u32[]{:S(2)}) async-start(f32[128,2,2,8,128]{4,3,2,1,0:T(8,128)} %copy.90), calls=%async_computation.2 | async-start | bytes 4194304 | tf_op jit(solution)/shard_map/all_to_all | solution.py:170
  101.5 31.4 %collective-permute-start.4 = (f32[8,384]{1,0:T(8,128)S(1)}, f32[8,384]{1,0:T(8,128)S(1)}, u32[]{:S(2)}, u32[]{:S(2)}) collective-permute-start(f32[8,384]{1,0:T(8,128)S(1)} %bitcast.87), channel_id=1, source_target_pairs={{0,8},{8,16},{16,24},{24,32},{32,40},{40,48},{48,56},{56,64},{64,7... | collective-permute-start | bytes 36872 | tf_op jit(solution)/shard_map/ppermute | solution.py:112
  104.7 28.3 %collective-permute-start.5 = (f32[8,384]{1,0:T(8,128)S(1)}, f32[8,384]{1,0:T(8,128)S(1)}, u32[]{:S(2)}, u32[]{:S(2)}) collective-permute-start(f32[8,384]{1,0:T(8,128)S(1)} %bitcast.88), channel_id=1, source_target_pairs={{8,0},{16,8},{24,16},{32,24},{40,32},{48,40},{56,48},{64,56},{72,6... | collective-permute-start | bytes 36872 | tf_op jit(solution)/shard_map/ppermute | solution.py:112
  111.2 21.7 %collective-permute-start.6 = (f32[128,8]{1,0:T(8,128)S(1)}, f32[128,8]{1,0:T(8,128)S(1)}, u32[]{:S(2)}, u32[]{:S(2)}) collective-permute-start(f32[128,8]{1,0:T(8,128)S(1)} %bitcast.80), channel_id=1, source_target_pairs={{0,1},{1,2},{2,3},{3,4},{4,5},{5,6},{6,7},{8,9},{9,10},{10,11},{11... | collective-permute-start | bytes 12296 | tf_op jit(solution)/shard_map/ppermute | solution.py:112
  116.0 16.9 %collective-permute-start.7 = (f32[128,8]{1,0:T(8,128)S(1)}, f32[128,8]{1,0:T(8,128)S(1)}, u32[]{:S(2)}, u32[]{:S(2)}) collective-permute-start(f32[128,8]{1,0:T(8,128)S(1)} %bitcast.81), channel_id=1, source_target_pairs={{1,0},{2,1},{3,2},{4,3},{5,4},{6,5},{7,6},{9,8},{10,9},{11,10},{12... | collective-permute-start | bytes 12296 | tf_op jit(solution)/shard_map/ppermute | solution.py:112
  132.9 0.8 copy-start.5
  132.9 0.8 copy-start.6
  132.9 0.8 copy-start.13
  132.9 0.8 copy-start.14
  139.7 15.6 %collective-permute-start.8 = (f32[8,384]{1,0:T(8,128)}, f32[8,384]{1,0:T(8,128)S(1)}, u32[]{:S(2)}, u32[]{:S(2)}) collective-permute-start(f32[8,384]{1,0:T(8,128)} %get-tuple-element.14), channel_id=1, source_target_pairs={{0,8},{8,16},{16,24},{24,32},{32,40},{40,48},{48,56},{56,64},{64,7... | collective-permute-start | bytes 36872 | tf_op jit(solution)/shard_map/ppermute | solution.py:112
  142.2 13.1 %collective-permute-start.9 = (f32[8,384]{1,0:T(8,128)}, f32[8,384]{1,0:T(8,128)S(1)}, u32[]{:S(2)}, u32[]{:S(2)}) collective-permute-start(f32[8,384]{1,0:T(8,128)} %get-tuple-element.15), channel_id=1, source_target_pairs={{8,0},{16,8},{24,16},{32,24},{40,32},{48,40},{56,48},{64,56},{72,6... | collective-permute-start | bytes 36872 | tf_op jit(solution)/shard_map/ppermute | solution.py:112
  147.1 5.3 %collective-permute-start.10 = (f32[128,8]{1,0:T(8,128)}, f32[128,8]{1,0:T(8,128)S(1)}, u32[]{:S(2)}, u32[]{:S(2)}) collective-permute-start(f32[128,8]{1,0:T(8,128)} %get-tuple-element.16), channel_id=1, source_target_pairs={{0,1},{1,2},{2,3},{3,4},{4,5},{5,6},{6,7},{8,9},{9,10},{10,11},{11... | collective-permute-start | bytes 12296 | tf_op jit(solution)/shard_map/ppermute | solution.py:112
  149.4 5.8 %collective-permute-start.11 = (f32[128,8]{1,0:T(8,128)}, f32[128,8]{1,0:T(8,128)S(1)}, u32[]{:S(2)}, u32[]{:S(2)}) collective-permute-start(f32[128,8]{1,0:T(8,128)} %get-tuple-element.17), channel_id=1, source_target_pairs={{1,0},{2,1},{3,2},{4,3},{5,4},{6,5},{7,6},{9,8},{10,9},{11,10},{12... | collective-permute-start | bytes 12296 | tf_op jit(solution)/shard_map/ppermute | solution.py:112
  152.4 2.9 %copy-start.8 = (f32[128,8]{1,0:T(8,128)}, f32[128,8]{1,0:T(8,128)S(1)}, u32[]{:S(2)}) copy-start(f32[128,8]{1,0:T(8,128)S(1)} %collective-permute-done.10.by_ref) | copy-start | bytes 12292
  155.2 0.6 copy-start.10
  155.2 0.6 copy-start.16
  155.2 0.6 copy-start.18
  161.9 15.7 %collective-permute-start.12 = (f32[8,384]{1,0:T(8,128)}, f32[8,384]{1,0:T(8,128)S(1)}, u32[]{:S(2)}, u32[]{:S(2)}) collective-permute-start(f32[8,384]{1,0:T(8,128)} %get-tuple-element.19), channel_id=1, source_target_pairs={{0,8},{8,16},{16,24},{24,32},{32,40},{40,48},{48,56},{56,64},{64,7... | collective-permute-start | bytes 36872 | tf_op jit(solution)/shard_map/ppermute | solution.py:112
  163.8 13.8 %collective-permute-start.13 = (f32[8,384]{1,0:T(8,128)}, f32[8,384]{1,0:T(8,128)S(1)}, u32[]{:S(2)}, u32[]{:S(2)}) collective-permute-start(f32[8,384]{1,0:T(8,128)} %get-tuple-element.20), channel_id=1, source_target_pairs={{8,0},{16,8},{24,16},{32,24},{40,32},{48,40},{56,48},{64,56},{72,6... | collective-permute-start | bytes 36872 | tf_op jit(solution)/shard_map/ppermute | solution.py:112
  169.3 4.5 %collective-permute-start.14 = (f32[128,8]{1,0:T(8,128)}, f32[128,8]{1,0:T(8,128)S(1)}, u32[]{:S(2)}, u32[]{:S(2)}) collective-permute-start(f32[128,8]{1,0:T(8,128)} %get-tuple-element.21), channel_id=1, source_target_pairs={{0,1},{1,2},{2,3},{3,4},{4,5},{5,6},{6,7},{8,9},{9,10},{10,11},{11... | collective-permute-start | bytes 12296 | tf_op jit(solution)/shard_map/ppermute | solution.py:112
  171.8 5.8 %collective-permute-start.15 = (f32[128,8]{1,0:T(8,128)}, f32[128,8]{1,0:T(8,128)S(1)}, u32[]{:S(2)}, u32[]{:S(2)}) collective-permute-start(f32[128,8]{1,0:T(8,128)} %get-tuple-element.22), channel_id=1, source_target_pairs={{1,0},{2,1},{3,2},{4,3},{5,4},{6,5},{7,6},{9,8},{10,9},{11,10},{12... | collective-permute-start | bytes 12296 | tf_op jit(solution)/shard_map/ppermute | solution.py:112
  173.7 3.9 %copy-start.7 = (f32[128,8]{1,0:T(8,128)}, f32[128,8]{1,0:T(8,128)S(1)}, u32[]{:S(2)}) copy-start(f32[128,8]{1,0:T(8,128)S(1)} %collective-permute-done.14.by_ref) | copy-start | bytes 12292
  177.6 0.6 copy-start.9
  177.6 0.6 copy-start.15
  177.6 0.6 copy-start.17

commit v15 on v14

--- a/solution.py
+++ b/solution.py
@@ -158,8 +158,9 @@
     rank = jnp.sum((same_owner & earlier).astype(jnp.int32), axis=1)
     slot_index = my_dest * CAP + rank
     send_select = (jnp.arange(devices * CAP)[:, None] == slot_index[None, :]).astype(jnp.float32)
-    both_states = jnp.stack([parent_field, new_parent]).reshape(2, levels, -1, STRIP)
-    picked = jnp.take(both_states, my_rows, axis=2)
+    picked = jnp.stack(
+        [jnp.take(state.reshape(levels, -1, STRIP), my_rows, axis=1) for state in (parent_field, new_parent)]
+    )
     outgoing_strips = jnp.einsum(
         "dsj,aljk->dsalk",
         send_select.reshape(devices, CAP, slots),

time: 185 us -> 189 us (1.022)
  local copies, waits for them, and re-layouts: 33.4 us -> 36.8 us
  other arithmetic: 17.6 us -> 15.6 us
    reshape x0 -> x4, local copies, waits for them, and re-layouts: none -> 9.7 us  [shards(): state.reshape(levels, -1, STRIP)]
    another operation x4 -> x0, local copies, waits for them, and re-layouts: 8.37 us -> none  [shards(): jnp.stack([parent_field, new_parent]).reshape(2, levels, -1, STRIP)]
    gather x1 -> x2, local copies, waits for them, and re-layouts: 2.87 us -> 5.27 us  [shards(): jnp.take(state.reshape(levels, -1, STRIP), my_rows, axis=1)]
  transfers between devices with their start and end apart: 19 -> 19, of which waited for: 4 -> 4; matrix products, arithmetic and copies ran while one was open for 26% -> 27% of each run, Pallas kernels for 0% -> 0%
where the time goes in v15:
time: 189 us; the launch traced here: 188 us
  starting transfers between devices  77 us (41%)
  local copies, waits for them, and re-layouts  36.8 us (19%)
  waiting for transfers between devices  27.8 us (15%)
  Pallas kernels  17.9 us (9%)
  other arithmetic  15.6 us (8%)
  matrix products  6.94 us (4%)
  between operations  5.83 us (3%)
    ppermute x12, starting transfers between devices, swap_edge(): return lax.ppermute(edge, axis, pairs)  37.8 us
    pallas_call x3, Pallas kernels, substep(): pl.pallas_call(functools.partial(substep_kernel, weight), out_shape=(jax....  17.9 us
    ppermute x4, starting transfers between devices, swap(): return lax.ppermute(edge, axis, pairs)  13.2 us
    all_to_all x1, waiting for transfers between devices, storm_rows(): gathered = lax.all_to_all(pieces, ('gx', 'gy'), 0, 0, tiled=True)  11.3 us
    all_to_all x1, waiting for transfers between devices, shards(): lax.all_to_all(outgoing_strips, ('gx', 'gy'), split_axis=0, concat_axis=0...  9.79 us
    all_to_all x1, starting transfers between devices, shards(): lax.all_to_all(outgoing_strips, ('gx', 'gy'), split_axis=0, concat_axis=0...  9.76 us
    reshape x4, local copies, waits for them, and re-layouts, shards(): state.reshape(levels, -1, STRIP)  9.7 us
    all_to_all x1, starting transfers between devices, storm_rows(): gathered = lax.all_to_all(pieces, ('gx', 'gy'), 0, 0, tiled=True)  9.25 us
  transfers between devices with their start and end apart: 19, of which 4 were waited for; matrix products, arithmetic and copies ran while one was open for 27% of the time, Pallas kernels for 0%

profile of v15, /device:TPU:33, one launch (start us, length us, event | category | flops | bytes accessed | tf_op | source)
XLA Modules:
  0.0 187.9 jit_solution(12144142933051642252)
XLA Ops:
  0.6 1.6 fusion.47
  2.2 0.2 copy.107
  2.4 3.9 %collective-permute-start.3 = (f32[8,128]{1,0:T(8,128)S(1)}, f32[8,128]{1,0:T(8,128)S(1)}, u32[]{:S(2)}, u32[]{:S(2)}) collective-permute-start(f32[8,128]{1,0:T(8,128)S(1)} %bitcast.94), channel_id=1, source_target_pairs={{0,1},{1,2},{2,3},{3,4},{4,5},{5,6},{6,7},{8,9},{9,10},{10,11},{11... | collective-permute-start | bytes 12296 | tf_op jit(solution)/shard_map/ppermute | solution.py:25
  6.3 0.2 copy.106
  6.5 1.9 %collective-permute-start.2 = (f32[8,128]{1,0:T(8,128)S(1)}, f32[8,128]{1,0:T(8,128)S(1)}, u32[]{:S(2)}, u32[]{:S(2)}) collective-permute-start(f32[8,128]{1,0:T(8,128)S(1)} %bitcast.96), channel_id=1, source_target_pairs={{1,0},{2,1},{3,2},{4,3},{5,4},{6,5},{7,6},{9,8},{10,9},{11,10},{12... | collective-permute-start | bytes 12296 | tf_op jit(solution)/shard_map/ppermute | solution.py:25
  8.5 3.1 %collective-permute-start.1 = (f32[8,512]{1,0:T(8,128)S(1)}, f32[8,512]{1,0:T(8,128)S(1)}, u32[]{:S(2)}, u32[]{:S(2)}) collective-permute-start(f32[8,512]{1,0:T(8,128)S(1)} %bitcast.88), channel_id=1, source_target_pairs={{0,8},{8,16},{16,24},{24,32},{32,40},{40,48},{48,56},{56,64},{64,7... | collective-permute-start | bytes 49160 | tf_op jit(solution)/shard_map/ppermute | solution.py:25
  11.6 4.3 %collective-permute-start = (f32[8,512]{1,0:T(8,128)S(1)}, f32[8,512]{1,0:T(8,128)S(1)}, u32[]{:S(2)}, u32[]{:S(2)}) collective-permute-start(f32[8,512]{1,0:T(8,128)S(1)} %bitcast.90), channel_id=1, source_target_pairs={{8,0},{16,8},{24,16},{32,24},{40,32},{48,40},{56,48},{64,56},{72,6... | collective-permute-start | bytes 49160 | tf_op jit(solution)/shard_map/ppermute | solution.py:25
  15.9 9.2 %all-to-all-start = ((f32[128,8,384]{2,1,0:T(8,128)}), f32[128,8,384]{2,1,0:T(8,128)}, u32[]{:S(2)}, u32[]{:S(2)}) async-start(f32[128,8,384]{2,1,0:T(8,128)} %bitcast.81), calls=%async_computation | async-start | bytes 3145728 | tf_op jit(solution)/shard_map/all_to_all | solution.py:51
  25.4 0.5 fusion.38
  25.9 0.6 constant_dynamic-slice_fusion.2
  30.4 0.6 multiply_bitcast_fusion.1
  31.0 0.8 fusion.48
  31.8 2.4 %fusion.49 = (f32[7,128,512]{2,1,0:T(8,128)}, f32[7,128,512]{2,1,0:T(8,128)}) fusion(f32[8,128,512]{2,1,0:T(8,128)S(1)} %copy-done), kind=kLoop, calls=%fused_computation.91 | loop fusion | bytes 7340032 | tf_op jit(solution)/shard_map/slice | solution.py:124
  34.2 2.7 %fusion.46 = (f32[8,128,511]{2,1,0:T(8,128)}, f32[8,128,511]{2,1,0:T(8,128)}) fusion(f32[8,128,512]{2,1,0:T(8,128)S(1)} %copy-done), kind=kLoop, calls=%fused_computation.88 | loop fusion | bytes 8372224 | tf_op jit(solution)/shard_map/slice | solution.py:38
  37.0 11.3 %all-to-all-done = f32[128,8,384]{2,1,0:T(8,128)} async-done(((f32[128,8,384]{2,1,0:T(8,128)}), f32[128,8,384]{2,1,0:T(8,128)}, u32[]{:S(2)}, u32[]{:S(2)}) %all-to-all-start) | async-done | bytes 1572896 | tf_op jit(solution)/shard_map/all_to_all | solution.py:51
  48.2 1.7 fusion.8
  50.0 1.4 fusion.7
  51.4 7.0 %all-to-all-start.1 = ((f32[128,8,384]{2,1,0:T(8,128)}), f32[128,8,384]{2,1,0:T(8,128)}, u32[]{:S(2)}, u32[]{:S(2)}) async-start(f32[128,8,384]{2,1,0:T(8,128)} %bitcast.80), calls=%async_computation.1 | async-start | bytes 3145728 | tf_op jit(solution)/shard_map/all_to_all | solution.py:56
  58.3 1.3 compare_and_fusion
  59.6 2.5 %fusion.44 = (f32[8,127,512]{2,1,0:T(8,128)}, f32[8,127,512]{2,1,0:T(8,128)}) fusion(f32[8,128,512]{2,1,0:T(8,128)S(1)} %copy-done), kind=kLoop, calls=%fused_computation.86 | loop fusion | bytes 8323072 | tf_op jit(solution)/shard_map/slice | solution.py:36
  62.1 0.6 multiply_add_fusion
  62.7 1.4 reshape.121
  64.1 4.1 %copy.89 = f32[8,512,128]{2,0,1:T(8,128)} copy(f32[8,512,128]{2,1,0:T(8,128)} %reshape.121) | data formatting | bytes 4194304 | tf_op jit(solution)/shard_map/reshape | solution.py:162
  68.2 3.0 %gather_fusion = f32[128,8,128]{2,1,0:T(8,128)} fusion(f32[8,512,128]{2,0,1:T(8,128)} %copy.89, s32[1024]{0:T(1024)S(1)} %pad_clamp_fusion), kind=kCustom, calls=%fused_computation.clone | custom fusion | bytes 1049088 | tf_op jit(solution)/shard_map/jit(_take)/gather | solution.py:162
  71.2 0.2 copy.84
  71.5 0.2 copy.82
  71.8 7.0 %fusion.4 = f32[8,128,512]{2,1,0:T(8,128)} fusion(f32[8,128,512]{2,1,0:T(8,128)S(1)} %copy-done, f32[1,128,512]{2,1,0:T(8,128)} %get-tuple-element.38, f32[7,128,512]{2,1,0:T(8,128)} %get-tuple-element.40, f32[7,128,512]{2,1,0:T(8,128)} %get-tuple-element.39, f32[1,128,512]{2,1,0:T(8,128)} %get-tuple-element.37, f32[8,128,511]{2,1,0:T(8,128)} %get-tuple-element.34, ...), kind=kLoop, calls=%fused_computation.15 | loop fusion | flops 13107200 | bytes 17039424 | tf_op jit(solution)/shard_map/add | solution.py:144
  78.8 1.6 reshape.123
  80.5 2.6 %copy.91 = f32[8,512,128]{2,0,1:T(8,128)} copy(f32[8,512,128]{2,1,0:T(8,128)S(1)} %reshape.123) | data formatting | bytes 4194304 | tf_op jit(solution)/shard_map/reshape | solution.py:162
  83.1 2.2 %gather_fusion.1 = f32[128,8,128]{2,1,0:T(8,128)S(1)} fusion(f32[8,512,128]{2,0,1:T(8,128)} %copy.91, s32[1024]{0:T(1024)S(1)} %pad_clamp_fusion), kind=kCustom, calls=%fused_computation.1.clone | custom fusion | bytes 1049088 | tf_op jit(solution)/shard_map/jit(_take)/gather | solution.py:162
  85.3 1.1 fusion.17
  86.4 1.2 slice.84
  88.3 1.8 convolution_add_fusion
  90.1 2.6 %copy.93 = f32[128,2,2,8,128]{4,3,2,1,0:T(8,128)} copy(f32[128,2,2,8,128]{4,0,3,2,1:T(8,128)S(1)} %convolution_add_fusion) | data formatting | bytes 4194304 | tf_op jit(solution)/shard_map/add | solution.py:170
  92.7 9.8 %all-to-all-start.2 = ((f32[128,2,2,8,128]{4,3,2,1,0:T(8,128)}), f32[128,2,2,8,128]{4,3,2,1,0:T(8,128)S(1)}, u32[]{:S(2)}, u32[]{:S(2)}) async-start(f32[128,2,2,8,128]{4,3,2,1,0:T(8,128)} %copy.93), calls=%async_computation.2 | async-start | bytes 4194304 | tf_op jit(solution)/shard_map/all_to_all | solution.py:171
  102.6 0.2 reduce_window_sum.11
  103.5 0.7 convert_add_fusion.1.factor_ref
  104.2 1.0 fusion.51
  105.2 3.1 %collective-permute-start.4 = (f32[8,384]{1,0:T(8,128)S(1)}, f32[8,384]{1,0:T(8,128)S(1)}, u32[]{:S(2)}, u32[]{:S(2)}) collective-permute-start(f32[8,384]{1,0:T(8,128)S(1)} %bitcast.92), channel_id=1, source_target_pairs={{0,8},{8,16},{16,24},{24,32},{32,40},{40,48},{48,56},{56,64},{64,7... | collective-permute-start | bytes 36872 | tf_op jit(solution)/shard_map/ppermute | solution.py:112
  108.3 4.3 %collective-permute-start.5 = (f32[8,384]{1,0:T(8,128)S(1)}, f32[8,384]{1,0:T(8,128)S(1)}, u32[]{:S(2)}, u32[]{:S(2)}) collective-permute-start(f32[8,384]{1,0:T(8,128)S(1)} %bitcast.93), channel_id=1, source_target_pairs={{8,0},{16,8},{24,16},{32,24},{40,32},{48,40},{56,48},{64,56},{72,6... | collective-permute-start | bytes 36872 | tf_op jit(solution)/shard_map/ppermute | solution.py:112
  112.6 1.4 fusion.50
  114.0 0.8 copy.110
  114.9 4.0 %collective-permute-start.6 = (f32[128,8]{1,0:T(8,128)S(1)}, f32[128,8]{1,0:T(8,128)S(1)}, u32[]{:S(2)}, u32[]{:S(2)}) collective-permute-start(f32[128,8]{1,0:T(8,128)S(1)} %bitcast.85), channel_id=1, source_target_pairs={{0,1},{1,2},{2,3},{3,4},{4,5},{5,6},{6,7},{8,9},{9,10},{10,11},{11... | collective-permute-start | bytes 12296 | tf_op jit(solution)/shard_map/ppermute | solution.py:112
  118.9 0.8 copy.111
  119.7 1.9 %collective-permute-start.7 = (f32[128,8]{1,0:T(8,128)S(1)}, f32[128,8]{1,0:T(8,128)S(1)}, u32[]{:S(2)}, u32[]{:S(2)}) collective-permute-start(f32[128,8]{1,0:T(8,128)S(1)} %bitcast.86), channel_id=1, source_target_pairs={{1,0},{2,1},{3,2},{4,3},{5,4},{6,5},{7,6},{9,8},{10,9},{11,10},{12... | collective-permute-start | bytes 12296 | tf_op jit(solution)/shard_map/ppermute | solution.py:112
  121.6 9.8 %all-to-all-done.2 = f32[128,2,2,8,128]{4,3,2,1,0:T(8,128)S(1)} async-done(((f32[128,2,2,8,128]{4,3,2,1,0:T(8,128)}), f32[128,2,2,8,128]{4,3,2,1,0:T(8,128)S(1)}, u32[]{:S(2)}, u32[]{:S(2)}) %all-to-all-start.2) | async-done | bytes 2097184 | tf_op jit(solution)/shard_map/all_to_all | solution.py:171
  131.4 2.0 %fusion.9 = f32[2,8,128,128]{2,3,0,1:T(8,128)S(1)} fusion(f32[128,2,2,8,128]{4,3,2,1,0:T(8,128)S(1)} %all-to-all-done.2, s32[128,2]{0,1:T(2,128)S(1)} %broadcast_select_fusion), kind=kOutput, calls=%fused_computation.21 | convolution fusion | flops 402685952 | bytes 3146752 | tf_op jit(solution)/shard_map/tqs,qsald->altd/dot_general | solution.py:181
  133.4 3.1 %fusion.14.bound_ref = f32[2,8,128,384]{3,2,1,0:T(8,128)} fusion(f32[2,8,128,128]{2,3,0,1:T(8,128)S(1)} %fusion.9, f32[128]{0:T(128)S(1)} %iota_convert_fusion, f32[384]{0:T(512)S(1)} %add_clamp_fusion), kind=kOutput, calls=%fused_computation.25 | convolution fusion | flops 604176384 | bytes 4196352 | tf_op jit(solution)/shard_map/altd,de->alte/dot_general | solution.py:188
  136.6 0.8 broadcast_in_dim.66.divisor_ref
  137.4 6.0 %shard_map.104 = (f32[8,128,384]{2,1,0:T(8,128)}, f32[8,384]{1,0:T(8,128)}, f32[8,384]{1,0:T(8,128)}, f32[128,8]{1,0:T(8,128)}, f32[128,8]{1,0:T(8,128)}) custom-call(f32[2,8]{1,0:T(2,128)} %wind_ref.5, f32[8,128,384]{2,1,0:T(8,128)} %bitcast.15.child_ref, f32[8,384]{1,0:T(8,128)} %copy-done.13, f32[8,384]{1,0:T(8,128)} %copy-done.14, f32[128,8]{1,0:T(8,128)} %copy-done.5, ...), custom_call_target="tpu_custom_call" | custom-call | flops 11796480 | bytes 6684672 | tf_op jit(solution)/shard_map/pallas_call | solution.py:90
  143.4 2.5 %collective-permute-start.8 = (f32[8,384]{1,0:T(8,128)}, f32[8,384]{1,0:T(8,128)S(1)}, u32[]{:S(2)}, u32[]{:S(2)}) collective-permute-start(f32[8,384]{1,0:T(8,128)} %get-tuple-element.15), channel_id=1, source_target_pairs={{0,8},{8,16},{16,24},{24,32},{32,40},{40,48},{48,56},{56,64},{64,7... | collective-permute-start | bytes 36872 | tf_op jit(solution)/shard_map/ppermute | solution.py:112
  145.8 4.9 %collective-permute-start.9 = (f32[8,384]{1,0:T(8,128)}, f32[8,384]{1,0:T(8,128)S(1)}, u32[]{:S(2)}, u32[]{:S(2)}) collective-permute-start(f32[8,384]{1,0:T(8,128)} %get-tuple-element.16), channel_id=1, source_target_pairs={{8,0},{16,8},{24,16},{32,24},{40,32},{48,40},{56,48},{64,56},{72,6... | collective-permute-start | bytes 36872 | tf_op jit(solution)/shard_map/ppermute | solution.py:112
  150.7 2.3 %collective-permute-start.10 = (f32[128,8]{1,0:T(8,128)}, f32[128,8]{1,0:T(8,128)S(1)}, u32[]{:S(2)}, u32[]{:S(2)}) collective-permute-start(f32[128,8]{1,0:T(8,128)} %get-tuple-element.17), channel_id=1, source_target_pairs={{0,1},{1,2},{2,3},{3,4},{4,5},{5,6},{6,7},{8,9},{9,10},{10,11},{11... | collective-permute-start | bytes 12296 | tf_op jit(solution)/shard_map/ppermute | solution.py:112
  153.1 2.9 %collective-permute-start.11 = (f32[128,8]{1,0:T(8,128)}, f32[128,8]{1,0:T(8,128)S(1)}, u32[]{:S(2)}, u32[]{:S(2)}) collective-permute-start(f32[128,8]{1,0:T(8,128)} %get-tuple-element.18), channel_id=1, source_target_pairs={{1,0},{2,1},{3,2},{4,3},{5,4},{6,5},{7,6},{9,8},{10,9},{11,10},{12... | collective-permute-start | bytes 12296 | tf_op jit(solution)/shard_map/ppermute | solution.py:112
  156.1 2.8 %collective-permute-done.11.ay_ref = f32[128,8]{1,0:T(8,128)S(1)} collective-permute-done((f32[128,8]{1,0:T(8,128)}, f32[128,8]{1,0:T(8,128)S(1)}, u32[]{:S(2)}, u32[]{:S(2)}) %collective-permute-start.11) | collective-permute-done | bytes 4128 | tf_op jit(solution)/shard_map/ppermute | solution.py:112
  158.9 0.6 copy-done.10
  159.5 6.0 %shard_map.105 = (f32[8,128,384]{2,1,0:T(8,128)}, f32[8,384]{1,0:T(8,128)}, f32[8,384]{1,0:T(8,128)}, f32[128,8]{1,0:T(8,128)}, f32[128,8]{1,0:T(8,128)}) custom-call(f32[2,8]{1,0:T(2,128)} %wind_ref.5, f32[8,128,384]{2,1,0:T(8,128)} %get-tuple-element.14.child_ref, f32[8,384]{1,0:T(8,128)} %copy-done.16, f32[8,384]{1,0:T(8,128)} %copy-done.18, ...), custom_call_target="tpu_custom_call" | custom-call | flops 11796480 | bytes 6684672 | tf_op jit(solution)/shard_map/pallas_call | solution.py:90
  165.5 1.9 %collective-permute-start.12 = (f32[8,384]{1,0:T(8,128)}, f32[8,384]{1,0:T(8,128)S(1)}, u32[]{:S(2)}, u32[]{:S(2)}) collective-permute-start(f32[8,384]{1,0:T(8,128)} %get-tuple-element.20), channel_id=1, source_target_pairs={{0,8},{8,16},{16,24},{24,32},{32,40},{40,48},{48,56},{56,64},{64,7... | collective-permute-start | bytes 36872 | tf_op jit(solution)/shard_map/ppermute | solution.py:112
  167.5 5.5 %collective-permute-start.13 = (f32[8,384]{1,0:T(8,128)}, f32[8,384]{1,0:T(8,128)S(1)}, u32[]{:S(2)}, u32[]{:S(2)}) collective-permute-start(f32[8,384]{1,0:T(8,128)} %get-tuple-element.21), channel_id=1, source_target_pairs={{8,0},{16,8},{24,16},{32,24},{40,32},{48,40},{56,48},{64,56},{72,6... | collective-permute-start | bytes 36872 | tf_op jit(solution)/shard_map/ppermute | solution.py:112
  172.9 2.5 %collective-permute-start.14 = (f32[128,8]{1,0:T(8,128)}, f32[128,8]{1,0:T(8,128)S(1)}, u32[]{:S(2)}, u32[]{:S(2)}) collective-permute-start(f32[128,8]{1,0:T(8,128)} %get-tuple-element.22), channel_id=1, source_target_pairs={{0,1},{1,2},{2,3},{3,4},{4,5},{5,6},{6,7},{8,9},{9,10},{10,11},{11... | collective-permute-start | bytes 12296 | tf_op jit(solution)/shard_map/ppermute | solution.py:112
  175.5 1.9 %collective-permute-start.15 = (f32[128,8]{1,0:T(8,128)}, f32[128,8]{1,0:T(8,128)S(1)}, u32[]{:S(2)}, u32[]{:S(2)}) collective-permute-start(f32[128,8]{1,0:T(8,128)} %get-tuple-element.23), channel_id=1, source_target_pairs={{1,0},{2,1},{3,2},{4,3},{5,4},{6,5},{7,6},{9,8},{10,9},{11,10},{12... | collective-permute-start | bytes 12296 | tf_op jit(solution)/shard_map/ppermute | solution.py:112
  177.4 3.8 %collective-permute-done.15.ay_ref = f32[128,8]{1,0:T(8,128)S(1)} collective-permute-done((f32[128,8]{1,0:T(8,128)}, f32[128,8]{1,0:T(8,128)S(1)}, u32[]{:S(2)}, u32[]{:S(2)}) %collective-permute-start.15) | collective-permute-done | bytes 4128 | tf_op jit(solution)/shard_map/ppermute | solution.py:112
  181.3 0.6 copy-done.9
  181.9 6.0 %shard_map.106 = (f32[8,128,384]{2,1,0:T(8,128)}, f32[8,384]{1,0:T(8,128)}, f32[8,384]{1,0:T(8,128)}, f32[128,8]{1,0:T(8,128)}, f32[128,8]{1,0:T(8,128)}) custom-call(f32[2,8]{1,0:T(2,128)} %wind_ref.5, f32[8,128,384]{2,1,0:T(8,128)} %get-tuple-element.19.child_ref, f32[8,384]{1,0:T(8,128)} %copy-done.15, f32[8,384]{1,0:T(8,128)} %copy-done.17, ...), custom_call_target="tpu_custom_call" | custom-call | flops 11796480 | bytes 6684672 | tf_op jit(solution)/shard_map/pallas_call | solution.py:90
  (83 shorter events, 1.2 us)
Async XLA Ops:
  0.6 7.8 %copy-start = (f32[8,128,512]{2,1,0:T(8,128)S(1)}, f32[8,128,512]{2,1,0:T(8,128)}, u32[]{:S(2)}) copy-start(f32[8,128,512]{2,1,0:T(8,128)} %param.11) | copy-start | bytes 6291460
  2.2 23.0 %copy-start.4 = (s32[16384,1]{0,1:T(1,128)S(1)}, s32[16384,1]{0,1:T(1,128)}, u32[]{:S(2)}) copy-start(s32[16384,1]{0,1:T(1,128)} %param.16) | copy-start | bytes 196612
  2.2 23.7 %copy-start.22 = (s32[2,4]{1,0:T(2,128)S(1)}, s32[2,4]{1,0:T(2,128)}, u32[]{:S(2)}) copy-start(s32[2,4]{1,0:T(2,128)} %param.19) | copy-start | bytes 100
  2.4 28.0 %copy-start.12 = (f32[2,8]{1,0:T(2,128)S(1)}, f32[2,8]{1,0:T(2,128)}, u32[]{:S(2)}) copy-start(f32[2,8]{1,0:T(2,128)} %wind_ref.5) | copy-start | bytes 196
  2.4 28.6 %copy-start.2 = (bf16[128,512]{1,0:T(8,128)(2,1)S(1)}, bf16[128,512]{1,0:T(8,128)(2,1)}, u32[]{:S(2)}) copy-start(bf16[128,512]{1,0:T(8,128)(2,1)} %param.12) | copy-start | bytes 393220
  2.4 68.8 %collective-permute-start.3 = (f32[8,128]{1,0:T(8,128)S(1)}, f32[8,128]{1,0:T(8,128)S(1)}, u32[]{:S(2)}, u32[]{:S(2)}) collective-permute-start(f32[8,128]{1,0:T(8,128)S(1)} %bitcast.94), channel_id=1, source_target_pairs={{0,1},{1,2},{2,3},{3,4},{4,5},{5,6},{6,7},{8,9},{9,10},{10,11},{11... | collective-permute-start | bytes 12296 | tf_op jit(solution)/shard_map/ppermute | solution.py:25
  6.5 65.0 %collective-permute-start.2 = (f32[8,128]{1,0:T(8,128)S(1)}, f32[8,128]{1,0:T(8,128)S(1)}, u32[]{:S(2)}, u32[]{:S(2)}) collective-permute-start(f32[8,128]{1,0:T(8,128)S(1)} %bitcast.96), channel_id=1, source_target_pairs={{1,0},{2,1},{3,2},{4,3},{5,4},{6,5},{7,6},{9,8},{10,9},{11,10},{12... | collective-permute-start | bytes 12296 | tf_op jit(solution)/shard_map/ppermute | solution.py:25
  8.5 63.2 %collective-permute-start.1 = (f32[8,512]{1,0:T(8,128)S(1)}, f32[8,512]{1,0:T(8,128)S(1)}, u32[]{:S(2)}, u32[]{:S(2)}) collective-permute-start(f32[8,512]{1,0:T(8,128)S(1)} %bitcast.88), channel_id=1, source_target_pairs={{0,8},{8,16},{16,24},{24,32},{32,40},{40,48},{48,56},{56,64},{64,7... | collective-permute-start | bytes 49160 | tf_op jit(solution)/shard_map/ppermute | solution.py:25
  11.6 60.1 %collective-permute-start = (f32[8,512]{1,0:T(8,128)S(1)}, f32[8,512]{1,0:T(8,128)S(1)}, u32[]{:S(2)}, u32[]{:S(2)}) collective-permute-start(f32[8,512]{1,0:T(8,128)S(1)} %bitcast.90), channel_id=1, source_target_pairs={{8,0},{16,8},{24,16},{32,24},{40,32},{48,40},{56,48},{64,56},{72,6... | collective-permute-start | bytes 49160 | tf_op jit(solution)/shard_map/ppermute | solution.py:25
  15.9 32.3 %all-to-all-start = ((f32[128,8,384]{2,1,0:T(8,128)}), f32[128,8,384]{2,1,0:T(8,128)}, u32[]{:S(2)}, u32[]{:S(2)}) async-start(f32[128,8,384]{2,1,0:T(8,128)} %bitcast.81), calls=%async_computation | async-start | bytes 3145728 | tf_op jit(solution)/shard_map/all_to_all | solution.py:51
  51.4 35.1 %all-to-all-start.1 = ((f32[128,8,384]{2,1,0:T(8,128)}), f32[128,8,384]{2,1,0:T(8,128)}, u32[]{:S(2)}, u32[]{:S(2)}) async-start(f32[128,8,384]{2,1,0:T(8,128)} %bitcast.80), calls=%async_computation.1 | async-start | bytes 3145728 | tf_op jit(solution)/shard_map/all_to_all | solution.py:56
  80.5 4.8 %copy-start.1 = (f32[128,8,128]{2,1,0:T(8,128)S(1)}, f32[128,8,128]{2,1,0:T(8,128)}, u32[]{:S(2)}) copy-start(f32[128,8,128]{2,1,0:T(8,128)} %gather_fusion) | copy-start | bytes 1572868
  80.5 4.8 %copy-start.19 = (pred[128]{0:T(512)(128)(4,1)S(1)}, pred[128]{0:T(512)(128)(4,1)}, u32[]{:S(2)}) copy-start(pred[128]{0:T(512)(128)(4,1)} %get-tuple-element.27) | copy-start | bytes 388
  83.0 5.2 %copy-start.20 = (s32[128]{0:T(128)S(1)}, s32[128]{0:T(128)}, u32[]{:S(2)}) copy-start(s32[128]{0:T(128)} %fusion.38) | copy-start | bytes 1540
  83.1 5.2 %copy-start.21 = (s32[128,2]{0,1:T(2,128)S(1)}, s32[128,2]{0,1:T(2,128)}, u32[]{:S(2)}) copy-start(s32[128,2]{0,1:T(2,128)} %multiply_add_fusion) | copy-start | bytes 3076
  92.7 10.3 %copy-start.11 = (s32[16384]{0:T(1024)S(1)}, s32[16384]{0:T(1024)}, u32[]{:S(2)}) copy-start(s32[16384]{0:T(1024)} %param.18) | copy-start | bytes 196612
  92.7 10.8 %copy-start.3 = (bf16[128,384]{1,0:T(8,128)(2,1)S(1)}, bf16[128,384]{1,0:T(8,128)(2,1)}, u32[]{:S(2)}) copy-start(bf16[128,384]{1,0:T(8,128)(2,1)} %param.14) | copy-start | bytes 294916
  92.7 38.7 %all-to-all-start.2 = ((f32[128,2,2,8,128]{4,3,2,1,0:T(8,128)}), f32[128,2,2,8,128]{4,3,2,1,0:T(8,128)S(1)}, u32[]{:S(2)}, u32[]{:S(2)}) async-start(f32[128,2,2,8,128]{4,3,2,1,0:T(8,128)} %copy.93), calls=%async_computation.2 | async-start | bytes 4194304 | tf_op jit(solution)/shard_map/all_to_all | solution.py:171
  105.2 31.4 %collective-permute-start.4 = (f32[8,384]{1,0:T(8,128)S(1)}, f32[8,384]{1,0:T(8,128)S(1)}, u32[]{:S(2)}, u32[]{:S(2)}) collective-permute-start(f32[8,384]{1,0:T(8,128)S(1)} %bitcast.92), channel_id=1, source_target_pairs={{0,8},{8,16},{16,24},{24,32},{32,40},{40,48},{48,56},{56,64},{64,7... | collective-permute-start | bytes 36872 | tf_op jit(solution)/shard_map/ppermute | solution.py:112
  108.3 28.3 %collective-permute-start.5 = (f32[8,384]{1,0:T(8,128)S(1)}, f32[8,384]{1,0:T(8,128)S(1)}, u32[]{:S(2)}, u32[]{:S(2)}) collective-permute-start(f32[8,384]{1,0:T(8,128)S(1)} %bitcast.93), channel_id=1, source_target_pairs={{8,0},{16,8},{24,16},{32,24},{40,32},{48,40},{56,48},{64,56},{72,6... | collective-permute-start | bytes 36872 | tf_op jit(solution)/shard_map/ppermute | solution.py:112
  114.9 21.7 %collective-permute-start.6 = (f32[128,8]{1,0:T(8,128)S(1)}, f32[128,8]{1,0:T(8,128)S(1)}, u32[]{:S(2)}, u32[]{:S(2)}) collective-permute-start(f32[128,8]{1,0:T(8,128)S(1)} %bitcast.85), channel_id=1, source_target_pairs={{0,1},{1,2},{2,3},{3,4},{4,5},{5,6},{6,7},{8,9},{9,10},{10,11},{11... | collective-permute-start | bytes 12296 | tf_op jit(solution)/shard_map/ppermute | solution.py:112
  119.7 16.9 %collective-permute-start.7 = (f32[128,8]{1,0:T(8,128)S(1)}, f32[128,8]{1,0:T(8,128)S(1)}, u32[]{:S(2)}, u32[]{:S(2)}) collective-permute-start(f32[128,8]{1,0:T(8,128)S(1)} %bitcast.86), channel_id=1, source_target_pairs={{1,0},{2,1},{3,2},{4,3},{5,4},{6,5},{7,6},{9,8},{10,9},{11,10},{12... | collective-permute-start | bytes 12296 | tf_op jit(solution)/shard_map/ppermute | solution.py:112
  136.5 0.8 copy-start.5
  136.6 0.8 copy-start.6
  136.6 0.8 copy-start.13
  136.6 0.8 copy-start.14
  143.4 15.5 %collective-permute-start.8 = (f32[8,384]{1,0:T(8,128)}, f32[8,384]{1,0:T(8,128)S(1)}, u32[]{:S(2)}, u32[]{:S(2)}) collective-permute-start(f32[8,384]{1,0:T(8,128)} %get-tuple-element.15), channel_id=1, source_target_pairs={{0,8},{8,16},{16,24},{24,32},{32,40},{40,48},{48,56},{56,64},{64,7... | collective-permute-start | bytes 36872 | tf_op jit(solution)/shard_map/ppermute | solution.py:112
  145.8 13.1 %collective-permute-start.9 = (f32[8,384]{1,0:T(8,128)}, f32[8,384]{1,0:T(8,128)S(1)}, u32[]{:S(2)}, u32[]{:S(2)}) collective-permute-start(f32[8,384]{1,0:T(8,128)} %get-tuple-element.16), channel_id=1, source_target_pairs={{8,0},{16,8},{24,16},{32,24},{40,32},{48,40},{56,48},{64,56},{72,6... | collective-permute-start | bytes 36872 | tf_op jit(solution)/shard_map/ppermute | solution.py:112
  150.7 5.3 %collective-permute-start.10 = (f32[128,8]{1,0:T(8,128)}, f32[128,8]{1,0:T(8,128)S(1)}, u32[]{:S(2)}, u32[]{:S(2)}) collective-permute-start(f32[128,8]{1,0:T(8,128)} %get-tuple-element.17), channel_id=1, source_target_pairs={{0,1},{1,2},{2,3},{3,4},{4,5},{5,6},{6,7},{8,9},{9,10},{10,11},{11... | collective-permute-start | bytes 12296 | tf_op jit(solution)/shard_map/ppermute | solution.py:112
  153.1 5.8 %collective-permute-start.11 = (f32[128,8]{1,0:T(8,128)}, f32[128,8]{1,0:T(8,128)S(1)}, u32[]{:S(2)}, u32[]{:S(2)}) collective-permute-start(f32[128,8]{1,0:T(8,128)} %get-tuple-element.18), channel_id=1, source_target_pairs={{1,0},{2,1},{3,2},{4,3},{5,4},{6,5},{7,6},{9,8},{10,9},{11,10},{12... | collective-permute-start | bytes 12296 | tf_op jit(solution)/shard_map/ppermute | solution.py:112
  156.1 2.9 %copy-start.8 = (f32[128,8]{1,0:T(8,128)}, f32[128,8]{1,0:T(8,128)S(1)}, u32[]{:S(2)}) copy-start(f32[128,8]{1,0:T(8,128)S(1)} %collective-permute-done.10.by_ref) | copy-start | bytes 12292
  158.9 0.6 copy-start.10
  158.9 0.6 copy-start.16
  158.9 0.6 copy-start.18
  165.5 15.7 %collective-permute-start.12 = (f32[8,384]{1,0:T(8,128)}, f32[8,384]{1,0:T(8,128)S(1)}, u32[]{:S(2)}, u32[]{:S(2)}) collective-permute-start(f32[8,384]{1,0:T(8,128)} %get-tuple-element.20), channel_id=1, source_target_pairs={{0,8},{8,16},{16,24},{24,32},{32,40},{40,48},{48,56},{56,64},{64,7... | collective-permute-start | bytes 36872 | tf_op jit(solution)/shard_map/ppermute | solution.py:112
  167.5 13.8 %collective-permute-start.13 = (f32[8,384]{1,0:T(8,128)}, f32[8,384]{1,0:T(8,128)S(1)}, u32[]{:S(2)}, u32[]{:S(2)}) collective-permute-start(f32[8,384]{1,0:T(8,128)} %get-tuple-element.21), channel_id=1, source_target_pairs={{8,0},{16,8},{24,16},{32,24},{40,32},{48,40},{56,48},{64,56},{72,6... | collective-permute-start | bytes 36872 | tf_op jit(solution)/shard_map/ppermute | solution.py:112
  172.9 4.5 %collective-permute-start.14 = (f32[128,8]{1,0:T(8,128)}, f32[128,8]{1,0:T(8,128)S(1)}, u32[]{:S(2)}, u32[]{:S(2)}) collective-permute-start(f32[128,8]{1,0:T(8,128)} %get-tuple-element.22), channel_id=1, source_target_pairs={{0,1},{1,2},{2,3},{3,4},{4,5},{5,6},{6,7},{8,9},{9,10},{10,11},{11... | collective-permute-start | bytes 12296 | tf_op jit(solution)/shard_map/ppermute | solution.py:112
  175.5 5.8 %collective-permute-start.15 = (f32[128,8]{1,0:T(8,128)}, f32[128,8]{1,0:T(8,128)S(1)}, u32[]{:S(2)}, u32[]{:S(2)}) collective-permute-start(f32[128,8]{1,0:T(8,128)} %get-tuple-element.23), channel_id=1, source_target_pairs={{1,0},{2,1},{3,2},{4,3},{5,4},{6,5},{7,6},{9,8},{10,9},{11,10},{12... | collective-permute-start | bytes 12296 | tf_op jit(solution)/shard_map/ppermute | solution.py:112
  177.4 3.9 %copy-start.7 = (f32[128,8]{1,0:T(8,128)}, f32[128,8]{1,0:T(8,128)S(1)}, u32[]{:S(2)}) copy-start(f32[128,8]{1,0:T(8,128)S(1)} %collective-permute-done.14.by_ref) | copy-start | bytes 12292
  181.3 0.6 copy-start.9
  181.3 0.6 copy-start.15
  181.3 0.6 copy-start.17
